TPU v7x, 32 devices: a whole 2x2x4 slice. The times are simulated.
32 devices in a mesh: groups: 2 (over y), seq: 4 (over z), chan: 2 (over x), rep: 2 (over core).
Axes of the slice: x: 2, y: 2, z: 4, core: 2. Of those that a mesh axis runs over, the one named last changes fastest.
Arguments:
- query_proj: bfloat16 [2048, 8192], P(('groups', 'seq'), ('chan', 'rep')), parts along dimension 0, may hold values from -6 to 6
- key_proj: bfloat16 [2048, 8192], P(('groups', 'seq'), ('chan', 'rep')), parts along dimension 0, may hold values from -6 to 6
- value_proj: bfloat16 [2048, 8192], P(('groups', 'seq'), ('chan', 'rep')), parts along dimension 0, may hold values from -6 to 6
- short_taps: bfloat16 [7, 8192], P(None, ('chan', 'rep')), may hold values from -2 to 2
- medium_taps: bfloat16 [128, 512], P(None, ('chan', 'rep')), may hold values from -0.5 to 0.5
- modal_poles: float32 [4, 512, 16], P(None, ('chan', 'rep')), may hold values from -3.1416 to 3.1416, as said below
- skip_gain: float32 [8192], P(('chan', 'rep')), may hold values from 0.5 to 1.5
- norm_gain: float32 [8192], P(('chan', 'rep')), may hold values from 0.5 to 1.5
- unembed: bfloat16 [8192, 512], P(('chan', 'rep')), may hold values from -0.1875 to 0.1875
- token_ids: int32 [2048], P(('groups', 'seq')), parts along dimension 0, may hold values from 0 to 511
- genome_lengths: int32 [16], P('groups'), parts along dimension 0, may hold values from 1 to 512, 1024 in all
Outputs:
- token_logprob: float32 [2048], P(('groups', 'seq')), parts along dimension 0
- genome_score: float32 [16], P('groups'), parts along dimension 0
There are 2 independent parts, one for each index of `groups`. A program takes and returns all parts, laid end to end along the dimension named above; an argument that names none is the same for every part. Nothing has to cross between parts.
Inputs may be any that keep to these rules, and one draw needn't show every extreme that they name: `genome_lengths`: the 8 genomes are packed end to end from position 0; their lengths sum to 1024. `modal_poles`: row 0 holds positive decay rates, row 1 angles, rows 2 and 3 residues.
All inputs are finite; a program needn't handle non-finite values.
Results may differ from a plain program's by a relative error of at most 0.0033.
Values may be sent and summed in bfloat16 or wider, within the bound.
No kernel may reach another device: no remote copies, remote signals or barrier semaphores. Data moves between devices by JAX's collectives and lax.ppermute only.
A program may use at most 128 MiB of HBM per device.

v0:
```python
import jax
import jax.numpy as jnp
from jax import lax
from jax.sharding import PartitionSpec as P

D = 8192
GROUP = 16


tile_rows = 128
short_margin = 8
norm_eps = 1e-05


def from_behind(shard, axis, by):
    count = lax.axis_size(axis)
    pairs = [(i, i + by) for i in range(count) if 0 <= i + by < count]
    return lax.ppermute(shard, axis, pairs)


def entering_2(part, axis, combine, identity):
    place = lax.axis_index(axis)
    lead = part[0].shape[0]
    flat = jnp.concatenate([a.reshape(lead, -1) for a in part], axis=1)
    gathered_flat = lax.all_gather(flat, axis)
    gathered = []
    offset = 0
    for a in part:
        width = a.size // lead
        gathered.append(gathered_flat[:, :, offset : offset + width].reshape((-1,) + a.shape))
        offset += width
    gathered = tuple(gathered)
    state = jax.tree.map(lambda a, e: jnp.zeros_like(a) + jnp.asarray(e, a.dtype), part, identity)

    def one(step, state):
        return combine(
            state, jax.tree.map(lambda a: lax.dynamic_index_in_dim(a, step, 0, False), gathered)
        )

    return lax.fori_loop(0, place, one, state)


def segment_ids(positions, genome_lengths):
    starts = jnp.cumsum(genome_lengths) - genome_lengths
    at_or_past = (positions[:, None] >= starts[None, :]).astype(jnp.int32)
    return jnp.sum(at_or_past, axis=1) - 1


def short_filter(keys_in, values_in, seg_list, out_rows, short_taps):
    gated = keys_in.astype(jnp.float32) * values_in.astype(jnp.float32)
    total_rows = keys_in.shape[0]
    lead_rows = total_rows - out_rows
    own_segs = seg_list[lead_rows:]
    result = jnp.zeros((out_rows, keys_in.shape[1]), jnp.float32)
    for lag_index in range(short_taps.shape[0]):
        shifted = gated[lead_rows - lag_index : total_rows - lag_index]
        same_genome = (seg_list[lead_rows - lag_index : total_rows - lag_index] == own_segs).astype(
            jnp.float32
        )
        result = (
            result
            + short_taps[lag_index].astype(jnp.float32)[None, :] * shifted * same_genome[:, None]
        )
    return result.astype(jnp.bfloat16)


def lag_select(table, rows, cols, shift):
    lag_count = table.shape[0]
    lag_ids = lax.optimization_barrier(jnp.arange(lag_count, dtype=jnp.int32))
    out_pos = jnp.arange(rows, dtype=jnp.int32)[:, None]
    in_pos = jnp.arange(cols, dtype=jnp.int32)[None, :]
    lag_grid = out_pos + shift - in_pos
    one_hot = (lag_grid[None] == lag_ids[:, None, None]).astype(table.dtype)
    picked = lax.dot_general(
        table, one_hot, (((0,), (0,)), ((), ())), preferred_element_type=jnp.float32
    )
    return picked.astype(table.dtype)


def medium_toeplitz(medium_taps):
    return lag_select(medium_taps, tile_rows, 2 * tile_rows, tile_rows)


def modal_tables(modal_poles):
    decay_rate = modal_poles[0]
    angles = modal_poles[1]
    residue_re = modal_poles[2]
    residue_im = modal_poles[3]
    powers = jnp.arange(tile_rows + 1).astype(jnp.float32)[:, None, None]
    magnitude = jnp.exp(-powers * decay_rate[None])
    power_re = magnitude * jnp.cos(powers * angles[None])
    power_im = magnitude * jnp.sin(powers * angles[None])
    kernel_re = residue_re[None] * power_re - residue_im[None] * power_im
    kernel_im = residue_re[None] * power_im + residue_im[None] * power_re
    kernel = jnp.sum(kernel_re[:tile_rows], axis=2)
    upper, lower = split_table(kernel)
    group_count = kernel.shape[1]
    both = lag_select(jnp.concatenate((upper, lower), axis=1), tile_rows, tile_rows, 0)
    toeplitz = (both[:group_count], both[group_count:])
    outward = jnp.transpose(jnp.concatenate((kernel_re[1:], -kernel_im[1:]), axis=2), (1, 0, 2))
    inward = jnp.transpose(
        jnp.concatenate((power_re[tile_rows - 1 :: -1], power_im[tile_rows - 1 :: -1]), axis=2),
        (1, 0, 2),
    )
    return (toeplitz, outward, inward, power_re[tile_rows], power_im[tile_rows])


def split_table(table):
    upper = table.astype(jnp.bfloat16)
    lower = (table - upper.astype(jnp.float32)).astype(jnp.bfloat16)
    return (upper, lower)


def complex_link(earlier, later):
    early_are, early_aim, early_sre, early_sim = earlier
    late_are, late_aim, late_sre, late_sim = later
    lead_re = late_are[..., None, :]
    lead_im = late_aim[..., None, :]
    return (
        late_are * early_are - late_aim * early_aim,
        late_are * early_aim + late_aim * early_are,
        lead_re * early_sre - lead_im * early_sim + late_sre,
        lead_re * early_sim + lead_im * early_sre + late_sim,
    )


def log_probs(logits, targets):
    vocab_ids = jnp.arange(logits.shape[1], dtype=jnp.int32)
    picked = jnp.sum(
        jnp.where(targets[:, None] == vocab_ids[None, :], logits, jnp.zeros_like(logits)), axis=1
    )
    return picked - jnp.log(jnp.sum(jnp.exp(logits), axis=1))


def channel_logits(normed_cols, unembed):
    return lax.dot_general(
        normed_cols, unembed, (((0,), (0,)), ((), ())), preferred_element_type=jnp.float32
    )


def per_device(
    query_proj,
    key_proj,
    value_proj,
    short_taps,
    medium_taps,
    modal_poles,
    skip_gain,
    norm_gain,
    unembed,
    token_ids,
    genome_lengths,
):
    highest = lax.Precision.HIGHEST
    row_count, chan_count = query_proj.shape
    group_count = chan_count // GROUP
    mode_count = modal_poles.shape[2]
    tile_count = row_count // tile_rows
    first_row = lax.axis_index("seq") * row_count
    segments = segment_ids(first_row + jnp.arange(row_count, dtype=jnp.int32), genome_lengths)
    edge_pair = from_behind(
        jnp.stack((key_proj[row_count - short_margin :], value_proj[row_count - short_margin :])),
        "seq",
        1,
    )
    ext_segs = segment_ids(
        first_row - short_margin + jnp.arange(row_count + short_margin, dtype=jnp.int32),
        genome_lengths,
    )
    filtered = short_filter(
        jnp.concatenate((edge_pair[0], key_proj)),
        jnp.concatenate((edge_pair[1], value_proj)),
        ext_segs,
        row_count,
        short_taps,
    )
    previous = from_behind(filtered[row_count - tile_rows :], "seq", 1)
    ext_short = jnp.concatenate((previous, filtered)).T.reshape(
        group_count, GROUP, row_count + tile_rows
    )
    medium_segs = segment_ids(
        first_row - tile_rows + jnp.arange(row_count + tile_rows, dtype=jnp.int32), genome_lengths
    )
    toeplitz = medium_toeplitz(medium_taps)

    def medium_block(tile_index):
        start = tile_index * tile_rows
        window = lax.dynamic_slice_in_dim(ext_short, start, 2 * tile_rows, 2)
        window_segs = lax.dynamic_slice_in_dim(medium_segs, start, 2 * tile_rows, 0)
        own_segs = lax.dynamic_slice_in_dim(segments, start, tile_rows, 0)
        same_genome = own_segs[:, None] == window_segs[None, :]
        matrix = jnp.where(same_genome[None], toeplitz, jnp.zeros_like(toeplitz))
        return jnp.einsum(
            "gts,gis->git", matrix, window, preferred_element_type=jnp.float32
        ).astype(jnp.bfloat16)

    signal = lax.map(medium_block, jnp.arange(tile_count, dtype=jnp.int32))
    long_toeplitz, outward, inward, decay_re, decay_im = modal_tables(modal_poles)
    toeplitz_upper, toeplitz_lower = long_toeplitz
    inward_upper, inward_lower = split_table(inward)
    tile_segs = segments.reshape(tile_count, tile_rows)
    before = segment_ids(
        first_row + jnp.arange(tile_count, dtype=jnp.int32) * tile_rows - 1, genome_lengths
    )

    def intra_block(inputs):
        block_in, own_segs = inputs
        same_genome = (own_segs[:, None] == own_segs[None, :])[None]
        upper = jnp.where(same_genome, toeplitz_upper, jnp.zeros_like(toeplitz_upper))
        lower = jnp.where(same_genome, toeplitz_lower, jnp.zeros_like(toeplitz_lower))
        return jnp.einsum(
            "gts,gis->git", upper, block_in, preferred_element_type=jnp.float32
        ) + jnp.einsum("gts,gis->git", lower, block_in, preferred_element_type=jnp.float32)

    local_part = lax.map(intra_block, (signal, tile_segs))
    end_keep = (tile_segs == tile_segs[:, -1:])[:, None, None, :]
    masked_signal = jnp.where(end_keep, signal, jnp.zeros_like(signal))
    states = jnp.einsum(
        "gsm,jgis->jgim", inward_upper, masked_signal, preferred_element_type=jnp.float32
    ) + jnp.einsum(
        "gsm,jgis->jgim", inward_lower, masked_signal, preferred_element_type=jnp.float32
    )
    carried = (tile_segs[:, -1] == before).astype(jnp.float32)

    def chain_link(carry_in, inputs):
        block_states, kept_flag = inputs
        step = (
            decay_re * kept_flag,
            decay_im * kept_flag,
            block_states[..., :mode_count],
            block_states[..., mode_count:],
        )
        return (complex_link(carry_in, step), carry_in)

    state_zero = jnp.zeros((group_count, GROUP, mode_count), jnp.float32)
    start_carry = (
        jnp.ones((group_count, mode_count), jnp.float32),
        jnp.zeros((group_count, mode_count), jnp.float32),
        state_zero,
        state_zero,
    )
    summary, entering = lax.scan(chain_link, start_carry, (states, carried))
    incoming = entering_2(
        (summary[0], summary[1], summary[2], summary[3]),
        "seq",
        complex_link,
        (start_carry[0], start_carry[1], start_carry[2], start_carry[3]),
    )
    incoming_re = incoming[2]
    incoming_im = incoming[3]
    reach_re = entering[0][:, :, None, :]
    reach_im = entering[1][:, :, None, :]
    full_re = entering[2] + reach_re * incoming_re - reach_im * incoming_im
    full_im = entering[3] + reach_re * incoming_im + reach_im * incoming_re
    keep_mask = (tile_segs == before[:, None]).astype(jnp.float32)
    carried_part = (
        jnp.einsum(
            "gtm,jgim->jgit",
            outward,
            jnp.concatenate((full_re, full_im), axis=3),
            precision=highest,
        )
        * keep_mask[:, None, None, :]
    )
    longconv = (
        local_part
        + carried_part
        + skip_gain.reshape(group_count, GROUP)[None, :, :, None] * signal.astype(jnp.float32)
    )
    long_cols = jnp.transpose(longconv, (1, 2, 0, 3)).reshape(chan_count, row_count)
    mixed = (query_proj.T.astype(jnp.float32) * long_cols).astype(jnp.bfloat16)
    mixed_wide = mixed.astype(jnp.float32)
    squares = lax.psum(jnp.sum(mixed_wide * mixed_wide, axis=0), ("chan", "rep"))
    normed = (mixed_wide * lax.rsqrt(squares / D + norm_eps)[None, :] * norm_gain[:, None]).astype(
        jnp.bfloat16
    )
    partial_value = channel_logits(normed, unembed)
    logits = lax.psum(partial_value, ("chan", "rep"))
    logprob = log_probs(logits, token_ids)
    genome_index = jnp.arange(genome_lengths.shape[0], dtype=jnp.int32)
    genome_part = jnp.sum(
        jnp.where(
            segments[:, None] == genome_index[None, :],
            logprob[:, None],
            jnp.zeros((row_count, genome_lengths.shape[0]), jnp.float32),
        ),
        axis=0,
    )
    totals = lax.psum(genome_part, "seq")
    return (logprob, totals / genome_lengths.astype(jnp.float32))


def solution(mesh):
    return jax.shard_map(
        per_device,
        mesh=mesh,
        in_specs=(
            P(("groups", "seq"), ("chan", "rep")),
            P(("groups", "seq"), ("chan", "rep")),
            P(("groups", "seq"), ("chan", "rep")),
            P(None, ("chan", "rep")),
            P(None, ("chan", "rep")),
            P(None, ("chan", "rep"), None),
            P(("chan", "rep")),
            P(("chan", "rep")),
            P(("chan", "rep"), None),
            P(("groups", "seq")),
            P("groups"),
        ),
        out_specs=(P(("groups", "seq")), P("groups")),
        check_vma=False,
    )
```

profile of v0, /device:TPU:0, one launch (start us, length us, event | category | flops | bytes accessed | tf_op | source)
XLA Modules:
  0.0 265.3 jit_solution(16015911143269287277)
XLA Ops:
  8.8 5.5 %collective-permute-start = (bf16[2,8,2048]{2,1,0:T(8,128)(2,1)}, bf16[2,8,2048]{2,1,0:T(8,128)(2,1)}, u32[]{:S(2)}, u32[]{:S(2)}) collective-permute-start(bf16[2,8,2048]{2,1,0:T(8,128)(2,1)} %pad_maximum_fusion.2), channel_id=1, source_target_pairs={{0,4},{4,8},{8,12},{1,5},{5,9},{9,13},{2,6},{6,10},{10,14},{3,7},{... | collective-permute-start | bytes 196616 | tf_op jit(solution)/shard_map/ppermute | solution.py:18
  16.6 9.4 %fusion.59 = (f32[129,128,16]{0,2,1:T(8,128)S(1)}, f32[129,128,16]{0,2,1:T(8,128)}, f32[129,128,16]{0,2,1:T(8,128)S(1)}) fusion(f32[128,16]{1,0:T(8,128)S(1)} %copy.88, f32[129]{0:T(256)S(1)} %iota_convert_fusion, f32[128,16]{1,0:T(8,128)S(1)} %copy.87, f32[129]{0:T(256)S(1)} %fusion.97, f32[128,16]{1,0:T(8,128)S(1)} %copy.89, f32[128,16]{1,0:T(8,128)S(1)} %copy.86), kind=kLoop, calls=%fused_computation.69 | loop fusion | flops 1849344 | bytes 3204104 | tf_op jit(solution)/shard_map/mul | solution.py:92
  33.7 9.4 %convert_bitcast_fusion = bf16[128,128,256]{0,2,1:T(8,128)(2,1)} fusion(s32[128]{0:T(128)S(1)} %iota.76, s32[128,256]{1,0:T(8,128)S(1)} %iota_subtract_fusion, bf16[128,128]{1,0:T(8,128)(2,1)} %param.23), kind=kOutput, calls=%fused_computation.52 | convolution fusion | flops 1082130432 | bytes 8552960 | tf_op jit(solution)/shard_map/dot_general | solution.py:74
  43.1 12.3 %copy.85 = bf16[128,128,256]{2,1,0:T(8,128)(2,1)} copy(bf16[128,128,256]{0,2,1:T(8,128)(2,1)} %convert_bitcast_fusion) | data formatting | bytes 16777216 | tf_op jit(solution)/shard_map/while | solution.py:197
  71.2 4.7 %copy.90 = bf16[128,128,128]{2,1,0:T(8,128)(2,1)} copy(bf16[128,128,128]{2,0,1:T(8,128)(2,1)S(1)} %get-tuple-element.485) | data formatting | bytes 8388608 | tf_op jit(solution)/shard_map/while | solution.py:215
  75.9 4.6 %copy.91 = bf16[128,128,128]{2,1,0:T(8,128)(2,1)} copy(bf16[128,128,128]{2,0,1:T(8,128)(2,1)S(1)} %get-tuple-element.484) | data formatting | bytes 8388608 | tf_op jit(solution)/shard_map/while | solution.py:215
  93.2 10.1 %collective-permute-done.1 = bf16[128,2048]{1,0:T(8,128)(2,1)S(1)} collective-permute-done((bf16[128,2048]{1,0:T(8,128)(2,1)S(1)}, bf16[128,2048]{1,0:T(8,128)(2,1)S(1)}, u32[]{:S(2)}, u32[]{:S(2)}) %collective-permute-start.1) | collective-permute-done | bytes 524320 | tf_op jit(solution)/shard_map/ppermute | solution.py:18
  107.3 15.3 %while.64 = (s32[]{:T(128)}, bf16[2,128,16,128]{3,2,1,0:T(8,128)(2,1)S(1)}, s32[2]{0:T(128)S(1)}, bf16[128,16,384]{2,1,0:T(8,128)(2,1)}, s32[256]{0:T(256)S(1)},...) while((s32[]{:T(128)}, bf16[2,128,16,128]{3,2,1,0:T(8,128)(2,1)S(1)}, ...), condition=%wide.region_5.6_spmd.clone, body=%wide.region_4.5_spmd.sunk.clone | while | flops 138706944 | bytes 10032308 | solution.py:197
  108.8 6.1 %fusion.132 = bf16[2,128,16,128]{3,2,1,0:T(8,128)(2,1)S(1)} fusion(bf16[2,128,16,128]{3,2,1,0:T(8,128)(2,1)S(1)} %get-tuple-element.874, s32[]{:T(128)} %get-tuple-element.873, bf16[128,128,256]{2,1,0:T(8,128)(2,1)} %get-tuple-element.887, pred[128,256]{1,0:T(8,128)(4,1)S(1)} %broadcast_compare_fusion.7, ...), kind=kOutput, calls=%fused_computation.6.clone.1.clone | convolution fusion | flops 138674176 | bytes 9994756 | tf_op jit(solution)/shard_map/while/body/eval_jaxpr/gts,gis->git/dot_general | solution.py:193
  116.5 6.1 %fusion.132 = bf16[2,128,16,128]{3,2,1,0:T(8,128)(2,1)S(1)} fusion(bf16[2,128,16,128]{3,2,1,0:T(8,128)(2,1)S(1)} %get-tuple-element.874, s32[]{:T(128)} %get-tuple-element.873, bf16[128,128,256]{2,1,0:T(8,128)(2,1)} %get-tuple-element.887, pred[128,256]{1,0:T(8,128)(4,1)S(1)} %broadcast_compare_fusion.7, ...), kind=kOutput, calls=%fused_computation.6.clone.1.clone | convolution fusion | flops 138674176 | bytes 9994756 | tf_op jit(solution)/shard_map/while/body/eval_jaxpr/gts,gis->git/dot_general | solution.py:193
  127.0 3.5 %copy.96 = f32[2,128,16,32]{1,3,2,0:T(8,128)} copy(f32[2,128,16,32]{3,2,0,1:T(8,128)} %add_bitcast_fusion) | data formatting | bytes 1048576
  130.5 7.3 %while.67 = (s32[]{:T(128)}, f32[128,16]{0,1:T(8,128)S(1)}, f32[128,16]{0,1:T(8,128)S(1)}, f32[128,16,16]{0,2,1:T(8,128)S(1)}, f32[128,16,16]{0,2,1:T(8,128)S(1)...) while((s32[]{:T(128)}, f32[128,16]{0,1:T(8,128)S(1)}, ...), condition=%wide.region_11.12_spmd.clone.clone, body=%wide.region_10.11_spmd.clone.sunk.clone | while | flops 421891 | bytes 2000031 | solution.py:242
  138.6 16.3 %while.65 = (s32[]{:T(128)}, f32[2,128,16,128]{3,2,0,1:T(8,128)}, bf16[2,128,16,128]{3,2,1,0:T(8,128)(2,1)S(1)}, s32[2,128]{1,0:T(2,128)S(1)}, bf16[128,128,128]{2,1,0:T(8,128)(2,1)}, /*index=5*/bf16[128,128,128]{2,1,0:T(8,128)(2,1)}) while((s32[]{:T(128)}, f32[2,128,16,128]{3,2,0,1:T(8,128)}, ...), condition=%wide.region_8.9_spmd.clone, body=%wide.region_7.8_spmd.sunk.clone | while | flops 138690560 | bytes 29411944 | solution.py:215
  138.7 4.6 %fusion.138 = f32[128,16,128]{2,1,0:T(8,128)S(1)} fusion(bf16[128,128,128]{2,1,0:T(8,128)(2,1)} %get-tuple-element.906, pred[128,128]{1,0:T(8,128)(4,1)S(1)} %broadcast_compare_fusion.8, bf16[2,128,16,128]{3,2,1,0:T(8,128)(2,1)S(1)} %get-tuple-element.903, s32[]{:T(128)} %get-tuple-element.895), kind=kOutput, calls=%fused_computation.11.clone.1.clone | convolution fusion | flops 69206016 | bytes 5783556 | tf_op jit(solution)/shard_map/while/body/eval_jaxpr/gts,gis->git/dot_general | solution.py:213
  143.4 3.4 %fusion.139 = f32[2,128,16,128]{3,2,0,1:T(8,128)} fusion(f32[2,128,16,128]{3,2,0,1:T(8,128)} %get-tuple-element.896, s32[]{:T(128)} %get-tuple-element.895, f32[128,16,128]{2,1,0:T(8,128)S(1)} %fusion.138, bf16[128,128,128]{2,1,0:T(8,128)(2,1)S(1)} %copy-done.4, pred[128,128]{1,0:T(8,128)(4,1)S(1)} %broadcast_compare_fusion.8, ...), kind=kOutput, calls=%fused_computation.21.clone.1.clone | convolution fusion | flops 69468160 | bytes 6833152 | tf_op jit(solution)/shard_map/while/body/eval_jaxpr/gts,gis->git/dot_general | solution.py:211
  146.9 4.7 %fusion.138 = f32[128,16,128]{2,1,0:T(8,128)S(1)} fusion(bf16[128,128,128]{2,1,0:T(8,128)(2,1)} %get-tuple-element.906, pred[128,128]{1,0:T(8,128)(4,1)S(1)} %broadcast_compare_fusion.8, bf16[2,128,16,128]{3,2,1,0:T(8,128)(2,1)S(1)} %get-tuple-element.903, s32[]{:T(128)} %get-tuple-element.895), kind=kOutput, calls=%fused_computation.11.clone.1.clone | convolution fusion | flops 69206016 | bytes 5783556 | tf_op jit(solution)/shard_map/while/body/eval_jaxpr/gts,gis->git/dot_general | solution.py:213
  151.5 3.4 %fusion.139 = f32[2,128,16,128]{3,2,0,1:T(8,128)} fusion(f32[2,128,16,128]{3,2,0,1:T(8,128)} %get-tuple-element.896, s32[]{:T(128)} %get-tuple-element.895, f32[128,16,128]{2,1,0:T(8,128)S(1)} %fusion.138, bf16[128,128,128]{2,1,0:T(8,128)(2,1)S(1)} %copy-done.4, pred[128,128]{1,0:T(8,128)(4,1)S(1)} %broadcast_compare_fusion.8, ...), kind=kOutput, calls=%fused_computation.21.clone.1.clone | convolution fusion | flops 69468160 | bytes 6833152 | tf_op jit(solution)/shard_map/while/body/eval_jaxpr/gts,gis->git/dot_general | solution.py:211
  154.9 16.0 %all-gather.3.cloned.1.call-done = f32[512,544]{0,1:T(8,128)} async-done(((f32[128,544]{0,1:T(8,128)}), f32[512,544]{0,1:T(8,128)}) %all-gather.3.cloned.1.call-update) | async-done | bytes 1114128 | tf_op jit(solution)/shard_map/all_gather | solution.py:25
  179.9 3.9 %copy.101 = f32[2,128,16,32]{3,2,0,1:T(8,128)} copy(f32[2,128,16,32]{1,3,2,0:T(8,128)} %pad_maximum_fusion) | data formatting | bytes 1048576 | tf_op jit(solution)/shard_map/concatenate | solution.py:260
  183.8 5.3 %fusion.78 = f32[128,16,2,128]{3,1,2,0:T(8,128)S(1)} fusion(f32[2,128,16,128]{3,2,0,1:T(8,128)} %get-tuple-element.216, f32[2,128,16,32]{3,2,0,1:T(8,128)} %copy.101, f32[128,128,16]{0,2,1:T(8,128)} %get-tuple-element.488, f32[128,128,16]{0,2,1:T(8,128)} %get-tuple-element.486, bf16[2,128,16,128]{3,2,1,0:T(8,128)(2,1)S(1)} %get-tuple-element.972, ...), kind=kOutput, calls=%fused_computation.99 | convolution fusion | flops 204472320 | bytes 7873536 | tf_op jit(solution)/shard_map/gtm,jgim->jgit/dot_general | solution.py:257
  191.9 6.0 %psum.21 = f32[256]{0:T(256)S(1)} all-reduce(f32[256]{0:T(256)S(1)} %fusion.55), channel_id=1, replica_groups=mesh['groups'=2,'seq'=4,'chan'=2,'rep'=2] {'chan','rep'}, use_global_device_ids=true, to_apply=%region_15.16 | all-reduce | flops 256 | bytes 2048 | tf_op jit(solution)/shard_map/psum | solution.py:273
  198.0 3.8 %fusion.85 = f32[256,512]{1,0:T(8,128)} fusion(bf16[2048,512]{1,0:T(8,128)(2,1)S(1)} %copy-done, f32[2048]{0:T(1024)S(1)} %copy-done.33, f32[256]{0:T(256)S(1)} %add_rsqrt_fusion, f32[256,8,2,128]{3,2,1,0:T(2,128)} %bitcast.200, bf16[256,2048]{0,1:T(8,128)(2,1)S(1)} %copy-done.5), kind=kOutput, calls=%fused_computation.109 | convolution fusion | flops 540540928 | bytes 5776384 | tf_op jit(solution)/shard_map/dot_general | solution.py:136
  201.9 42.9 %all-reduce.2.cloned.1.call-done = f32[256,512]{1,0:T(8,128)} async-done(((f32[256,512]{1,0:T(8,128)}), f32[256,512]{1,0:T(8,128)}) %all-reduce.2.cloned.1.call-update) | async-done | bytes 524304 | tf_op jit(solution)/shard_map/psum | solution.py:278
  246.2 11.7 %psum.23 = f32[8]{0:T(128)S(1)} all-reduce(f32[8]{0:T(128)S(1)} %select_reduce_fusion.1), channel_id=1, replica_groups=mesh['groups'=2,'seq'=4,'chan'=2,'rep'=2] {'seq'}, use_global_device_ids=true, to_apply=%region_20.21 | all-reduce | flops 8 | bytes 64 | tf_op jit(solution)/shard_map/psum | solution.py:289
  (192 shorter events, 72.0 us)
Async XLA Ops:
  7.2 190.8 %copy-start = (bf16[2048,512]{1,0:T(8,128)(2,1)S(1)}, bf16[2048,512]{1,0:T(8,128)(2,1)}, u32[]{:S(2)}) copy-start(bf16[2048,512]{1,0:T(8,128)(2,1)} %param.27) | copy-start | bytes 6291460
  7.2 163.7 %all-gather.3.cloned.1.call-start = ((), (), s32[]{:S(2)}) async-start(), calls=%async_computation.1 | async-start | bytes 1392640 | tf_op jit(solution)/shard_map/all_gather | solution.py:25
  8.8 74.8 %collective-permute-start = (bf16[2,8,2048]{2,1,0:T(8,128)(2,1)}, bf16[2,8,2048]{2,1,0:T(8,128)(2,1)}, u32[]{:S(2)}, u32[]{:S(2)}) collective-permute-start(bf16[2,8,2048]{2,1,0:T(8,128)(2,1)} %pad_maximum_fusion.2), channel_id=1, source_target_pairs={{0,4},{4,8},{8,12},{1,5},{5,9},{9,13},{2,6},{6,10},{10,14},{3,7},{... | collective-permute-start | bytes 196616 | tf_op jit(solution)/shard_map/ppermute | solution.py:18
  30.9 29.1 %copy-start.15 = (s32[8]{0:T(128)}, s32[8]{0:T(128)S(1)}, u32[]{:S(2)}) copy-start(s32[8]{0:T(128)S(1)} %bitcast_subtract_fusion) | copy-start | bytes 100
  33.0 26.9 %copy-start.28 = (s32[2,128]{1,0:T(2,128)}, s32[2,128]{1,0:T(2,128)S(1)}, u32[]{:S(2)}) copy-start(s32[2,128]{1,0:T(2,128)S(1)} %get-tuple-element.892) | copy-start | bytes 3076
  55.3 4.8 %copy-start.37 = (s32[2]{0:T(128)S(1)}, s32[2]{0:T(128)}, u32[]{:S(2)}) copy-start(s32[2]{0:T(128)} %add_add_fusion.1) | copy-start | bytes 28
  75.9 4.7 %copy-start.14 = (f32[2048]{0:T(1024)S(1)}, f32[2048]{0:T(1024)}, u32[]{:S(2)}) copy-start(f32[2048]{0:T(1024)} %param.25) | copy-start | bytes 24580
  86.5 5.9 %copy-start.16 = (s32[8]{0:T(128)S(1)}, s32[8]{0:T(128)}, u32[]{:S(2)}) copy-start(s32[8]{0:T(128)} %copy-done.15) | copy-start | bytes 100
  86.6 6.0 %copy-start.31 = (s32[2]{0:T(128)S(1)}, s32[2]{0:T(128)}, u32[]{:S(2)}) copy-start(s32[2]{0:T(128)} %copy-done.30) | copy-start | bytes 28
  86.6 6.0 %copy-start.32 = (s32[2]{0:T(128)S(1)}, s32[2]{0:T(128)}, u32[]{:S(2)}) copy-start(s32[2]{0:T(128)} %broadcast_add_fusion.3) | copy-start | bytes 28
  89.6 13.8 %collective-permute-start.1 = (bf16[128,2048]{1,0:T(8,128)(2,1)S(1)}, bf16[128,2048]{1,0:T(8,128)(2,1)S(1)}, u32[]{:S(2)}, u32[]{:S(2)}) collective-permute-start(bf16[128,2048]{1,0:T(8,128)(2,1)S(1)} %slice.197), channel_id=1, source_target_pairs={{0,4},{4,8},{8,12},{1,5},{5,9},{9,13},{2,6},{6,10},{10,14},{3,7},{... | collective-permute-start | bytes 1572872 | tf_op jit(solution)/shard_map/ppermute | solution.py:18
  127.0 3.5 %copy-start.13 = (f32[2,128,16]{1,2,0:T(8,128)S(1)}, f32[2,128,16]{1,2,0:T(8,128)}, u32[]{:S(2)}) copy-start(f32[2,128,16]{1,2,0:T(8,128)} %custom-call.5) | copy-start | bytes 49156
  127.0 3.5 %copy-start.36 = (f32[2]{0:T(128)S(1)}, f32[2]{0:T(128)}, u32[]{:S(2)}) copy-start(f32[2]{0:T(128)} %compare_convert_fusion.1) | copy-start | bytes 28
  130.5 8.1 %copy-start.29 = (s32[2,128]{1,0:T(2,128)S(1)}, s32[2,128]{1,0:T(2,128)}, u32[]{:S(2)}) copy-start(s32[2,128]{1,0:T(2,128)} %copy-done.28) | copy-start | bytes 3076
  138.6 106.3 %all-reduce.2.cloned.1.call-start = ((), (), s32[]{:S(2)}) async-start(), calls=%async_computation | async-start | bytes 1048576 | tf_op jit(solution)/shard_map/psum | solution.py:278
  138.7 4.6 %copy-start.4 = (bf16[128,128,128]{2,1,0:T(8,128)(2,1)S(1)}, bf16[128,128,128]{2,1,0:T(8,128)(2,1)}, u32[]{:S(2)}) copy-start(bf16[128,128,128]{2,1,0:T(8,128)(2,1)} %get-tuple-element.905) | copy-start | bytes 12582916 | tf_op jit(solution)/shard_map/while
  146.9 4.7 %copy-start.4 = (bf16[128,128,128]{2,1,0:T(8,128)(2,1)S(1)}, bf16[128,128,128]{2,1,0:T(8,128)(2,1)}, u32[]{:S(2)}) copy-start(bf16[128,128,128]{2,1,0:T(8,128)(2,1)} %get-tuple-element.905) | copy-start | bytes 12582916 | tf_op jit(solution)/shard_map/while
  179.0 4.8 %copy-start.6 = (f32[128,16]{1,0:T(8,128)S(1)}, f32[128,16]{1,0:T(8,128)}, u32[]{:S(2)}) copy-start(f32[128,16]{1,0:T(8,128)} %mul.500) | copy-start | bytes 24580
  179.0 4.8 %copy-start.17 = (f32[2,128]{1,0:T(2,128)S(1)}, f32[2,128]{1,0:T(2,128)}, u32[]{:S(2)}) copy-start(f32[2,128]{1,0:T(2,128)} %get-tuple-element.519) | copy-start | bytes 3076
  190.3 7.7 %copy-start.33 = (f32[2048]{0:T(1024)S(1)}, f32[2048]{0:T(1024)}, u32[]{:S(2)}) copy-start(f32[2048]{0:T(1024)} %param.26) | copy-start | bytes 24580
  198.0 46.8 %copy-start.27 = (s32[256]{0:T(256)S(1)}, s32[256]{0:T(256)}, u32[]{:S(2)}) copy-start(s32[256]{0:T(256)} %param.28) | copy-start | bytes 3076
  198.0 48.1 %copy-start.25 = (s32[256]{0:T(256)S(1)}, s32[256]{0:T(256)}, u32[]{:S(2)}) copy-start(s32[256]{0:T(256)} %get-tuple-element.869) | copy-start | bytes 3076
  198.0 59.9 %copy-start.35 = (s32[8]{0:T(128)S(1)}, s32[8]{0:T(128)}, u32[]{:S(2)}) copy-start(s32[8]{0:T(128)} %param.29) | copy-start | bytes 100
  246.1 12.3 %copy-start.26 = (f32[256]{0:T(256)}, f32[256]{0:T(256)S(1)}, u32[]{:S(2)}) copy-start(f32[256]{0:T(256)S(1)} %log_subtract_fusion) | copy-start | bytes 3076
  (19 other events, 37.7 us)
Sparse Core Ops, SparseCore 0:
  138.7 32.1 all-gather.2
  202.0 42.7 all-reduce.1
where the time goes:
time: 267 us; the launch traced here: 265 us
  waiting for transfers between devices  69.1 us (26%)
  local copies, waits for them, and re-layouts  62.8 us (24%)
  matrix products  53.6 us (20%)
  other arithmetic  37.7 us (14%)
  blocking collectives  17.7 us (7%)
  between operations  14.6 us (5%)
  starting transfers between devices  8.52 us (3%)
    psum x1, waiting for transfers between devices, per_device(): logits = lax.psum(partial_value, ('chan', 'rep'))  42.9 us
    all_gather x1, waiting for transfers between devices, entering_2(): gathered_flat = lax.all_gather(flat, axis)  16 us
    while x1, local copies, waits for them, and re-layouts, per_device(): signal = lax.map(medium_block, jnp.arange(tile_count, dtype=jnp.int32))  12.3 us
    dot_general x2, matrix products, medium_block(): jnp.einsum('gts,gis->git', matrix, window, preferred_element_type=jnp.flo...  12.2 us
    dot_general x2, matrix products, lag_select(): lax.dot_general(table, one_hot, (((0,), (0,)), ((), ())), preferred_eleme...  11.8 us
    psum x1, blocking collectives, per_device(): totals = lax.psum(genome_part, 'seq')  11.7 us
    ppermute x2, waiting for transfers between devices, from_behind(): return lax.ppermute(shard, axis, pairs)  10.1 us
    mul x1, other arithmetic, modal_tables(): power_im = magnitude * jnp.sin(powers * angles[None])  9.36 us
  transfers between devices with their start and end apart: 4, of which 3 were waited for; matrix products, arithmetic and copies ran while one was open for 32% of the time, Pallas kernels for 0%

commit v1 on v0

--- a/solution.py
+++ b/solution.py
@@ -158,26 +158,24 @@
     tile_count = row_count // tile_rows
     first_row = lax.axis_index("seq") * row_count
     segments = segment_ids(first_row + jnp.arange(row_count, dtype=jnp.int32), genome_lengths)
+    halo = tile_rows + short_margin
     edge_pair = from_behind(
-        jnp.stack((key_proj[row_count - short_margin :], value_proj[row_count - short_margin :])),
+        jnp.stack((key_proj[row_count - halo :], value_proj[row_count - halo :])),
         "seq",
         1,
     )
     ext_segs = segment_ids(
-        first_row - short_margin + jnp.arange(row_count + short_margin, dtype=jnp.int32),
+        first_row - halo + jnp.arange(row_count + halo, dtype=jnp.int32),
         genome_lengths,
     )
     filtered = short_filter(
         jnp.concatenate((edge_pair[0], key_proj)),
         jnp.concatenate((edge_pair[1], value_proj)),
         ext_segs,
-        row_count,
+        row_count + tile_rows,
         short_taps,
     )
-    previous = from_behind(filtered[row_count - tile_rows :], "seq", 1)
-    ext_short = jnp.concatenate((previous, filtered)).T.reshape(
-        group_count, GROUP, row_count + tile_rows
-    )
+    ext_short = filtered.T.reshape(group_count, GROUP, row_count + tile_rows)
     medium_segs = segment_ids(
         first_row - tile_rows + jnp.arange(row_count + tile_rows, dtype=jnp.int32), genome_lengths
     )
@@ -275,19 +273,26 @@
         jnp.bfloat16
     )
     partial_value = channel_logits(normed, unembed)
-    logits = lax.psum(partial_value, ("chan", "rep"))
-    logprob = log_probs(logits, token_ids)
+    lanes = ("chan", "rep")
+    lane_count = lax.axis_size(lanes)
+    piece = row_count // lane_count
+    piece_at = lax.axis_index(lanes) * piece
+    logits = lax.psum_scatter(partial_value, lanes, scatter_dimension=0, tiled=True)
+    logprob = log_probs(logits, lax.dynamic_slice_in_dim(token_ids, piece_at, piece, 0))
+    piece_segs = lax.dynamic_slice_in_dim(segments, piece_at, piece, 0)
     genome_index = jnp.arange(genome_lengths.shape[0], dtype=jnp.int32)
     genome_part = jnp.sum(
         jnp.where(
-            segments[:, None] == genome_index[None, :],
+            piece_segs[:, None] == genome_index[None, :],
             logprob[:, None],
-            jnp.zeros((row_count, genome_lengths.shape[0]), jnp.float32),
+            jnp.zeros((piece, genome_lengths.shape[0]), jnp.float32),
         ),
         axis=0,
     )
-    totals = lax.psum(genome_part, "seq")
-    return (logprob, totals / genome_lengths.astype(jnp.float32))
+    packed = lax.all_gather(jnp.concatenate((logprob, genome_part)), ("seq",) + lanes)
+    own = lax.dynamic_slice_in_dim(packed, lax.axis_index("seq") * lane_count, lane_count, 0)
+    totals = jnp.sum(packed[:, piece:], axis=0)
+    return (own[:, :piece].reshape(row_count), totals / genome_lengths.astype(jnp.float32))
 
 
 def solution(mesh):

time: 267 us -> 253 us (0.948)
  waiting for transfers between devices: 69.1 us -> 37.3 us
  blocking collectives: 17.7 us -> 38.7 us
    psum x1 -> x0, waiting for transfers between devices: 42.9 us -> none  [per_device(): logits = lax.psum(partial_value, ('chan', 'rep'))]
    unnamed x0 -> x1, blocking collectives: none -> 32.7 us
    reduce_scatter x0 -> x1, waiting for transfers between devices: none -> 23.1 us  [per_device(): lax.psum_scatter(partial_value, lanes, scatter_dimension=0, tiled=True)]
    psum x1 -> x0, blocking collectives: 11.7 us -> none  [per_device(): totals = lax.psum(genome_part, 'seq')]
    ppermute x2 -> x1, waiting for transfers between devices: 10.1 us -> 0.01 us  [from_behind(): return lax.ppermute(shard, axis, pairs)]
    transpose x1, other arithmetic: 1.35 us -> 5.11 us  [per_device(): ext_short = filtered.T.reshape(group_count, GROUP, row_count + tile_rows)]
    convert_element_type x1 -> x0, other arithmetic: 2.93 us -> none  [short_filter(): return result.astype(jnp.bfloat16)]
    ppermute x2 -> x1, starting transfers between devices: 8.45 us -> 5.94 us  [from_behind(): return lax.ppermute(shard, axis, pairs)]
  transfers between devices with their start and end apart: 4 -> 3, of which waited for: 3 -> 2; matrix products, arithmetic and copies ran while one was open for 32% -> 33% of each run, Pallas kernels for 0% -> 0%
where the time goes in v1:
time: 253 us; the launch traced here: 252 us
  local copies, waits for them, and re-layouts  64.4 us (25%)
  matrix products  52.7 us (21%)
  blocking collectives  38.7 us (15%)
  waiting for transfers between devices  37.3 us (15%)
  other arithmetic  36.2 us (14%)
  between operations  15.1 us (6%)
  starting transfers between devices  6.02 us (2%)
    unnamed x1, blocking collectives  32.7 us
    reduce_scatter x1, waiting for transfers between devices, per_device(): lax.psum_scatter(partial_value, lanes, scatter_dimension=0, tiled=True)  23.1 us
    all_gather x1, waiting for transfers between devices, entering_2(): gathered_flat = lax.all_gather(flat, axis)  14.2 us
    while x1, local copies, waits for them, and re-layouts, per_device(): signal = lax.map(medium_block, jnp.arange(tile_count, dtype=jnp.int32))  12.3 us
    dot_general x2, matrix products, medium_block(): jnp.einsum('gts,gis->git', matrix, window, preferred_element_type=jnp.flo...  12.2 us
    dot_general x2, matrix products, lag_select(): lax.dot_general(table, one_hot, (((0,), (0,)), ((), ())), preferred_eleme...  11 us
    mul x1, other arithmetic, modal_tables(): power_im = magnitude * jnp.sin(powers * angles[None])  9.35 us
    while x2, local copies, waits for them, and re-layouts, per_device(): local_part = lax.map(intra_block, (signal, tile_segs))  9.28 us
  transfers between devices with their start and end apart: 3, of which 2 were waited for; matrix products, arithmetic and copies ran while one was open for 33% of the time, Pallas kernels for 0%

profile of v1, /device:TPU:0, one launch (start us, length us, event | category | flops | bytes accessed | tf_op | source)
XLA Modules:
  0.0 252.1 jit_solution(71615114541046645)
XLA Ops:
  9.8 5.9 %collective-permute-start = (bf16[2,136,2048]{2,1,0:T(8,128)(2,1)}, bf16[2,136,2048]{2,1,0:T(8,128)(2,1)}, u32[]{:S(2)}, u32[]{:S(2)}) collective-permute-start(bf16[2,136,2048]{2,1,0:T(8,128)(2,1)} %pad_maximum_fusion), channel_id=1, source_target_pairs={{0,4},{4,8},{8,12},{1,5},{5,9},{9,13},{2,6},{6,10},{10,14},{3,7},{... | collective-permute-start | bytes 3342344 | tf_op jit(solution)/shard_map/ppermute | solution.py:18
  16.2 9.4 %fusion.72 = (f32[129,128,16]{0,2,1:T(8,128)S(1)}, f32[129,128,16]{0,2,1:T(8,128)}, f32[129,128,16]{0,2,1:T(8,128)S(1)}) fusion(f32[128,16]{1,0:T(8,128)S(1)} %copy.110, f32[129]{0:T(256)S(1)} %iota_convert_fusion, f32[128,16]{1,0:T(8,128)S(1)} %copy.109, f32[129]{0:T(256)S(1)} %fusion.104, f32[128,16]{1,0:T(8,128)S(1)} %copy.111, f32[128,16]{1,0:T(8,128)S(1)} %copy.108), kind=kLoop, calls=%fused_computation.89 | loop fusion | flops 1849344 | bytes 3204104 | tf_op jit(solution)/shard_map/mul | solution.py:92
  31.5 8.5 %convert_bitcast_fusion = bf16[128,128,256]{0,2,1:T(8,128)(2,1)} fusion(s32[128]{0:T(128)S(1)} %iota.76, s32[128,256]{1,0:T(8,128)S(1)} %iota_subtract_fusion, bf16[128,128]{1,0:T(8,128)(2,1)S(1)} %copy-done.9), kind=kOutput, calls=%fused_computation.52 | convolution fusion | flops 1082130432 | bytes 8552960 | tf_op jit(solution)/shard_map/dot_general | solution.py:74
  40.0 12.3 %copy.107 = bf16[128,128,256]{2,1,0:T(8,128)(2,1)} copy(bf16[128,128,256]{0,2,1:T(8,128)(2,1)} %convert_bitcast_fusion) | data formatting | bytes 16777216 | tf_op jit(solution)/shard_map/while | solution.py:195
  68.7 4.7 %copy.112 = bf16[128,128,128]{2,1,0:T(8,128)(2,1)} copy(bf16[128,128,128]{2,0,1:T(8,128)(2,1)S(1)} %get-tuple-element.519) | data formatting | bytes 8388608 | tf_op jit(solution)/shard_map/while | solution.py:213
  73.4 4.6 %copy.113 = bf16[128,128,128]{2,1,0:T(8,128)(2,1)} copy(bf16[128,128,128]{2,0,1:T(8,128)(2,1)S(1)} %get-tuple-element.518) | data formatting | bytes 8388608 | tf_op jit(solution)/shard_map/while | solution.py:213
  85.8 5.1 %fusion.80 = bf16[2048,384]{0,1:T(8,128)(2,1)} fusion(f32[384]{0:T(512)S(1)} %get-tuple-element.552, f32[392,2048]{1,0:T(8,128)S(1)} %convert_multiply_fusion, f32[2048]{0:T(1024)S(1)} %bitcast.215, f32[384]{0:T(512)S(1)} %get-tuple-element.548, f32[2048]{0:T(1024)S(1)} %bitcast.216, f32[384]{0:T(512)S(1)} %get-tuple-element.549, f32[2048]{0:T(1024)S(1)} %bitcast.211, ...), kind=kLoop, calls=%fused_computation.105 | loop fusion | flops 15728640 | bytes 23659520 | tf_op jit(solution)/shard_map/transpose | solution.py:178
  93.5 15.3 %while.64 = (s32[]{:T(128)}, bf16[2,128,16,128]{3,2,1,0:T(8,128)(2,1)S(1)}, s32[2]{0:T(128)S(1)}, bf16[128,16,384]{2,1,0:T(8,128)(2,1)}, s32[256]{0:T(256)S(1)},...) while((s32[]{:T(128)}, bf16[2,128,16,128]{3,2,1,0:T(8,128)(2,1)S(1)}, ...), condition=%wide.region_5.6_spmd.clone, body=%wide.region_4.5_spmd.sunk.clone | while | flops 138706944 | bytes 10032308 | solution.py:195
  95.0 6.1 %fusion.139 = bf16[2,128,16,128]{3,2,1,0:T(8,128)(2,1)S(1)} fusion(bf16[2,128,16,128]{3,2,1,0:T(8,128)(2,1)S(1)} %get-tuple-element.908, s32[]{:T(128)} %get-tuple-element.907, bf16[128,128,256]{2,1,0:T(8,128)(2,1)} %get-tuple-element.921, pred[128,256]{1,0:T(8,128)(4,1)S(1)} %broadcast_compare_fusion.7, ...), kind=kOutput, calls=%fused_computation.6.clone.1.clone | convolution fusion | flops 138674176 | bytes 9994756 | tf_op jit(solution)/shard_map/while/body/eval_jaxpr/gts,gis->git/dot_general | solution.py:191
  102.6 6.1 %fusion.139 = bf16[2,128,16,128]{3,2,1,0:T(8,128)(2,1)S(1)} fusion(bf16[2,128,16,128]{3,2,1,0:T(8,128)(2,1)S(1)} %get-tuple-element.908, s32[]{:T(128)} %get-tuple-element.907, bf16[128,128,256]{2,1,0:T(8,128)(2,1)} %get-tuple-element.921, pred[128,256]{1,0:T(8,128)(4,1)S(1)} %broadcast_compare_fusion.7, ...), kind=kOutput, calls=%fused_computation.6.clone.1.clone | convolution fusion | flops 138674176 | bytes 9994756 | tf_op jit(solution)/shard_map/while/body/eval_jaxpr/gts,gis->git/dot_general | solution.py:191
  113.3 3.5 %copy.118 = f32[2,128,16,32]{1,3,2,0:T(8,128)} copy(f32[2,128,16,32]{3,2,0,1:T(8,128)} %add_bitcast_fusion) | data formatting | bytes 1048576
  116.8 7.6 %while.67 = (s32[]{:T(128)}, f32[128,16]{0,1:T(8,128)S(1)}, f32[128,16]{0,1:T(8,128)S(1)}, f32[128,16,16]{0,2,1:T(8,128)S(1)}, f32[128,16,16]{0,2,1:T(8,128)S(1)...) while((s32[]{:T(128)}, f32[128,16]{0,1:T(8,128)S(1)}, ...), condition=%wide.region_11.12_spmd.clone.clone, body=%wide.region_10.11_spmd.clone.sunk.clone | while | flops 421891 | bytes 2000031 | solution.py:240
  125.2 16.3 %while.65 = (s32[]{:T(128)}, f32[2,128,16,128]{3,2,0,1:T(8,128)}, bf16[2,128,16,128]{3,2,1,0:T(8,128)(2,1)S(1)}, s32[2,128]{1,0:T(2,128)S(1)}, bf16[128,128,128]{2,1,0:T(8,128)(2,1)}, /*index=5*/bf16[128,128,128]{2,1,0:T(8,128)(2,1)}) while((s32[]{:T(128)}, f32[2,128,16,128]{3,2,0,1:T(8,128)}, ...), condition=%wide.region_8.9_spmd.clone, body=%wide.region_7.8_spmd.sunk.clone | while | flops 138690560 | bytes 29411944 | solution.py:213
  125.3 4.6 %fusion.145 = f32[128,16,128]{2,1,0:T(8,128)S(1)} fusion(bf16[128,128,128]{2,1,0:T(8,128)(2,1)} %get-tuple-element.940, pred[128,128]{1,0:T(8,128)(4,1)S(1)} %broadcast_compare_fusion.8, bf16[2,128,16,128]{3,2,1,0:T(8,128)(2,1)S(1)} %get-tuple-element.937, s32[]{:T(128)} %get-tuple-element.929), kind=kOutput, calls=%fused_computation.11.clone.1.clone | convolution fusion | flops 69206016 | bytes 5783556 | tf_op jit(solution)/shard_map/while/body/eval_jaxpr/gts,gis->git/dot_general | solution.py:211
  130.0 3.4 %fusion.146 = f32[2,128,16,128]{3,2,0,1:T(8,128)} fusion(f32[2,128,16,128]{3,2,0,1:T(8,128)} %get-tuple-element.930, s32[]{:T(128)} %get-tuple-element.929, f32[128,16,128]{2,1,0:T(8,128)S(1)} %fusion.145, bf16[128,128,128]{2,1,0:T(8,128)(2,1)S(1)} %copy-done.4, pred[128,128]{1,0:T(8,128)(4,1)S(1)} %broadcast_compare_fusion.8, ...), kind=kOutput, calls=%fused_computation.21.clone.1.clone | convolution fusion | flops 69468160 | bytes 6833152 | tf_op jit(solution)/shard_map/while/body/eval_jaxpr/gts,gis->git/dot_general | solution.py:209
  133.5 4.6 %fusion.145 = f32[128,16,128]{2,1,0:T(8,128)S(1)} fusion(bf16[128,128,128]{2,1,0:T(8,128)(2,1)} %get-tuple-element.940, pred[128,128]{1,0:T(8,128)(4,1)S(1)} %broadcast_compare_fusion.8, bf16[2,128,16,128]{3,2,1,0:T(8,128)(2,1)S(1)} %get-tuple-element.937, s32[]{:T(128)} %get-tuple-element.929), kind=kOutput, calls=%fused_computation.11.clone.1.clone | convolution fusion | flops 69206016 | bytes 5783556 | tf_op jit(solution)/shard_map/while/body/eval_jaxpr/gts,gis->git/dot_general | solution.py:211
  138.1 3.4 %fusion.146 = f32[2,128,16,128]{3,2,0,1:T(8,128)} fusion(f32[2,128,16,128]{3,2,0,1:T(8,128)} %get-tuple-element.930, s32[]{:T(128)} %get-tuple-element.929, f32[128,16,128]{2,1,0:T(8,128)S(1)} %fusion.145, bf16[128,128,128]{2,1,0:T(8,128)(2,1)S(1)} %copy-done.4, pred[128,128]{1,0:T(8,128)(4,1)S(1)} %broadcast_compare_fusion.8, ...), kind=kOutput, calls=%fused_computation.21.clone.1.clone | convolution fusion | flops 69468160 | bytes 6833152 | tf_op jit(solution)/shard_map/while/body/eval_jaxpr/gts,gis->git/dot_general | solution.py:209
  141.5 14.2 %all-gather.4.cloned.1.call-done = f32[512,544]{0,1:T(8,128)} async-done(((f32[128,544]{0,1:T(8,128)}), f32[512,544]{0,1:T(8,128)}) %all-gather.4.cloned.1.call-update) | async-done | bytes 1114128 | tf_op jit(solution)/shard_map/all_gather | solution.py:25
  163.3 3.9 %copy.123 = f32[2,128,16,32]{3,2,0,1:T(8,128)} copy(f32[2,128,16,32]{1,3,2,0:T(8,128)} %pad_maximum_fusion.1) | data formatting | bytes 1048576 | tf_op jit(solution)/shard_map/concatenate | solution.py:258
  167.2 5.3 %fusion.78 = f32[128,16,2,128]{3,1,2,0:T(8,128)S(1)} fusion(f32[2,128,16,128]{3,2,0,1:T(8,128)} %get-tuple-element.216, f32[2,128,16,32]{3,2,0,1:T(8,128)} %copy.123, f32[128,128,16]{0,2,1:T(8,128)} %get-tuple-element.522, f32[128,128,16]{0,2,1:T(8,128)} %get-tuple-element.520, bf16[2,128,16,128]{3,2,1,0:T(8,128)(2,1)S(1)} %get-tuple-element.1006, ...), kind=kOutput, calls=%fused_computation.99 | convolution fusion | flops 204472320 | bytes 7873536 | tf_op jit(solution)/shard_map/gtm,jgim->jgit/dot_general | solution.py:255
  175.3 6.0 %psum.7 = f32[256]{0:T(256)S(1)} all-reduce(f32[256]{0:T(256)S(1)} %fusion.68), channel_id=1, replica_groups=mesh['groups'=2,'seq'=4,'chan'=2,'rep'=2] {'chan','rep'}, use_global_device_ids=true, to_apply=%region_15.16 | all-reduce | flops 256 | bytes 2048 | tf_op jit(solution)/shard_map/psum | solution.py:271
  181.4 3.8 %fusion.86 = f32[256,512]{1,0:T(8,128)} fusion(bf16[2048,512]{1,0:T(8,128)(2,1)S(1)} %copy-done, f32[2048]{0:T(1024)S(1)} %copy-done.19, f32[256]{0:T(256)S(1)} %add_rsqrt_fusion, f32[256,8,2,128]{3,2,1,0:T(2,128)} %bitcast.202, bf16[256,2048]{0,1:T(8,128)(2,1)S(1)} %copy-done.5), kind=kOutput, calls=%fused_computation.110 | convolution fusion | flops 540540928 | bytes 5776384 | tf_op jit(solution)/shard_map/dot_general | solution.py:136
  186.6 23.1 %reduce-scatter.2.cloned.1.call-done = f32[64,512]{1,0:T(8,128)} async-done(((f32[256,512]{1,0:T(8,128)}), f32[64,512]{1,0:T(8,128)}) %reduce-scatter.2.cloned.1.call-update) | async-done | bytes 131088 | tf_op jit(solution)/shard_map/reduce_scatter | solution.py:280
  211.2 32.7 %all-reduce = f32[1152]{0:T(1024)S(1)} all-reduce(f32[1152]{0:T(1024)S(1)} %maximum_dynamic-update-slice_fusion), channel_id=3, replica_groups=mesh['groups'=2,'seq'=4,'chan'=2,'rep'=2] {'seq','chan','rep'}, use_global_device_ids=true, to_apply=%add | all-reduce | flops 1152 | bytes 9216
  (173 shorter events, 64.3 us)
Async XLA Ops:
  7.2 174.2 %copy-start = (bf16[2048,512]{1,0:T(8,128)(2,1)S(1)}, bf16[2048,512]{1,0:T(8,128)(2,1)}, u32[]{:S(2)}) copy-start(bf16[2048,512]{1,0:T(8,128)(2,1)} %param.27) | copy-start | bytes 6291460
  7.2 8.6 %copy-start.10 = (f32[4,128,16]{1,2,0:T(8,128)S(1)}, f32[4,128,16]{1,2,0:T(8,128)}, u32[]{:S(2)}) copy-start(f32[4,128,16]{1,2,0:T(8,128)} %param.24) | copy-start | bytes 98308
  7.2 148.5 %all-gather.4.cloned.1.call-start = ((), (), s32[]{:S(2)}) async-start(), calls=%async_computation.2 | async-start | bytes 1392640 | tf_op jit(solution)/shard_map/all_gather | solution.py:25
  9.8 74.1 %collective-permute-start = (bf16[2,136,2048]{2,1,0:T(8,128)(2,1)}, bf16[2,136,2048]{2,1,0:T(8,128)(2,1)}, u32[]{:S(2)}, u32[]{:S(2)}) collective-permute-start(bf16[2,136,2048]{2,1,0:T(8,128)(2,1)} %pad_maximum_fusion), channel_id=1, source_target_pairs={{0,4},{4,8},{8,12},{1,5},{5,9},{9,13},{2,6},{6,10},{10,14},{3,7},{... | collective-permute-start | bytes 3342344 | tf_op jit(solution)/shard_map/ppermute | solution.py:18
  31.3 25.5 %copy-start.16 = (s32[2,128]{1,0:T(2,128)}, s32[2,128]{1,0:T(2,128)S(1)}, u32[]{:S(2)}) copy-start(s32[2,128]{1,0:T(2,128)S(1)} %get-tuple-element.926) | copy-start | bytes 3076
  78.0 3.1 %copy-start.18 = (s32[2]{0:T(128)S(1)}, s32[2]{0:T(128)}, u32[]{:S(2)}) copy-start(s32[2]{0:T(128)} %slice_reduce_fusion.2) | copy-start | bytes 28
  78.0 5.8 %copy-start.8 = (bf16[7,2048]{1,0:T(8,128)(2,1)S(1)}, bf16[7,2048]{1,0:T(8,128)(2,1)}, u32[]{:S(2)}) copy-start(bf16[7,2048]{1,0:T(8,128)(2,1)} %param.22) | copy-start | bytes 86020
  81.1 4.1 %copy-start.6 = (bf16[256,2048]{1,0:T(8,128)(2,1)S(1)}, bf16[256,2048]{1,0:T(8,128)(2,1)}, u32[]{:S(2)}) copy-start(bf16[256,2048]{1,0:T(8,128)(2,1)} %param.20) | copy-start | bytes 3145732
  81.1 4.2 %copy-start.7 = (bf16[256,2048]{1,0:T(8,128)(2,1)S(1)}, bf16[256,2048]{1,0:T(8,128)(2,1)}, u32[]{:S(2)}) copy-start(bf16[256,2048]{1,0:T(8,128)(2,1)} %param.21) | copy-start | bytes 3145732
  90.9 2.6 %copy-start.14 = (s32[256]{0:T(256)S(1)}, s32[256]{0:T(256)}, u32[]{:S(2)}) copy-start(s32[256]{0:T(256)} %get-tuple-element.903) | copy-start | bytes 3076
  93.5 15.4 %copy-start.12 = (pred[2,128]{1,0:T(4,128)(4,1)S(1)}, pred[2,128]{1,0:T(4,128)(4,1)}, u32[]{:S(2)}) copy-start(pred[2,128]{1,0:T(4,128)(4,1)} %get-tuple-element.554) | copy-start | bytes 772
  113.3 3.5 %copy-start.11 = (f32[2,128,16]{1,2,0:T(8,128)S(1)}, f32[2,128,16]{1,2,0:T(8,128)}, u32[]{:S(2)}) copy-start(f32[2,128,16]{1,2,0:T(8,128)} %custom-call.5) | copy-start | bytes 49156
  113.3 3.5 %copy-start.24 = (f32[2]{0:T(128)S(1)}, f32[2]{0:T(128)}, u32[]{:S(2)}) copy-start(f32[2]{0:T(128)} %compare_convert_fusion.1) | copy-start | bytes 28
  116.8 8.4 %copy-start.17 = (s32[2,128]{1,0:T(2,128)S(1)}, s32[2,128]{1,0:T(2,128)}, u32[]{:S(2)}) copy-start(s32[2,128]{1,0:T(2,128)} %copy-done.16) | copy-start | bytes 3076
  125.2 84.6 %reduce-scatter.2.cloned.1.call-start = ((), (), s32[]{:S(2)}) async-start(), calls=%async_computation.1 | async-start | bytes 655360 | tf_op jit(solution)/shard_map/reduce_scatter | solution.py:280
  125.3 4.6 %copy-start.4 = (bf16[128,128,128]{2,1,0:T(8,128)(2,1)S(1)}, bf16[128,128,128]{2,1,0:T(8,128)(2,1)}, u32[]{:S(2)}) copy-start(bf16[128,128,128]{2,1,0:T(8,128)(2,1)} %get-tuple-element.939) | copy-start | bytes 12582916 | tf_op jit(solution)/shard_map/while
  133.4 4.6 %copy-start.4 = (bf16[128,128,128]{2,1,0:T(8,128)(2,1)S(1)}, bf16[128,128,128]{2,1,0:T(8,128)(2,1)}, u32[]{:S(2)}) copy-start(bf16[128,128,128]{2,1,0:T(8,128)(2,1)} %get-tuple-element.939) | copy-start | bytes 12582916 | tf_op jit(solution)/shard_map/while
  162.4 4.7 %copy-start.13 = (f32[2,128]{1,0:T(2,128)S(1)}, f32[2,128]{1,0:T(2,128)}, u32[]{:S(2)}) copy-start(f32[2,128]{1,0:T(2,128)} %get-tuple-element.553) | copy-start | bytes 3076
  172.5 2.4 copy-start.5
  173.6 7.7 %copy-start.19 = (f32[2048]{0:T(1024)S(1)}, f32[2048]{0:T(1024)}, u32[]{:S(2)}) copy-start(f32[2048]{0:T(1024)} %param.26) | copy-start | bytes 24580
  181.3 3.9 %copy-start.15 = (s32[256]{0:T(256)S(1)}, s32[256]{0:T(256)}, u32[]{:S(2)}) copy-start(s32[256]{0:T(256)} %get-tuple-element.903) | copy-start | bytes 3076
  181.3 4.0 %copy-start.20 = (s32[256]{0:T(256)S(1)}, s32[256]{0:T(256)}, u32[]{:S(2)}) copy-start(s32[256]{0:T(256)} %param.28) | copy-start | bytes 3076
  181.3 4.1 %copy-start.23 = (u32[32]{0:T(128)S(1)}, u32[32]{0:T(128)}, u32[]{:S(2)}) copy-start(u32[32]{0:T(128)} %constant.132) | copy-start | bytes 388
  181.4 63.4 %copy-start.22 = (s32[8]{0:T(128)S(1)}, s32[8]{0:T(128)}, u32[]{:S(2)}) copy-start(s32[8]{0:T(128)} %param.29) | copy-start | bytes 100
  (6 other events, 10.2 us)
Sparse Core Ops, SparseCore 0:
  125.3 30.3 all-gather.3
  185.4 24.3 reduce-scatter.1

commit v2 on v1

--- a/solution.py
+++ b/solution.py
@@ -278,21 +278,19 @@
     piece = row_count // lane_count
     piece_at = lax.axis_index(lanes) * piece
     logits = lax.psum_scatter(partial_value, lanes, scatter_dimension=0, tiled=True)
-    logprob = log_probs(logits, lax.dynamic_slice_in_dim(token_ids, piece_at, piece, 0))
-    piece_segs = lax.dynamic_slice_in_dim(segments, piece_at, piece, 0)
+    logprob_piece = log_probs(logits, lax.dynamic_slice_in_dim(token_ids, piece_at, piece, 0))
+    logprob = lax.all_gather(logprob_piece, lanes, tiled=True)
     genome_index = jnp.arange(genome_lengths.shape[0], dtype=jnp.int32)
     genome_part = jnp.sum(
         jnp.where(
-            piece_segs[:, None] == genome_index[None, :],
+            segments[:, None] == genome_index[None, :],
             logprob[:, None],
-            jnp.zeros((piece, genome_lengths.shape[0]), jnp.float32),
+            jnp.zeros((row_count, genome_lengths.shape[0]), jnp.float32),
         ),
         axis=0,
     )
-    packed = lax.all_gather(jnp.concatenate((logprob, genome_part)), ("seq",) + lanes)
-    own = lax.dynamic_slice_in_dim(packed, lax.axis_index("seq") * lane_count, lane_count, 0)
-    totals = jnp.sum(packed[:, piece:], axis=0)
-    return (own[:, :piece].reshape(row_count), totals / genome_lengths.astype(jnp.float32))
+    totals = lax.psum(genome_part, "seq")
+    return (logprob, totals / genome_lengths.astype(jnp.float32))
 
 
 def solution(mesh):

time: 253 us -> 237 us (0.937)
  blocking collectives: 38.7 us -> 23.6 us
    unnamed x1, blocking collectives: 32.7 us -> 5.73 us
    psum x0 -> x1, blocking collectives: none -> 11.9 us  [per_device(): totals = lax.psum(genome_part, 'seq')]
    unnamed x54 -> x56, local copies, waits for them, and re-layouts: 8.33 us -> 8.34 us
  transfers between devices with their start and end apart: 3 -> 3, of which waited for: 2 -> 2; matrix products, arithmetic and copies ran while one was open for 33% -> 36% of each run, Pallas kernels for 0% -> 0%
where the time goes in v2:
time: 237 us; the launch traced here: 236 us
  local copies, waits for them, and re-layouts  63.6 us (27%)
  matrix products  52.7 us (22%)
  waiting for transfers between devices  37.4 us (16%)
  other arithmetic  35.8 us (15%)
  blocking collectives  23.6 us (10%)
  between operations  15.1 us (6%)
  starting transfers between devices  6.02 us (3%)
    reduce_scatter x1, waiting for transfers between devices, per_device(): lax.psum_scatter(partial_value, lanes, scatter_dimension=0, tiled=True)  23.2 us
    all_gather x1, waiting for transfers between devices, entering_2(): gathered_flat = lax.all_gather(flat, axis)  14.2 us
    while x1, local copies, waits for them, and re-layouts, per_device(): signal = lax.map(medium_block, jnp.arange(tile_count, dtype=jnp.int32))  12.4 us
    dot_general x2, matrix products, medium_block(): jnp.einsum('gts,gis->git', matrix, window, preferred_element_type=jnp.flo...  12.2 us
    psum x1, blocking collectives, per_device(): totals = lax.psum(genome_part, 'seq')  11.9 us
    dot_general x2, matrix products, lag_select(): lax.dot_general(table, one_hot, (((0,), (0,)), ((), ())), preferred_eleme...  11 us
    mul x1, other arithmetic, modal_tables(): power_im = magnitude * jnp.sin(powers * angles[None])  9.36 us
    while x2, local copies, waits for them, and re-layouts, per_device(): local_part = lax.map(intra_block, (signal, tile_segs))  9.31 us
  transfers between devices with their start and end apart: 3, of which 2 were waited for; matrix products, arithmetic and copies ran while one was open for 36% of the time, Pallas kernels for 0%

profile of v2, /device:TPU:0, one launch (start us, length us, event | category | flops | bytes accessed | tf_op | source)
XLA Modules:
  0.0 235.8 jit_solution(225362090778139897)
XLA Ops:
  9.8 5.9 %collective-permute-start = (bf16[2,136,2048]{2,1,0:T(8,128)(2,1)}, bf16[2,136,2048]{2,1,0:T(8,128)(2,1)}, u32[]{:S(2)}, u32[]{:S(2)}) collective-permute-start(bf16[2,136,2048]{2,1,0:T(8,128)(2,1)} %pad_maximum_fusion), channel_id=1, source_target_pairs={{0,4},{4,8},{8,12},{1,5},{5,9},{9,13},{2,6},{6,10},{10,14},{3,7},{... | collective-permute-start | bytes 3342344 | tf_op jit(solution)/shard_map/ppermute | solution.py:18
  16.2 9.4 %fusion.72 = (f32[129,128,16]{0,2,1:T(8,128)S(1)}, f32[129,128,16]{0,2,1:T(8,128)}, f32[129,128,16]{0,2,1:T(8,128)S(1)}) fusion(f32[128,16]{1,0:T(8,128)S(1)} %copy.88, f32[129]{0:T(256)S(1)} %iota_convert_fusion, f32[128,16]{1,0:T(8,128)S(1)} %copy.87, f32[129]{0:T(256)S(1)} %fusion.104, f32[128,16]{1,0:T(8,128)S(1)} %copy.89, f32[128,16]{1,0:T(8,128)S(1)} %copy.86), kind=kLoop, calls=%fused_computation.89 | loop fusion | flops 1849344 | bytes 3204104 | tf_op jit(solution)/shard_map/mul | solution.py:92
  31.5 8.5 %convert_bitcast_fusion = bf16[128,128,256]{0,2,1:T(8,128)(2,1)} fusion(s32[128]{0:T(128)S(1)} %iota.76, s32[128,256]{1,0:T(8,128)S(1)} %iota_subtract_fusion, bf16[128,128]{1,0:T(8,128)(2,1)S(1)} %copy-done.9), kind=kOutput, calls=%fused_computation.52 | convolution fusion | flops 1082130432 | bytes 8552960 | tf_op jit(solution)/shard_map/dot_general | solution.py:74
  40.0 12.4 %copy.85 = bf16[128,128,256]{2,1,0:T(8,128)(2,1)} copy(bf16[128,128,256]{0,2,1:T(8,128)(2,1)} %convert_bitcast_fusion) | data formatting | bytes 16777216 | tf_op jit(solution)/shard_map/while | solution.py:195
  68.9 4.7 %copy.90 = bf16[128,128,128]{2,1,0:T(8,128)(2,1)} copy(bf16[128,128,128]{2,0,1:T(8,128)(2,1)S(1)} %get-tuple-element.485) | data formatting | bytes 8388608 | tf_op jit(solution)/shard_map/while | solution.py:213
  73.5 4.6 %copy.91 = bf16[128,128,128]{2,1,0:T(8,128)(2,1)} copy(bf16[128,128,128]{2,0,1:T(8,128)(2,1)S(1)} %get-tuple-element.484) | data formatting | bytes 8388608 | tf_op jit(solution)/shard_map/while | solution.py:213
  86.0 5.1 %fusion.80 = bf16[2048,384]{0,1:T(8,128)(2,1)} fusion(f32[384]{0:T(512)S(1)} %get-tuple-element.518, f32[392,2048]{1,0:T(8,128)S(1)} %convert_multiply_fusion, f32[2048]{0:T(1024)S(1)} %bitcast.214, f32[384]{0:T(512)S(1)} %get-tuple-element.514, f32[2048]{0:T(1024)S(1)} %bitcast.215, f32[384]{0:T(512)S(1)} %get-tuple-element.515, f32[2048]{0:T(1024)S(1)} %bitcast.210, ...), kind=kLoop, calls=%fused_computation.105 | loop fusion | flops 15728640 | bytes 23659520 | tf_op jit(solution)/shard_map/transpose | solution.py:178
  93.7 15.4 %while.64 = (s32[]{:T(128)}, bf16[2,128,16,128]{3,2,1,0:T(8,128)(2,1)S(1)}, s32[2]{0:T(128)S(1)}, bf16[128,16,384]{2,1,0:T(8,128)(2,1)}, s32[256]{0:T(256)S(1)},...) while((s32[]{:T(128)}, bf16[2,128,16,128]{3,2,1,0:T(8,128)(2,1)S(1)}, ...), condition=%wide.region_5.6_spmd.clone, body=%wide.region_4.5_spmd.sunk.clone | while | flops 138706944 | bytes 10032308 | solution.py:195
  95.3 6.1 %fusion.139 = bf16[2,128,16,128]{3,2,1,0:T(8,128)(2,1)S(1)} fusion(bf16[2,128,16,128]{3,2,1,0:T(8,128)(2,1)S(1)} %get-tuple-element.874, s32[]{:T(128)} %get-tuple-element.873, bf16[128,128,256]{2,1,0:T(8,128)(2,1)} %get-tuple-element.887, pred[128,256]{1,0:T(8,128)(4,1)S(1)} %broadcast_compare_fusion.7, ...), kind=kOutput, calls=%fused_computation.6.clone.1.clone | convolution fusion | flops 138674176 | bytes 9994756 | tf_op jit(solution)/shard_map/while/body/eval_jaxpr/gts,gis->git/dot_general | solution.py:191
  102.9 6.1 %fusion.139 = bf16[2,128,16,128]{3,2,1,0:T(8,128)(2,1)S(1)} fusion(bf16[2,128,16,128]{3,2,1,0:T(8,128)(2,1)S(1)} %get-tuple-element.874, s32[]{:T(128)} %get-tuple-element.873, bf16[128,128,256]{2,1,0:T(8,128)(2,1)} %get-tuple-element.887, pred[128,256]{1,0:T(8,128)(4,1)S(1)} %broadcast_compare_fusion.7, ...), kind=kOutput, calls=%fused_computation.6.clone.1.clone | convolution fusion | flops 138674176 | bytes 9994756 | tf_op jit(solution)/shard_map/while/body/eval_jaxpr/gts,gis->git/dot_general | solution.py:191
  113.6 3.5 %copy.96 = f32[2,128,16,32]{1,3,2,0:T(8,128)} copy(f32[2,128,16,32]{3,2,0,1:T(8,128)} %add_bitcast_fusion) | data formatting | bytes 1048576
  117.1 7.1 %while.67 = (s32[]{:T(128)}, f32[128,16]{0,1:T(8,128)S(1)}, f32[128,16]{0,1:T(8,128)S(1)}, f32[128,16,16]{0,2,1:T(8,128)S(1)}, f32[128,16,16]{0,2,1:T(8,128)S(1)...) while((s32[]{:T(128)}, f32[128,16]{0,1:T(8,128)S(1)}, ...), condition=%wide.region_11.12_spmd.clone.clone, body=%wide.region_10.11_spmd.clone.sunk.clone | while | flops 421891 | bytes 2000031 | solution.py:240
  125.0 16.3 %while.65 = (s32[]{:T(128)}, f32[2,128,16,128]{3,2,0,1:T(8,128)}, bf16[2,128,16,128]{3,2,1,0:T(8,128)(2,1)S(1)}, s32[2,128]{1,0:T(2,128)S(1)}, bf16[128,128,128]{2,1,0:T(8,128)(2,1)}, /*index=5*/bf16[128,128,128]{2,1,0:T(8,128)(2,1)}) while((s32[]{:T(128)}, f32[2,128,16,128]{3,2,0,1:T(8,128)}, ...), condition=%wide.region_8.9_spmd.clone, body=%wide.region_7.8_spmd.sunk.clone | while | flops 138690560 | bytes 29411944 | solution.py:213
  125.1 4.6 %fusion.145 = f32[128,16,128]{2,1,0:T(8,128)S(1)} fusion(bf16[128,128,128]{2,1,0:T(8,128)(2,1)} %get-tuple-element.906, pred[128,128]{1,0:T(8,128)(4,1)S(1)} %broadcast_compare_fusion.8, bf16[2,128,16,128]{3,2,1,0:T(8,128)(2,1)S(1)} %get-tuple-element.903, s32[]{:T(128)} %get-tuple-element.895), kind=kOutput, calls=%fused_computation.11.clone.1.clone | convolution fusion | flops 69206016 | bytes 5783556 | tf_op jit(solution)/shard_map/while/body/eval_jaxpr/gts,gis->git/dot_general | solution.py:211
  133.2 4.6 %fusion.145 = f32[128,16,128]{2,1,0:T(8,128)S(1)} fusion(bf16[128,128,128]{2,1,0:T(8,128)(2,1)} %get-tuple-element.906, pred[128,128]{1,0:T(8,128)(4,1)S(1)} %broadcast_compare_fusion.8, bf16[2,128,16,128]{3,2,1,0:T(8,128)(2,1)S(1)} %get-tuple-element.903, s32[]{:T(128)} %get-tuple-element.895), kind=kOutput, calls=%fused_computation.11.clone.1.clone | convolution fusion | flops 69206016 | bytes 5783556 | tf_op jit(solution)/shard_map/while/body/eval_jaxpr/gts,gis->git/dot_general | solution.py:211
  137.8 3.4 %fusion.146 = f32[2,128,16,128]{3,2,0,1:T(8,128)} fusion(f32[2,128,16,128]{3,2,0,1:T(8,128)} %get-tuple-element.896, s32[]{:T(128)} %get-tuple-element.895, f32[128,16,128]{2,1,0:T(8,128)S(1)} %fusion.145, bf16[128,128,128]{2,1,0:T(8,128)(2,1)S(1)} %copy-done.4, pred[128,128]{1,0:T(8,128)(4,1)S(1)} %broadcast_compare_fusion.8, ...), kind=kOutput, calls=%fused_computation.21.clone.1.clone | convolution fusion | flops 69468160 | bytes 6833152 | tf_op jit(solution)/shard_map/while/body/eval_jaxpr/gts,gis->git/dot_general | solution.py:209
  141.2 14.2 %all-gather.3.cloned.1.call-done = f32[512,544]{0,1:T(8,128)} async-done(((f32[128,544]{0,1:T(8,128)}), f32[512,544]{0,1:T(8,128)}) %all-gather.3.cloned.1.call-update) | async-done | bytes 1114128 | tf_op jit(solution)/shard_map/all_gather | solution.py:25
  163.1 3.9 %copy.101 = f32[2,128,16,32]{3,2,0,1:T(8,128)} copy(f32[2,128,16,32]{1,3,2,0:T(8,128)} %pad_maximum_fusion.1) | data formatting | bytes 1048576 | tf_op jit(solution)/shard_map/concatenate | solution.py:258
  166.9 5.3 %fusion.78 = f32[128,16,2,128]{3,1,2,0:T(8,128)S(1)} fusion(f32[2,128,16,128]{3,2,0,1:T(8,128)} %get-tuple-element.216, f32[2,128,16,32]{3,2,0,1:T(8,128)} %copy.101, f32[128,128,16]{0,2,1:T(8,128)} %get-tuple-element.488, f32[128,128,16]{0,2,1:T(8,128)} %get-tuple-element.486, bf16[2,128,16,128]{3,2,1,0:T(8,128)(2,1)S(1)} %get-tuple-element.972, ...), kind=kOutput, calls=%fused_computation.99 | convolution fusion | flops 204472320 | bytes 7873536 | tf_op jit(solution)/shard_map/gtm,jgim->jgit/dot_general | solution.py:255
  175.0 6.0 %psum.14 = f32[256]{0:T(256)S(1)} all-reduce(f32[256]{0:T(256)S(1)} %fusion.68), channel_id=1, replica_groups=mesh['groups'=2,'seq'=4,'chan'=2,'rep'=2] {'chan','rep'}, use_global_device_ids=true, to_apply=%region_15.16 | all-reduce | flops 256 | bytes 2048 | tf_op jit(solution)/shard_map/psum | solution.py:271
  181.1 3.8 %fusion.86 = f32[256,512]{1,0:T(8,128)} fusion(bf16[2048,512]{1,0:T(8,128)(2,1)S(1)} %copy-done, f32[2048]{0:T(1024)S(1)} %copy-done.20, f32[256]{0:T(256)S(1)} %add_rsqrt_fusion, f32[256,8,2,128]{3,2,1,0:T(2,128)} %bitcast.201, bf16[256,2048]{0,1:T(8,128)(2,1)S(1)} %copy-done.5), kind=kOutput, calls=%fused_computation.110 | convolution fusion | flops 540540928 | bytes 5776384 | tf_op jit(solution)/shard_map/dot_general | solution.py:136
  186.3 23.2 %reduce-scatter.2.cloned.1.call-done = f32[64,512]{1,0:T(8,128)} async-done(((f32[256,512]{1,0:T(8,128)}), f32[64,512]{1,0:T(8,128)}) %reduce-scatter.2.cloned.1.call-update) | async-done | bytes 131088 | tf_op jit(solution)/shard_map/reduce_scatter | solution.py:280
  210.7 5.7 %all-reduce = f32[256]{0:T(256)S(1)} all-reduce(f32[256]{0:T(256)S(1)} %subtract_dynamic-update-slice_fusion), channel_id=1, replica_groups=mesh['groups'=2,'seq'=4,'chan'=2,'rep'=2] {'chan','rep'}, use_global_device_ids=true, to_apply=%add | all-reduce | flops 256 | bytes 2048
  216.5 11.9 %psum.15 = f32[8]{0:T(128)S(1)} all-reduce(f32[8]{0:T(128)S(1)} %select_reduce_fusion.1), channel_id=1, replica_groups=mesh['groups'=2,'seq'=4,'chan'=2,'rep'=2] {'seq'}, use_global_device_ids=true, to_apply=%region_20.21 | all-reduce | flops 8 | bytes 64 | tf_op jit(solution)/shard_map/psum | solution.py:292
  (170 shorter events, 66.1 us)
Async XLA Ops:
  7.2 173.9 %copy-start = (bf16[2048,512]{1,0:T(8,128)(2,1)S(1)}, bf16[2048,512]{1,0:T(8,128)(2,1)}, u32[]{:S(2)}) copy-start(bf16[2048,512]{1,0:T(8,128)(2,1)} %param.27) | copy-start | bytes 6291460
  7.2 8.6 %copy-start.10 = (f32[4,128,16]{1,2,0:T(8,128)S(1)}, f32[4,128,16]{1,2,0:T(8,128)}, u32[]{:S(2)}) copy-start(f32[4,128,16]{1,2,0:T(8,128)} %param.24) | copy-start | bytes 98308
  7.2 148.2 %all-gather.3.cloned.1.call-start = ((), (), s32[]{:S(2)}) async-start(), calls=%async_computation.2 | async-start | bytes 1392640 | tf_op jit(solution)/shard_map/all_gather | solution.py:25
  9.8 74.3 %collective-permute-start = (bf16[2,136,2048]{2,1,0:T(8,128)(2,1)}, bf16[2,136,2048]{2,1,0:T(8,128)(2,1)}, u32[]{:S(2)}, u32[]{:S(2)}) collective-permute-start(bf16[2,136,2048]{2,1,0:T(8,128)(2,1)} %pad_maximum_fusion), channel_id=1, source_target_pairs={{0,4},{4,8},{8,12},{1,5},{5,9},{9,13},{2,6},{6,10},{10,14},{3,7},{... | collective-permute-start | bytes 3342344 | tf_op jit(solution)/shard_map/ppermute | solution.py:18
  31.3 25.6 %copy-start.17 = (s32[2,128]{1,0:T(2,128)}, s32[2,128]{1,0:T(2,128)S(1)}, u32[]{:S(2)}) copy-start(s32[2,128]{1,0:T(2,128)S(1)} %get-tuple-element.892) | copy-start | bytes 3076
  78.2 3.1 %copy-start.19 = (s32[2]{0:T(128)S(1)}, s32[2]{0:T(128)}, u32[]{:S(2)}) copy-start(s32[2]{0:T(128)} %slice_reduce_fusion.1) | copy-start | bytes 28
  78.2 5.8 %copy-start.8 = (bf16[7,2048]{1,0:T(8,128)(2,1)S(1)}, bf16[7,2048]{1,0:T(8,128)(2,1)}, u32[]{:S(2)}) copy-start(bf16[7,2048]{1,0:T(8,128)(2,1)} %param.22) | copy-start | bytes 86020
  81.3 4.1 %copy-start.6 = (bf16[256,2048]{1,0:T(8,128)(2,1)S(1)}, bf16[256,2048]{1,0:T(8,128)(2,1)}, u32[]{:S(2)}) copy-start(bf16[256,2048]{1,0:T(8,128)(2,1)} %param.20) | copy-start | bytes 3145732
  81.3 4.2 %copy-start.7 = (bf16[256,2048]{1,0:T(8,128)(2,1)S(1)}, bf16[256,2048]{1,0:T(8,128)(2,1)}, u32[]{:S(2)}) copy-start(bf16[256,2048]{1,0:T(8,128)(2,1)} %param.21) | copy-start | bytes 3145732
  91.1 2.6 %copy-start.14 = (s32[256]{0:T(256)S(1)}, s32[256]{0:T(256)}, u32[]{:S(2)}) copy-start(s32[256]{0:T(256)} %get-tuple-element.869) | copy-start | bytes 3076
  93.7 15.4 %copy-start.12 = (pred[2,128]{1,0:T(4,128)(4,1)S(1)}, pred[2,128]{1,0:T(4,128)(4,1)}, u32[]{:S(2)}) copy-start(pred[2,128]{1,0:T(4,128)(4,1)} %get-tuple-element.520) | copy-start | bytes 772
  113.6 3.5 %copy-start.11 = (f32[2,128,16]{1,2,0:T(8,128)S(1)}, f32[2,128,16]{1,2,0:T(8,128)}, u32[]{:S(2)}) copy-start(f32[2,128,16]{1,2,0:T(8,128)} %custom-call.5) | copy-start | bytes 49156
  113.6 3.5 %copy-start.25 = (f32[2]{0:T(128)S(1)}, f32[2]{0:T(128)}, u32[]{:S(2)}) copy-start(f32[2]{0:T(128)} %compare_convert_fusion.1) | copy-start | bytes 28
  117.1 7.9 %copy-start.18 = (s32[2,128]{1,0:T(2,128)S(1)}, s32[2,128]{1,0:T(2,128)}, u32[]{:S(2)}) copy-start(s32[2,128]{1,0:T(2,128)} %copy-done.17) | copy-start | bytes 3076
  124.9 84.6 %reduce-scatter.2.cloned.1.call-start = ((), (), s32[]{:S(2)}) async-start(), calls=%async_computation.1 | async-start | bytes 655360 | tf_op jit(solution)/shard_map/reduce_scatter | solution.py:280
  125.1 4.6 %copy-start.4 = (bf16[128,128,128]{2,1,0:T(8,128)(2,1)S(1)}, bf16[128,128,128]{2,1,0:T(8,128)(2,1)}, u32[]{:S(2)}) copy-start(bf16[128,128,128]{2,1,0:T(8,128)(2,1)} %get-tuple-element.905) | copy-start | bytes 12582916 | tf_op jit(solution)/shard_map/while
  133.2 4.6 %copy-start.4 = (bf16[128,128,128]{2,1,0:T(8,128)(2,1)S(1)}, bf16[128,128,128]{2,1,0:T(8,128)(2,1)}, u32[]{:S(2)}) copy-start(bf16[128,128,128]{2,1,0:T(8,128)(2,1)} %get-tuple-element.905) | copy-start | bytes 12582916 | tf_op jit(solution)/shard_map/while
  162.2 4.8 %copy-start.13 = (f32[2,128]{1,0:T(2,128)S(1)}, f32[2,128]{1,0:T(2,128)}, u32[]{:S(2)}) copy-start(f32[2,128]{1,0:T(2,128)} %get-tuple-element.519) | copy-start | bytes 3076
  173.4 7.7 %copy-start.20 = (f32[2048]{0:T(1024)S(1)}, f32[2048]{0:T(1024)}, u32[]{:S(2)}) copy-start(f32[2048]{0:T(1024)} %param.26) | copy-start | bytes 24580
  181.1 3.9 %copy-start.21 = (s32[256]{0:T(256)S(1)}, s32[256]{0:T(256)}, u32[]{:S(2)}) copy-start(s32[256]{0:T(256)} %param.28) | copy-start | bytes 3076
  181.1 4.0 %copy-start.24 = (u32[32]{0:T(128)S(1)}, u32[32]{0:T(128)}, u32[]{:S(2)}) copy-start(u32[32]{0:T(128)} %constant.128) | copy-start | bytes 388
  181.1 35.3 %copy-start.15 = (s32[256]{0:T(256)S(1)}, s32[256]{0:T(256)}, u32[]{:S(2)}) copy-start(s32[256]{0:T(256)} %get-tuple-element.869) | copy-start | bytes 3076
  181.1 47.3 %copy-start.23 = (s32[8]{0:T(128)S(1)}, s32[8]{0:T(128)}, u32[]{:S(2)}) copy-start(s32[8]{0:T(128)} %param.29) | copy-start | bytes 100
  216.4 12.5 %copy-start.16 = (f32[256]{0:T(256)}, f32[256]{0:T(256)S(1)}, u32[]{:S(2)}) copy-start(f32[256]{0:T(256)S(1)} %all-reduce) | copy-start | bytes 3076
  (7 other events, 12.6 us)
Sparse Core Ops, SparseCore 0:
  125.0 30.3 all-gather.2
  185.1 24.3 reduce-scatter.1

commit v3 on v2

--- a/solution.py
+++ b/solution.py
@@ -20,24 +20,32 @@
 
 def entering_2(part, axis, combine, identity):
     place = lax.axis_index(axis)
+    count = lax.axis_size(axis)
     lead = part[0].shape[0]
-    flat = jnp.concatenate([a.reshape(lead, -1) for a in part], axis=1)
-    gathered_flat = lax.all_gather(flat, axis)
-    gathered = []
-    offset = 0
-    for a in part:
-        width = a.size // lead
-        gathered.append(gathered_flat[:, :, offset : offset + width].reshape((-1,) + a.shape))
-        offset += width
-    gathered = tuple(gathered)
-    state = jax.tree.map(lambda a, e: jnp.zeros_like(a) + jnp.asarray(e, a.dtype), part, identity)
-
-    def one(step, state):
-        return combine(
-            state, jax.tree.map(lambda a: lax.dynamic_index_in_dim(a, step, 0, False), gathered)
-        )
-
-    return lax.fori_loop(0, place, one, state)
+    widths = [a.size // lead for a in part]
+
+    def pack(t):
+        return jnp.concatenate([a.reshape(lead, -1) for a in t], axis=1)
+
+    def unpack(flat):
+        pieces = []
+        offset = 0
+        for a, width in zip(part, widths):
+            pieces.append(flat[:, offset : offset + width].reshape(a.shape))
+            offset += width
+        return tuple(pieces)
+
+    ident = tuple(jnp.zeros_like(a) + jnp.asarray(e, a.dtype) for a, e in zip(part, identity))
+    before = ident
+    upto = tuple(part)
+    shift = 1
+    while shift < count:
+        arrived = unpack(from_behind(pack(upto), axis, shift))
+        arrived = tuple(jnp.where(place >= shift, r, i) for r, i in zip(arrived, ident))
+        before = combine(arrived, before)
+        upto = combine(arrived, upto)
+        shift *= 2
+    return before
 
 
 def segment_ids(positions, genome_lengths):

time: 237 us -> 229 us (0.966)
  waiting for transfers between devices: 37.4 us -> 18.6 us
  starting transfers between devices: 6.02 us -> 12.1 us
  matrix products: 52.7 us -> 56.6 us
  other arithmetic: 35.8 us -> 38.5 us
    all_gather x1 -> x0, waiting for transfers between devices: 14.2 us -> none  [entering_2(): gathered_flat = lax.all_gather(flat, axis)]
    ppermute x1 -> x3, starting transfers between devices: 5.94 us -> 12.1 us  [from_behind(): return lax.ppermute(shard, axis, pairs)]
    reduce_scatter x1, waiting for transfers between devices: 23.2 us -> 18.6 us  [per_device(): lax.psum_scatter(partial_value, lanes, scatter_dimension=0, tiled=True)]
    dot_general x2, matrix products: 11 us -> 14.9 us  [lag_select(): lax.dot_general(table, one_hot, (((0,), (0,)), ((), ())), preferred_eleme...]
    slice x2 -> x0, local copies, waits for them, and re-layouts: 3.02 us -> none  [entering_2(): gathered_flat[:, :, offset:offset + width].reshape((-1,) + a.shape)]
    slice x1, local copies, waits for them, and re-layouts: 0.84 us -> 3.82 us  [modal_tables(): toeplitz = (both[:group_count], both[group_count:])]
    all_gather x1 -> x0, local copies, waits for them, and re-layouts: 2.58 us -> none  [entering_2(): gathered_flat = lax.all_gather(flat, axis)]
    unnamed x56 -> x58, local copies, waits for them, and re-layouts: 8.34 us -> 8.1 us
  transfers between devices with their start and end apart: 3 -> 4, of which waited for: 2 -> 1; matrix products, arithmetic and copies ran while one was open for 36% -> 40% of each run, Pallas kernels for 0% -> 0%
where the time goes in v3:
time: 229 us; the launch traced here: 228 us
  local copies, waits for them, and re-layouts  61.7 us (27%)
  matrix products  56.6 us (25%)
  other arithmetic  38.5 us (17%)
  blocking collectives  23.6 us (10%)
  waiting for transfers between devices  18.6 us (8%)
  between operations  15.1 us (7%)
  starting transfers between devices  12.1 us (5%)
    reduce_scatter x1, waiting for transfers between devices, per_device(): lax.psum_scatter(partial_value, lanes, scatter_dimension=0, tiled=True)  18.6 us
    dot_general x2, matrix products, lag_select(): lax.dot_general(table, one_hot, (((0,), (0,)), ((), ())), preferred_eleme...  14.9 us
    while x1, local copies, waits for them, and re-layouts, per_device(): signal = lax.map(medium_block, jnp.arange(tile_count, dtype=jnp.int32))  12.6 us
    dot_general x2, matrix products, medium_block(): jnp.einsum('gts,gis->git', matrix, window, preferred_element_type=jnp.flo...  12.2 us
    ppermute x3, starting transfers between devices, from_behind(): return lax.ppermute(shard, axis, pairs)  12.1 us
    psum x1, blocking collectives, per_device(): totals = lax.psum(genome_part, 'seq')  11.9 us
    mul x1, other arithmetic, modal_tables(): power_im = magnitude * jnp.sin(powers * angles[None])  9.39 us
    while x2, local copies, waits for them, and re-layouts, per_device(): local_part = lax.map(intra_block, (signal, tile_segs))  9.32 us
  transfers between devices with their start and end apart: 4, of which 1 were waited for; matrix products, arithmetic and copies ran while one was open for 40% of the time, Pallas kernels for 0%

profile of v3, /device:TPU:0, one launch (start us, length us, event | category | flops | bytes accessed | tf_op | source)
XLA Modules:
  0.0 227.8 jit_solution(5506170593089953487)
XLA Ops:
  9.8 5.9 %collective-permute-start = (bf16[2,136,2048]{2,1,0:T(8,128)(2,1)}, bf16[2,136,2048]{2,1,0:T(8,128)(2,1)}, u32[]{:S(2)}, u32[]{:S(2)}) collective-permute-start(bf16[2,136,2048]{2,1,0:T(8,128)(2,1)} %pad_maximum_fusion), channel_id=1, source_target_pairs={{0,4},{4,8},{8,12},{1,5},{5,9},{9,13},{2,6},{6,10},{10,14},{3,7},{... | collective-permute-start | bytes 3342344 | tf_op jit(solution)/shard_map/ppermute | solution.py:18
  16.2 9.4 %fusion.72 = (f32[129,128,16]{0,2,1:T(8,128)S(1)}, f32[129,128,16]{0,2,1:T(8,128)}, f32[129,128,16]{0,2,1:T(8,128)S(1)}) fusion(f32[128,16]{1,0:T(8,128)S(1)} %copy.80, f32[129]{0:T(256)S(1)} %iota_convert_fusion, f32[128,16]{1,0:T(8,128)S(1)} %copy.79, f32[129]{0:T(256)S(1)} %fusion.104, f32[128,16]{1,0:T(8,128)S(1)} %copy.81, f32[128,16]{1,0:T(8,128)S(1)} %copy.78), kind=kLoop, calls=%fused_computation.83 | loop fusion | flops 1849344 | bytes 3204104 | tf_op jit(solution)/shard_map/mul | solution.py:100
  36.8 8.4 %convert_bitcast_fusion = bf16[128,128,256]{0,2,1:T(8,128)(2,1)} fusion(s32[128]{0:T(128)S(1)} %iota.76, s32[128,256]{1,0:T(8,128)S(1)} %iota_subtract_fusion, bf16[128,128]{1,0:T(8,128)(2,1)S(1)} %copy-done.12), kind=kOutput, calls=%fused_computation.46 | convolution fusion | flops 1082130432 | bytes 8552960 | tf_op jit(solution)/shard_map/dot_general | solution.py:82
  45.2 12.6 %copy.77 = bf16[128,128,256]{2,1,0:T(8,128)(2,1)} copy(bf16[128,128,256]{0,2,1:T(8,128)(2,1)} %convert_bitcast_fusion) | data formatting | bytes 16777216 | tf_op jit(solution)/shard_map/while | solution.py:203
  65.7 6.4 %fusion.48 = bf16[256,128,128]{2,0,1:T(8,128)(2,1)} fusion(s32[128,128]{1,0:T(8,128)S(1)} %iota_subtract_fusion.1, s32[128]{0:T(128)S(1)} %iota.76, bf16[128,128]{0,1:T(8,128)(2,1)S(1)} %get-tuple-element.358, bf16[128,128]{0,1:T(8,128)(2,1)} %get-tuple-element.359), kind=kOutput, calls=%fused_computation.51 | convolution fusion | flops 1080164352 | bytes 8520192 | tf_op jit(solution)/shard_map/dot_general | solution.py:82
  74.6 5.1 %fusion.80 = bf16[2048,384]{0,1:T(8,128)(2,1)} fusion(f32[384]{0:T(512)S(1)} %get-tuple-element.410, f32[392,2048]{1,0:T(8,128)S(1)} %convert_multiply_fusion, f32[2048]{0:T(1024)S(1)} %bitcast.194, f32[384]{0:T(512)S(1)} %get-tuple-element.406, f32[2048]{0:T(1024)S(1)} %bitcast.195, f32[384]{0:T(512)S(1)} %get-tuple-element.407, f32[2048]{0:T(1024)S(1)} %bitcast.190, ...), kind=kLoop, calls=%fused_computation.99 | loop fusion | flops 15728640 | bytes 23659520 | tf_op jit(solution)/shard_map/transpose | solution.py:186
  82.3 15.3 %while.48 = (s32[]{:T(128)}, bf16[2,128,16,128]{3,2,1,0:T(8,128)(2,1)S(1)}, s32[2]{0:T(128)S(1)}, bf16[128,16,384]{2,1,0:T(8,128)(2,1)}, s32[256]{0:T(256)S(1)},...) while((s32[]{:T(128)}, bf16[2,128,16,128]{3,2,1,0:T(8,128)(2,1)S(1)}, ...), condition=%wide.region_5.6_spmd.clone, body=%wide.region_4.5_spmd.sunk.clone | while | flops 138706944 | bytes 10032308 | solution.py:203
  83.8 6.1 %fusion.137 = bf16[2,128,16,128]{3,2,1,0:T(8,128)(2,1)S(1)} fusion(bf16[2,128,16,128]{3,2,1,0:T(8,128)(2,1)S(1)} %get-tuple-element.677, s32[]{:T(128)} %get-tuple-element.676, bf16[128,128,256]{2,1,0:T(8,128)(2,1)} %get-tuple-element.690, pred[128,256]{1,0:T(8,128)(4,1)S(1)} %broadcast_compare_fusion.7, ...), kind=kOutput, calls=%fused_computation.6.clone.1.clone | convolution fusion | flops 138674176 | bytes 9994756 | tf_op jit(solution)/shard_map/while/body/eval_jaxpr/gts,gis->git/dot_general | solution.py:199
  91.4 6.1 %fusion.137 = bf16[2,128,16,128]{3,2,1,0:T(8,128)(2,1)S(1)} fusion(bf16[2,128,16,128]{3,2,1,0:T(8,128)(2,1)S(1)} %get-tuple-element.677, s32[]{:T(128)} %get-tuple-element.676, bf16[128,128,256]{2,1,0:T(8,128)(2,1)} %get-tuple-element.690, pred[128,256]{1,0:T(8,128)(4,1)S(1)} %broadcast_compare_fusion.7, ...), kind=kOutput, calls=%fused_computation.6.clone.1.clone | convolution fusion | flops 138674176 | bytes 9994756 | tf_op jit(solution)/shard_map/while/body/eval_jaxpr/gts,gis->git/dot_general | solution.py:199
  102.1 3.5 %copy.88 = f32[2,128,16,32]{1,3,2,0:T(8,128)} copy(f32[2,128,16,32]{3,2,0,1:T(8,128)} %add_bitcast_fusion) | data formatting | bytes 1048576
  105.6 7.1 %while.50 = (s32[]{:T(128)}, f32[128,16]{0,1:T(8,128)S(1)}, f32[128,16]{0,1:T(8,128)S(1)}, f32[128,16,16]{0,2,1:T(8,128)S(1)}, f32[128,16,16]{0,2,1:T(8,128)S(1)...) while((s32[]{:T(128)}, f32[128,16]{0,1:T(8,128)S(1)}, ...), condition=%wide.region_11.12_spmd.clone.clone, body=%wide.region_10.11_spmd.clone.sunk.clone | while | flops 421891 | bytes 2000031 | solution.py:248
  116.7 3.8 %fusion.111 = (bf16[128,128,128]{2,0,1:T(8,128)(2,1)S(1)}, bf16[128,128,128]{2,0,1:T(8,128)(2,1)S(1)}) fusion(bf16[256,128,128]{2,0,1:T(8,128)(2,1)} %fusion.48), kind=kLoop, calls=%fused_computation.202 | loop fusion | bytes 16777216 | tf_op jit(solution)/shard_map/slice | solution.py:107
  120.5 4.7 %copy.82 = bf16[128,128,128]{2,1,0:T(8,128)(2,1)} copy(bf16[128,128,128]{2,0,1:T(8,128)(2,1)S(1)} %get-tuple-element.367) | data formatting | bytes 8388608 | tf_op jit(solution)/shard_map/while | solution.py:221
  125.2 4.7 %copy.83 = bf16[128,128,128]{2,1,0:T(8,128)(2,1)} copy(bf16[128,128,128]{2,0,1:T(8,128)(2,1)S(1)} %get-tuple-element.366) | data formatting | bytes 8388608 | tf_op jit(solution)/shard_map/while | solution.py:221
  138.9 17.6 %while.49 = (s32[]{:T(128)}, f32[2,128,16,128]{3,2,0,1:T(8,128)}, bf16[2,128,16,128]{3,2,1,0:T(8,128)(2,1)S(1)}, s32[2,128]{1,0:T(2,128)}, bf16[128,128,128]{2,1,0:T(8,128)(2,1)}, /*index=5*/bf16[128,128,128]{2,1,0:T(8,128)(2,1)}) while((s32[]{:T(128)}, f32[2,128,16,128]{3,2,0,1:T(8,128)}, bf16[2,128,16,128]{3,2,1,0:T(8,128)(2,1)S(1)}, ...), condition=%wide.region_8.9_spmd.clone, body=%wide.region_7.8_spmd.sunk.clone | while | flops 138690560 | bytes 29411944 | solution.py:221
  139.7 4.6 %fusion.143 = f32[128,16,128]{2,1,0:T(8,128)S(1)} fusion(bf16[128,128,128]{2,1,0:T(8,128)(2,1)} %get-tuple-element.709, pred[128,128]{1,0:T(8,128)(4,1)S(1)} %broadcast_compare_fusion.8, bf16[2,128,16,128]{3,2,1,0:T(8,128)(2,1)S(1)} %get-tuple-element.706, s32[]{:T(128)} %get-tuple-element.698), kind=kOutput, calls=%fused_computation.11.clone.1.clone | convolution fusion | flops 69206016 | bytes 5783556 | tf_op jit(solution)/shard_map/while/body/eval_jaxpr/gts,gis->git/dot_general | solution.py:219
  148.5 4.6 %fusion.143 = f32[128,16,128]{2,1,0:T(8,128)S(1)} fusion(bf16[128,128,128]{2,1,0:T(8,128)(2,1)} %get-tuple-element.709, pred[128,128]{1,0:T(8,128)(4,1)S(1)} %broadcast_compare_fusion.8, bf16[2,128,16,128]{3,2,1,0:T(8,128)(2,1)S(1)} %get-tuple-element.706, s32[]{:T(128)} %get-tuple-element.698), kind=kOutput, calls=%fused_computation.11.clone.1.clone | convolution fusion | flops 69206016 | bytes 5783556 | tf_op jit(solution)/shard_map/while/body/eval_jaxpr/gts,gis->git/dot_general | solution.py:219
  159.6 3.9 %copy.89 = f32[2,128,16,32]{3,2,0,1:T(8,128)} copy(f32[2,128,16,32]{1,3,2,0:T(8,128)} %pad_maximum_fusion.1) | data formatting | bytes 1048576 | tf_op jit(solution)/shard_map/concatenate | solution.py:266
  163.5 5.3 %fusion.78 = f32[128,16,2,128]{3,1,2,0:T(8,128)S(1)} fusion(f32[2,128,16,128]{3,2,0,1:T(8,128)} %get-tuple-element.146, f32[2,128,16,32]{3,2,0,1:T(8,128)} %copy.89, f32[128,128,16]{0,2,1:T(8,128)} %get-tuple-element.370, f32[128,128,16]{0,2,1:T(8,128)} %get-tuple-element.368, bf16[2,128,16,128]{3,2,1,0:T(8,128)(2,1)S(1)} %get-tuple-element.750, ...), kind=kOutput, calls=%fused_computation.93 | convolution fusion | flops 204472320 | bytes 7873536 | tf_op jit(solution)/shard_map/gtm,jgim->jgit/dot_general | solution.py:263
  171.6 6.0 %psum.14 = f32[256]{0:T(256)S(1)} all-reduce(f32[256]{0:T(256)S(1)} %fusion.68), channel_id=1, replica_groups=mesh['groups'=2,'seq'=4,'chan'=2,'rep'=2] {'chan','rep'}, use_global_device_ids=true, to_apply=%region_13.14 | all-reduce | flops 256 | bytes 2048 | tf_op jit(solution)/shard_map/psum | solution.py:279
  177.7 3.8 %fusion.86 = f32[256,512]{1,0:T(8,128)} fusion(bf16[2048,512]{1,0:T(8,128)(2,1)S(1)} %copy-done, f32[2048]{0:T(1024)S(1)} %copy-done.22, f32[256]{0:T(256)S(1)} %add_rsqrt_fusion, f32[256,8,2,128]{3,2,1,0:T(2,128)} %bitcast.177, bf16[256,2048]{0,1:T(8,128)(2,1)S(1)} %copy-done.5), kind=kOutput, calls=%fused_computation.104 | convolution fusion | flops 540540928 | bytes 5776384 | tf_op jit(solution)/shard_map/dot_general | solution.py:144
  182.9 18.6 %reduce-scatter.2.cloned.1.call-done = f32[64,512]{1,0:T(8,128)} async-done(((f32[256,512]{1,0:T(8,128)}), f32[64,512]{1,0:T(8,128)}) %reduce-scatter.2.cloned.1.call-update) | async-done | bytes 131088 | tf_op jit(solution)/shard_map/reduce_scatter | solution.py:288
  202.7 5.7 %all-reduce = f32[256]{0:T(256)S(1)} all-reduce(f32[256]{0:T(256)S(1)} %subtract_dynamic-update-slice_fusion), channel_id=1, replica_groups=mesh['groups'=2,'seq'=4,'chan'=2,'rep'=2] {'chan','rep'}, use_global_device_ids=true, to_apply=%add | all-reduce | flops 256 | bytes 2048
  208.5 11.9 %psum.15 = f32[8]{0:T(128)S(1)} all-reduce(f32[8]{0:T(128)S(1)} %select_reduce_fusion.1), channel_id=1, replica_groups=mesh['groups'=2,'seq'=4,'chan'=2,'rep'=2] {'seq'}, use_global_device_ids=true, to_apply=%region_18.19 | all-reduce | flops 8 | bytes 64 | tf_op jit(solution)/shard_map/psum | solution.py:300
  (173 shorter events, 70.1 us)
Async XLA Ops:
  7.2 170.5 %copy-start = (bf16[2048,512]{1,0:T(8,128)(2,1)S(1)}, bf16[2048,512]{1,0:T(8,128)(2,1)}, u32[]{:S(2)}) copy-start(bf16[2048,512]{1,0:T(8,128)(2,1)} %param.25) | copy-start | bytes 6291460
  7.2 8.6 %copy-start.15 = (f32[4,128,16]{1,2,0:T(8,128)S(1)}, f32[4,128,16]{1,2,0:T(8,128)}, u32[]{:S(2)}) copy-start(f32[4,128,16]{1,2,0:T(8,128)} %param.22) | copy-start | bytes 98308
  7.2 194.3 %reduce-scatter.2.cloned.1.call-start = ((), (), s32[]{:S(2)}) async-start(), calls=%async_computation.1 | async-start | bytes 655360 | tf_op jit(solution)/shard_map/reduce_scatter | solution.py:288
  9.8 62.4 %collective-permute-start = (bf16[2,136,2048]{2,1,0:T(8,128)(2,1)}, bf16[2,136,2048]{2,1,0:T(8,128)(2,1)}, u32[]{:S(2)}, u32[]{:S(2)}) collective-permute-start(bf16[2,136,2048]{2,1,0:T(8,128)(2,1)} %pad_maximum_fusion), channel_id=1, source_target_pairs={{0,4},{4,8},{8,12},{1,5},{5,9},{9,13},{2,6},{6,10},{10,14},{3,7},{... | collective-permute-start | bytes 3342344 | tf_op jit(solution)/shard_map/ppermute | solution.py:18
  30.2 6.6 %copy-start.12 = (bf16[128,128]{1,0:T(8,128)(2,1)S(1)}, bf16[128,128]{1,0:T(8,128)(2,1)}, u32[]{:S(2)}) copy-start(bf16[128,128]{1,0:T(8,128)(2,1)} %param.21) | copy-start | bytes 98308
  31.2 5.0 %copy-start.21 = (s32[2,128]{1,0:T(2,128)}, s32[2,128]{1,0:T(2,128)S(1)}, u32[]{:S(2)}) copy-start(s32[2,128]{1,0:T(2,128)S(1)} %get-tuple-element.695) | copy-start | bytes 3076
  65.7 6.4 %copy-start.11 = (bf16[7,2048]{1,0:T(8,128)(2,1)S(1)}, bf16[7,2048]{1,0:T(8,128)(2,1)}, u32[]{:S(2)}) copy-start(bf16[7,2048]{1,0:T(8,128)(2,1)} %param.20) | copy-start | bytes 86020
  102.1 3.5 %copy-start.27 = (f32[2]{0:T(128)S(1)}, f32[2]{0:T(128)}, u32[]{:S(2)}) copy-start(f32[2]{0:T(128)} %compare_convert_fusion.1) | copy-start | bytes 28
  113.4 19.4 %collective-permute-start.1 = (f32[128,544]{0,1:T(8,128)}, f32[128,544]{0,1:T(8,128)}, u32[]{:S(2)}, u32[]{:S(2)}) collective-permute-start(f32[128,544]{0,1:T(8,128)} %pad_maximum_fusion.2), channel_id=1, source_target_pairs={{0,4},{4,8},{8,12},{1,5},{5,9},{9,13},{2,6},{6,10},{10,14},{3,7},{... | collective-permute-start | bytes 835592 | tf_op jit(solution)/shard_map/ppermute | solution.py:18
  125.2 4.7 %copy-start.16 = (f32[2048]{0:T(1024)S(1)}, f32[2048]{0:T(1024)}, u32[]{:S(2)}) copy-start(f32[2048]{0:T(1024)} %param.23) | copy-start | bytes 24580
  135.9 20.6 %collective-permute-start.2 = (f32[128,544]{0,1:T(8,128)}, f32[128,544]{0,1:T(8,128)}, u32[]{:S(2)}, u32[]{:S(2)}) collective-permute-start(f32[128,544]{0,1:T(8,128)} %pad_maximum_fusion.3), channel_id=1, source_target_pairs={{0,8},{4,12},{1,9},{5,13},{2,10},{6,14},{3,11},{7,15},{16,24},{20,... | collective-permute-start | bytes 835592 | tf_op jit(solution)/shard_map/ppermute | solution.py:18
  138.9 18.6 %copy-start.9 = (f32[128,256]{0,1:T(8,128)S(1)}, f32[128,256]{0,1:T(8,128)}, u32[]{:S(2)}) copy-start(f32[128,256]{0,1:T(8,128)} %copy-done.8) | copy-start | bytes 393220
  138.9 18.6 %copy-start.13 = (f32[128,16]{0,1:T(8,128)S(1)}, f32[128,16]{0,1:T(8,128)}, u32[]{:S(2)}) copy-start(f32[128,16]{0,1:T(8,128)} %get-tuple-element.381) | copy-start | bytes 24580
  138.9 18.6 %copy-start.14 = (f32[128,16]{0,1:T(8,128)S(1)}, f32[128,16]{0,1:T(8,128)}, u32[]{:S(2)}) copy-start(f32[128,16]{0,1:T(8,128)} %get-tuple-element.382) | copy-start | bytes 24580
  139.7 4.6 %copy-start.4 = (bf16[128,128,128]{2,1,0:T(8,128)(2,1)S(1)}, bf16[128,128,128]{2,1,0:T(8,128)(2,1)}, u32[]{:S(2)}) copy-start(bf16[128,128,128]{2,1,0:T(8,128)(2,1)} %get-tuple-element.708) | copy-start | bytes 12582916 | tf_op jit(solution)/shard_map/while
  148.5 4.6 %copy-start.4 = (bf16[128,128,128]{2,1,0:T(8,128)(2,1)S(1)}, bf16[128,128,128]{2,1,0:T(8,128)(2,1)}, u32[]{:S(2)}) copy-start(bf16[128,128,128]{2,1,0:T(8,128)(2,1)} %get-tuple-element.708) | copy-start | bytes 12582916 | tf_op jit(solution)/shard_map/while
  158.7 4.8 %copy-start.10 = (f32[128,16]{1,0:T(8,128)S(1)}, f32[128,16]{1,0:T(8,128)}, u32[]{:S(2)}) copy-start(f32[128,16]{1,0:T(8,128)} %mul.578) | copy-start | bytes 24580
  158.7 4.7 %copy-start.17 = (f32[2,128]{1,0:T(2,128)S(1)}, f32[2,128]{1,0:T(2,128)}, u32[]{:S(2)}) copy-start(f32[2,128]{1,0:T(2,128)} %get-tuple-element.411) | copy-start | bytes 3076
  169.9 7.7 %copy-start.22 = (f32[2048]{0:T(1024)S(1)}, f32[2048]{0:T(1024)}, u32[]{:S(2)}) copy-start(f32[2048]{0:T(1024)} %param.24) | copy-start | bytes 24580
  177.6 3.9 %copy-start.23 = (s32[256]{0:T(256)S(1)}, s32[256]{0:T(256)}, u32[]{:S(2)}) copy-start(s32[256]{0:T(256)} %param.26) | copy-start | bytes 3076
  177.7 4.0 %copy-start.26 = (u32[32]{0:T(128)S(1)}, u32[32]{0:T(128)}, u32[]{:S(2)}) copy-start(u32[32]{0:T(128)} %constant.111) | copy-start | bytes 388
  177.7 30.7 %copy-start.19 = (s32[256]{0:T(256)S(1)}, s32[256]{0:T(256)}, u32[]{:S(2)}) copy-start(s32[256]{0:T(256)} %get-tuple-element.672) | copy-start | bytes 3076
  177.7 42.7 %copy-start.25 = (s32[8]{0:T(128)S(1)}, s32[8]{0:T(128)}, u32[]{:S(2)}) copy-start(s32[8]{0:T(128)} %param.27) | copy-start | bytes 100
  208.4 12.5 %copy-start.20 = (f32[256]{0:T(256)}, f32[256]{0:T(256)S(1)}, u32[]{:S(2)}) copy-start(f32[256]{0:T(256)S(1)} %all-reduce) | copy-start | bytes 3076
  (9 other events, 17.1 us)
Sparse Core Ops, SparseCore 0:
  181.7 19.7 reduce-scatter.1

commit v4 on v3

--- a/solution.py
+++ b/solution.py
@@ -78,11 +78,11 @@
     out_pos = jnp.arange(rows, dtype=jnp.int32)[:, None]
     in_pos = jnp.arange(cols, dtype=jnp.int32)[None, :]
     lag_grid = out_pos + shift - in_pos
-    one_hot = (lag_grid[None] == lag_ids[:, None, None]).astype(table.dtype)
-    picked = lax.dot_general(
-        table, one_hot, (((0,), (0,)), ((), ())), preferred_element_type=jnp.float32
-    )
-    return picked.astype(table.dtype)
+    one_hot = (lag_grid.reshape(1, rows * cols) == lag_ids[:, None]).astype(table.dtype)
+    width = table.shape[1]
+    lead = jnp.concatenate((table.T, jnp.zeros((max(256 - width, 0), lag_count), table.dtype)))
+    picked = jnp.dot(lead, one_hot, preferred_element_type=jnp.float32)[:width]
+    return picked.astype(table.dtype).reshape(width, rows, cols)
 
 
 def medium_toeplitz(medium_taps):

time: 229 us -> 226 us (0.987)
  other arithmetic: 38.5 us -> 35.8 us
    while x9 -> x6, local copies, waits for them, and re-layouts: 21.9 us -> 0.01 us  [the longest x1 12.6 us: per_device(): signal = lax.map(medium_block, jnp.arange(tile_count, dtype=jnp.int32))]
    unnamed x58 -> x65, local copies, waits for them, and re-layouts: 8.1 us -> 27.6 us
    slice x1, local copies, waits for them, and re-layouts: 3.82 us -> 7.35 us  [lag_select(): picked = jnp.dot(lead, one_hot, preferred_element_type=jnp.float32)[:width]]
where the time goes in v4:
time: 226 us; the launch traced here: 225 us
  local copies, waits for them, and re-layouts  62.8 us (28%)
  matrix products  55.5 us (25%)
  other arithmetic  35.8 us (16%)
  blocking collectives  23.6 us (10%)
  waiting for transfers between devices  18.6 us (8%)
  between operations  15.2 us (7%)
  starting transfers between devices  12.4 us (5%)
    unnamed x65, local copies, waits for them, and re-layouts  27.6 us
    reduce_scatter x1, waiting for transfers between devices, per_device(): lax.psum_scatter(partial_value, lanes, scatter_dimension=0, tiled=True)  18.5 us
    dot_general x2, matrix products, lag_select(): picked = jnp.dot(lead, one_hot, preferred_element_type=jnp.float32)[:width]  13.9 us
    ppermute x3, starting transfers between devices, from_behind(): return lax.ppermute(shard, axis, pairs)  12.3 us
    dot_general x2, matrix products, medium_block(): jnp.einsum('gts,gis->git', matrix, window, preferred_element_type=jnp.flo...  12.2 us
    psum x1, blocking collectives, per_device(): totals = lax.psum(genome_part, 'seq')  11.9 us
    mul x1, other arithmetic, modal_tables(): power_im = magnitude * jnp.sin(powers * angles[None])  9.37 us
    dot_general x2, matrix products, intra_block(): jnp.einsum('gts,gis->git', lower, block_in, preferred_element_type=jnp.fl...  9.22 us
  transfers between devices with their start and end apart: 4, of which 1 were waited for; matrix products, arithmetic and copies ran while one was open for 40% of the time, Pallas kernels for 0%

profile of v4, /device:TPU:0, one launch (start us, length us, event | category | flops | bytes accessed | tf_op | source)
XLA Modules:
  0.0 225.2 jit_solution(7509894498725809986)
XLA Ops:
  9.9 5.9 %collective-permute-start = (bf16[2,136,2048]{2,1,0:T(8,128)(2,1)}, bf16[2,136,2048]{2,1,0:T(8,128)(2,1)}, u32[]{:S(2)}, u32[]{:S(2)}) collective-permute-start(bf16[2,136,2048]{2,1,0:T(8,128)(2,1)} %pad_maximum_fusion), channel_id=1, source_target_pairs={{0,4},{4,8},{8,12},{1,5},{5,9},{9,13},{2,6},{6,10},{10,14},{3,7},{... | collective-permute-start | bytes 3342344 | tf_op jit(solution)/shard_map/ppermute | solution.py:18
  16.3 9.4 %fusion.66 = (f32[129,128,16]{0,2,1:T(8,128)S(1)}, f32[129,128,16]{0,2,1:T(8,128)}, f32[129,128,16]{0,2,1:T(8,128)S(1)}) fusion(f32[128,16]{1,0:T(8,128)S(1)} %copy.70, f32[129]{0:T(256)S(1)} %iota_convert_fusion, f32[128,16]{1,0:T(8,128)S(1)} %copy.69, f32[129]{0:T(256)S(1)} %fusion.99, f32[128,16]{1,0:T(8,128)S(1)} %copy.71, f32[128,16]{1,0:T(8,128)S(1)} %copy.68), kind=kLoop, calls=%fused_computation.84 | loop fusion | flops 1849344 | bytes 3204104 | tf_op jit(solution)/shard_map/mul | solution.py:100
  31.1 8.2 %fusion.42 = bf16[256,32768]{1,0:T(8,128)(2,1)} fusion(s32[32768]{0:T(1024)S(1)} %bitcast.193, s32[128]{0:T(128)S(1)} %iota.65, bf16[128,128]{0,1:T(8,128)(2,1)S(1)} %bitcast.207), kind=kOutput, calls=%fused_computation.46 | convolution fusion | flops 2151677952 | bytes 16941568 | tf_op jit(solution)/shard_map/dot_general | solution.py:84
  39.3 7.4 %slice.366 = bf16[128,32768]{1,0:T(8,128)(2,1)} slice(bf16[256,32768]{1,0:T(8,128)(2,1)} %fusion.42), slice={[0:128], [0:32768]} | slice | bytes 16777216 | tf_op jit(solution)/shard_map/slice | solution.py:84
  46.7 9.1 %copy.92 = bf16[16,8,128,256]{3,2,1,0:T(8,128)(2,1)} copy(bf16[16,8,128,256]{3,1,2,0:T(8,128)(2,1)} %bitcast.180) | data formatting | bytes 16777216
  67.9 5.7 %convolution_convert_fusion = bf16[256,16384]{1,0:T(8,128)(2,1)} fusion(s32[16384]{0:T(1024)S(1)} %subtract_bitcast_fusion.1, s32[128]{0:T(128)S(1)} %iota.65, bf16[128,128]{0,1:T(8,128)(2,1)S(1)} %get-tuple-element.306, bf16[128,128]{0,1:T(8,128)(2,1)S(1)} %get-tuple-element.307), kind=kOutput, calls=%fused_computation.44 | convolution fusion | flops 1080164352 | bytes 8520192 | tf_op jit(solution)/shard_map/dot_general | solution.py:84
  76.0 5.1 %fusion.74 = bf16[2048,384]{0,1:T(8,128)(2,1)} fusion(f32[384]{0:T(512)S(1)} %get-tuple-element.358, f32[392,2048]{1,0:T(8,128)S(1)} %convert_multiply_fusion, f32[2048]{0:T(1024)S(1)} %bitcast.205, f32[384]{0:T(512)S(1)} %get-tuple-element.354, f32[2048]{0:T(1024)S(1)} %bitcast.206, f32[384]{0:T(512)S(1)} %get-tuple-element.355, f32[2048]{0:T(1024)S(1)} %bitcast.201, ...), kind=kLoop, calls=%fused_computation.100 | loop fusion | flops 15728640 | bytes 23659520 | tf_op jit(solution)/shard_map/transpose | solution.py:186
  83.7 15.0 %while.48 = (s32[]{:T(128)}, bf16[2,128,16,128]{3,2,1,0:T(8,128)(2,1)S(1)}, s32[2]{0:T(128)S(1)}, bf16[128,16,384]{2,1,0:T(8,128)(2,1)}, s32[256]{0:T(256)S(1)},...) while((s32[]{:T(128)}, bf16[2,128,16,128]{3,2,1,0:T(8,128)(2,1)S(1)}, ...), condition=%wide.region_5.6_spmd.clone, body=%wide.region_4.5_spmd.sunk.clone | while | flops 138706944 | bytes 10032308 | solution.py:203
  85.1 6.1 %fusion.132 = bf16[2,128,16,128]{3,2,1,0:T(8,128)(2,1)S(1)} fusion(bf16[2,128,16,128]{3,2,1,0:T(8,128)(2,1)S(1)} %get-tuple-element.625, s32[]{:T(128)} %get-tuple-element.624, bf16[128,128,256]{2,1,0:T(8,128)(2,1)} %get-tuple-element.638, pred[128,256]{1,0:T(8,128)(4,1)S(1)} %broadcast_compare_fusion.7, ...), kind=kOutput, calls=%fused_computation.6.clone.1.clone | convolution fusion | flops 138674176 | bytes 9994756 | tf_op jit(solution)/shard_map/while/body/eval_jaxpr/gts,gis->git/dot_general | solution.py:199
  92.7 6.1 %fusion.132 = bf16[2,128,16,128]{3,2,1,0:T(8,128)(2,1)S(1)} fusion(bf16[2,128,16,128]{3,2,1,0:T(8,128)(2,1)S(1)} %get-tuple-element.625, s32[]{:T(128)} %get-tuple-element.624, bf16[128,128,256]{2,1,0:T(8,128)(2,1)} %get-tuple-element.638, pred[128,256]{1,0:T(8,128)(4,1)S(1)} %broadcast_compare_fusion.7, ...), kind=kOutput, calls=%fused_computation.6.clone.1.clone | convolution fusion | flops 138674176 | bytes 9994756 | tf_op jit(solution)/shard_map/while/body/eval_jaxpr/gts,gis->git/dot_general | solution.py:199
  103.2 3.5 %copy.76 = f32[2,128,16,32]{1,3,2,0:T(8,128)} copy(f32[2,128,16,32]{3,2,0,1:T(8,128)} %add_bitcast_fusion) | data formatting | bytes 1048576
  106.7 6.1 %while.50 = (s32[]{:T(128)}, f32[128,16]{0,1:T(8,128)S(1)}, f32[128,16]{0,1:T(8,128)S(1)}, f32[128,16,16]{0,2,1:T(8,128)S(1)}, f32[128,16,16]{0,2,1:T(8,128)S(1)...) while((s32[]{:T(128)}, f32[128,16]{0,1:T(8,128)S(1)}, ...), condition=%wide.region_11.12_spmd.clone.clone, body=%wide.region_10.11_spmd.clone.sunk.clone | while | flops 421891 | bytes 1999523 | solution.py:248
  116.8 3.9 %slice_bitcast_fusion = (bf16[16,8,128,128]{3,1,2,0:T(8,128)(2,1)S(1)}, bf16[16,8,128,128]{3,1,2,0:T(8,128)(2,1)S(1)}) fusion(bf16[256,16384]{1,0:T(8,128)(2,1)} %convolution_convert_fusion), kind=kLoop, calls=%fused_computation.51 | loop fusion | bytes 16777216
  136.4 17.5 %while.49 = (s32[]{:T(128)}, f32[2,128,16,128]{3,2,0,1:T(8,128)}, bf16[2,128,16,128]{3,2,1,0:T(8,128)(2,1)S(1)}, s32[2,128]{1,0:T(2,128)}, bf16[128,128,128]{2,1,0:T(8,128)(2,1)}, /*index=5*/bf16[128,128,128]{2,1,0:T(8,128)(2,1)}) while((s32[]{:T(128)}, f32[2,128,16,128]{3,2,0,1:T(8,128)}, bf16[2,128,16,128]{3,2,1,0:T(8,128)(2,1)S(1)}, ...), condition=%wide.region_8.9_spmd.clone, body=%wide.region_7.8_spmd.sunk.clone | while | flops 138690560 | bytes 29411944 | solution.py:221
  137.3 4.6 %fusion.138 = f32[128,16,128]{2,1,0:T(8,128)S(1)} fusion(bf16[128,128,128]{2,1,0:T(8,128)(2,1)} %get-tuple-element.657, pred[128,128]{1,0:T(8,128)(4,1)S(1)} %broadcast_compare_fusion.8, bf16[2,128,16,128]{3,2,1,0:T(8,128)(2,1)S(1)} %get-tuple-element.654, s32[]{:T(128)} %get-tuple-element.646), kind=kOutput, calls=%fused_computation.11.clone.1.clone | convolution fusion | flops 69206016 | bytes 5783556 | tf_op jit(solution)/shard_map/while/body/eval_jaxpr/gts,gis->git/dot_general | solution.py:219
  146.0 4.6 %fusion.138 = f32[128,16,128]{2,1,0:T(8,128)S(1)} fusion(bf16[128,128,128]{2,1,0:T(8,128)(2,1)} %get-tuple-element.657, pred[128,128]{1,0:T(8,128)(4,1)S(1)} %broadcast_compare_fusion.8, bf16[2,128,16,128]{3,2,1,0:T(8,128)(2,1)S(1)} %get-tuple-element.654, s32[]{:T(128)} %get-tuple-element.646), kind=kOutput, calls=%fused_computation.11.clone.1.clone | convolution fusion | flops 69206016 | bytes 5783556 | tf_op jit(solution)/shard_map/while/body/eval_jaxpr/gts,gis->git/dot_general | solution.py:219
  150.6 3.4 %fusion.139 = f32[2,128,16,128]{3,2,0,1:T(8,128)} fusion(f32[2,128,16,128]{3,2,0,1:T(8,128)} %get-tuple-element.647, s32[]{:T(128)} %get-tuple-element.646, f32[128,16,128]{2,1,0:T(8,128)S(1)} %fusion.138, bf16[128,128,128]{2,1,0:T(8,128)(2,1)S(1)} %copy-done.4, pred[128,128]{1,0:T(8,128)(4,1)S(1)} %broadcast_compare_fusion.8, ...), kind=kOutput, calls=%fused_computation.21.clone.1.clone | convolution fusion | flops 69468160 | bytes 6833152 | tf_op jit(solution)/shard_map/while/body/eval_jaxpr/gts,gis->git/dot_general | solution.py:217
  157.1 3.9 %copy.77 = f32[2,128,16,32]{3,2,0,1:T(8,128)} copy(f32[2,128,16,32]{1,3,2,0:T(8,128)} %pad_maximum_fusion.1) | data formatting | bytes 1048576 | tf_op jit(solution)/shard_map/concatenate | solution.py:266
  161.0 5.3 %fusion.72 = f32[128,16,2,128]{3,1,2,0:T(8,128)S(1)} fusion(f32[2,128,16,128]{3,2,0,1:T(8,128)} %get-tuple-element.146, f32[2,128,16,32]{3,2,0,1:T(8,128)} %copy.77, f32[128,128,16]{0,2,1:T(8,128)} %get-tuple-element.318, f32[128,128,16]{0,2,1:T(8,128)} %get-tuple-element.316, bf16[2,128,16,128]{3,2,1,0:T(8,128)(2,1)S(1)} %get-tuple-element.698, ...), kind=kOutput, calls=%fused_computation.94 | convolution fusion | flops 204472320 | bytes 7873536 | tf_op jit(solution)/shard_map/gtm,jgim->jgit/dot_general | solution.py:263
  169.1 6.0 %psum.14 = f32[256]{0:T(256)S(1)} all-reduce(f32[256]{0:T(256)S(1)} %fusion.62), channel_id=1, replica_groups=mesh['groups'=2,'seq'=4,'chan'=2,'rep'=2] {'chan','rep'}, use_global_device_ids=true, to_apply=%region_13.14 | all-reduce | flops 256 | bytes 2048 | tf_op jit(solution)/shard_map/psum | solution.py:279
  175.2 3.8 %fusion.80 = f32[256,512]{1,0:T(8,128)} fusion(bf16[2048,512]{1,0:T(8,128)(2,1)S(1)} %copy-done, f32[2048]{0:T(1024)S(1)} %copy-done.24, f32[256]{0:T(256)S(1)} %add_rsqrt_fusion, f32[256,8,2,128]{3,2,1,0:T(2,128)} %bitcast.185, bf16[256,2048]{0,1:T(8,128)(2,1)S(1)} %copy-done.5), kind=kOutput, calls=%fused_computation.105 | convolution fusion | flops 540540928 | bytes 5776384 | tf_op jit(solution)/shard_map/dot_general | solution.py:144
  180.4 18.5 %reduce-scatter.2.cloned.1.call-done = f32[64,512]{1,0:T(8,128)} async-done(((f32[256,512]{1,0:T(8,128)}), f32[64,512]{1,0:T(8,128)}) %reduce-scatter.2.cloned.1.call-update) | async-done | bytes 131088 | tf_op jit(solution)/shard_map/reduce_scatter | solution.py:288
  200.1 5.7 %all-reduce.1 = f32[256]{0:T(256)S(1)} all-reduce(f32[256]{0:T(256)S(1)} %subtract_dynamic-update-slice_fusion), channel_id=1, replica_groups=mesh['groups'=2,'seq'=4,'chan'=2,'rep'=2] {'chan','rep'}, use_global_device_ids=true, to_apply=%add.1 | all-reduce | flops 256 | bytes 2048
  206.0 11.9 %psum.15 = f32[8]{0:T(128)S(1)} all-reduce(f32[8]{0:T(128)S(1)} %select_reduce_fusion.1), channel_id=1, replica_groups=mesh['groups'=2,'seq'=4,'chan'=2,'rep'=2] {'seq'}, use_global_device_ids=true, to_apply=%region_18.19 | all-reduce | flops 8 | bytes 64 | tf_op jit(solution)/shard_map/psum | solution.py:300
  (177 shorter events, 70.7 us)
Async XLA Ops:
  7.2 168.0 %copy-start = (bf16[2048,512]{1,0:T(8,128)(2,1)S(1)}, bf16[2048,512]{1,0:T(8,128)(2,1)}, u32[]{:S(2)}) copy-start(bf16[2048,512]{1,0:T(8,128)(2,1)} %param.25) | copy-start | bytes 6291460
  7.2 8.7 %copy-start.15 = (f32[4,128,16]{1,2,0:T(8,128)S(1)}, f32[4,128,16]{1,2,0:T(8,128)}, u32[]{:S(2)}) copy-start(f32[4,128,16]{1,2,0:T(8,128)} %param.22) | copy-start | bytes 98308
  7.2 191.7 %reduce-scatter.2.cloned.1.call-start = ((), (), s32[]{:S(2)}) async-start(), calls=%async_computation.1 | async-start | bytes 655360 | tf_op jit(solution)/shard_map/reduce_scatter | solution.py:288
  9.9 63.7 %collective-permute-start = (bf16[2,136,2048]{2,1,0:T(8,128)(2,1)}, bf16[2,136,2048]{2,1,0:T(8,128)(2,1)}, u32[]{:S(2)}, u32[]{:S(2)}) collective-permute-start(bf16[2,136,2048]{2,1,0:T(8,128)(2,1)} %pad_maximum_fusion), channel_id=1, source_target_pairs={{0,4},{4,8},{8,12},{1,5},{5,9},{9,13},{2,6},{6,10},{10,14},{3,7},{... | collective-permute-start | bytes 3342344 | tf_op jit(solution)/shard_map/ppermute | solution.py:18
  30.8 29.5 %copy-start.23 = (s32[2,128]{1,0:T(2,128)}, s32[2,128]{1,0:T(2,128)S(1)}, u32[]{:S(2)}) copy-start(s32[2,128]{1,0:T(2,128)S(1)} %get-tuple-element.643) | copy-start | bytes 3076
  67.9 5.7 %copy-start.11 = (bf16[7,2048]{1,0:T(8,128)(2,1)S(1)}, bf16[7,2048]{1,0:T(8,128)(2,1)}, u32[]{:S(2)}) copy-start(bf16[7,2048]{1,0:T(8,128)(2,1)} %param.20) | copy-start | bytes 86020
  112.8 7.9 %copy-start.16 = (f32[2,128,16]{1,2,0:T(8,128)}, f32[2,128,16]{1,2,0:T(8,128)S(1)}, u32[]{:S(2)}) copy-start(f32[2,128,16]{1,2,0:T(8,128)S(1)} %get-tuple-element.148) | copy-start | bytes 49156
  112.8 7.9 %copy-start.17 = (f32[2,128,16]{1,2,0:T(8,128)}, f32[2,128,16]{1,2,0:T(8,128)S(1)}, u32[]{:S(2)}) copy-start(f32[2,128,16]{1,2,0:T(8,128)S(1)} %get-tuple-element.153) | copy-start | bytes 49156
  113.6 16.6 %collective-permute-start.1 = (f32[128,544]{0,1:T(8,128)}, f32[128,544]{0,1:T(8,128)}, u32[]{:S(2)}, u32[]{:S(2)}) collective-permute-start(f32[128,544]{0,1:T(8,128)} %pad_maximum_fusion.2), channel_id=1, source_target_pairs={{0,4},{4,8},{8,12},{1,5},{5,9},{9,13},{2,6},{6,10},{10,14},{3,7},{... | collective-permute-start | bytes 835592 | tf_op jit(solution)/shard_map/ppermute | solution.py:18
  124.0 3.2 %copy-start.18 = (f32[2048]{0:T(1024)S(1)}, f32[2048]{0:T(1024)}, u32[]{:S(2)}) copy-start(f32[2048]{0:T(1024)} %param.23) | copy-start | bytes 24580
  133.3 20.7 %collective-permute-start.2 = (f32[128,544]{0,1:T(8,128)}, f32[128,544]{0,1:T(8,128)}, u32[]{:S(2)}, u32[]{:S(2)}) collective-permute-start(f32[128,544]{0,1:T(8,128)} %pad_maximum_fusion.3), channel_id=1, source_target_pairs={{0,8},{4,12},{1,9},{5,13},{2,10},{6,14},{3,11},{7,15},{16,24},{20,... | collective-permute-start | bytes 835592 | tf_op jit(solution)/shard_map/ppermute | solution.py:18
  136.4 18.5 %copy-start.9 = (f32[128,256]{0,1:T(8,128)S(1)}, f32[128,256]{0,1:T(8,128)}, u32[]{:S(2)}) copy-start(f32[128,256]{0,1:T(8,128)} %copy-done.8) | copy-start | bytes 393220
  136.4 18.5 %copy-start.13 = (f32[128,16]{0,1:T(8,128)S(1)}, f32[128,16]{0,1:T(8,128)}, u32[]{:S(2)}) copy-start(f32[128,16]{0,1:T(8,128)} %get-tuple-element.329) | copy-start | bytes 24580
  136.4 18.5 %copy-start.14 = (f32[128,16]{0,1:T(8,128)S(1)}, f32[128,16]{0,1:T(8,128)}, u32[]{:S(2)}) copy-start(f32[128,16]{0,1:T(8,128)} %get-tuple-element.330) | copy-start | bytes 24580
  137.3 4.6 %copy-start.4 = (bf16[128,128,128]{2,1,0:T(8,128)(2,1)S(1)}, bf16[128,128,128]{2,1,0:T(8,128)(2,1)}, u32[]{:S(2)}) copy-start(bf16[128,128,128]{2,1,0:T(8,128)(2,1)} %get-tuple-element.656) | copy-start | bytes 12582916 | tf_op jit(solution)/shard_map/while
  146.0 4.6 %copy-start.4 = (bf16[128,128,128]{2,1,0:T(8,128)(2,1)S(1)}, bf16[128,128,128]{2,1,0:T(8,128)(2,1)}, u32[]{:S(2)}) copy-start(bf16[128,128,128]{2,1,0:T(8,128)(2,1)} %get-tuple-element.656) | copy-start | bytes 12582916 | tf_op jit(solution)/shard_map/while
  156.2 4.8 %copy-start.10 = (f32[128,16]{1,0:T(8,128)S(1)}, f32[128,16]{1,0:T(8,128)}, u32[]{:S(2)}) copy-start(f32[128,16]{1,0:T(8,128)} %mul.578) | copy-start | bytes 24580
  156.2 4.8 %copy-start.19 = (f32[2,128]{1,0:T(2,128)S(1)}, f32[2,128]{1,0:T(2,128)}, u32[]{:S(2)}) copy-start(f32[2,128]{1,0:T(2,128)} %get-tuple-element.359) | copy-start | bytes 3076
  167.4 7.7 %copy-start.24 = (f32[2048]{0:T(1024)S(1)}, f32[2048]{0:T(1024)}, u32[]{:S(2)}) copy-start(f32[2048]{0:T(1024)} %param.24) | copy-start | bytes 24580
  175.1 3.9 %copy-start.25 = (s32[256]{0:T(256)S(1)}, s32[256]{0:T(256)}, u32[]{:S(2)}) copy-start(s32[256]{0:T(256)} %param.26) | copy-start | bytes 3076
  175.2 4.0 %copy-start.28 = (u32[32]{0:T(128)S(1)}, u32[32]{0:T(128)}, u32[]{:S(2)}) copy-start(u32[32]{0:T(128)} %constant.114) | copy-start | bytes 388
  175.2 30.7 %copy-start.21 = (s32[256]{0:T(256)S(1)}, s32[256]{0:T(256)}, u32[]{:S(2)}) copy-start(s32[256]{0:T(256)} %copy-done.20) | copy-start | bytes 3076
  175.2 42.7 %copy-start.27 = (s32[8]{0:T(128)S(1)}, s32[8]{0:T(128)}, u32[]{:S(2)}) copy-start(s32[8]{0:T(128)} %param.27) | copy-start | bytes 100
  205.9 12.5 %copy-start.22 = (f32[256]{0:T(256)}, f32[256]{0:T(256)S(1)}, u32[]{:S(2)}) copy-start(f32[256]{0:T(256)S(1)} %all-reduce.1) | copy-start | bytes 3076
  (10 other events, 18.8 us)
Sparse Core Ops, SparseCore 0:
  179.2 19.6 reduce-scatter.1

commit v5 on v4

--- a/solution.py
+++ b/solution.py
@@ -72,21 +72,15 @@
     return result.astype(jnp.bfloat16)
 
 
-def lag_select(table, rows, cols, shift):
-    lag_count = table.shape[0]
+def circulants(table):
+    lag_count, width = table.shape
     lag_ids = lax.optimization_barrier(jnp.arange(lag_count, dtype=jnp.int32))
-    out_pos = jnp.arange(rows, dtype=jnp.int32)[:, None]
-    in_pos = jnp.arange(cols, dtype=jnp.int32)[None, :]
-    lag_grid = out_pos + shift - in_pos
-    one_hot = (lag_grid.reshape(1, rows * cols) == lag_ids[:, None]).astype(table.dtype)
-    width = table.shape[1]
-    lead = jnp.concatenate((table.T, jnp.zeros((max(256 - width, 0), lag_count), table.dtype)))
-    picked = jnp.dot(lead, one_hot, preferred_element_type=jnp.float32)[:width]
-    return picked.astype(table.dtype).reshape(width, rows, cols)
-
-
-def medium_toeplitz(medium_taps):
-    return lag_select(medium_taps, tile_rows, 2 * tile_rows, tile_rows)
+    out_pos = jnp.arange(tile_rows, dtype=jnp.int32)[:, None]
+    in_pos = jnp.arange(tile_rows, dtype=jnp.int32)[None, :]
+    lag_grid = (out_pos - in_pos + tile_rows) % tile_rows
+    one_hot = (lag_grid.reshape(1, tile_rows * tile_rows) == lag_ids[:, None]).astype(table.dtype)
+    picked = jnp.dot(table.T, one_hot, preferred_element_type=jnp.float32)
+    return picked.astype(table.dtype).reshape(width, tile_rows, tile_rows)
 
 
 def modal_tables(modal_poles):
@@ -101,10 +95,7 @@
     kernel_re = residue_re[None] * power_re - residue_im[None] * power_im
     kernel_im = residue_re[None] * power_im + residue_im[None] * power_re
     kernel = jnp.sum(kernel_re[:tile_rows], axis=2)
-    upper, lower = split_table(kernel)
-    group_count = kernel.shape[1]
-    both = lag_select(jnp.concatenate((upper, lower), axis=1), tile_rows, tile_rows, 0)
-    toeplitz = (both[:group_count], both[group_count:])
+    toeplitz = split_table(kernel)
     outward = jnp.transpose(jnp.concatenate((kernel_re[1:], -kernel_im[1:]), axis=2), (1, 0, 2))
     inward = jnp.transpose(
         jnp.concatenate((power_re[tile_rows - 1 :: -1], power_im[tile_rows - 1 :: -1]), axis=2),
@@ -187,22 +178,31 @@
     medium_segs = segment_ids(
         first_row - tile_rows + jnp.arange(row_count + tile_rows, dtype=jnp.int32), genome_lengths
     )
-    toeplitz = medium_toeplitz(medium_taps)
+
+    long_toeplitz, outward, inward, decay_re, decay_im = modal_tables(modal_poles)
+    circ = circulants(jnp.concatenate((medium_taps, long_toeplitz[0], long_toeplitz[1]), axis=1))
+    circ_medium = jnp.concatenate((circ[:group_count], circ[:group_count]), axis=2)
+    toeplitz_upper = circ[group_count : 2 * group_count]
+    toeplitz_lower = circ[2 * group_count :]
+    lag_band = (
+        jnp.arange(tile_rows, dtype=jnp.int32)[:, None] + tile_rows
+        - jnp.arange(2 * tile_rows, dtype=jnp.int32)[None, :]
+    )
+    medium_band = (lag_band >= 0) & (lag_band < medium_taps.shape[0])
+    long_band = lag_band[:, tile_rows:] >= 0
 
     def medium_block(tile_index):
         start = tile_index * tile_rows
         window = lax.dynamic_slice_in_dim(ext_short, start, 2 * tile_rows, 2)
         window_segs = lax.dynamic_slice_in_dim(medium_segs, start, 2 * tile_rows, 0)
         own_segs = lax.dynamic_slice_in_dim(segments, start, tile_rows, 0)
-        same_genome = own_segs[:, None] == window_segs[None, :]
-        matrix = jnp.where(same_genome[None], toeplitz, jnp.zeros_like(toeplitz))
+        same_genome = (own_segs[:, None] == window_segs[None, :]) & medium_band
+        matrix = jnp.where(same_genome[None], circ_medium, jnp.zeros_like(circ_medium))
         return jnp.einsum(
             "gts,gis->git", matrix, window, preferred_element_type=jnp.float32
         ).astype(jnp.bfloat16)
 
     signal = lax.map(medium_block, jnp.arange(tile_count, dtype=jnp.int32))
-    long_toeplitz, outward, inward, decay_re, decay_im = modal_tables(modal_poles)
-    toeplitz_upper, toeplitz_lower = long_toeplitz
     inward_upper, inward_lower = split_table(inward)
     tile_segs = segments.reshape(tile_count, tile_rows)
     before = segment_ids(
@@ -211,7 +211,7 @@
 
     def intra_block(inputs):
         block_in, own_segs = inputs
-        same_genome = (own_segs[:, None] == own_segs[None, :])[None]
+        same_genome = ((own_segs[:, None] == own_segs[None, :]) & long_band)[None]
         upper = jnp.where(same_genome, toeplitz_upper, jnp.zeros_like(toeplitz_upper))
         lower = jnp.where(same_genome, toeplitz_lower, jnp.zeros_like(toeplitz_lower))
         return jnp.einsum(

time: 226 us -> 222 us (0.982)
  other arithmetic: 35.8 us -> 47.6 us
  matrix products: 55.5 us -> 45.5 us
  local copies, waits for them, and re-layouts: 62.8 us -> 56.5 us
    dot_general x2 -> x1, matrix products: 13.9 us -> 3.81 us  [circulants(): picked = jnp.dot(table.T, one_hot, preferred_element_type=jnp.float32)]
    concatenate x0 -> x1, other arithmetic: none -> 8.6 us  [per_device(): jnp.concatenate((circ[:group_count], circ[:group_count]), axis=2)]
    slice x1 -> x0, local copies, waits for them, and re-layouts: 7.35 us -> none  [lag_select(): picked = jnp.dot(lead, one_hot, preferred_element_type=jnp.float32)[:width]]
  transfers between devices with their start and end apart: 4 -> 4, of which waited for: 1 -> 1; matrix products, arithmetic and copies ran while one was open for 40% -> 38% of each run, Pallas kernels for 0% -> 0%
where the time goes in v5:
time: 222 us; the launch traced here: 221 us
  local copies, waits for them, and re-layouts  56.5 us (25%)
  other arithmetic  47.6 us (21%)
  matrix products  45.5 us (20%)
  blocking collectives  23.6 us (11%)
  waiting for transfers between devices  18.6 us (8%)
  between operations  15.1 us (7%)
  starting transfers between devices  12.1 us (5%)
    unnamed x65, local copies, waits for them, and re-layouts  27.3 us
    reduce_scatter x1, waiting for transfers between devices, per_device(): lax.psum_scatter(partial_value, lanes, scatter_dimension=0, tiled=True)  18.6 us
    dot_general x2, matrix products, medium_block(): jnp.einsum('gts,gis->git', matrix, window, preferred_element_type=jnp.flo...  12.2 us
    ppermute x3, starting transfers between devices, from_behind(): return lax.ppermute(shard, axis, pairs)  12.1 us
    psum x1, blocking collectives, per_device(): totals = lax.psum(genome_part, 'seq')  11.9 us
    mul x1, other arithmetic, modal_tables(): power_im = magnitude * jnp.sin(powers * angles[None])  9.48 us
    dot_general x2, matrix products, intra_block(): jnp.einsum('gts,gis->git', lower, block_in, preferred_element_type=jnp.fl...  9.22 us
    concatenate x1, other arithmetic, per_device(): jnp.concatenate((circ[:group_count], circ[:group_count]), axis=2)  8.6 us
  transfers between devices with their start and end apart: 4, of which 1 were waited for; matrix products, arithmetic and copies ran while one was open for 38% of the time, Pallas kernels for 0%

profile of v5, /device:TPU:0, one launch (start us, length us, event | category | flops | bytes accessed | tf_op | source)
XLA Modules:
  0.0 220.6 jit_solution(15880490417131114398)
XLA Ops:
  9.8 6.0 %collective-permute-start = (bf16[2,136,2048]{2,1,0:T(8,128)(2,1)}, bf16[2,136,2048]{2,1,0:T(8,128)(2,1)}, u32[]{:S(2)}, u32[]{:S(2)}) collective-permute-start(bf16[2,136,2048]{2,1,0:T(8,128)(2,1)} %pad_maximum_fusion.1), channel_id=1, source_target_pairs={{0,4},{4,8},{8,12},{1,5},{5,9},{9,13},{2,6},{6,10},{10,14},{3,7},{... | collective-permute-start | bytes 3342344 | tf_op jit(solution)/shard_map/ppermute | solution.py:18
  16.6 9.5 %fusion.68 = (f32[129,128,16]{0,2,1:T(8,128)}, f32[129,128,16]{0,2,1:T(8,128)S(1)}, f32[129,128,16]{0,2,1:T(8,128)}) fusion(f32[128,16]{1,0:T(8,128)S(1)} %copy.71, f32[129]{0:T(256)S(1)} %iota_convert_fusion, f32[128,16]{1,0:T(8,128)S(1)} %copy.70, f32[129]{0:T(256)S(1)} %fusion.104, f32[128,16]{1,0:T(8,128)S(1)} %copy.72, f32[128,16]{1,0:T(8,128)S(1)} %copy.69), kind=kLoop, calls=%fused_computation.86 | loop fusion | flops 1849344 | bytes 3204104 | tf_op jit(solution)/shard_map/mul | solution.py:94
  27.6 3.8 %convolution_convert_fusion = bf16[384,16384]{1,0:T(8,128)(2,1)S(1)} fusion(s32[16384]{0:T(1024)S(1)} %add_select_fusion, s32[128]{0:T(128)S(1)} %iota.67, bf16[128,128]{0,1:T(8,128)(2,1)S(1)} %get-tuple-element.339, bf16[128,128]{0,1:T(8,128)(2,1)S(1)} %get-tuple-element.340, bf16[128,128]{0,1:T(8,128)(2,1)S(1)} %copy.73), kind=kOutput, calls=%fused_computation.49 | convolution fusion | flops 1619296256 | bytes 12747264 | tf_op jit(solution)/shard_map/dot_general | solution.py:82
  31.4 4.8 %slice_bitcast_fusion = (bf16[16,8,128,128]{3,1,2,0:T(8,128)(2,1)}, bf16[16,8,128,128]{3,1,2,0:T(8,128)(2,1)}, bf16[16,8,128,128]{3,1,2,0:T(8,128)(2,1)}) fusion(bf16[384,16384]{1,0:T(8,128)(2,1)S(1)} %convolution_convert_fusion), kind=kLoop, calls=%fused_computation.52 | loop fusion | bytes 25165824
  36.9 4.5 %fusion.85 = (f32[128,128,16]{0,2,1:T(8,128)}, f32[128,128,16]{0,2,1:T(8,128)}, f32[128,128,16]{0,2,1:T(8,128)}) fusion(f32[129,128,16]{0,2,1:T(8,128)} %get-tuple-element.375, f32[129,128,16]{0,2,1:T(8,128)} %get-tuple-element.373, f32[128,16]{1,0:T(8,128)S(1)} %copy.72, f32[128,16]{1,0:T(8,128)S(1)} %copy.69), kind=kLoop, calls=%fused_computation.110 | loop fusion | flops 1048576 | bytes 7356416 | tf_op jit(solution)/shard_map/neg | solution.py:99
  45.5 5.5 %copy.93 = bf16[16,8,128,128]{3,2,1,0:T(8,128)(2,1)} copy(bf16[16,8,128,128]{3,1,2,0:T(8,128)(2,1)} %get-tuple-element.349) | data formatting | bytes 8388608
  58.9 8.6 %pad_maximum_fusion = bf16[128,128,256]{2,1,0:T(8,128)(2,1)} fusion(bf16[128,128,128]{2,1,0:T(8,128)(2,1)} %bitcast.181), kind=kLoop, calls=%fused_computation.50 | loop fusion | flops 16777216 | bytes 12582912 | tf_op jit(solution)/shard_map/concatenate | solution.py:184
  69.9 5.3 %fusion.76 = bf16[2048,384]{0,1:T(8,128)(2,1)} fusion(f32[384]{0:T(512)S(1)} %get-tuple-element.392, f32[392,2048]{1,0:T(8,128)S(1)} %convert_multiply_fusion, f32[2048]{0:T(1024)S(1)} %bitcast.202, f32[384]{0:T(512)S(1)} %get-tuple-element.388, f32[2048]{0:T(1024)S(1)} %bitcast.203, f32[384]{0:T(512)S(1)} %get-tuple-element.389, f32[2048]{0:T(1024)S(1)} %bitcast.198, ...), kind=kLoop, calls=%fused_computation.102 | loop fusion | flops 15728640 | bytes 23659520 | tf_op jit(solution)/shard_map/transpose | solution.py:177
  77.8 15.3 %while.50 = (s32[]{:T(128)}, bf16[2,128,16,128]{3,2,1,0:T(8,128)(2,1)S(1)}, s32[2]{0:T(128)S(1)}, bf16[128,16,384]{2,1,0:T(8,128)(2,1)}, s32[256]{0:T(256)S(1)},...) while((s32[]{:T(128)}, ...), condition=%wide.region_6.7_spmd.clone.clone, body=%wide.region_5.6_spmd.clone.sunk.clone | while | flops 138870784 | bytes 10032828 | solution.py:205
  79.3 6.1 %fusion.146 = bf16[2,128,16,128]{3,2,1,0:T(8,128)(2,1)S(1)} fusion(bf16[2,128,16,128]{3,2,1,0:T(8,128)(2,1)S(1)} %get-tuple-element.676, s32[]{:T(128)} %get-tuple-element.675, bf16[128,128,256]{2,1,0:T(8,128)(2,1)} %get-tuple-element.690, pred[128,256]{1,0:T(8,128)(4,1)S(1)} %fusion.145, bf16[128,16,384]{2,1,0:T(8,128)(2,1)} %get-tuple-element.687, ...), kind=kOutput, calls=%fused_computation.29.clone.1.clone | convolution fusion | flops 138674176 | bytes 9994756 | tf_op jit(solution)/shard_map/while/body/eval_jaxpr/gts,gis->git/dot_general | solution.py:201
  87.0 6.1 %fusion.146 = bf16[2,128,16,128]{3,2,1,0:T(8,128)(2,1)S(1)} fusion(bf16[2,128,16,128]{3,2,1,0:T(8,128)(2,1)S(1)} %get-tuple-element.676, s32[]{:T(128)} %get-tuple-element.675, bf16[128,128,256]{2,1,0:T(8,128)(2,1)} %get-tuple-element.690, pred[128,256]{1,0:T(8,128)(4,1)S(1)} %fusion.145, bf16[128,16,384]{2,1,0:T(8,128)(2,1)} %get-tuple-element.687, ...), kind=kOutput, calls=%fused_computation.29.clone.1.clone | convolution fusion | flops 138674176 | bytes 9994756 | tf_op jit(solution)/shard_map/while/body/eval_jaxpr/gts,gis->git/dot_general | solution.py:201
  97.6 3.4 %copy.78 = f32[2,128,16,32]{1,3,2,0:T(8,128)} copy(f32[2,128,16,32]{3,2,0,1:T(8,128)} %add_bitcast_fusion) | data formatting | bytes 1048576
  101.0 6.2 %while.51 = (s32[]{:T(128)}, f32[128,16]{0,1:T(8,128)S(1)}, f32[128,16]{0,1:T(8,128)S(1)}, f32[128,16,16]{0,2,1:T(8,128)S(1)}, f32[128,16,16]{0,2,1:T(8,128)S(1)...) while((s32[]{:T(128)}, f32[128,16]{0,1:T(8,128)S(1)}, ...), condition=%wide.region_11.12_spmd.clone.clone, body=%wide.region_10.11_spmd.clone.sunk.clone | while | flops 421891 | bytes 1999523 | solution.py:248
  111.2 5.5 %copy.94 = bf16[16,8,128,128]{3,2,1,0:T(8,128)(2,1)} copy(bf16[16,8,128,128]{3,1,2,0:T(8,128)(2,1)} %get-tuple-element.348) | data formatting | bytes 8388608
  129.6 18.9 %while.49 = (s32[]{:T(128)}, f32[2,128,16,128]{3,2,0,1:T(8,128)}, bf16[2,128,16,128]{3,2,1,0:T(8,128)(2,1)S(1)}, s32[2,128]{1,0:T(2,128)}, pred[128,128]{1,0:T(8...) while((s32[]{:T(128)}, f32[2,128,16,128]{3,2,0,1:T(8,128)}, ...), condition=%wide.region_8.9_spmd.clone, body=%wide.region_7.8_spmd.sunk.clone | while | flops 138706944 | bytes 29428336 | solution.py:221
  131.2 4.6 %fusion.141 = f32[128,16,128]{2,1,0:T(8,128)S(1)} fusion(bf16[128,128,128]{2,1,0:T(8,128)(2,1)} %get-tuple-element.713, pred[128,128]{1,0:T(8,128)(4,1)S(1)} %compare_and_fusion.3, bf16[2,128,16,128]{3,2,1,0:T(8,128)(2,1)S(1)} %get-tuple-element.709, s32[]{:T(128)} %get-tuple-element.700), kind=kOutput, calls=%fused_computation.1.clone.1.clone | convolution fusion | flops 69206016 | bytes 5783556 | tf_op jit(solution)/shard_map/while/body/eval_jaxpr/gts,gis->git/dot_general | solution.py:219
  140.6 4.6 %fusion.141 = f32[128,16,128]{2,1,0:T(8,128)S(1)} fusion(bf16[128,128,128]{2,1,0:T(8,128)(2,1)} %get-tuple-element.713, pred[128,128]{1,0:T(8,128)(4,1)S(1)} %compare_and_fusion.3, bf16[2,128,16,128]{3,2,1,0:T(8,128)(2,1)S(1)} %get-tuple-element.709, s32[]{:T(128)} %get-tuple-element.700), kind=kOutput, calls=%fused_computation.1.clone.1.clone | convolution fusion | flops 69206016 | bytes 5783556 | tf_op jit(solution)/shard_map/while/body/eval_jaxpr/gts,gis->git/dot_general | solution.py:219
  152.4 3.9 %copy.79 = f32[2,128,16,32]{3,2,0,1:T(8,128)} copy(f32[2,128,16,32]{1,3,2,0:T(8,128)} %pad_maximum_fusion.2) | data formatting | bytes 1048576 | tf_op jit(solution)/shard_map/concatenate | solution.py:266
  156.3 5.3 %fusion.74 = f32[128,16,2,128]{3,1,2,0:T(8,128)S(1)} fusion(f32[2,128,16,128]{3,2,0,1:T(8,128)} %get-tuple-element.156, f32[2,128,16,32]{3,2,0,1:T(8,128)} %copy.79, f32[128,128,16]{0,2,1:T(8,128)} %get-tuple-element.352, f32[128,128,16]{0,2,1:T(8,128)} %get-tuple-element.350, bf16[2,128,16,128]{3,2,1,0:T(8,128)(2,1)S(1)} %get-tuple-element.754, ...), kind=kOutput, calls=%fused_computation.96 | convolution fusion | flops 204472320 | bytes 7873536 | tf_op jit(solution)/shard_map/gtm,jgim->jgit/dot_general | solution.py:263
  164.4 6.0 %psum.14 = f32[256]{0:T(256)S(1)} all-reduce(f32[256]{0:T(256)S(1)} %fusion.64), channel_id=1, replica_groups=mesh['groups'=2,'seq'=4,'chan'=2,'rep'=2] {'chan','rep'}, use_global_device_ids=true, to_apply=%region_13.14 | all-reduce | flops 256 | bytes 2048 | tf_op jit(solution)/shard_map/psum | solution.py:279
  170.5 3.8 %fusion.82 = f32[256,512]{1,0:T(8,128)} fusion(bf16[2048,512]{1,0:T(8,128)(2,1)S(1)} %copy-done, f32[2048]{0:T(1024)S(1)} %copy-done.24, f32[256]{0:T(256)S(1)} %add_rsqrt_fusion, f32[256,8,2,128]{3,2,1,0:T(2,128)} %bitcast.183, bf16[256,2048]{0,1:T(8,128)(2,1)S(1)} %copy-done.7), kind=kOutput, calls=%fused_computation.107 | convolution fusion | flops 540540928 | bytes 5776384 | tf_op jit(solution)/shard_map/dot_general | solution.py:135
  175.7 18.6 %reduce-scatter.2.cloned.1.call-done = f32[64,512]{1,0:T(8,128)} async-done(((f32[256,512]{1,0:T(8,128)}), f32[64,512]{1,0:T(8,128)}) %reduce-scatter.2.cloned.1.call-update) | async-done | bytes 131088 | tf_op jit(solution)/shard_map/reduce_scatter | solution.py:288
  195.5 5.7 %all-reduce = f32[256]{0:T(256)S(1)} all-reduce(f32[256]{0:T(256)S(1)} %subtract_dynamic-update-slice_fusion), channel_id=1, replica_groups=mesh['groups'=2,'seq'=4,'chan'=2,'rep'=2] {'chan','rep'}, use_global_device_ids=true, to_apply=%add | all-reduce | flops 256 | bytes 2048
  201.3 11.9 %psum.15 = f32[8]{0:T(128)S(1)} all-reduce(f32[8]{0:T(128)S(1)} %select_reduce_fusion.1), channel_id=1, replica_groups=mesh['groups'=2,'seq'=4,'chan'=2,'rep'=2] {'seq'}, use_global_device_ids=true, to_apply=%region_18.19 | all-reduce | flops 8 | bytes 64 | tf_op jit(solution)/shard_map/psum | solution.py:300
  (176 shorter events, 70.5 us)
Async XLA Ops:
  7.2 163.3 %copy-start = (bf16[2048,512]{1,0:T(8,128)(2,1)S(1)}, bf16[2048,512]{1,0:T(8,128)(2,1)}, u32[]{:S(2)}) copy-start(bf16[2048,512]{1,0:T(8,128)(2,1)} %param.25) | copy-start | bytes 6291460
  7.2 8.7 %copy-start.26 = (s32[8]{0:T(128)S(1)}, s32[8]{0:T(128)}, u32[]{:S(2)}) copy-start(s32[8]{0:T(128)} %param.27) | copy-start | bytes 100
  7.2 9.0 %copy-start.14 = (f32[4,128,16]{1,2,0:T(8,128)S(1)}, f32[4,128,16]{1,2,0:T(8,128)}, u32[]{:S(2)}) copy-start(f32[4,128,16]{1,2,0:T(8,128)} %param.22) | copy-start | bytes 98308
  7.2 187.1 %reduce-scatter.2.cloned.1.call-start = ((), (), s32[]{:S(2)}) async-start(), calls=%async_computation.1 | async-start | bytes 655360 | tf_op jit(solution)/shard_map/reduce_scatter | solution.py:288
  9.8 57.7 %collective-permute-start = (bf16[2,136,2048]{2,1,0:T(8,128)(2,1)}, bf16[2,136,2048]{2,1,0:T(8,128)(2,1)}, u32[]{:S(2)}, u32[]{:S(2)}) collective-permute-start(bf16[2,136,2048]{2,1,0:T(8,128)(2,1)} %pad_maximum_fusion.1), channel_id=1, source_target_pairs={{0,4},{4,8},{8,12},{1,5},{5,9},{9,13},{2,6},{6,10},{10,14},{3,7},{... | collective-permute-start | bytes 3342344 | tf_op jit(solution)/shard_map/ppermute | solution.py:18
  53.3 5.5 %copy-start.13 = (bf16[7,2048]{1,0:T(8,128)(2,1)S(1)}, bf16[7,2048]{1,0:T(8,128)(2,1)}, u32[]{:S(2)}) copy-start(bf16[7,2048]{1,0:T(8,128)(2,1)} %param.20) | copy-start | bytes 86020
  107.2 9.4 %copy-start.16 = (f32[2,128,16]{1,2,0:T(8,128)}, f32[2,128,16]{1,2,0:T(8,128)S(1)}, u32[]{:S(2)}) copy-start(f32[2,128,16]{1,2,0:T(8,128)S(1)} %get-tuple-element.158) | copy-start | bytes 49156
  107.3 9.4 %copy-start.17 = (f32[2,128,16]{1,2,0:T(8,128)}, f32[2,128,16]{1,2,0:T(8,128)S(1)}, u32[]{:S(2)}) copy-start(f32[2,128,16]{1,2,0:T(8,128)S(1)} %get-tuple-element.163) | copy-start | bytes 49156
  108.0 15.6 %collective-permute-start.1 = (f32[128,544]{0,1:T(8,128)}, f32[128,544]{0,1:T(8,128)}, u32[]{:S(2)}, u32[]{:S(2)}) collective-permute-start(f32[128,544]{0,1:T(8,128)} %pad_maximum_fusion.3), channel_id=1, source_target_pairs={{0,4},{4,8},{8,12},{1,5},{5,9},{9,13},{2,6},{6,10},{10,14},{3,7},{... | collective-permute-start | bytes 835592 | tf_op jit(solution)/shard_map/ppermute | solution.py:18
  111.2 5.5 %copy-start.1 = (bf16[16,8,128,128]{3,1,2,0:T(8,128)(2,1)S(1)}, bf16[16,8,128,128]{3,1,2,0:T(8,128)(2,1)}, u32[]{:S(2)}) copy-start(bf16[16,8,128,128]{3,1,2,0:T(8,128)(2,1)} %get-tuple-element.347) | copy-start | bytes 12582916
  116.7 3.2 %copy-start.18 = (f32[2048]{0:T(1024)S(1)}, f32[2048]{0:T(1024)}, u32[]{:S(2)}) copy-start(f32[2048]{0:T(1024)} %param.23) | copy-start | bytes 24580
  126.7 21.9 %collective-permute-start.2 = (f32[128,544]{0,1:T(8,128)}, f32[128,544]{0,1:T(8,128)}, u32[]{:S(2)}, u32[]{:S(2)}) collective-permute-start(f32[128,544]{0,1:T(8,128)} %pad_maximum_fusion.4), channel_id=1, source_target_pairs={{0,8},{4,12},{1,9},{5,13},{2,10},{6,14},{3,11},{7,15},{16,24},{20,... | collective-permute-start | bytes 835592 | tf_op jit(solution)/shard_map/ppermute | solution.py:18
  129.6 19.9 %copy-start.11 = (f32[128,256]{0,1:T(8,128)S(1)}, f32[128,256]{0,1:T(8,128)}, u32[]{:S(2)}) copy-start(f32[128,256]{0,1:T(8,128)} %copy-done.10) | copy-start | bytes 393220
  131.2 4.6 %copy-start.6 = (bf16[128,128,128]{2,1,0:T(8,128)(2,1)S(1)}, bf16[128,128,128]{2,1,0:T(8,128)(2,1)}, u32[]{:S(2)}) copy-start(bf16[128,128,128]{2,1,0:T(8,128)(2,1)} %get-tuple-element.712) | copy-start | bytes 12582916 | tf_op jit(solution)/shard_map/while
  140.6 4.6 %copy-start.6 = (bf16[128,128,128]{2,1,0:T(8,128)(2,1)S(1)}, bf16[128,128,128]{2,1,0:T(8,128)(2,1)}, u32[]{:S(2)}) copy-start(bf16[128,128,128]{2,1,0:T(8,128)(2,1)} %get-tuple-element.712) | copy-start | bytes 12582916 | tf_op jit(solution)/shard_map/while
  151.5 4.8 %copy-start.12 = (f32[128,16]{1,0:T(8,128)S(1)}, f32[128,16]{1,0:T(8,128)}, u32[]{:S(2)}) copy-start(f32[128,16]{1,0:T(8,128)} %mul.578) | copy-start | bytes 24580
  151.5 4.8 %copy-start.19 = (f32[2,128]{1,0:T(2,128)S(1)}, f32[2,128]{1,0:T(2,128)}, u32[]{:S(2)}) copy-start(f32[2,128]{1,0:T(2,128)} %get-tuple-element.393) | copy-start | bytes 3076
  161.6 2.4 %copy-start.7 = (bf16[256,2048]{0,1:T(8,128)(2,1)S(1)}, bf16[256,2048]{0,1:T(8,128)(2,1)}, u32[]{:S(2)}) copy-start(bf16[256,2048]{0,1:T(8,128)(2,1)} %copy.67) | copy-start | bytes 3145732
  162.7 7.7 %copy-start.24 = (f32[2048]{0:T(1024)S(1)}, f32[2048]{0:T(1024)}, u32[]{:S(2)}) copy-start(f32[2048]{0:T(1024)} %param.24) | copy-start | bytes 24580
  170.4 3.9 %copy-start.25 = (s32[256]{0:T(256)S(1)}, s32[256]{0:T(256)}, u32[]{:S(2)}) copy-start(s32[256]{0:T(256)} %param.26) | copy-start | bytes 3076
  170.4 4.0 %copy-start.28 = (u32[32]{0:T(128)S(1)}, u32[32]{0:T(128)}, u32[]{:S(2)}) copy-start(u32[32]{0:T(128)} %constant.127) | copy-start | bytes 388
  170.5 30.7 %copy-start.21 = (s32[256]{0:T(256)S(1)}, s32[256]{0:T(256)}, u32[]{:S(2)}) copy-start(s32[256]{0:T(256)} %copy-done.20) | copy-start | bytes 3076
  170.5 42.7 %copy-start.27 = (s32[8]{0:T(128)S(1)}, s32[8]{0:T(128)}, u32[]{:S(2)}) copy-start(s32[8]{0:T(128)} %param.27) | copy-start | bytes 100
  201.2 12.5 %copy-start.22 = (f32[256]{0:T(256)}, f32[256]{0:T(256)S(1)}, u32[]{:S(2)}) copy-start(f32[256]{0:T(256)S(1)} %all-reduce) | copy-start | bytes 3076
  (10 other events, 17.7 us)
Sparse Core Ops, SparseCore 0:
  174.5 19.7 reduce-scatter.1

commit v6 on v5

--- a/solution.py
+++ b/solution.py
@@ -180,10 +180,10 @@
     )
 
     long_toeplitz, outward, inward, decay_re, decay_im = modal_tables(modal_poles)
-    circ = circulants(jnp.concatenate((medium_taps, long_toeplitz[0], long_toeplitz[1]), axis=1))
-    circ_medium = jnp.concatenate((circ[:group_count], circ[:group_count]), axis=2)
-    toeplitz_upper = circ[group_count : 2 * group_count]
-    toeplitz_lower = circ[2 * group_count :]
+    circ_medium = circulants(medium_taps)
+    circ_long = circulants(jnp.concatenate(long_toeplitz, axis=1))
+    toeplitz_upper = circ_long[:group_count]
+    toeplitz_lower = circ_long[group_count:]
     lag_band = (
         jnp.arange(tile_rows, dtype=jnp.int32)[:, None] + tile_rows
         - jnp.arange(2 * tile_rows, dtype=jnp.int32)[None, :]
@@ -197,10 +197,16 @@
         window_segs = lax.dynamic_slice_in_dim(medium_segs, start, 2 * tile_rows, 0)
         own_segs = lax.dynamic_slice_in_dim(segments, start, tile_rows, 0)
         same_genome = (own_segs[:, None] == window_segs[None, :]) & medium_band
-        matrix = jnp.where(same_genome[None], circ_medium, jnp.zeros_like(circ_medium))
-        return jnp.einsum(
-            "gts,gis->git", matrix, window, preferred_element_type=jnp.float32
-        ).astype(jnp.bfloat16)
+        halves = []
+        for half in range(2):
+            cols = slice(half * tile_rows, (half + 1) * tile_rows)
+            matrix = jnp.where(same_genome[None, :, cols], circ_medium, jnp.zeros_like(circ_medium))
+            halves.append(
+                jnp.einsum(
+                    "gts,gis->git", matrix, window[:, :, cols], preferred_element_type=jnp.float32
+                )
+            )
+        return (halves[0] + halves[1]).astype(jnp.bfloat16)
 
     signal = lax.map(medium_block, jnp.arange(tile_count, dtype=jnp.int32))
     inward_upper, inward_lower = split_table(inward)

time: 222 us -> 227 us (1.023)
  matrix products: 45.5 us -> 56.8 us
  other arithmetic: 47.6 us -> 38.8 us
    concatenate x1 -> x0, other arithmetic: 8.6 us -> none  [per_device(): jnp.concatenate((circ[:group_count], circ[:group_count]), axis=2)]
    dot_general x1 -> x2, matrix products: 3.81 us -> 10.8 us  [circulants(): picked = jnp.dot(table.T, one_hot, preferred_element_type=jnp.float32)]
    dot_general x2 -> x4, matrix products: 12.2 us -> 16.4 us  [medium_block(): jnp.einsum('gts,gis->git', matrix, window[:, :, cols], preferred_element_...]
    unnamed x65 -> x68, local copies, waits for them, and re-layouts: 27.3 us -> 29.4 us
  transfers between devices with their start and end apart: 4 -> 4, of which waited for: 1 -> 1; matrix products, arithmetic and copies ran while one was open for 38% -> 37% of each run, Pallas kernels for 0% -> 0%
where the time goes in v6:
time: 227 us; the launch traced here: 225 us
  local copies, waits for them, and re-layouts  58.6 us (26%)
  matrix products  56.8 us (25%)
  other arithmetic  38.8 us (17%)
  blocking collectives  23.6 us (10%)
  waiting for transfers between devices  18.6 us (8%)
  between operations  15.1 us (7%)
  starting transfers between devices  12.3 us (5%)
    unnamed x68, local copies, waits for them, and re-layouts  29.4 us
    reduce_scatter x1, waiting for transfers between devices, per_device(): lax.psum_scatter(partial_value, lanes, scatter_dimension=0, tiled=True)  18.6 us
    dot_general x4, matrix products, medium_block(): jnp.einsum('gts,gis->git', matrix, window[:, :, cols], preferred_element_...  16.4 us
    ppermute x3, starting transfers between devices, from_behind(): return lax.ppermute(shard, axis, pairs)  12.3 us
    psum x1, blocking collectives, per_device(): totals = lax.psum(genome_part, 'seq')  11.9 us
    dot_general x2, matrix products, circulants(): picked = jnp.dot(table.T, one_hot, preferred_element_type=jnp.float32)  10.8 us
    dot_general x2, matrix products, intra_block(): jnp.einsum('gts,gis->git', lower, block_in, preferred_element_type=jnp.fl...  9.22 us
    mul x1, other arithmetic, modal_tables(): power_im = magnitude * jnp.sin(powers * angles[None])  7.98 us
  transfers between devices with their start and end apart: 4, of which 1 were waited for; matrix products, arithmetic and copies ran while one was open for 37% of the time, Pallas kernels for 0%

profile of v6, /device:TPU:0, one launch (start us, length us, event | category | flops | bytes accessed | tf_op | source)
XLA Modules:
  0.0 225.3 jit_solution(4984934244830057682)
XLA Ops:
  9.9 5.9 %collective-permute-start = (bf16[2,136,2048]{2,1,0:T(8,128)(2,1)}, bf16[2,136,2048]{2,1,0:T(8,128)(2,1)}, u32[]{:S(2)}, u32[]{:S(2)}) collective-permute-start(bf16[2,136,2048]{2,1,0:T(8,128)(2,1)} %pad_maximum_fusion), channel_id=1, source_target_pairs={{0,4},{4,8},{8,12},{1,5},{5,9},{9,13},{2,6},{6,10},{10,14},{3,7},{... | collective-permute-start | bytes 3342344 | tf_op jit(solution)/shard_map/ppermute | solution.py:18
  19.0 8.0 %fusion.81 = (f32[129,128,16]{0,2,1:T(8,128)S(1)}, f32[129,128,16]{0,2,1:T(8,128)S(1)}, f32[129,128,16]{0,2,1:T(8,128)S(1)}) fusion(f32[128,16]{1,0:T(8,128)S(1)} %copy.74, f32[129]{0:T(256)S(1)} %iota_convert_fusion, f32[128,16]{1,0:T(8,128)S(1)} %copy.73, f32[129]{0:T(256)S(1)} %fusion.115, f32[128,16]{1,0:T(8,128)S(1)} %copy.75, f32[128,16]{1,0:T(8,128)S(1)} %copy.72), kind=kLoop, calls=%fused_computation.96 | loop fusion | flops 1849344 | bytes 3204104 | tf_op jit(solution)/shard_map/mul | solution.py:94
  31.8 4.4 %convolution_convert_fusion.1 = bf16[16384,128]{1,0:T(8,128)(2,1)} fusion(bf16[128,128]{1,0:T(8,128)(2,1)S(1)} %copy-done.17, s32[16384]{0:T(1024)S(1)} %add_select_fusion, s32[128]{0:T(128)S(1)} %iota.69), kind=kOutput, calls=%fused_computation.58 | convolution fusion | flops 541065216 | bytes 4293120 | tf_op jit(solution)/shard_map/dot_general | solution.py:82
  39.7 6.6 %copy.71 = bf16[128,128,128]{2,1,0:T(8,128)(2,1)} copy(bf16[128,128,128]{0,2,1:T(8,128)(2,1)} %bitcast.180) | data formatting | bytes 8388608
  54.2 6.4 %convolution_convert_fusion = bf16[256,16384]{1,0:T(8,128)(2,1)} fusion(s32[16384]{0:T(1024)S(1)} %add_select_fusion, s32[128]{0:T(128)S(1)} %iota.69, bf16[128,128]{0,1:T(8,128)(2,1)S(1)} %get-tuple-element.371, bf16[128,128]{0,1:T(8,128)(2,1)} %get-tuple-element.372), kind=kOutput, calls=%fused_computation.57 | convolution fusion | flops 1080164352 | bytes 8520192 | tf_op jit(solution)/shard_map/dot_general | solution.py:82
  63.1 5.3 %fusion.89 = bf16[2048,384]{0,1:T(8,128)(2,1)} fusion(f32[384]{0:T(512)S(1)} %get-tuple-element.425, f32[392,2048]{1,0:T(8,128)S(1)} %convert_multiply_fusion, f32[2048]{0:T(1024)S(1)} %bitcast.203, f32[384]{0:T(512)S(1)} %get-tuple-element.421, f32[2048]{0:T(1024)S(1)} %bitcast.204, f32[384]{0:T(512)S(1)} %get-tuple-element.422, f32[2048]{0:T(1024)S(1)} %bitcast.199, ...), kind=kLoop, calls=%fused_computation.112 | loop fusion | flops 15728640 | bytes 23659520 | tf_op jit(solution)/shard_map/transpose | solution.py:177
  70.9 19.5 %while.50 = (s32[]{:T(128)}, bf16[2,128,16,128]{3,2,1,0:T(8,128)(2,1)S(1)}, s32[2]{0:T(128)S(1)}, bf16[128,16,384]{2,1,0:T(8,128)(2,1)}, s32[256]{0:T(256)S(1)},...) while((s32[]{:T(128)}, ...), condition=%wide.region_5.6_spmd.clone.clone, body=%wide.region_4.5_spmd.clone.sunk.clone | while | flops 139132928 | bytes 28972776 | solution.py:211
  72.5 4.8 %fusion.170 = f32[128,16,128]{2,1,0:T(8,128)S(1)} fusion(bf16[128,128,128]{2,1,0:T(8,128)(2,1)} %get-tuple-element.730, pred[128,128]{1,0:T(8,128)(4,1)S(1)} %get-tuple-element.651, bf16[128,16,384]{2,1,0:T(8,128)(2,1)} %get-tuple-element.727, s32[]{:T(128)S(6)} %add.412), kind=kOutput, calls=%fused_computation.23.clone.1.clone | convolution fusion | flops 69206016 | bytes 5783556 | tf_op jit(solution)/shard_map/while/body/eval_jaxpr/gts,gis->git/dot_general | solution.py:205
  77.3 3.4 %fusion.171 = bf16[2,128,16,128]{3,2,1,0:T(8,128)(2,1)S(1)} fusion(bf16[2,128,16,128]{3,2,1,0:T(8,128)(2,1)S(1)} %get-tuple-element.716, s32[]{:T(128)} %get-tuple-element.715, f32[128,16,128]{2,1,0:T(8,128)S(1)} %fusion.170, bf16[128,128,128]{2,1,0:T(8,128)(2,1)S(1)} %copy-done.8, pred[128,128]{1,0:T(8,128)(4,1)S(1)} %get-tuple-element.652, ...), kind=kOutput, calls=%fused_computation.34.clone.1.clone | convolution fusion | flops 69730304 | bytes 6308356 | tf_op jit(solution)/shard_map/while/body/eval_jaxpr/gts,gis->git/dot_general | solution.py:205
  82.3 4.8 %fusion.170 = f32[128,16,128]{2,1,0:T(8,128)S(1)} fusion(bf16[128,128,128]{2,1,0:T(8,128)(2,1)} %get-tuple-element.730, pred[128,128]{1,0:T(8,128)(4,1)S(1)} %get-tuple-element.651, bf16[128,16,384]{2,1,0:T(8,128)(2,1)} %get-tuple-element.727, s32[]{:T(128)S(6)} %add.412), kind=kOutput, calls=%fused_computation.23.clone.1.clone | convolution fusion | flops 69206016 | bytes 5783556 | tf_op jit(solution)/shard_map/while/body/eval_jaxpr/gts,gis->git/dot_general | solution.py:205
  95.0 3.4 %copy.80 = f32[2,128,16,32]{1,3,2,0:T(8,128)} copy(f32[2,128,16,32]{3,2,0,1:T(8,128)} %add_bitcast_fusion) | data formatting | bytes 1048576
  98.4 7.4 %while.51 = (s32[]{:T(128)}, f32[128,16]{0,1:T(8,128)S(1)}, f32[128,16]{0,1:T(8,128)S(1)}, f32[128,16,16]{0,2,1:T(8,128)S(1)}, f32[128,16,16]{0,2,1:T(8,128)S(1)...) while((s32[]{:T(128)}, f32[128,16]{0,1:T(8,128)S(1)}, ...), condition=%wide.region_11.12_spmd.clone.clone, body=%wide.region_10.11_spmd.clone.sunk.clone | while | flops 421891 | bytes 2000031 | solution.py:254
  109.7 5.8 %slice_bitcast_fusion = (bf16[16,8,128,128]{3,1,2,0:T(8,128)(2,1)}, bf16[16,8,128,128]{3,1,2,0:T(8,128)(2,1)}) fusion(bf16[256,16384]{1,0:T(8,128)(2,1)} %convolution_convert_fusion), kind=kLoop, calls=%fused_computation.61 | loop fusion | bytes 16777216
  115.6 5.5 %copy.95 = bf16[16,8,128,128]{3,2,1,0:T(8,128)(2,1)} copy(bf16[16,8,128,128]{3,1,2,0:T(8,128)(2,1)} %get-tuple-element.382) | data formatting | bytes 8388608
  134.3 19.1 %while.49 = (s32[]{:T(128)}, f32[2,128,16,128]{3,2,0,1:T(8,128)}, bf16[2,128,16,128]{3,2,1,0:T(8,128)(2,1)S(1)}, s32[2,128]{1,0:T(2,128)}, pred[128,128]{1,0:T(8...) while((s32[]{:T(128)}, f32[2,128,16,128]{3,2,0,1:T(8,128)}, ...), condition=%wide.region_8.9_spmd.clone, body=%wide.region_7.8_spmd.sunk.clone | while | flops 138706944 | bytes 29428336 | solution.py:227
  135.8 4.6 %fusion.162 = f32[128,16,128]{2,1,0:T(8,128)S(1)} fusion(bf16[128,128,128]{2,1,0:T(8,128)(2,1)} %get-tuple-element.753, pred[128,128]{1,0:T(8,128)(4,1)S(1)} %compare_and_fusion.3, bf16[2,128,16,128]{3,2,1,0:T(8,128)(2,1)S(1)} %get-tuple-element.749, s32[]{:T(128)} %get-tuple-element.740), kind=kOutput, calls=%fused_computation.1.clone.1.clone | convolution fusion | flops 69206016 | bytes 5783556 | tf_op jit(solution)/shard_map/while/body/eval_jaxpr/gts,gis->git/dot_general | solution.py:225
  145.3 4.6 %fusion.162 = f32[128,16,128]{2,1,0:T(8,128)S(1)} fusion(bf16[128,128,128]{2,1,0:T(8,128)(2,1)} %get-tuple-element.753, pred[128,128]{1,0:T(8,128)(4,1)S(1)} %compare_and_fusion.3, bf16[2,128,16,128]{3,2,1,0:T(8,128)(2,1)S(1)} %get-tuple-element.749, s32[]{:T(128)} %get-tuple-element.740), kind=kOutput, calls=%fused_computation.1.clone.1.clone | convolution fusion | flops 69206016 | bytes 5783556 | tf_op jit(solution)/shard_map/while/body/eval_jaxpr/gts,gis->git/dot_general | solution.py:225
  157.2 3.9 %copy.81 = f32[2,128,16,32]{3,2,0,1:T(8,128)} copy(f32[2,128,16,32]{1,3,2,0:T(8,128)} %pad_maximum_fusion.1) | data formatting | bytes 1048576 | tf_op jit(solution)/shard_map/concatenate | solution.py:272
  161.1 5.3 %fusion.87 = f32[128,16,2,128]{3,1,2,0:T(8,128)S(1)} fusion(f32[2,128,16,128]{3,2,0,1:T(8,128)} %get-tuple-element.156, f32[2,128,16,32]{3,2,0,1:T(8,128)} %copy.81, f32[128,128,16]{0,2,1:T(8,128)} %get-tuple-element.385, f32[128,128,16]{0,2,1:T(8,128)} %get-tuple-element.383, bf16[2,128,16,128]{3,2,1,0:T(8,128)(2,1)S(1)} %get-tuple-element.794, ...), kind=kOutput, calls=%fused_computation.106 | convolution fusion | flops 204472320 | bytes 7873536 | tf_op jit(solution)/shard_map/gtm,jgim->jgit/dot_general | solution.py:269
  169.2 6.0 %psum.14 = f32[256]{0:T(256)S(1)} all-reduce(f32[256]{0:T(256)S(1)} %fusion.77), channel_id=1, replica_groups=mesh['groups'=2,'seq'=4,'chan'=2,'rep'=2] {'chan','rep'}, use_global_device_ids=true, to_apply=%region_13.14 | all-reduce | flops 256 | bytes 2048 | tf_op jit(solution)/shard_map/psum | solution.py:285
  175.3 3.8 %fusion.95 = f32[256,512]{1,0:T(8,128)} fusion(bf16[2048,512]{1,0:T(8,128)(2,1)S(1)} %copy-done, f32[2048]{0:T(1024)S(1)} %copy-done.26, f32[256]{0:T(256)S(1)} %add_rsqrt_fusion, f32[256,8,2,128]{3,2,1,0:T(2,128)} %bitcast.184, bf16[256,2048]{0,1:T(8,128)(2,1)S(1)} %copy-done.10), kind=kOutput, calls=%fused_computation.117 | convolution fusion | flops 540540928 | bytes 5776384 | tf_op jit(solution)/shard_map/dot_general | solution.py:135
  180.5 18.6 %reduce-scatter.2.cloned.1.call-done = f32[64,512]{1,0:T(8,128)} async-done(((f32[256,512]{1,0:T(8,128)}), f32[64,512]{1,0:T(8,128)}) %reduce-scatter.2.cloned.1.call-update) | async-done | bytes 131088 | tf_op jit(solution)/shard_map/reduce_scatter | solution.py:294
  200.2 5.7 %all-reduce = f32[256]{0:T(256)S(1)} all-reduce(f32[256]{0:T(256)S(1)} %subtract_dynamic-update-slice_fusion), channel_id=1, replica_groups=mesh['groups'=2,'seq'=4,'chan'=2,'rep'=2] {'chan','rep'}, use_global_device_ids=true, to_apply=%add | all-reduce | flops 256 | bytes 2048
  206.1 11.9 %psum.15 = f32[8]{0:T(128)S(1)} all-reduce(f32[8]{0:T(128)S(1)} %select_reduce_fusion.1), channel_id=1, replica_groups=mesh['groups'=2,'seq'=4,'chan'=2,'rep'=2] {'seq'}, use_global_device_ids=true, to_apply=%region_18.19 | all-reduce | flops 8 | bytes 64 | tf_op jit(solution)/shard_map/psum | solution.py:306
  (187 shorter events, 80.0 us)
Async XLA Ops:
  7.2 168.1 %copy-start = (bf16[2048,512]{1,0:T(8,128)(2,1)S(1)}, bf16[2048,512]{1,0:T(8,128)(2,1)}, u32[]{:S(2)}) copy-start(bf16[2048,512]{1,0:T(8,128)(2,1)} %param.25) | copy-start | bytes 6291460
  7.2 8.7 %copy-start.28 = (s32[8]{0:T(128)S(1)}, s32[8]{0:T(128)}, u32[]{:S(2)}) copy-start(s32[8]{0:T(128)} %param.27) | copy-start | bytes 100
  7.2 9.8 %copy-start.18 = (f32[4,128,16]{1,2,0:T(8,128)S(1)}, f32[4,128,16]{1,2,0:T(8,128)}, u32[]{:S(2)}) copy-start(f32[4,128,16]{1,2,0:T(8,128)} %param.22) | copy-start | bytes 98308
  7.2 191.8 %reduce-scatter.2.cloned.1.call-start = ((), (), s32[]{:S(2)}) async-start(), calls=%async_computation.1 | async-start | bytes 655360 | tf_op jit(solution)/shard_map/reduce_scatter | solution.py:294
  9.9 50.8 %collective-permute-start = (bf16[2,136,2048]{2,1,0:T(8,128)(2,1)}, bf16[2,136,2048]{2,1,0:T(8,128)(2,1)}, u32[]{:S(2)}, u32[]{:S(2)}) collective-permute-start(bf16[2,136,2048]{2,1,0:T(8,128)(2,1)} %pad_maximum_fusion), channel_id=1, source_target_pairs={{0,4},{4,8},{8,12},{1,5},{5,9},{9,13},{2,6},{6,10},{10,14},{3,7},{... | collective-permute-start | bytes 3342344 | tf_op jit(solution)/shard_map/ppermute | solution.py:18
  16.9 10.2 %copy-start.25 = (s32[2,128]{1,0:T(2,128)}, s32[2,128]{1,0:T(2,128)S(1)}, u32[]{:S(2)}) copy-start(s32[2,128]{1,0:T(2,128)S(1)} %get-tuple-element.736) | copy-start | bytes 3076
  54.2 6.5 %copy-start.16 = (bf16[7,2048]{1,0:T(8,128)(2,1)S(1)}, bf16[7,2048]{1,0:T(8,128)(2,1)}, u32[]{:S(2)}) copy-start(bf16[7,2048]{1,0:T(8,128)(2,1)} %param.20) | copy-start | bytes 86020
  70.9 19.5 %copy-start.20 = (pred[2,128]{1,0:T(4,128)(4,1)S(1)}, pred[2,128]{1,0:T(4,128)(4,1)}, u32[]{:S(2)}) copy-start(pred[2,128]{1,0:T(4,128)(4,1)} %get-tuple-element.427) | copy-start | bytes 772
  72.5 4.8 %copy-start.8 = (bf16[128,128,128]{2,1,0:T(8,128)(2,1)S(1)}, bf16[128,128,128]{2,1,0:T(8,128)(2,1)}, u32[]{:S(2)}) copy-start(bf16[128,128,128]{2,1,0:T(8,128)(2,1)} %get-tuple-element.730) | copy-start | bytes 12582916 | tf_op jit(solution)/shard_map/while
  82.3 4.8 %copy-start.8 = (bf16[128,128,128]{2,1,0:T(8,128)(2,1)S(1)}, bf16[128,128,128]{2,1,0:T(8,128)(2,1)}, u32[]{:S(2)}) copy-start(bf16[128,128,128]{2,1,0:T(8,128)(2,1)} %get-tuple-element.730) | copy-start | bytes 12582916 | tf_op jit(solution)/shard_map/while
  106.5 21.5 %collective-permute-start.1 = (f32[128,544]{0,1:T(8,128)}, f32[128,544]{0,1:T(8,128)}, u32[]{:S(2)}, u32[]{:S(2)}) collective-permute-start(f32[128,544]{0,1:T(8,128)} %pad_maximum_fusion.2), channel_id=1, source_target_pairs={{0,4},{4,8},{8,12},{1,5},{5,9},{9,13},{2,6},{6,10},{10,14},{3,7},{... | collective-permute-start | bytes 835592 | tf_op jit(solution)/shard_map/ppermute | solution.py:18
  115.6 5.5 %copy-start.1 = (bf16[16,8,128,128]{3,1,2,0:T(8,128)(2,1)S(1)}, bf16[16,8,128,128]{3,1,2,0:T(8,128)(2,1)}, u32[]{:S(2)}) copy-start(bf16[16,8,128,128]{3,1,2,0:T(8,128)(2,1)} %get-tuple-element.381) | copy-start | bytes 12582916
  131.2 22.2 %collective-permute-start.2 = (f32[128,544]{0,1:T(8,128)}, f32[128,544]{0,1:T(8,128)}, u32[]{:S(2)}, u32[]{:S(2)}) collective-permute-start(f32[128,544]{0,1:T(8,128)} %pad_maximum_fusion.3), channel_id=1, source_target_pairs={{0,8},{4,12},{1,9},{5,13},{2,10},{6,14},{3,11},{7,15},{16,24},{20,... | collective-permute-start | bytes 835592 | tf_op jit(solution)/shard_map/ppermute | solution.py:18
  134.3 20.1 %copy-start.14 = (f32[128,256]{0,1:T(8,128)S(1)}, f32[128,256]{0,1:T(8,128)}, u32[]{:S(2)}) copy-start(f32[128,256]{0,1:T(8,128)} %copy-done.13) | copy-start | bytes 393220
  135.8 4.6 %copy-start.9 = (bf16[128,128,128]{2,1,0:T(8,128)(2,1)S(1)}, bf16[128,128,128]{2,1,0:T(8,128)(2,1)}, u32[]{:S(2)}) copy-start(bf16[128,128,128]{2,1,0:T(8,128)(2,1)} %get-tuple-element.752) | copy-start | bytes 12582916 | tf_op jit(solution)/shard_map/while
  145.3 4.6 %copy-start.9 = (bf16[128,128,128]{2,1,0:T(8,128)(2,1)S(1)}, bf16[128,128,128]{2,1,0:T(8,128)(2,1)}, u32[]{:S(2)}) copy-start(bf16[128,128,128]{2,1,0:T(8,128)(2,1)} %get-tuple-element.752) | copy-start | bytes 12582916 | tf_op jit(solution)/shard_map/while
  156.3 4.7 %copy-start.15 = (f32[128,16]{1,0:T(8,128)S(1)}, f32[128,16]{1,0:T(8,128)}, u32[]{:S(2)}) copy-start(f32[128,16]{1,0:T(8,128)} %mul.578) | copy-start | bytes 24580
  156.3 4.7 %copy-start.21 = (f32[2,128]{1,0:T(2,128)S(1)}, f32[2,128]{1,0:T(2,128)}, u32[]{:S(2)}) copy-start(f32[2,128]{1,0:T(2,128)} %get-tuple-element.426) | copy-start | bytes 3076
  167.5 7.7 %copy-start.26 = (f32[2048]{0:T(1024)S(1)}, f32[2048]{0:T(1024)}, u32[]{:S(2)}) copy-start(f32[2048]{0:T(1024)} %param.24) | copy-start | bytes 24580
  175.2 3.9 %copy-start.27 = (s32[256]{0:T(256)S(1)}, s32[256]{0:T(256)}, u32[]{:S(2)}) copy-start(s32[256]{0:T(256)} %param.26) | copy-start | bytes 3076
  175.2 4.0 %copy-start.30 = (u32[32]{0:T(128)S(1)}, u32[32]{0:T(128)}, u32[]{:S(2)}) copy-start(u32[32]{0:T(128)} %constant.130) | copy-start | bytes 388
  175.2 30.7 %copy-start.23 = (s32[256]{0:T(256)S(1)}, s32[256]{0:T(256)}, u32[]{:S(2)}) copy-start(s32[256]{0:T(256)} %get-tuple-element.710) | copy-start | bytes 3076
  175.3 42.7 %copy-start.29 = (s32[8]{0:T(128)S(1)}, s32[8]{0:T(128)}, u32[]{:S(2)}) copy-start(s32[8]{0:T(128)} %param.27) | copy-start | bytes 100
  205.9 12.5 %copy-start.24 = (f32[256]{0:T(256)}, f32[256]{0:T(256)S(1)}, u32[]{:S(2)}) copy-start(f32[256]{0:T(256)S(1)} %all-reduce) | copy-start | bytes 3076
  (14 other events, 32.2 us)
Sparse Core Ops, SparseCore 0:
  179.2 19.7 reduce-scatter.1

commit v7 on v5

--- a/solution.py
+++ b/solution.py
@@ -83,24 +83,41 @@
     return picked.astype(table.dtype).reshape(width, tile_rows, tile_rows)
 
 
+def pole_powers(decay_rate, angles, exponents):
+    e = exponents.astype(jnp.float32)[:, None, None]
+    magnitude = jnp.exp(-e * decay_rate[None])
+    return (magnitude * jnp.cos(e * angles[None]), magnitude * jnp.sin(e * angles[None]))
+
+
+def power_products(high, low):
+    high_re, high_im = high[0][:, None], high[1][:, None]
+    low_re, low_im = low[0][None], low[1][None]
+    out_re = high_re * low_re - high_im * low_im
+    out_im = high_re * low_im + high_im * low_re
+    return (out_re.reshape((-1,) + out_re.shape[2:]), out_im.reshape((-1,) + out_im.shape[2:]))
+
+
 def modal_tables(modal_poles):
     decay_rate = modal_poles[0]
     angles = modal_poles[1]
     residue_re = modal_poles[2]
     residue_im = modal_poles[3]
-    powers = jnp.arange(tile_rows + 1).astype(jnp.float32)[:, None, None]
-    magnitude = jnp.exp(-powers * decay_rate[None])
-    power_re = magnitude * jnp.cos(powers * angles[None])
-    power_im = magnitude * jnp.sin(powers * angles[None])
+    step = 16
+    spans = tile_rows // step
+    low = pole_powers(decay_rate, angles, jnp.arange(step))
+    high = pole_powers(decay_rate, angles, jnp.arange(spans + 1) * step)
+    forward = power_products(high, low)
+    power_re = forward[0][: tile_rows + 1]
+    power_im = forward[1][: tile_rows + 1]
+    backward = power_products(
+        (high[0][spans - 1 :: -1], high[1][spans - 1 :: -1]), (low[0][::-1], low[1][::-1])
+    )
     kernel_re = residue_re[None] * power_re - residue_im[None] * power_im
     kernel_im = residue_re[None] * power_im + residue_im[None] * power_re
     kernel = jnp.sum(kernel_re[:tile_rows], axis=2)
     toeplitz = split_table(kernel)
     outward = jnp.transpose(jnp.concatenate((kernel_re[1:], -kernel_im[1:]), axis=2), (1, 0, 2))
-    inward = jnp.transpose(
-        jnp.concatenate((power_re[tile_rows - 1 :: -1], power_im[tile_rows - 1 :: -1]), axis=2),
-        (1, 0, 2),
-    )
+    inward = jnp.transpose(jnp.concatenate(backward, axis=2), (1, 0, 2))
     return (toeplitz, outward, inward, power_re[tile_rows], power_im[tile_rows])
 
 

time: 222 us -> 259 us (1.17)
  local copies, waits for them, and re-layouts: 56.5 us -> 76.1 us
  other arithmetic: 47.6 us -> 59.6 us
    mul x1 -> x2, other arithmetic: 9.48 us -> 0.89 us  [pole_powers(): magnitude * jnp.cos(e * angles[None])]
    sub x0 -> x3, other arithmetic: none -> 6.9 us  [the longest x2 4.37 us: power_products(): out_re = high_re * low_re - high_im * low_im]
    unnamed x65 -> x73, local copies, waits for them, and re-layouts: 27.3 us -> 32.5 us
    sub x0 -> x1, local copies, waits for them, and re-layouts: none -> 2.8 us  [power_products(): out_re = high_re * low_re - high_im * low_im]
    add x0 -> x1, local copies, waits for them, and re-layouts: none -> 2.79 us  [power_products(): out_im = high_re * low_im + high_im * low_re]
  transfers between devices with their start and end apart: 4 -> 4, of which waited for: 1 -> 2; matrix products, arithmetic and copies ran while one was open for 38% -> 41% of each run, Pallas kernels for 0% -> 0%
where the time goes in v7:
time: 259 us; the launch traced here: 257 us
  local copies, waits for them, and re-layouts  76.1 us (29%)
  other arithmetic  59.6 us (23%)
  matrix products  46.3 us (18%)
  blocking collectives  23.3 us (9%)
  waiting for transfers between devices  20.9 us (8%)
  between operations  15.1 us (6%)
  starting transfers between devices  14.6 us (6%)
    unnamed x73, local copies, waits for them, and re-layouts  32.5 us
    reduce_scatter x1, waiting for transfers between devices, per_device(): lax.psum_scatter(partial_value, lanes, scatter_dimension=0, tiled=True)  18.9 us
    ppermute x3, starting transfers between devices, from_behind(): return lax.ppermute(shard, axis, pairs)  14.5 us
    dot_general x2, matrix products, medium_block(): jnp.einsum('gts,gis->git', matrix, window, preferred_element_type=jnp.flo...  12.2 us
    psum x1, blocking collectives, per_device(): totals = lax.psum(genome_part, 'seq')  11.9 us
    dot_general x2, matrix products, intra_block(): jnp.einsum('gts,gis->git', lower, block_in, preferred_element_type=jnp.fl...  9.22 us
    concatenate x1, other arithmetic, per_device(): jnp.concatenate((circ[:group_count], circ[:group_count]), axis=2)  8.56 us
    dot_general x2, matrix products, intra_block(): jnp.einsum('gts,gis->git', upper, block_in, preferred_element_type=jnp.fl...  6.81 us
  transfers between devices with their start and end apart: 4, of which 2 were waited for; matrix products, arithmetic and copies ran while one was open for 41% of the time, Pallas kernels for 0%

profile of v7, /device:TPU:0, one launch (start us, length us, event | category | flops | bytes accessed | tf_op | source)
XLA Modules:
  0.0 257.4 jit_solution(1472304107086639858)
XLA Ops:
  9.8 6.0 %collective-permute-start = (bf16[2,136,2048]{2,1,0:T(8,128)(2,1)}, bf16[2,136,2048]{2,1,0:T(8,128)(2,1)}, u32[]{:S(2)}, u32[]{:S(2)}) collective-permute-start(bf16[2,136,2048]{2,1,0:T(8,128)(2,1)} %pad_maximum_fusion.1), channel_id=1, source_target_pairs={{0,4},{4,8},{8,12},{1,5},{5,9},{9,13},{2,6},{6,10},{10,14},{3,7},{... | collective-permute-start | bytes 3342344 | tf_op jit(solution)/shard_map/ppermute | solution.py:18
  41.5 4.6 %convolution_convert_fusion = bf16[384,16384]{1,0:T(8,128)(2,1)S(1)} fusion(s32[16384]{0:T(1024)} %add_select_fusion, s32[128]{0:T(128)S(1)} %iota.77, bf16[128,128]{0,1:T(8,128)(2,1)} %get-tuple-element.339, bf16[128,128]{0,1:T(8,128)(2,1)} %get-tuple-element.340, bf16[128,128]{0,1:T(8,128)(2,1)} %copy.75), kind=kOutput, calls=%fused_computation.49 | convolution fusion | flops 1619296256 | bytes 12747264 | tf_op jit(solution)/shard_map/dot_general | solution.py:82
  46.1 3.9 %slice_bitcast_fusion = (bf16[16,8,128,128]{3,1,2,0:T(8,128)(2,1)}, bf16[16,8,128,128]{3,1,2,0:T(8,128)(2,1)}, bf16[16,8,128,128]{3,1,2,0:T(8,128)(2,1)S(1)}) fusion(bf16[384,16384]{1,0:T(8,128)(2,1)S(1)} %convolution_convert_fusion), kind=kLoop, calls=%fused_computation.52 | loop fusion | bytes 25165824
  74.7 5.6 %copy.98 = bf16[16,8,128,128]{3,2,1,0:T(8,128)(2,1)} copy(bf16[16,8,128,128]{3,1,2,0:T(8,128)(2,1)} %get-tuple-element.348) | data formatting | bytes 8388608
  91.3 8.6 %pad_maximum_fusion = bf16[128,128,256]{2,1,0:T(8,128)(2,1)} fusion(bf16[128,128,128]{2,1,0:T(8,128)(2,1)} %bitcast.187), kind=kLoop, calls=%fused_computation.50 | loop fusion | flops 16777216 | bytes 12582912 | tf_op jit(solution)/shard_map/concatenate | solution.py:201
  102.5 5.4 %fusion.74 = bf16[2048,384]{0,1:T(8,128)(2,1)} fusion(f32[384]{0:T(512)S(1)} %copy-done.21, f32[392,2048]{1,0:T(8,128)S(1)} %convert_multiply_fusion, f32[2048]{0:T(1024)S(1)} %bitcast.212, f32[384]{0:T(512)S(1)} %copy-done.17, f32[2048]{0:T(1024)S(1)} %bitcast.213, f32[384]{0:T(512)S(1)} %copy-done.18, f32[2048]{0:T(1024)S(1)} %bitcast.208, ...), kind=kLoop, calls=%fused_computation.97 | loop fusion | flops 15728640 | bytes 23659520 | tf_op jit(solution)/shard_map/transpose | solution.py:194
  111.0 21.7 %while.50 = (s32[]{:T(128)}, bf16[2,128,16,128]{3,2,1,0:T(8,128)(2,1)S(1)}, s32[2]{0:T(128)}, bf16[128,16,384]{2,1,0:T(8,128)(2,1)}, s32[256]{0:T(256)}, /*index...) while((s32[]{:T(128)}, ...), condition=%wide.region_6.7_spmd.clone.clone, body=%wide.region_5.6_spmd.clone.sunk.clone | while | flops 138870784 | bytes 10032828 | solution.py:222
  115.8 6.1 %fusion.149 = bf16[2,128,16,128]{3,2,1,0:T(8,128)(2,1)S(1)} fusion(bf16[2,128,16,128]{3,2,1,0:T(8,128)(2,1)S(1)} %get-tuple-element.680, s32[]{:T(128)} %get-tuple-element.679, bf16[128,128,256]{2,1,0:T(8,128)(2,1)} %get-tuple-element.694, pred[128,256]{1,0:T(8,128)(4,1)S(1)} %fusion.148, bf16[128,16,384]{2,1,0:T(8,128)(2,1)} %get-tuple-element.691, ...), kind=kOutput, calls=%fused_computation.29.clone.1.clone | convolution fusion | flops 138674176 | bytes 9994756 | tf_op jit(solution)/shard_map/while/body/eval_jaxpr/gts,gis->git/dot_general | solution.py:218
  126.7 6.1 %fusion.149 = bf16[2,128,16,128]{3,2,1,0:T(8,128)(2,1)S(1)} fusion(bf16[2,128,16,128]{3,2,1,0:T(8,128)(2,1)S(1)} %get-tuple-element.680, s32[]{:T(128)} %get-tuple-element.679, bf16[128,128,256]{2,1,0:T(8,128)(2,1)} %get-tuple-element.694, pred[128,256]{1,0:T(8,128)(4,1)S(1)} %fusion.148, bf16[128,16,384]{2,1,0:T(8,128)(2,1)} %get-tuple-element.691, ...), kind=kOutput, calls=%fused_computation.29.clone.1.clone | convolution fusion | flops 138674176 | bytes 9994756 | tf_op jit(solution)/shard_map/while/body/eval_jaxpr/gts,gis->git/dot_general | solution.py:218
  137.2 3.4 %copy.80 = f32[2,128,16,32]{1,3,2,0:T(8,128)} copy(f32[2,128,16,32]{3,2,0,1:T(8,128)} %add_bitcast_fusion) | data formatting | bytes 1048576
  140.6 10.2 %while.51 = (s32[]{:T(128)}, f32[128,16]{0,1:T(8,128)S(1)}, f32[128,16]{0,1:T(8,128)S(1)}, f32[128,16,16]{0,2,1:T(8,128)S(1)}, f32[128,16,16]{0,2,1:T(8,128)S(1)...) while((s32[]{:T(128)}, f32[128,16]{0,1:T(8,128)S(1)}, ...), condition=%wide.region_11.12_spmd.clone.clone, body=%wide.region_10.11_spmd.clone.sunk.clone | while | flops 421891 | bytes 2000031 | solution.py:265
  153.4 3.6 %fusion.83 = f32[128,128,16]{0,2,1:T(8,128)} fusion(f32[129,128,16]{0,2,1:T(8,128)} %copy.90, f32[129,128,16]{0,2,1:T(8,128)} %copy.91, f32[128,16]{1,0:T(8,128)S(1)} %copy.73, f32[128,16]{1,0:T(8,128)S(1)} %copy.71), kind=kLoop, calls=%fused_computation.107 | loop fusion | flops 1048576 | bytes 3162112 | tf_op jit(solution)/shard_map/neg | solution.py:119
  160.4 6.1 %collective-permute-start.2 = (f32[128,544]{0,1:T(8,128)}, f32[128,544]{0,1:T(8,128)}, u32[]{:S(2)}, u32[]{:S(2)}) collective-permute-start(f32[128,544]{0,1:T(8,128)} %pad_maximum_fusion.4), channel_id=1, source_target_pairs={{0,8},{4,12},{1,9},{5,13},{2,10},{6,14},{3,11},{7,15},{16,24},{20,... | collective-permute-start | bytes 835592 | tf_op jit(solution)/shard_map/ppermute | solution.py:18
  166.5 19.1 %while.49 = (s32[]{:T(128)}, f32[2,128,16,128]{3,2,0,1:T(8,128)}, bf16[2,128,16,128]{3,2,1,0:T(8,128)(2,1)S(1)}, s32[2,128]{1,0:T(2,128)}, pred[128,128]{1,0:T(8...) while((s32[]{:T(128)}, f32[2,128,16,128]{3,2,0,1:T(8,128)}, ...), condition=%wide.region_8.9_spmd.clone, body=%wide.region_7.8_spmd.sunk.clone | while | flops 138706944 | bytes 29428336 | solution.py:238
  168.0 4.6 %fusion.144 = f32[128,16,128]{2,1,0:T(8,128)S(1)} fusion(bf16[128,128,128]{2,1,0:T(8,128)(2,1)} %get-tuple-element.717, pred[128,128]{1,0:T(8,128)(4,1)S(1)} %compare_and_fusion.3, bf16[2,128,16,128]{3,2,1,0:T(8,128)(2,1)S(1)} %get-tuple-element.713, s32[]{:T(128)} %get-tuple-element.704), kind=kOutput, calls=%fused_computation.1.clone.1.clone | convolution fusion | flops 69206016 | bytes 5783556 | tf_op jit(solution)/shard_map/while/body/eval_jaxpr/gts,gis->git/dot_general | solution.py:236
  172.6 3.4 %fusion.145 = f32[2,128,16,128]{3,2,0,1:T(8,128)} fusion(f32[2,128,16,128]{3,2,0,1:T(8,128)} %get-tuple-element.705, s32[]{:T(128)} %get-tuple-element.704, f32[128,16,128]{2,1,0:T(8,128)S(1)} %fusion.144, bf16[128,128,128]{2,1,0:T(8,128)(2,1)S(1)} %copy-done.6, pred[128,128]{1,0:T(8,128)(4,1)S(1)} %compare_and_fusion.3, ...), kind=kOutput, calls=%fused_computation.11.clone.1.clone | convolution fusion | flops 69468160 | bytes 6833152 | tf_op jit(solution)/shard_map/while/body/eval_jaxpr/gts,gis->git/dot_general | solution.py:234
  177.5 4.6 %fusion.144 = f32[128,16,128]{2,1,0:T(8,128)S(1)} fusion(bf16[128,128,128]{2,1,0:T(8,128)(2,1)} %get-tuple-element.717, pred[128,128]{1,0:T(8,128)(4,1)S(1)} %compare_and_fusion.3, bf16[2,128,16,128]{3,2,1,0:T(8,128)(2,1)S(1)} %get-tuple-element.713, s32[]{:T(128)} %get-tuple-element.704), kind=kOutput, calls=%fused_computation.1.clone.1.clone | convolution fusion | flops 69206016 | bytes 5783556 | tf_op jit(solution)/shard_map/while/body/eval_jaxpr/gts,gis->git/dot_general | solution.py:236
  189.3 3.9 %copy.81 = f32[2,128,16,32]{3,2,0,1:T(8,128)} copy(f32[2,128,16,32]{1,3,2,0:T(8,128)} %pad_maximum_fusion.2) | data formatting | bytes 1048576 | tf_op jit(solution)/shard_map/concatenate | solution.py:283
  193.2 5.3 %fusion.72 = f32[128,16,2,128]{3,1,2,0:T(8,128)S(1)} fusion(f32[2,128,16,128]{3,2,0,1:T(8,128)} %get-tuple-element.156, f32[2,128,16,32]{3,2,0,1:T(8,128)} %copy.81, f32[128,128,16]{0,2,1:T(8,128)} %fusion.83, f32[128,128,16]{0,2,1:T(8,128)} %get-tuple-element.350, bf16[2,128,16,128]{3,2,1,0:T(8,128)(2,1)S(1)} %get-tuple-element.758, ...), kind=kOutput, calls=%fused_computation.92 | convolution fusion | flops 204472320 | bytes 7873536 | tf_op jit(solution)/shard_map/gtm,jgim->jgit/dot_general | solution.py:280
  201.3 5.7 %psum.14 = f32[256]{0:T(256)S(1)} all-reduce(f32[256]{0:T(256)S(1)} %fusion.64), channel_id=1, replica_groups=mesh['groups'=2,'seq'=4,'chan'=2,'rep'=2] {'chan','rep'}, use_global_device_ids=true, to_apply=%region_13.14 | all-reduce | flops 256 | bytes 2048 | tf_op jit(solution)/shard_map/psum | solution.py:296
  207.0 3.8 %fusion.80 = f32[256,512]{1,0:T(8,128)} fusion(bf16[2048,512]{1,0:T(8,128)(2,1)S(1)} %copy-done, f32[2048]{0:T(1024)S(1)} %copy-done.27, f32[256]{0:T(256)S(1)} %add_rsqrt_fusion, f32[256,8,2,128]{3,2,1,0:T(2,128)} %bitcast.189, bf16[256,2048]{0,1:T(8,128)(2,1)S(1)} %copy-done.7), kind=kOutput, calls=%fused_computation.104 | convolution fusion | flops 540540928 | bytes 5776384 | tf_op jit(solution)/shard_map/dot_general | solution.py:152
  212.2 18.9 %reduce-scatter.2.cloned.1.call-done = f32[64,512]{1,0:T(8,128)} async-done(((f32[256,512]{1,0:T(8,128)}), f32[64,512]{1,0:T(8,128)}) %reduce-scatter.2.cloned.1.call-update) | async-done | bytes 131088 | tf_op jit(solution)/shard_map/reduce_scatter | solution.py:305
  232.3 5.7 %all-reduce = f32[256]{0:T(256)S(1)} all-reduce(f32[256]{0:T(256)S(1)} %subtract_dynamic-update-slice_fusion), channel_id=1, replica_groups=mesh['groups'=2,'seq'=4,'chan'=2,'rep'=2] {'chan','rep'}, use_global_device_ids=true, to_apply=%add | all-reduce | flops 256 | bytes 2048
  238.2 11.9 %psum.15 = f32[8]{0:T(128)S(1)} all-reduce(f32[8]{0:T(128)S(1)} %select_reduce_fusion.1), channel_id=1, replica_groups=mesh['groups'=2,'seq'=4,'chan'=2,'rep'=2] {'seq'}, use_global_device_ids=true, to_apply=%region_18.19 | all-reduce | flops 8 | bytes 64 | tf_op jit(solution)/shard_map/psum | solution.py:317
  (193 shorter events, 113.7 us)
Async XLA Ops:
  7.2 199.8 %copy-start = (bf16[2048,512]{1,0:T(8,128)(2,1)S(1)}, bf16[2048,512]{1,0:T(8,128)(2,1)}, u32[]{:S(2)}) copy-start(bf16[2048,512]{1,0:T(8,128)(2,1)} %param.25) | copy-start | bytes 6291460
  7.2 9.9 %copy-start.13 = (f32[4,128,16]{1,2,0:T(8,128)S(1)}, f32[4,128,16]{1,2,0:T(8,128)}, u32[]{:S(2)}) copy-start(f32[4,128,16]{1,2,0:T(8,128)} %param.22) | copy-start | bytes 98308
  7.2 223.9 %reduce-scatter.2.cloned.1.call-start = ((), (), s32[]{:S(2)}) async-start(), calls=%async_computation.1 | async-start | bytes 655360 | tf_op jit(solution)/shard_map/reduce_scatter | solution.py:305
  9.8 90.1 %collective-permute-start = (bf16[2,136,2048]{2,1,0:T(8,128)(2,1)}, bf16[2,136,2048]{2,1,0:T(8,128)(2,1)}, u32[]{:S(2)}, u32[]{:S(2)}) collective-permute-start(bf16[2,136,2048]{2,1,0:T(8,128)(2,1)} %pad_maximum_fusion.1), channel_id=1, source_target_pairs={{0,4},{4,8},{8,12},{1,5},{5,9},{9,13},{2,6},{6,10},{10,14},{3,7},{... | collective-permute-start | bytes 3342344 | tf_op jit(solution)/shard_map/ppermute | solution.py:18
  22.9 3.4 %copy-start.5 = (f32[9,16,128,16]{2,3,1,0:T(8,128)S(1)}, f32[9,16,128,16]{2,3,1,0:T(8,128)}, u32[]{:S(2)}) copy-start(f32[9,16,128,16]{2,3,1,0:T(8,128)} %get-tuple-element.357) | copy-start | bytes 3538948
  74.7 5.6 %copy-start.1 = (bf16[16,8,128,128]{3,1,2,0:T(8,128)(2,1)S(1)}, bf16[16,8,128,128]{3,1,2,0:T(8,128)(2,1)}, u32[]{:S(2)}) copy-start(bf16[16,8,128,128]{3,1,2,0:T(8,128)(2,1)} %get-tuple-element.347) | copy-start | bytes 12582916
  80.3 3.2 %copy-start.14 = (s32[128]{0:T(128)S(1)}, s32[128]{0:T(128)}, u32[]{:S(2)}) copy-start(s32[128]{0:T(128)} %iota_add_fusion.3) | copy-start | bytes 1540
  132.8 2.4 copy-start.2
  132.8 2.4 copy-start.3
  132.8 2.4 copy-start.23
  150.9 8.1 %collective-permute-start.1 = (f32[128,544]{0,1:T(8,128)S(1)}, f32[128,544]{0,1:T(8,128)S(1)}, u32[]{:S(2)}, u32[]{:S(2)}) collective-permute-start(f32[128,544]{0,1:T(8,128)S(1)} %pad_maximum_fusion.3), channel_id=1, source_target_pairs={{0,4},{4,8},{8,12},{1,5},{5,9},{9,13},{2,6},{6,10},{10,14},{3,7},{... | collective-permute-start | bytes 835592 | tf_op jit(solution)/shard_map/ppermute | solution.py:18
  160.4 25.2 %collective-permute-start.2 = (f32[128,544]{0,1:T(8,128)}, f32[128,544]{0,1:T(8,128)}, u32[]{:S(2)}, u32[]{:S(2)}) collective-permute-start(f32[128,544]{0,1:T(8,128)} %pad_maximum_fusion.4), channel_id=1, source_target_pairs={{0,8},{4,12},{1,9},{5,13},{2,10},{6,14},{3,11},{7,15},{16,24},{20,... | collective-permute-start | bytes 835592 | tf_op jit(solution)/shard_map/ppermute | solution.py:18
  166.5 20.1 %copy-start.11 = (f32[128,256]{0,1:T(8,128)S(1)}, f32[128,256]{0,1:T(8,128)}, u32[]{:S(2)}) copy-start(f32[128,256]{0,1:T(8,128)} %copy-done.10) | copy-start | bytes 393220
  168.0 4.6 %copy-start.6 = (bf16[128,128,128]{2,1,0:T(8,128)(2,1)S(1)}, bf16[128,128,128]{2,1,0:T(8,128)(2,1)}, u32[]{:S(2)}) copy-start(bf16[128,128,128]{2,1,0:T(8,128)(2,1)} %get-tuple-element.716) | copy-start | bytes 12582916 | tf_op jit(solution)/shard_map/while
  177.5 4.6 %copy-start.6 = (bf16[128,128,128]{2,1,0:T(8,128)(2,1)S(1)}, bf16[128,128,128]{2,1,0:T(8,128)(2,1)}, u32[]{:S(2)}) copy-start(bf16[128,128,128]{2,1,0:T(8,128)(2,1)} %get-tuple-element.716) | copy-start | bytes 12582916 | tf_op jit(solution)/shard_map/while
  188.5 4.7 %copy-start.12 = (f32[128,16]{1,0:T(8,128)S(1)}, f32[128,16]{1,0:T(8,128)}, u32[]{:S(2)}) copy-start(f32[128,16]{1,0:T(8,128)} %mul.802) | copy-start | bytes 24580
  188.5 4.7 %copy-start.24 = (f32[2,128]{1,0:T(2,128)S(1)}, f32[2,128]{1,0:T(2,128)}, u32[]{:S(2)}) copy-start(f32[2,128]{1,0:T(2,128)} %get-tuple-element.395) | copy-start | bytes 3076
  198.5 2.4 copy-start.7
  199.7 7.3 %copy-start.27 = (f32[2048]{0:T(1024)S(1)}, f32[2048]{0:T(1024)}, u32[]{:S(2)}) copy-start(f32[2048]{0:T(1024)} %param.24) | copy-start | bytes 24580
  207.0 3.9 %copy-start.28 = (s32[256]{0:T(256)S(1)}, s32[256]{0:T(256)}, u32[]{:S(2)}) copy-start(s32[256]{0:T(256)} %param.26) | copy-start | bytes 3076
  207.0 4.0 %copy-start.30 = (u32[32]{0:T(128)S(1)}, u32[32]{0:T(128)}, u32[]{:S(2)}) copy-start(u32[32]{0:T(128)} %constant.129) | copy-start | bytes 388
  207.0 31.0 %copy-start.25 = (s32[256]{0:T(256)S(1)}, s32[256]{0:T(256)}, u32[]{:S(2)}) copy-start(s32[256]{0:T(256)} %get-tuple-element.764) | copy-start | bytes 3076
  207.0 43.0 %copy-start.29 = (s32[8]{0:T(128)S(1)}, s32[8]{0:T(128)}, u32[]{:S(2)}) copy-start(s32[8]{0:T(128)} %param.27) | copy-start | bytes 100
  238.1 12.5 %copy-start.26 = (f32[256]{0:T(256)}, f32[256]{0:T(256)S(1)}, u32[]{:S(2)}) copy-start(f32[256]{0:T(256)S(1)} %all-reduce) | copy-start | bytes 3076
  (13 other events, 12.0 us)
Sparse Core Ops, SparseCore 0:
  211.0 20.0 reduce-scatter.1

commit v8 on v5

--- a/solution.py
+++ b/solution.py
@@ -16,6 +16,17 @@
     count = lax.axis_size(axis)
     pairs = [(i, i + by) for i in range(count) if 0 <= i + by < count]
     return lax.ppermute(shard, axis, pairs)
+
+
+def sum_over(part, axis):
+    count = lax.axis_size(axis)
+    if count & (count - 1):
+        return lax.psum(part, axis)
+    bit = 1
+    while bit < count:
+        part = part + lax.ppermute(part, axis, [(i, i ^ bit) for i in range(count)])
+        bit *= 2
+    return part
 
 
 def entering_2(part, axis, combine, identity):
@@ -202,7 +213,7 @@
             "gts,gis->git", matrix, window, preferred_element_type=jnp.float32
         ).astype(jnp.bfloat16)
 
-    signal = lax.map(medium_block, jnp.arange(tile_count, dtype=jnp.int32))
+    signal = jnp.stack([medium_block(tile_index) for tile_index in range(tile_count)])
     inward_upper, inward_lower = split_table(inward)
     tile_segs = segments.reshape(tile_count, tile_rows)
     before = segment_ids(
@@ -218,7 +229,7 @@
             "gts,gis->git", upper, block_in, preferred_element_type=jnp.float32
         ) + jnp.einsum("gts,gis->git", lower, block_in, preferred_element_type=jnp.float32)
 
-    local_part = lax.map(intra_block, (signal, tile_segs))
+    local_part = jnp.stack([intra_block((signal[j], tile_segs[j])) for j in range(tile_count)])
     end_keep = (tile_segs == tile_segs[:, -1:])[:, None, None, :]
     masked_signal = jnp.where(end_keep, signal, jnp.zeros_like(signal))
     states = jnp.einsum(
@@ -297,7 +308,7 @@
         ),
         axis=0,
     )
-    totals = lax.psum(genome_part, "seq")
+    totals = sum_over(genome_part, "seq")
     return (logprob, totals / genome_lengths.astype(jnp.float32))
 
 

time: 222 us -> 216 us (0.973)
  waiting for transfers between devices: 18.6 us -> 32.9 us
  blocking collectives: 23.6 us -> 11.4 us
  other arithmetic: 47.6 us -> 42.6 us
  starting transfers between devices: 12.1 us -> 16.2 us
  matrix products: 45.5 us -> 41.6 us
    psum x1 -> x0, blocking collectives: 11.9 us -> none  [per_device(): totals = lax.psum(genome_part, 'seq')]
    concatenate x1 -> x0, other arithmetic: 8.6 us -> none  [per_device(): jnp.concatenate((circ[:group_count], circ[:group_count]), axis=2)]
    reduce_scatter x1, waiting for transfers between devices: 18.6 us -> 27 us  [per_device(): lax.psum_scatter(partial_value, lanes, scatter_dimension=0, tiled=True)]
    select_n x0 -> x1, other arithmetic: none -> 6.92 us  [intra_block(): jnp.where(same_genome, toeplitz_upper, jnp.zeros_like(toeplitz_upper))]
    concatenate x0 -> x1, local copies, waits for them, and re-layouts: none -> 5.06 us  [per_device(): jnp.concatenate((circ[:group_count], circ[:group_count]), axis=2)]
    ppermute x0 -> x2, starting transfers between devices: none -> 4.32 us  [sum_over(): part = part + lax.ppermute(part, axis, [(i, i ^ bit) for i in range(count)])]
    ppermute x0 -> x2, waiting for transfers between devices: none -> 3.72 us  [sum_over(): part = part + lax.ppermute(part, axis, [(i, i ^ bit) for i in range(count)])]
    dot_general x2, matrix products: 9.22 us -> 6.59 us  [intra_block(): jnp.einsum('gts,gis->git', lower, block_in, preferred_element_type=jnp.fl...]
  transfers between devices with their start and end apart: 4 -> 6, of which waited for: 1 -> 4; matrix products, arithmetic and copies ran while one was open for 38% -> 38% of each run, Pallas kernels for 0% -> 0%
where the time goes in v8:
time: 216 us
  local copies, waits for them, and re-layouts  55.5 us (26%)
  other arithmetic  42.6 us (20%)
  matrix products  41.6 us (19%)
  waiting for transfers between devices  32.9 us (15%)
  starting transfers between devices  16.2 us (8%)
  between operations  15.3 us (7%)
  blocking collectives  11.4 us (5%)
    reduce_scatter x1, waiting for transfers between devices, per_device(): lax.psum_scatter(partial_value, lanes, scatter_dimension=0, tiled=True)  27 us
    unnamed x108, local copies, waits for them, and re-layouts  26.9 us
    dot_general x2, matrix products, medium_block(): jnp.einsum('gts,gis->git', matrix, window, preferred_element_type=jnp.flo...  11.9 us
    ppermute x3, starting transfers between devices, from_behind(): return lax.ppermute(shard, axis, pairs)  11.9 us
    mul x1, other arithmetic, modal_tables(): power_im = magnitude * jnp.sin(powers * angles[None])  9.37 us
    select_n x1, other arithmetic, intra_block(): jnp.where(same_genome, toeplitz_upper, jnp.zeros_like(toeplitz_upper))  6.92 us
    dot_general x2, matrix products, intra_block(): jnp.einsum('gts,gis->git', upper, block_in, preferred_element_type=jnp.fl...  6.73 us
    dot_general x2, matrix products, intra_block(): jnp.einsum('gts,gis->git', lower, block_in, preferred_element_type=jnp.fl...  6.59 us
  transfers between devices with their start and end apart: 6, of which 4 were waited for; matrix products, arithmetic and copies ran while one was open for 38% of the time, Pallas kernels for 0%

profile of v8, /device:TPU:0, one launch (start us, length us, event | category | flops | bytes accessed | tf_op | source)
XLA Modules:
  0.0 215.6 jit_solution(14178917983510365971)
XLA Ops:
  9.8 5.9 %collective-permute-start = (bf16[2,136,2048]{2,1,0:T(8,128)(2,1)}, bf16[2,136,2048]{2,1,0:T(8,128)(2,1)}, u32[]{:S(2)}, u32[]{:S(2)}) collective-permute-start(bf16[2,136,2048]{2,1,0:T(8,128)(2,1)} %pad_maximum_fusion), channel_id=1, source_target_pairs={{0,4},{4,8},{8,12},{1,5},{5,9},{9,13},{2,6},{6,10},{10,14},{3,7},{... | collective-permute-start | bytes 3342344 | tf_op jit(solution)/shard_map/ppermute | solution.py:18
  17.3 9.4 %fusion.28 = (f32[129,128,16]{0,2,1:T(8,128)S(1)}, f32[129,128,16]{0,2,1:T(8,128)}, f32[129,128,16]{0,2,1:T(8,128)S(1)}) fusion(f32[128,16]{1,0:T(8,128)S(1)} %copy.89, f32[129]{0:T(256)S(1)} %iota_convert_fusion, f32[128,16]{1,0:T(8,128)S(1)} %copy.88, f32[129]{0:T(256)S(1)} %fusion.73, f32[128,16]{1,0:T(8,128)S(1)} %copy.90, f32[128,16]{1,0:T(8,128)S(1)} %copy.87), kind=kLoop, calls=%fused_computation.59 | loop fusion | flops 1849344 | bytes 3204104 | tf_op jit(solution)/shard_map/mul | solution.py:105
  33.3 3.2 %fusion.82 = (f32[128,128,16]{0,2,1:T(8,128)}, f32[128,128]{0,1:T(8,128)S(1)}) fusion(f32[129,128,16]{0,2,1:T(8,128)} %get-tuple-element.263), kind=kLoop, calls=%fused_computation.201 | loop fusion | flops 245760 | bytes 3211264 | tf_op jit(solution)/shard_map/slice | solution.py:110
  38.0 4.6 %convolution_convert_fusion = bf16[384,16384]{1,0:T(8,128)(2,1)S(1)} fusion(s32[16384]{0:T(1024)S(1)} %add_select_fusion, s32[128]{0:T(128)S(1)} %iota.77, bf16[128,128]{0,1:T(8,128)(2,1)S(1)} %get-tuple-element.224, bf16[128,128]{0,1:T(8,128)(2,1)} %get-tuple-element.225, bf16[128,128]{0,1:T(8,128)(2,1)S(1)} %copy.91), kind=kOutput, calls=%fused_computation.11 | convolution fusion | flops 1619296256 | bytes 12747264 | tf_op jit(solution)/shard_map/dot_general | solution.py:93
  42.6 3.9 %slice_bitcast_fusion = (bf16[16,8,128,128]{3,1,2,0:T(8,128)(2,1)}, bf16[16,8,128,128]{3,1,2,0:T(8,128)(2,1)}, bf16[16,8,128,128]{3,1,2,0:T(8,128)(2,1)S(1)}) fusion(bf16[384,16384]{1,0:T(8,128)(2,1)S(1)} %convolution_convert_fusion), kind=kLoop, calls=%fused_computation.23 | loop fusion | bytes 25165824
  61.1 5.6 %copy.106 = bf16[16,8,128,128]{3,2,1,0:T(8,128)(2,1)} copy(bf16[16,8,128,128]{3,1,2,0:T(8,128)(2,1)} %get-tuple-element.233) | data formatting | bytes 8388608
  66.7 3.2 %copy.107 = bf16[16,8,128,128]{3,2,1,0:T(8,128)(2,1)} copy(bf16[16,8,128,128]{3,1,2,0:T(8,128)(2,1)S(1)} %copy-done.3) | data formatting | bytes 8388608
  73.2 5.1 %constant_dynamic-update-slice_fusion = bf16[128,128,256]{2,1,0:T(8,128)(2,1)} fusion(bf16[128,128,256]{2,1,0:T(8,128)(2,1)} %constant_dynamic-update-slice_fusion.1, bf16[128,128,128]{2,1,0:T(8,128)(2,1)} %bitcast.152), kind=kLoop, calls=%fused_computation.159 | loop fusion | bytes 8388608 | tf_op jit(solution)/shard_map/concatenate | solution.py:195
  79.4 6.9 %bitcast_select_fusion.3 = (bf16[128,128,128]{2,1,0:T(8,128)(2,1)}, bf16[128,128,128]{2,1,0:T(8,128)(2,1)}, bf16[128,128,128]{2,1,0:T(8,128)(2,1)}, bf16[128,128,128]{2,1,0:T(8,128)(2,1)}) fusion(bf16[16,8,128,128]{3,2,1,0:T(8,128)(2,1)S(1)} %copy-done.4, pred[128,128]{1,0:T(8,128)(4,1)S(1)} %get-tuple-element.222, ...), kind=kLoop, calls=%fused_computation.22 | loop fusion | flops 8388608 | bytes 25198592 | tf_op jit(solution)/shard_map/jit(_where)/select_n | solution.py:226
  88.5 5.3 %fusion.36 = bf16[2048,384]{0,1:T(8,128)(2,1)} fusion(f32[384]{0:T(512)S(1)} %copy-done.34, f32[392,2048]{1,0:T(8,128)S(1)} %convert_multiply_fusion, f32[2048]{0:T(1024)S(1)} %bitcast.180, f32[384]{0:T(512)S(1)} %copy-done.30, f32[2048]{0:T(1024)S(1)} %bitcast.181, f32[384]{0:T(512)S(1)} %copy-done.31, f32[2048]{0:T(1024)S(1)} %bitcast.176, ...), kind=kLoop, calls=%fused_computation.75 | loop fusion | flops 15728640 | bytes 23659520 | tf_op jit(solution)/shard_map/transpose | solution.py:188
  96.3 6.1 %fusion.39 = bf16[128,16,128]{2,1,0:T(8,128)(2,1)S(1)} fusion(bf16[128,128,256]{2,1,0:T(8,128)(2,1)} %constant_dynamic-update-slice_fusion, pred[128,256]{1,0:T(8,128)(4,1)S(1)} %get-tuple-element.292, bf16[128,16,384]{2,1,0:T(8,128)(2,1)} %bitcast.163), kind=kOutput, calls=%fused_computation.80 | convolution fusion | flops 138674176 | bytes 9994240 | tf_op jit(solution)/shard_map/gts,gis->git/dot_general | solution.py:212
  102.5 5.8 %fusion.42 = bf16[128,16,128]{2,1,0:T(8,128)(2,1)S(1)} fusion(bf16[128,128,256]{2,1,0:T(8,128)(2,1)} %constant_dynamic-update-slice_fusion, pred[128,256]{1,0:T(8,128)(4,1)S(1)} %get-tuple-element.293, bf16[128,16,384]{2,1,0:T(8,128)(2,1)S(1)} %bitcast.164), kind=kOutput, calls=%fused_computation.81 | convolution fusion | flops 138674176 | bytes 9994240 | tf_op jit(solution)/shard_map/gts,gis->git/dot_general | solution.py:212
  111.0 3.5 %copy.96 = f32[2,128,16,32]{1,3,2,0:T(8,128)} copy(f32[2,128,16,32]{3,2,0,1:T(8,128)} %add_bitcast_fusion) | data formatting | bytes 1048576
  114.5 6.2 %while.25 = (s32[]{:T(128)}, f32[128,16]{0,1:T(8,128)S(1)}, f32[128,16]{0,1:T(8,128)S(1)}, f32[128,16,16]{0,2,1:T(8,128)S(1)}, f32[128,16,16]{0,2,1:T(8,128)S(1)...) while((s32[]{:T(128)}, f32[128,16]{0,1:T(8,128)S(1)}, ...), condition=%wide.region_7.8_spmd.clone, body=%wide.region_6.7_spmd.clone.sunk | while | flops 421891 | bytes 1999539 | solution.py:259
  123.6 4.5 %fusion.85 = f32[128,16,128]{2,1,0:T(8,128)S(1)} fusion(bf16[128,16,128]{2,1,0:T(8,128)(2,1)S(1)} %fusion.39, bf16[128,128,128]{2,1,0:T(8,128)(2,1)} %get-tuple-element.237), kind=kOutput, calls=%fused_computation.204 | convolution fusion | flops 67108864 | bytes 5767168 | tf_op jit(solution)/shard_map/gts,gis->git/dot_general | solution.py:228
  128.0 3.3 %fusion.38 = f32[1,128,16,128]{3,2,1,0:T(8,128)} fusion(f32[128,16,128]{2,1,0:T(8,128)S(1)} %fusion.85, bf16[128,16,128]{2,1,0:T(8,128)(2,1)S(1)} %fusion.39, bf16[128,128,128]{2,1,0:T(8,128)(2,1)S(1)} %copy-done.7), kind=kOutput, calls=%fused_computation.79 | convolution fusion | flops 67371008 | bytes 6815744 | tf_op jit(solution)/shard_map/gts,gis->git/dot_general | solution.py:230
  133.8 3.2 %collective-permute-start.2 = (f32[128,544]{0,1:T(8,128)S(1)}, f32[128,544]{0,1:T(8,128)S(1)}, u32[]{:S(2)}, u32[]{:S(2)}) collective-permute-start(f32[128,544]{0,1:T(8,128)S(1)} %pad_maximum_fusion.4), channel_id=1, source_target_pairs={{0,8},{4,12},{1,9},{5,13},{2,10},{6,14},{3,11},{7,15},{16,24},{20,... | collective-permute-start | bytes 835592 | tf_op jit(solution)/shard_map/ppermute | solution.py:18
  137.0 3.3 %fusion.37 = f32[1,128,16,128]{3,2,1,0:T(8,128)} fusion(f32[128,16,128]{2,1,0:T(8,128)S(1)} %fusion.86, bf16[128,16,128]{2,1,0:T(8,128)(2,1)S(1)} %fusion.42, bf16[128,128,128]{2,1,0:T(8,128)(2,1)S(1)} %copy-done.6), kind=kOutput, calls=%fused_computation.77 | convolution fusion | flops 67371008 | bytes 6815744 | tf_op jit(solution)/shard_map/gts,gis->git/dot_general | solution.py:230
  143.4 3.1 %copy.102 = f32[2,128,16,32]{3,2,1,0:T(8,128)} copy(f32[2,128,16,32]{1,3,2,0:T(8,128)} %pad_maximum_fusion.2) | data formatting | bytes 1048576 | tf_op jit(solution)/shard_map/concatenate | solution.py:277
  146.5 5.3 %fusion.31 = f32[128,16,2,128]{3,1,0,2:T(8,128)S(1)} fusion(f32[1,128,16,128]{3,2,1,0:T(8,128)} %fusion.37, f32[1,128,16,128]{3,2,1,0:T(8,128)} %fusion.38, f32[2,128,16,32]{3,2,1,0:T(8,128)} %copy.102, f32[128,128,16]{0,2,1:T(8,128)} %get-tuple-element.241, f32[128,128,16]{0,2,1:T(8,128)} %get-tuple-element.239, f32[128,16]{1,0:T(8,128)S(1)} %mul.572, ...), kind=kOutput, calls=%fused_computation.64 | convolution fusion | flops 205520896 | bytes 7873536 | tf_op jit(solution)/shard_map/gtm,jgim->jgit/dot_general | solution.py:274
  155.2 5.7 %psum.7 = f32[256]{0:T(256)S(1)} all-reduce(f32[256]{0:T(256)S(1)} %fusion.24), channel_id=1, replica_groups=mesh['groups'=2,'seq'=4,'chan'=2,'rep'=2] {'chan','rep'}, use_global_device_ids=true, to_apply=%region_9.10 | all-reduce | flops 256 | bytes 2048 | tf_op jit(solution)/shard_map/psum | solution.py:290
  160.9 3.8 %fusion.50 = f32[256,512]{1,0:T(8,128)} fusion(bf16[2048,512]{1,0:T(8,128)(2,1)S(1)} %copy-done, f32[2048]{0:T(1024)S(1)} %copy-done.44, f32[256]{0:T(256)S(1)} %add_rsqrt_fusion, f32[256,8,2,128]{3,2,1,0:T(2,128)} %bitcast.162, bf16[256,2048]{0,1:T(8,128)(2,1)S(1)} %copy-done.11), kind=kOutput, calls=%fused_computation.86 | convolution fusion | flops 540540928 | bytes 5776384 | tf_op jit(solution)/shard_map/dot_general | solution.py:146
  166.1 27.0 %reduce-scatter.2.cloned.1.call-done = f32[64,512]{1,0:T(8,128)} async-done(((f32[256,512]{1,0:T(8,128)}), f32[64,512]{1,0:T(8,128)}) %reduce-scatter.2.cloned.1.call-update) | async-done | bytes 131088 | tf_op jit(solution)/shard_map/reduce_scatter | solution.py:299
  194.3 5.7 %all-reduce = f32[256]{0:T(256)S(1)} all-reduce(f32[256]{0:T(256)S(1)} %subtract_dynamic-update-slice_fusion), channel_id=1, replica_groups=mesh['groups'=2,'seq'=4,'chan'=2,'rep'=2] {'chan','rep'}, use_global_device_ids=true, to_apply=%add | all-reduce | flops 256 | bytes 2048
  (207 shorter events, 67.0 us)
Async XLA Ops:
  7.2 153.7 %copy-start = (bf16[2048,512]{1,0:T(8,128)(2,1)S(1)}, bf16[2048,512]{1,0:T(8,128)(2,1)}, u32[]{:S(2)}) copy-start(bf16[2048,512]{1,0:T(8,128)(2,1)} %param.21) | copy-start | bytes 6291460
  7.2 9.7 %copy-start.26 = (f32[4,128,16]{1,2,0:T(8,128)S(1)}, f32[4,128,16]{1,2,0:T(8,128)}, u32[]{:S(2)}) copy-start(f32[4,128,16]{1,2,0:T(8,128)} %param.18) | copy-start | bytes 98308
  7.2 185.9 %reduce-scatter.2.cloned.1.call-start = ((), (), s32[]{:S(2)}) async-start(), calls=%async_computation.1 | async-start | bytes 655360 | tf_op jit(solution)/shard_map/reduce_scatter | solution.py:299
  9.8 76.5 %collective-permute-start = (bf16[2,136,2048]{2,1,0:T(8,128)(2,1)}, bf16[2,136,2048]{2,1,0:T(8,128)(2,1)}, u32[]{:S(2)}, u32[]{:S(2)}) collective-permute-start(bf16[2,136,2048]{2,1,0:T(8,128)(2,1)} %pad_maximum_fusion), channel_id=1, source_target_pairs={{0,4},{4,8},{8,12},{1,5},{5,9},{9,13},{2,6},{6,10},{10,14},{3,7},{... | collective-permute-start | bytes 3342344 | tf_op jit(solution)/shard_map/ppermute | solution.py:18
  61.1 5.6 %copy-start.3 = (bf16[16,8,128,128]{3,1,2,0:T(8,128)(2,1)S(1)}, bf16[16,8,128,128]{3,1,2,0:T(8,128)(2,1)}, u32[]{:S(2)}) copy-start(bf16[16,8,128,128]{3,1,2,0:T(8,128)(2,1)} %get-tuple-element.232) | copy-start | bytes 12582916
  73.2 6.2 %copy-start.5 = (bf16[16,8,128,128]{3,2,1,0:T(8,128)(2,1)S(1)}, bf16[16,8,128,128]{3,2,1,0:T(8,128)(2,1)}, u32[]{:S(2)}) copy-start(bf16[16,8,128,128]{3,2,1,0:T(8,128)(2,1)} %copy.107) | copy-start | bytes 12582916
  79.4 8.2 %copy-start.12 = (bf16[256,2048]{1,0:T(8,128)(2,1)S(1)}, bf16[256,2048]{1,0:T(8,128)(2,1)}, u32[]{:S(2)}) copy-start(bf16[256,2048]{1,0:T(8,128)(2,1)} %param.14) | copy-start | bytes 3145732
  79.4 8.2 %copy-start.13 = (bf16[256,2048]{1,0:T(8,128)(2,1)S(1)}, bf16[256,2048]{1,0:T(8,128)(2,1)}, u32[]{:S(2)}) copy-start(bf16[256,2048]{1,0:T(8,128)(2,1)} %param.15) | copy-start | bytes 3145732
  96.3 6.1 %copy-start.14 = (bf16[2048,384]{1,0:T(8,128)(2,1)S(1)}, bf16[2048,384]{1,0:T(8,128)(2,1)}, u32[]{:S(2)}) copy-start(bf16[2048,384]{1,0:T(8,128)(2,1)} %copy.86) | copy-start | bytes 4718596
  102.4 5.8 %copy-start.8 = (f32[128,128,16]{0,2,1:T(8,128)S(1)}, f32[128,128,16]{0,2,1:T(8,128)}, u32[]{:S(2)}) copy-start(f32[128,128,16]{0,2,1:T(8,128)} %rev.6) | copy-start | bytes 3145732
  102.4 5.8 %copy-start.9 = (f32[128,128,16]{0,2,1:T(8,128)S(1)}, f32[128,128,16]{0,2,1:T(8,128)}, u32[]{:S(2)}) copy-start(f32[128,128,16]{0,2,1:T(8,128)} %rev.7) | copy-start | bytes 3145732
  102.4 5.8 %copy-start.38 = (pred[2,128]{1,0:T(4,128)(4,1)S(1)}, pred[2,128]{1,0:T(4,128)(4,1)}, u32[]{:S(2)}) copy-start(pred[2,128]{1,0:T(4,128)(4,1)} %get-tuple-element.287) | copy-start | bytes 772
  109.0 5.5 %copy-start.27 = (f32[2,128,16]{1,2,0:T(8,128)S(1)}, f32[2,128,16]{1,2,0:T(8,128)}, u32[]{:S(2)}) copy-start(f32[2,128,16]{1,2,0:T(8,128)} %custom-call.5) | copy-start | bytes 49156
  109.0 5.5 %copy-start.28 = (f32[2,128,16]{1,2,0:T(8,128)S(1)}, f32[2,128,16]{1,2,0:T(8,128)}, u32[]{:S(2)}) copy-start(f32[2,128,16]{1,2,0:T(8,128)} %custom-call.6) | copy-start | bytes 49156
  120.7 7.3 %copy-start.7 = (bf16[128,128,128]{2,1,0:T(8,128)(2,1)S(1)}, bf16[128,128,128]{2,1,0:T(8,128)(2,1)}, u32[]{:S(2)}) copy-start(bf16[128,128,128]{2,1,0:T(8,128)(2,1)} %get-tuple-element.266) | copy-start | bytes 12582916
  120.8 12.9 %collective-permute-start.1 = (f32[128,544]{0,1:T(8,128)S(1)}, f32[128,544]{0,1:T(8,128)S(1)}, u32[]{:S(2)}, u32[]{:S(2)}) collective-permute-start(f32[128,544]{0,1:T(8,128)S(1)} %pad_maximum_fusion.3), channel_id=1, source_target_pairs={{0,4},{4,8},{8,12},{1,5},{5,9},{9,13},{2,6},{6,10},{10,14},{3,7},{... | collective-permute-start | bytes 835592 | tf_op jit(solution)/shard_map/ppermute | solution.py:18
  131.4 5.6 %copy-start.6 = (bf16[128,128,128]{2,1,0:T(8,128)(2,1)S(1)}, bf16[128,128,128]{2,1,0:T(8,128)(2,1)}, u32[]{:S(2)}) copy-start(bf16[128,128,128]{2,1,0:T(8,128)(2,1)} %get-tuple-element.265) | copy-start | bytes 12582916
  133.8 8.6 %collective-permute-start.2 = (f32[128,544]{0,1:T(8,128)S(1)}, f32[128,544]{0,1:T(8,128)S(1)}, u32[]{:S(2)}, u32[]{:S(2)}) collective-permute-start(f32[128,544]{0,1:T(8,128)S(1)} %pad_maximum_fusion.4), channel_id=1, source_target_pairs={{0,8},{4,12},{1,9},{5,13},{2,10},{6,14},{3,11},{7,15},{16,24},{20,... | collective-permute-start | bytes 835592 | tf_op jit(solution)/shard_map/ppermute | solution.py:18
  140.3 6.3 %copy-start.39 = (f32[2,128]{1,0:T(2,128)S(1)}, f32[2,128]{1,0:T(2,128)}, u32[]{:S(2)}) copy-start(f32[2,128]{1,0:T(2,128)} %get-tuple-element.286) | copy-start | bytes 3076
  151.8 9.0 %copy-start.44 = (f32[2048]{0:T(1024)S(1)}, f32[2048]{0:T(1024)}, u32[]{:S(2)}) copy-start(f32[2048]{0:T(1024)} %param.20) | copy-start | bytes 24580
  160.9 47.3 %copy-start.43 = (s32[8]{0:T(128)S(1)}, s32[8]{0:T(128)}, u32[]{:S(2)}) copy-start(s32[8]{0:T(128)} %param.23) | copy-start | bytes 100
  200.1 8.7 %copy-start.40 = (f32[256]{0:T(256)}, f32[256]{0:T(256)S(1)}, u32[]{:S(2)}) copy-start(f32[256]{0:T(256)S(1)} %all-reduce) | copy-start | bytes 3076
  200.2 3.6 %collective-permute-start.3 = (f32[8]{0:T(128)S(1)}, f32[8]{0:T(128)S(1)}, u32[]{:S(2)}, u32[]{:S(2)}) collective-permute-start(f32[8]{0:T(128)S(1)} %select_reduce_fusion.1), channel_id=1, source_target_pairs={{0,4},{4,0},{8,12},{12,8},{1,5},{5,1},{9,13},{13,9},{2,6},{6,2},{1... | collective-permute-start | bytes 104 | tf_op jit(solution)/shard_map/ppermute | solution.py:27
  203.8 4.4 %collective-permute-start.4 = (f32[8]{0:T(128)S(1)}, f32[8]{0:T(128)S(1)}, u32[]{:S(2)}, u32[]{:S(2)}) collective-permute-start(f32[8]{0:T(128)S(1)} %add.282), channel_id=1, source_target_pairs={{0,8},{4,12},{8,0},{12,4},{1,9},{5,13},{9,1},{13,5},{2,10},{6,14},... | collective-permute-start | bytes 104 | tf_op jit(solution)/shard_map/ppermute | solution.py:27
  (31 other events, 76.6 us)
Sparse Core Ops, SparseCore 0:
  164.9 28.2 reduce-scatter.1

commit v9 on v8

--- a/solution.py
+++ b/solution.py
@@ -16,6 +16,22 @@
     count = lax.axis_size(axis)
     pairs = [(i, i + by) for i in range(count) if 0 <= i + by < count]
     return lax.ppermute(shard, axis, pairs)
+
+
+def scatter_sum(part, axes):
+    count = lax.axis_size(axes)
+    if count & (count - 1):
+        return lax.psum_scatter(part, axes, scatter_dimension=0, tiled=True)
+    place = lax.axis_index(axes)
+    bit = count // 2
+    while bit >= 1:
+        half = part.shape[0] // 2
+        upper = (place & bit) != 0
+        keep = jnp.where(upper, part[half:], part[:half])
+        give = jnp.where(upper, part[:half], part[half:])
+        part = keep + lax.ppermute(give, axes, [(i, i ^ bit) for i in range(count)])
+        bit //= 2
+    return part
 
 
 def sum_over(part, axis):
@@ -296,7 +312,7 @@
     lane_count = lax.axis_size(lanes)
     piece = row_count // lane_count
     piece_at = lax.axis_index(lanes) * piece
-    logits = lax.psum_scatter(partial_value, lanes, scatter_dimension=0, tiled=True)
+    logits = scatter_sum(partial_value, lanes)
     logprob_piece = log_probs(logits, lax.dynamic_slice_in_dim(token_ids, piece_at, piece, 0))
     logprob = lax.all_gather(logprob_piece, lanes, tiled=True)
     genome_index = jnp.arange(genome_lengths.shape[0], dtype=jnp.int32)

time: 216 us -> 191 us (0.88)
  waiting for transfers between devices: 32.9 us -> 11.5 us
  between operations: 15.3 us -> 1.95 us
  starting transfers between devices: 16.2 us -> 23 us
    reduce_scatter x1 -> x0, waiting for transfers between devices: 27 us -> none  [per_device(): lax.psum_scatter(partial_value, lanes, scatter_dimension=0, tiled=True)]
    ppermute x0 -> x2, waiting for transfers between devices: none -> 6.34 us  [scatter_sum(): part = keep + lax.ppermute(give, axes, [(i, i ^ bit) for i in range(count)])]
    ppermute x2, starting transfers between devices: 4.32 us -> 9.3 us  [sum_over(): part = part + lax.ppermute(part, axis, [(i, i ^ bit) for i in range(count)])]
    unnamed x108 -> x112, local copies, waits for them, and re-layouts: 26.9 us -> 27.7 us
  transfers between devices with their start and end apart: 6 -> 7, of which waited for: 4 -> 4; matrix products, arithmetic and copies ran while one was open for 38% -> 43% of each run, Pallas kernels for 0% -> 0%
where the time goes in v9:
time: 191 us; the launch traced here: 190 us
  local copies, waits for them, and re-layouts  56.3 us (29%)
  other arithmetic  43.4 us (23%)
  matrix products  40.7 us (21%)
  starting transfers between devices  23 us (12%)
  blocking collectives  12.9 us (7%)
  waiting for transfers between devices  11.5 us (6%)
  between operations  1.95 us (1%)
    unnamed x112, local copies, waits for them, and re-layouts  27.7 us
    dot_general x2, matrix products, medium_block(): jnp.einsum('gts,gis->git', matrix, window, preferred_element_type=jnp.flo...  11.9 us
    ppermute x3, starting transfers between devices, from_behind(): return lax.ppermute(shard, axis, pairs)  11.9 us
    mul x1, other arithmetic, modal_tables(): power_im = magnitude * jnp.sin(powers * angles[None])  9.38 us
    ppermute x2, starting transfers between devices, sum_over(): part = part + lax.ppermute(part, axis, [(i, i ^ bit) for i in range(count)])  9.3 us
    unnamed x1, blocking collectives  7.2 us
    select_n x1, other arithmetic, intra_block(): jnp.where(same_genome, toeplitz_upper, jnp.zeros_like(toeplitz_upper))  6.93 us
    dot_general x2, matrix products, intra_block(): jnp.einsum('gts,gis->git', upper, block_in, preferred_element_type=jnp.fl...  6.73 us
  transfers between devices with their start and end apart: 7, of which 4 were waited for; matrix products, arithmetic and copies ran while one was open for 43% of the time, Pallas kernels for 0%

profile of v9, /device:TPU:0, one launch (start us, length us, event | category | flops | bytes accessed | tf_op | source)
XLA Modules:
  0.0 189.9 jit_solution(5543026404329945336)
XLA Ops:
  3.2 5.9 %collective-permute-start = (bf16[2,136,2048]{2,1,0:T(8,128)(2,1)}, bf16[2,136,2048]{2,1,0:T(8,128)(2,1)}, u32[]{:S(2)}, u32[]{:S(2)}) collective-permute-start(bf16[2,136,2048]{2,1,0:T(8,128)(2,1)} %pad_maximum_fusion), channel_id=1, source_target_pairs={{0,4},{4,8},{8,12},{1,5},{5,9},{9,13},{2,6},{6,10},{10,14},{3,7},{... | collective-permute-start | bytes 3342344 | tf_op jit(solution)/shard_map/ppermute | solution.py:18
  10.7 9.4 %fusion.28 = (f32[129,128,16]{0,2,1:T(8,128)S(1)}, f32[129,128,16]{0,2,1:T(8,128)}, f32[129,128,16]{0,2,1:T(8,128)S(1)}) fusion(f32[128,16]{1,0:T(8,128)S(1)} %copy.89, f32[129]{0:T(256)S(1)} %iota_convert_fusion, f32[128,16]{1,0:T(8,128)S(1)} %copy.88, f32[129]{0:T(256)S(1)} %fusion.73, f32[128,16]{1,0:T(8,128)S(1)} %copy.90, f32[128,16]{1,0:T(8,128)S(1)} %copy.87), kind=kLoop, calls=%fused_computation.59 | loop fusion | flops 1849344 | bytes 3204104 | tf_op jit(solution)/shard_map/mul | solution.py:121
  26.8 3.2 %fusion.82 = (f32[128,128,16]{0,2,1:T(8,128)}, f32[128,128]{0,1:T(8,128)S(1)}) fusion(f32[129,128,16]{0,2,1:T(8,128)} %get-tuple-element.263), kind=kLoop, calls=%fused_computation.205 | loop fusion | flops 245760 | bytes 3211264 | tf_op jit(solution)/shard_map/slice | solution.py:126
  31.4 4.6 %convolution_convert_fusion = bf16[384,16384]{1,0:T(8,128)(2,1)S(1)} fusion(s32[16384]{0:T(1024)S(1)} %add_select_fusion, s32[128]{0:T(128)S(1)} %iota.77, bf16[128,128]{0,1:T(8,128)(2,1)S(1)} %get-tuple-element.224, bf16[128,128]{0,1:T(8,128)(2,1)} %get-tuple-element.225, bf16[128,128]{0,1:T(8,128)(2,1)S(1)} %copy.91), kind=kOutput, calls=%fused_computation.11 | convolution fusion | flops 1619296256 | bytes 12747264 | tf_op jit(solution)/shard_map/dot_general | solution.py:109
  36.0 3.9 %slice_bitcast_fusion = (bf16[16,8,128,128]{3,1,2,0:T(8,128)(2,1)}, bf16[16,8,128,128]{3,1,2,0:T(8,128)(2,1)}, bf16[16,8,128,128]{3,1,2,0:T(8,128)(2,1)S(1)}) fusion(bf16[384,16384]{1,0:T(8,128)(2,1)S(1)} %convolution_convert_fusion), kind=kLoop, calls=%fused_computation.23 | loop fusion | bytes 25165824
  54.5 5.6 %copy.106 = bf16[16,8,128,128]{3,2,1,0:T(8,128)(2,1)} copy(bf16[16,8,128,128]{3,1,2,0:T(8,128)(2,1)} %get-tuple-element.233) | data formatting | bytes 8388608
  60.1 3.2 %copy.107 = bf16[16,8,128,128]{3,2,1,0:T(8,128)(2,1)} copy(bf16[16,8,128,128]{3,1,2,0:T(8,128)(2,1)S(1)} %copy-done.3) | data formatting | bytes 8388608
  67.1 5.1 %constant_dynamic-update-slice_fusion = bf16[128,128,256]{2,1,0:T(8,128)(2,1)} fusion(bf16[128,128,256]{2,1,0:T(8,128)(2,1)} %constant_dynamic-update-slice_fusion.1, bf16[128,128,128]{2,1,0:T(8,128)(2,1)} %bitcast.152), kind=kLoop, calls=%fused_computation.163 | loop fusion | bytes 8388608 | tf_op jit(solution)/shard_map/concatenate | solution.py:211
  73.4 6.9 %bitcast_select_fusion.3 = (bf16[128,128,128]{2,1,0:T(8,128)(2,1)}, bf16[128,128,128]{2,1,0:T(8,128)(2,1)}, bf16[128,128,128]{2,1,0:T(8,128)(2,1)}, bf16[128,128,128]{2,1,0:T(8,128)(2,1)}) fusion(bf16[16,8,128,128]{3,2,1,0:T(8,128)(2,1)S(1)} %copy-done.4, pred[128,128]{1,0:T(8,128)(4,1)S(1)} %get-tuple-element.222, ...), kind=kLoop, calls=%fused_computation.22 | loop fusion | flops 8388608 | bytes 25198592 | tf_op jit(solution)/shard_map/jit(_where)/select_n | solution.py:242
  82.5 5.3 %fusion.36 = bf16[2048,384]{0,1:T(8,128)(2,1)} fusion(f32[384]{0:T(512)S(1)} %copy-done.36, f32[392,2048]{1,0:T(8,128)S(1)} %convert_multiply_fusion, f32[2048]{0:T(1024)S(1)} %bitcast.180, f32[384]{0:T(512)S(1)} %copy-done.32, f32[2048]{0:T(1024)S(1)} %bitcast.181, f32[384]{0:T(512)S(1)} %copy-done.33, f32[2048]{0:T(1024)S(1)} %bitcast.176, ...), kind=kLoop, calls=%fused_computation.75 | loop fusion | flops 15728640 | bytes 23659520 | tf_op jit(solution)/shard_map/transpose | solution.py:204
  90.4 6.1 %fusion.39 = bf16[128,16,128]{2,1,0:T(8,128)(2,1)S(1)} fusion(bf16[128,128,256]{2,1,0:T(8,128)(2,1)} %constant_dynamic-update-slice_fusion, pred[128,256]{1,0:T(8,128)(4,1)S(1)} %copy-done.28, bf16[128,16,384]{2,1,0:T(8,128)(2,1)} %bitcast.163), kind=kOutput, calls=%fused_computation.80 | convolution fusion | flops 138674176 | bytes 9994240 | tf_op jit(solution)/shard_map/gts,gis->git/dot_general | solution.py:228
  96.5 5.8 %fusion.42 = bf16[128,16,128]{2,1,0:T(8,128)(2,1)S(1)} fusion(bf16[128,128,256]{2,1,0:T(8,128)(2,1)} %constant_dynamic-update-slice_fusion, pred[128,256]{1,0:T(8,128)(4,1)S(1)} %get-tuple-element.293, bf16[128,16,384]{2,1,0:T(8,128)(2,1)S(1)} %bitcast.164), kind=kOutput, calls=%fused_computation.81 | convolution fusion | flops 138674176 | bytes 9994240 | tf_op jit(solution)/shard_map/gts,gis->git/dot_general | solution.py:228
  105.0 3.5 %copy.96 = f32[2,128,16,32]{1,3,2,0:T(8,128)} copy(f32[2,128,16,32]{3,2,0,1:T(8,128)} %add_bitcast_fusion) | data formatting | bytes 1048576
  108.5 6.2 %while.25 = (s32[]{:T(128)}, f32[128,16]{0,1:T(8,128)S(1)}, f32[128,16]{0,1:T(8,128)S(1)}, f32[128,16,16]{0,2,1:T(8,128)S(1)}, f32[128,16,16]{0,2,1:T(8,128)S(1)...) while((s32[]{:T(128)}, f32[128,16]{0,1:T(8,128)S(1)}, ...), condition=%wide.region_7.8_spmd.clone, body=%wide.region_6.7_spmd.clone.sunk | while | flops 421891 | bytes 1999539 | solution.py:275
  117.6 4.5 %fusion.85 = f32[128,16,128]{2,1,0:T(8,128)S(1)} fusion(bf16[128,16,128]{2,1,0:T(8,128)(2,1)S(1)} %fusion.39, bf16[128,128,128]{2,1,0:T(8,128)(2,1)} %get-tuple-element.237), kind=kOutput, calls=%fused_computation.208 | convolution fusion | flops 67108864 | bytes 5767168 | tf_op jit(solution)/shard_map/gts,gis->git/dot_general | solution.py:244
  122.1 3.3 %fusion.38 = f32[1,128,16,128]{3,2,1,0:T(8,128)} fusion(f32[128,16,128]{2,1,0:T(8,128)S(1)} %fusion.85, bf16[128,16,128]{2,1,0:T(8,128)(2,1)S(1)} %fusion.39, bf16[128,128,128]{2,1,0:T(8,128)(2,1)S(1)} %copy-done.7), kind=kOutput, calls=%fused_computation.79 | convolution fusion | flops 67371008 | bytes 6815744 | tf_op jit(solution)/shard_map/gts,gis->git/dot_general | solution.py:246
  127.8 3.1 %collective-permute-start.2 = (f32[128,544]{0,1:T(8,128)S(1)}, f32[128,544]{0,1:T(8,128)S(1)}, u32[]{:S(2)}, u32[]{:S(2)}) collective-permute-start(f32[128,544]{0,1:T(8,128)S(1)} %pad_maximum_fusion.4), channel_id=1, source_target_pairs={{0,8},{4,12},{1,9},{5,13},{2,10},{6,14},{3,11},{7,15},{16,24},{20,... | collective-permute-start | bytes 835592 | tf_op jit(solution)/shard_map/ppermute | solution.py:18
  131.0 3.3 %fusion.37 = f32[1,128,16,128]{3,2,1,0:T(8,128)} fusion(f32[128,16,128]{2,1,0:T(8,128)S(1)} %fusion.86, bf16[128,16,128]{2,1,0:T(8,128)(2,1)S(1)} %fusion.42, bf16[128,128,128]{2,1,0:T(8,128)(2,1)S(1)} %copy-done.6), kind=kOutput, calls=%fused_computation.77 | convolution fusion | flops 67371008 | bytes 6815744 | tf_op jit(solution)/shard_map/gts,gis->git/dot_general | solution.py:246
  140.5 5.3 %fusion.31 = f32[128,16,2,128]{3,1,0,2:T(8,128)S(1)} fusion(f32[1,128,16,128]{3,2,1,0:T(8,128)} %fusion.37, f32[1,128,16,128]{3,2,1,0:T(8,128)} %fusion.38, f32[2,128,16,32]{3,2,1,0:T(8,128)} %copy.102, f32[128,128,16]{0,2,1:T(8,128)} %get-tuple-element.241, f32[128,128,16]{0,2,1:T(8,128)} %get-tuple-element.239, f32[128,16]{1,0:T(8,128)S(1)} %mul.573, ...), kind=kOutput, calls=%fused_computation.64 | convolution fusion | flops 205520896 | bytes 7873536 | tf_op jit(solution)/shard_map/gtm,jgim->jgit/dot_general | solution.py:290
  149.2 5.7 %psum.7 = f32[256]{0:T(256)S(1)} all-reduce(f32[256]{0:T(256)S(1)} %fusion.24), channel_id=1, replica_groups=mesh['groups'=2,'seq'=4,'chan'=2,'rep'=2] {'chan','rep'}, use_global_device_ids=true, to_apply=%region_9.10 | all-reduce | flops 256 | bytes 2048 | tf_op jit(solution)/shard_map/psum | solution.py:306
  160.5 6.3 %collective-permute-done.3 = f32[128,512]{1,0:T(8,128)S(1)} collective-permute-done((f32[128,512]{1,0:T(8,128)S(1)}, f32[128,512]{1,0:T(8,128)S(1)}, u32[]{:S(2)}, u32[]{:S(2)}) %collective-permute-start.3) | collective-permute-done | bytes 262176 | tf_op jit(solution)/shard_map/ppermute | solution.py:32
  169.7 7.2 %all-reduce = f32[256]{0:T(256)S(1)} all-reduce(f32[256]{0:T(256)S(1)} %subtract_dynamic-update-slice_fusion), channel_id=1, replica_groups=mesh['groups'=2,'seq'=4,'chan'=2,'rep'=2] {'chan','rep'}, use_global_device_ids=true, to_apply=%add | all-reduce | flops 256 | bytes 2048
  177.0 5.9 %collective-permute-start.5 = (f32[8]{0:T(128)S(1)}, f32[8]{0:T(128)S(1)}, u32[]{:S(2)}, u32[]{:S(2)}) collective-permute-start(f32[8]{0:T(128)S(1)} %select_reduce_fusion.1), channel_id=1, source_target_pairs={{0,4},{4,0},{8,12},{12,8},{1,5},{5,1},{9,13},{13,9},{2,6},{6,2},{1... | collective-permute-start | bytes 104 | tf_op jit(solution)/shard_map/ppermute | solution.py:43
  184.5 3.4 %collective-permute-start.6 = (f32[8]{0:T(128)S(1)}, f32[8]{0:T(128)S(1)}, u32[]{:S(2)}, u32[]{:S(2)}) collective-permute-start(f32[8]{0:T(128)S(1)} %add.289), channel_id=1, source_target_pairs={{0,8},{4,12},{8,0},{12,4},{1,9},{5,13},{9,1},{13,5},{2,10},{6,14},... | collective-permute-start | bytes 104 | tf_op jit(solution)/shard_map/ppermute | solution.py:43
  (215 shorter events, 71.5 us)
Async XLA Ops:
  0.6 154.2 %copy-start = (bf16[2048,512]{1,0:T(8,128)(2,1)S(1)}, bf16[2048,512]{1,0:T(8,128)(2,1)}, u32[]{:S(2)}) copy-start(bf16[2048,512]{1,0:T(8,128)(2,1)} %param.21) | copy-start | bytes 6291460
  0.6 9.6 %copy-start.27 = (f32[4,128,16]{1,2,0:T(8,128)S(1)}, f32[4,128,16]{1,2,0:T(8,128)}, u32[]{:S(2)}) copy-start(f32[4,128,16]{1,2,0:T(8,128)} %param.18) | copy-start | bytes 98308
  3.2 77.1 %collective-permute-start = (bf16[2,136,2048]{2,1,0:T(8,128)(2,1)}, bf16[2,136,2048]{2,1,0:T(8,128)(2,1)}, u32[]{:S(2)}, u32[]{:S(2)}) collective-permute-start(bf16[2,136,2048]{2,1,0:T(8,128)(2,1)} %pad_maximum_fusion), channel_id=1, source_target_pairs={{0,4},{4,8},{8,12},{1,5},{5,9},{9,13},{2,6},{6,10},{10,14},{3,7},{... | collective-permute-start | bytes 3342344 | tf_op jit(solution)/shard_map/ppermute | solution.py:18
  54.5 5.6 %copy-start.3 = (bf16[16,8,128,128]{3,1,2,0:T(8,128)(2,1)S(1)}, bf16[16,8,128,128]{3,1,2,0:T(8,128)(2,1)}, u32[]{:S(2)}) copy-start(bf16[16,8,128,128]{3,1,2,0:T(8,128)(2,1)} %get-tuple-element.232) | copy-start | bytes 12582916
  67.1 6.2 %copy-start.5 = (bf16[16,8,128,128]{3,2,1,0:T(8,128)(2,1)S(1)}, bf16[16,8,128,128]{3,2,1,0:T(8,128)(2,1)}, u32[]{:S(2)}) copy-start(bf16[16,8,128,128]{3,2,1,0:T(8,128)(2,1)} %copy.107) | copy-start | bytes 12582916
  73.4 8.2 %copy-start.12 = (bf16[256,2048]{1,0:T(8,128)(2,1)S(1)}, bf16[256,2048]{1,0:T(8,128)(2,1)}, u32[]{:S(2)}) copy-start(bf16[256,2048]{1,0:T(8,128)(2,1)} %param.14) | copy-start | bytes 3145732
  73.4 8.2 %copy-start.13 = (bf16[256,2048]{1,0:T(8,128)(2,1)S(1)}, bf16[256,2048]{1,0:T(8,128)(2,1)}, u32[]{:S(2)}) copy-start(bf16[256,2048]{1,0:T(8,128)(2,1)} %param.15) | copy-start | bytes 3145732
  90.4 6.1 %copy-start.15 = (bf16[2048,384]{1,0:T(8,128)(2,1)S(1)}, bf16[2048,384]{1,0:T(8,128)(2,1)}, u32[]{:S(2)}) copy-start(bf16[2048,384]{1,0:T(8,128)(2,1)} %copy.86) | copy-start | bytes 4718596
  96.4 5.8 %copy-start.8 = (f32[128,128,16]{0,2,1:T(8,128)S(1)}, f32[128,128,16]{0,2,1:T(8,128)}, u32[]{:S(2)}) copy-start(f32[128,128,16]{0,2,1:T(8,128)} %rev.6) | copy-start | bytes 3145732
  96.5 5.8 %copy-start.9 = (f32[128,128,16]{0,2,1:T(8,128)S(1)}, f32[128,128,16]{0,2,1:T(8,128)}, u32[]{:S(2)}) copy-start(f32[128,128,16]{0,2,1:T(8,128)} %rev.7) | copy-start | bytes 3145732
  96.5 5.8 %copy-start.40 = (pred[2,128]{1,0:T(4,128)(4,1)S(1)}, pred[2,128]{1,0:T(4,128)(4,1)}, u32[]{:S(2)}) copy-start(pred[2,128]{1,0:T(4,128)(4,1)} %get-tuple-element.287) | copy-start | bytes 772
  114.8 7.3 %copy-start.7 = (bf16[128,128,128]{2,1,0:T(8,128)(2,1)S(1)}, bf16[128,128,128]{2,1,0:T(8,128)(2,1)}, u32[]{:S(2)}) copy-start(bf16[128,128,128]{2,1,0:T(8,128)(2,1)} %get-tuple-element.266) | copy-start | bytes 12582916
  114.8 12.9 %collective-permute-start.1 = (f32[128,544]{0,1:T(8,128)S(1)}, f32[128,544]{0,1:T(8,128)S(1)}, u32[]{:S(2)}, u32[]{:S(2)}) collective-permute-start(f32[128,544]{0,1:T(8,128)S(1)} %pad_maximum_fusion.3), channel_id=1, source_target_pairs={{0,4},{4,8},{8,12},{1,5},{5,9},{9,13},{2,6},{6,10},{10,14},{3,7},{... | collective-permute-start | bytes 835592 | tf_op jit(solution)/shard_map/ppermute | solution.py:18
  127.8 8.6 %collective-permute-start.2 = (f32[128,544]{0,1:T(8,128)S(1)}, f32[128,544]{0,1:T(8,128)S(1)}, u32[]{:S(2)}, u32[]{:S(2)}) collective-permute-start(f32[128,544]{0,1:T(8,128)S(1)} %pad_maximum_fusion.4), channel_id=1, source_target_pairs={{0,8},{4,12},{1,9},{5,13},{2,10},{6,14},{3,11},{7,15},{16,24},{20,... | collective-permute-start | bytes 835592 | tf_op jit(solution)/shard_map/ppermute | solution.py:18
  134.2 6.3 %copy-start.41 = (f32[2,128]{1,0:T(2,128)S(1)}, f32[2,128]{1,0:T(2,128)}, u32[]{:S(2)}) copy-start(f32[2,128]{1,0:T(2,128)} %get-tuple-element.286) | copy-start | bytes 3076
  145.8 9.0 %copy-start.46 = (f32[2048]{0:T(1024)S(1)}, f32[2048]{0:T(1024)}, u32[]{:S(2)}) copy-start(f32[2048]{0:T(1024)} %param.20) | copy-start | bytes 24580
  154.8 13.2 %copy-start.47 = (s32[256]{0:T(256)S(1)}, s32[256]{0:T(256)}, u32[]{:S(2)}) copy-start(s32[256]{0:T(256)} %param.22) | copy-start | bytes 3076
  154.8 13.3 %copy-start.48 = (u32[32]{0:T(128)S(1)}, u32[32]{0:T(128)}, u32[]{:S(2)}) copy-start(u32[32]{0:T(128)} %constant.98) | copy-start | bytes 388
  154.8 34.5 %copy-start.45 = (s32[8]{0:T(128)S(1)}, s32[8]{0:T(128)}, u32[]{:S(2)}) copy-start(s32[8]{0:T(128)} %param.23) | copy-start | bytes 100
  158.7 8.1 %collective-permute-start.3 = (f32[128,512]{1,0:T(8,128)S(1)}, f32[128,512]{1,0:T(8,128)S(1)}, u32[]{:S(2)}, u32[]{:S(2)}) collective-permute-start(f32[128,512]{1,0:T(8,128)S(1)} %slice_select_fusion), channel_id=1, source_target_pairs={{0,2},{1,3},{2,0},{3,1},{4,6},{5,7},{6,4},{7,5},{8,10},{9,11},{10,... | collective-permute-start | bytes 786440 | tf_op jit(solution)/shard_map/ppermute | solution.py:32
  168.0 1.4 collective-permute-start.4
  176.9 13.0 %copy-start.42 = (f32[256]{0:T(256)}, f32[256]{0:T(256)S(1)}, u32[]{:S(2)}) copy-start(f32[256]{0:T(256)S(1)} %all-reduce) | copy-start | bytes 3076
  177.0 7.4 %collective-permute-start.5 = (f32[8]{0:T(128)S(1)}, f32[8]{0:T(128)S(1)}, u32[]{:S(2)}, u32[]{:S(2)}) collective-permute-start(f32[8]{0:T(128)S(1)} %select_reduce_fusion.1), channel_id=1, source_target_pairs={{0,4},{4,0},{8,12},{12,8},{1,5},{5,1},{9,13},{13,9},{2,6},{6,2},{1... | collective-permute-start | bytes 104 | tf_op jit(solution)/shard_map/ppermute | solution.py:43
  184.5 4.9 %collective-permute-start.6 = (f32[8]{0:T(128)S(1)}, f32[8]{0:T(128)S(1)}, u32[]{:S(2)}, u32[]{:S(2)}) collective-permute-start(f32[8]{0:T(128)S(1)} %add.289), channel_id=1, source_target_pairs={{0,8},{4,12},{8,0},{12,4},{1,9},{5,13},{9,1},{13,5},{2,10},{6,14},... | collective-permute-start | bytes 104 | tf_op jit(solution)/shard_map/ppermute | solution.py:43
  (34 other events, 88.7 us)

commit v10 on v9

--- a/solution.py
+++ b/solution.py
@@ -115,20 +115,37 @@
     angles = modal_poles[1]
     residue_re = modal_poles[2]
     residue_im = modal_poles[3]
-    powers = jnp.arange(tile_rows + 1).astype(jnp.float32)[:, None, None]
-    magnitude = jnp.exp(-powers * decay_rate[None])
-    power_re = magnitude * jnp.cos(powers * angles[None])
-    power_im = magnitude * jnp.sin(powers * angles[None])
+
+    def pole_powers(exponents):
+        magnitude = jnp.exp(-exponents * decay_rate[None])
+        return (
+            magnitude * jnp.cos(exponents * angles[None]),
+            magnitude * jnp.sin(exponents * angles[None]),
+        )
+
+    power_re, power_im = pole_powers(jnp.arange(tile_rows).astype(jnp.float32)[:, None, None])
+    last_re, last_im = pole_powers(jnp.full((1, 1, 1), tile_rows, jnp.float32))
     kernel_re = residue_re[None] * power_re - residue_im[None] * power_im
     kernel_im = residue_re[None] * power_im + residue_im[None] * power_re
-    kernel = jnp.sum(kernel_re[:tile_rows], axis=2)
+    end_re = residue_re[None] * last_re - residue_im[None] * last_im
+    end_im = residue_re[None] * last_im + residue_im[None] * last_re
+    kernel = jnp.sum(kernel_re, axis=2)
     toeplitz = split_table(kernel)
-    outward = jnp.transpose(jnp.concatenate((kernel_re[1:], -kernel_im[1:]), axis=2), (1, 0, 2))
+    outward = jnp.transpose(
+        jnp.concatenate(
+            (
+                jnp.concatenate((kernel_re[1:], end_re), axis=0),
+                -jnp.concatenate((kernel_im[1:], end_im), axis=0),
+            ),
+            axis=2,
+        ),
+        (1, 0, 2),
+    )
     inward = jnp.transpose(
         jnp.concatenate((power_re[tile_rows - 1 :: -1], power_im[tile_rows - 1 :: -1]), axis=2),
         (1, 0, 2),
     )
-    return (toeplitz, outward, inward, power_re[tile_rows], power_im[tile_rows])
+    return (toeplitz, outward, inward, last_re[0], last_im[0])
 
 
 def split_table(table):

time: 191 us -> 199 us (1.042)
  local copies, waits for them, and re-layouts: 56.3 us -> 60.7 us
  other arithmetic: 43.4 us -> 46.4 us
    mul x1 -> x0, other arithmetic: 9.38 us -> none  [modal_tables(): power_im = magnitude * jnp.sin(powers * angles[None])]
    sub x0 -> x2, other arithmetic: none -> 8.19 us  [the longest x1 7.51 us: modal_tables(): kernel_re = residue_re[None] * power_re - residue_im[None] * power_im]
    slice x1 -> x0, other arithmetic: 3.18 us -> none  [modal_tables(): kernel_re[1:]]
    add x0 -> x1, other arithmetic: none -> 3.1 us  [modal_tables(): kernel_im = residue_re[None] * power_im + residue_im[None] * power_re]
    slice x4 -> x1, local copies, waits for them, and re-layouts: 5.44 us -> 2.54 us  [modal_tables(): kernel_re[1:]]
    add x0 -> x1, local copies, waits for them, and re-layouts: none -> 2.24 us  [modal_tables(): end_im = residue_re[None] * last_im + residue_im[None] * last_re]
    sub x0 -> x1, local copies, waits for them, and re-layouts: none -> 2.08 us  [modal_tables(): end_re = residue_re[None] * last_re - residue_im[None] * last_im]
  transfers between devices with their start and end apart: 7 -> 7, of which waited for: 4 -> 4; matrix products, arithmetic and copies ran while one was open for 43% -> 46% of each run, Pallas kernels for 0% -> 0%
where the time goes in v10:
time: 199 us; the launch traced here: 198 us
  local copies, waits for them, and re-layouts  60.7 us (31%)
  other arithmetic  46.4 us (23%)
  matrix products  41.1 us (21%)
  starting transfers between devices  23 us (12%)
  blocking collectives  12.9 us (6%)
  waiting for transfers between devices  11.5 us (6%)
    unnamed x112, local copies, waits for them, and re-layouts  28.1 us
    dot_general x2, matrix products, medium_block(): jnp.einsum('gts,gis->git', matrix, window, preferred_element_type=jnp.flo...  11.9 us
    ppermute x3, starting transfers between devices, from_behind(): return lax.ppermute(shard, axis, pairs)  11.8 us
    ppermute x2, starting transfers between devices, sum_over(): part = part + lax.ppermute(part, axis, [(i, i ^ bit) for i in range(count)])  9.3 us
    sub x1, other arithmetic, modal_tables(): kernel_re = residue_re[None] * power_re - residue_im[None] * power_im  7.51 us
    unnamed x1, blocking collectives  7.2 us
    select_n x1, other arithmetic, intra_block(): jnp.where(same_genome, toeplitz_upper, jnp.zeros_like(toeplitz_upper))  6.93 us
    dot_general x2, matrix products, intra_block(): jnp.einsum('gts,gis->git', upper, block_in, preferred_element_type=jnp.fl...  6.73 us
  transfers between devices with their start and end apart: 7, of which 4 were waited for; matrix products, arithmetic and copies ran while one was open for 46% of the time, Pallas kernels for 0%

profile of v10, /device:TPU:0, one launch (start us, length us, event | category | flops | bytes accessed | tf_op | source)
XLA Modules:
  0.0 197.7 jit_solution(3640524859059632844)
XLA Ops:
  3.2 5.9 %collective-permute-start = (bf16[2,136,2048]{2,1,0:T(8,128)(2,1)}, bf16[2,136,2048]{2,1,0:T(8,128)(2,1)}, u32[]{:S(2)}, u32[]{:S(2)}) collective-permute-start(bf16[2,136,2048]{2,1,0:T(8,128)(2,1)} %pad_maximum_fusion), channel_id=1, source_target_pairs={{0,4},{4,8},{8,12},{1,5},{5,9},{9,13},{2,6},{6,10},{10,14},{3,7},{... | collective-permute-start | bytes 3342344 | tf_op jit(solution)/shard_map/ppermute | solution.py:18
  14.3 7.5 %multiply_subtract_fusion.1 = (f32[128,128,16]{0,2,1:T(8,128)}, f32[128,128]{0,1:T(8,128)}, f32[128,128,16]{0,2,1:T(8,128)S(1)}, f32[128,128,16]{0,2,1:T(8,128)}) fusion(f32[128,16]{1,0:T(8,128)S(1)} %copy.137, f32[128,16]{1,0:T(8,128)S(1)} %copy.134, f32[128,16]{1,0:T(8,128)} %copy.136, f32[128]{0:T(128)} %iota_convert_fusion, f32[128,16]{1,0:T(8,128)} %copy.135, ...), kind=kLoop, calls=%fused_computation.96 | loop fusion | flops 2080768 | bytes 3245056 | tf_op jit(solution)/shard_map/sub | solution.py:128
  34.2 4.6 %convolution_convert_fusion = bf16[384,16384]{1,0:T(8,128)(2,1)S(1)} fusion(s32[16384]{0:T(1024)} %add_select_fusion, s32[128]{0:T(128)S(1)} %iota.77, bf16[128,128]{0,1:T(8,128)(2,1)S(1)} %get-tuple-element.237, bf16[128,128]{0,1:T(8,128)(2,1)S(1)} %get-tuple-element.238, bf16[128,128]{0,1:T(8,128)(2,1)S(1)} %copy.138), kind=kOutput, calls=%fused_computation.11 | convolution fusion | flops 1619296256 | bytes 12747264 | tf_op jit(solution)/shard_map/dot_general | solution.py:109
  38.8 3.9 %slice_bitcast_fusion = (bf16[16,8,128,128]{3,1,2,0:T(8,128)(2,1)}, bf16[16,8,128,128]{3,1,2,0:T(8,128)(2,1)}, bf16[16,8,128,128]{3,1,2,0:T(8,128)(2,1)S(1)}) fusion(bf16[384,16384]{1,0:T(8,128)(2,1)S(1)} %convolution_convert_fusion), kind=kLoop, calls=%fused_computation.23 | loop fusion | bytes 25165824
  50.2 5.5 %copy.153 = bf16[16,8,128,128]{3,2,1,0:T(8,128)(2,1)} copy(bf16[16,8,128,128]{3,1,2,0:T(8,128)(2,1)} %get-tuple-element.246) | data formatting | bytes 8388608
  55.7 3.2 %copy.154 = bf16[16,8,128,128]{3,2,1,0:T(8,128)(2,1)} copy(bf16[16,8,128,128]{3,1,2,0:T(8,128)(2,1)S(1)} %copy-done.5) | data formatting | bytes 8388608
  74.6 5.1 %constant_dynamic-update-slice_fusion = bf16[128,128,256]{2,1,0:T(8,128)(2,1)} fusion(bf16[128,128,256]{2,1,0:T(8,128)(2,1)} %constant_dynamic-update-slice_fusion.1, bf16[128,128,128]{2,1,0:T(8,128)(2,1)} %bitcast.154), kind=kLoop, calls=%fused_computation.169 | loop fusion | bytes 8388608 | tf_op jit(solution)/shard_map/concatenate | solution.py:228
  80.8 6.9 %bitcast_select_fusion.3 = (bf16[128,128,128]{2,1,0:T(8,128)(2,1)}, bf16[128,128,128]{2,1,0:T(8,128)(2,1)}, bf16[128,128,128]{2,1,0:T(8,128)(2,1)}, bf16[128,128,128]{2,1,0:T(8,128)(2,1)}) fusion(bf16[16,8,128,128]{3,2,1,0:T(8,128)(2,1)S(1)} %copy-done.3, pred[128,128]{1,0:T(8,128)(4,1)S(1)} %get-tuple-element.235, ...), kind=kLoop, calls=%fused_computation.22 | loop fusion | flops 8388608 | bytes 25198592 | tf_op jit(solution)/shard_map/jit(_where)/select_n | solution.py:259
  89.9 5.3 %fusion.36 = bf16[2048,384]{0,1:T(8,128)(2,1)} fusion(f32[384]{0:T(512)S(1)} %copy-done.39, f32[392,2048]{1,0:T(8,128)S(1)} %convert_multiply_fusion, f32[2048]{0:T(1024)S(1)} %bitcast.180, f32[384]{0:T(512)S(1)} %copy-done.35, f32[2048]{0:T(1024)S(1)} %bitcast.181, f32[384]{0:T(512)S(1)} %copy-done.36, f32[2048]{0:T(1024)S(1)} %bitcast.176, ...), kind=kLoop, calls=%fused_computation.71 | loop fusion | flops 15728640 | bytes 23659520 | tf_op jit(solution)/shard_map/transpose | solution.py:221
  97.8 6.1 %fusion.39 = bf16[128,16,128]{2,1,0:T(8,128)(2,1)S(1)} fusion(bf16[128,128,256]{2,1,0:T(8,128)(2,1)} %constant_dynamic-update-slice_fusion, pred[128,256]{1,0:T(8,128)(4,1)S(1)} %get-tuple-element.305, bf16[128,16,384]{2,1,0:T(8,128)(2,1)} %bitcast.165), kind=kOutput, calls=%fused_computation.78 | convolution fusion | flops 138674176 | bytes 9994240 | tf_op jit(solution)/shard_map/gts,gis->git/dot_general | solution.py:245
  103.9 5.8 %fusion.42 = bf16[128,16,128]{2,1,0:T(8,128)(2,1)S(1)} fusion(bf16[128,128,256]{2,1,0:T(8,128)(2,1)} %constant_dynamic-update-slice_fusion, pred[128,256]{1,0:T(8,128)(4,1)S(1)} %get-tuple-element.306, bf16[128,16,384]{2,1,0:T(8,128)(2,1)S(1)} %bitcast.166), kind=kOutput, calls=%fused_computation.79 | convolution fusion | flops 138674176 | bytes 9994240 | tf_op jit(solution)/shard_map/gts,gis->git/dot_general | solution.py:245
  112.5 3.5 %copy.141 = f32[2,128,16,32]{1,3,2,0:T(8,128)} copy(f32[2,128,16,32]{3,2,0,1:T(8,128)} %add_bitcast_fusion) | data formatting | bytes 1048576
  116.0 6.2 %while.25 = (s32[]{:T(128)}, f32[128,16]{0,1:T(8,128)S(1)}, f32[128,16]{0,1:T(8,128)S(1)}, f32[128,16,16]{0,2,1:T(8,128)S(1)}, f32[128,16,16]{0,2,1:T(8,128)S(1)...) while((s32[]{:T(128)}, f32[128,16]{0,1:T(8,128)S(1)}, ...), condition=%wide.region_7.8_spmd.clone, body=%wide.region_6.7_spmd.clone.sunk | while | flops 421891 | bytes 1999539 | solution.py:292
  125.0 4.5 %fusion.88 = f32[128,16,128]{2,1,0:T(8,128)S(1)} fusion(bf16[128,16,128]{2,1,0:T(8,128)(2,1)S(1)} %fusion.39, bf16[128,128,128]{2,1,0:T(8,128)(2,1)} %get-tuple-element.250), kind=kOutput, calls=%fused_computation.216 | convolution fusion | flops 67108864 | bytes 5767168 | tf_op jit(solution)/shard_map/gts,gis->git/dot_general | solution.py:261
  129.5 3.3 %fusion.38 = f32[1,128,16,128]{3,2,1,0:T(8,128)} fusion(f32[128,16,128]{2,1,0:T(8,128)S(1)} %fusion.88, bf16[128,16,128]{2,1,0:T(8,128)(2,1)S(1)} %fusion.39, bf16[128,128,128]{2,1,0:T(8,128)(2,1)S(1)} %copy-done.7), kind=kOutput, calls=%fused_computation.77 | convolution fusion | flops 67371008 | bytes 6815744 | tf_op jit(solution)/shard_map/gts,gis->git/dot_general | solution.py:263
  135.2 3.2 %collective-permute-start.2 = (f32[128,544]{0,1:T(8,128)S(1)}, f32[128,544]{0,1:T(8,128)S(1)}, u32[]{:S(2)}, u32[]{:S(2)}) collective-permute-start(f32[128,544]{0,1:T(8,128)S(1)} %pad_maximum_fusion.4), channel_id=1, source_target_pairs={{0,8},{4,12},{1,9},{5,13},{2,10},{6,14},{3,11},{7,15},{16,24},{20,... | collective-permute-start | bytes 835592 | tf_op jit(solution)/shard_map/ppermute | solution.py:18
  138.4 3.3 %fusion.37 = f32[1,128,16,128]{3,2,1,0:T(8,128)} fusion(f32[128,16,128]{2,1,0:T(8,128)S(1)} %fusion.89, bf16[128,16,128]{2,1,0:T(8,128)(2,1)S(1)} %fusion.42, bf16[128,128,128]{2,1,0:T(8,128)(2,1)S(1)} %copy-done.6), kind=kOutput, calls=%fused_computation.75 | convolution fusion | flops 67371008 | bytes 6815744 | tf_op jit(solution)/shard_map/gts,gis->git/dot_general | solution.py:263
  144.8 3.1 %copy.149 = f32[2,128,16,32]{3,2,1,0:T(8,128)} copy(f32[2,128,16,32]{1,3,2,0:T(8,128)} %pad_maximum_fusion.2) | data formatting | bytes 1048576 | tf_op jit(solution)/shard_map/concatenate | solution.py:310
  148.0 5.6 %fusion.29 = f32[128,16,2,128]{3,1,0,2:T(8,128)S(1)} fusion(f32[1,128,16,128]{3,2,1,0:T(8,128)} %fusion.37, f32[1,128,16,128]{3,2,1,0:T(8,128)} %fusion.38, f32[2,128,16,32]{3,2,1,0:T(8,128)} %copy.149, f32[128,128,16]{0,2,1:T(8,128)} %maximum_negate_fusion, f32[1,128,16]{0,2,1:T(8,128)} %copy.142, f32[127,128,16]{0,2,1:T(8,128)} %slice.238, ...), kind=kOutput, calls=%fused_computation.60 | convolution fusion | flops 206045184 | bytes 7873536 | tf_op jit(solution)/shard_map/gtm,jgim->jgit/dot_general | solution.py:307
  156.9 5.7 %psum.7 = f32[256]{0:T(256)S(1)} all-reduce(f32[256]{0:T(256)S(1)} %fusion.24), channel_id=1, replica_groups=mesh['groups'=2,'seq'=4,'chan'=2,'rep'=2] {'chan','rep'}, use_global_device_ids=true, to_apply=%region_9.10 | all-reduce | flops 256 | bytes 2048 | tf_op jit(solution)/shard_map/psum | solution.py:323
  168.3 6.4 %collective-permute-done.3 = f32[128,512]{1,0:T(8,128)S(1)} collective-permute-done((f32[128,512]{1,0:T(8,128)S(1)}, f32[128,512]{1,0:T(8,128)S(1)}, u32[]{:S(2)}, u32[]{:S(2)}) %collective-permute-start.3) | collective-permute-done | bytes 262176 | tf_op jit(solution)/shard_map/ppermute | solution.py:32
  177.5 7.2 %all-reduce = f32[256]{0:T(256)S(1)} all-reduce(f32[256]{0:T(256)S(1)} %subtract_dynamic-update-slice_fusion), channel_id=1, replica_groups=mesh['groups'=2,'seq'=4,'chan'=2,'rep'=2] {'chan','rep'}, use_global_device_ids=true, to_apply=%add | all-reduce | flops 256 | bytes 2048
  184.8 5.9 %collective-permute-start.5 = (f32[8]{0:T(128)S(1)}, f32[8]{0:T(128)S(1)}, u32[]{:S(2)}, u32[]{:S(2)}) collective-permute-start(f32[8]{0:T(128)S(1)} %select_reduce_fusion.1), channel_id=1, source_target_pairs={{0,4},{4,0},{8,12},{12,8},{1,5},{5,1},{9,13},{13,9},{2,6},{6,2},{1... | collective-permute-start | bytes 104 | tf_op jit(solution)/shard_map/ppermute | solution.py:43
  192.3 3.4 %collective-permute-start.6 = (f32[8]{0:T(128)S(1)}, f32[8]{0:T(128)S(1)}, u32[]{:S(2)}, u32[]{:S(2)}) collective-permute-start(f32[8]{0:T(128)S(1)} %add.293), channel_id=1, source_target_pairs={{0,8},{4,12},{8,0},{12,4},{1,9},{5,13},{9,1},{13,5},{2,10},{6,14},... | collective-permute-start | bytes 104 | tf_op jit(solution)/shard_map/ppermute | solution.py:43
  (214 shorter events, 80.9 us)
Async XLA Ops:
  0.6 162.0 %copy-start = (bf16[2048,512]{1,0:T(8,128)(2,1)S(1)}, bf16[2048,512]{1,0:T(8,128)(2,1)}, u32[]{:S(2)}) copy-start(bf16[2048,512]{1,0:T(8,128)(2,1)} %param.21) | copy-start | bytes 6291460
  0.6 11.3 %copy-start.29 = (f32[4,128,16]{1,2,0:T(8,128)S(1)}, f32[4,128,16]{1,2,0:T(8,128)}, u32[]{:S(2)}) copy-start(f32[4,128,16]{1,2,0:T(8,128)} %param.18) | copy-start | bytes 98308
  3.2 84.5 %collective-permute-start = (bf16[2,136,2048]{2,1,0:T(8,128)(2,1)}, bf16[2,136,2048]{2,1,0:T(8,128)(2,1)}, u32[]{:S(2)}, u32[]{:S(2)}) collective-permute-start(bf16[2,136,2048]{2,1,0:T(8,128)(2,1)} %pad_maximum_fusion), channel_id=1, source_target_pairs={{0,4},{4,8},{8,12},{1,5},{5,9},{9,13},{2,6},{6,10},{10,14},{3,7},{... | collective-permute-start | bytes 3342344 | tf_op jit(solution)/shard_map/ppermute | solution.py:18
  47.5 8.3 %copy-start.32 = (s32[256]{0:T(256)}, s32[256]{0:T(256)S(1)}, u32[]{:S(2)}) copy-start(s32[256]{0:T(256)S(1)} %get-tuple-element.302) | copy-start | bytes 3076
  48.0 10.9 %copy-start.40 = (s32[128]{0:T(128)}, s32[128]{0:T(128)S(1)}, u32[]{:S(2)}) copy-start(s32[128]{0:T(128)S(1)} %get-tuple-element.307) | copy-start | bytes 1540
  59.0 13.0 %copy-start.11 = (f32[127,128,16]{0,2,1:T(8,128)S(1)}, f32[127,128,16]{0,2,1:T(8,128)}, u32[]{:S(2)}) copy-start(f32[127,128,16]{0,2,1:T(8,128)} %fusion.54) | copy-start | bytes 3121156
  74.6 6.2 %copy-start.4 = (bf16[16,8,128,128]{3,2,1,0:T(8,128)(2,1)S(1)}, bf16[16,8,128,128]{3,2,1,0:T(8,128)(2,1)}, u32[]{:S(2)}) copy-start(bf16[16,8,128,128]{3,2,1,0:T(8,128)(2,1)} %copy.154) | copy-start | bytes 12582916
  80.8 8.2 %copy-start.13 = (bf16[256,2048]{1,0:T(8,128)(2,1)S(1)}, bf16[256,2048]{1,0:T(8,128)(2,1)}, u32[]{:S(2)}) copy-start(bf16[256,2048]{1,0:T(8,128)(2,1)} %param.14) | copy-start | bytes 3145732
  80.8 8.2 %copy-start.14 = (bf16[256,2048]{1,0:T(8,128)(2,1)S(1)}, bf16[256,2048]{1,0:T(8,128)(2,1)}, u32[]{:S(2)}) copy-start(bf16[256,2048]{1,0:T(8,128)(2,1)} %param.15) | copy-start | bytes 3145732
  122.2 7.3 %copy-start.7 = (bf16[128,128,128]{2,1,0:T(8,128)(2,1)S(1)}, bf16[128,128,128]{2,1,0:T(8,128)(2,1)}, u32[]{:S(2)}) copy-start(bf16[128,128,128]{2,1,0:T(8,128)(2,1)} %get-tuple-element.275) | copy-start | bytes 12582916
  122.2 12.8 %collective-permute-start.1 = (f32[128,544]{0,1:T(8,128)S(1)}, f32[128,544]{0,1:T(8,128)S(1)}, u32[]{:S(2)}, u32[]{:S(2)}) collective-permute-start(f32[128,544]{0,1:T(8,128)S(1)} %pad_maximum_fusion.3), channel_id=1, source_target_pairs={{0,4},{4,8},{8,12},{1,5},{5,9},{9,13},{2,6},{6,10},{10,14},{3,7},{... | collective-permute-start | bytes 835592 | tf_op jit(solution)/shard_map/ppermute | solution.py:18
  135.2 8.6 %collective-permute-start.2 = (f32[128,544]{0,1:T(8,128)S(1)}, f32[128,544]{0,1:T(8,128)S(1)}, u32[]{:S(2)}, u32[]{:S(2)}) collective-permute-start(f32[128,544]{0,1:T(8,128)S(1)} %pad_maximum_fusion.4), channel_id=1, source_target_pairs={{0,8},{4,12},{1,9},{5,13},{2,10},{6,14},{3,11},{7,15},{16,24},{20,... | collective-permute-start | bytes 835592 | tf_op jit(solution)/shard_map/ppermute | solution.py:18
  141.7 6.3 %copy-start.19 = (f32[128,16]{1,0:T(8,128)S(1)}, f32[128,16]{1,0:T(8,128)}, u32[]{:S(2)}) copy-start(f32[128,16]{1,0:T(8,128)} %mul.610) | copy-start | bytes 24580
  141.7 6.3 %copy-start.43 = (f32[2,128]{1,0:T(2,128)S(1)}, f32[2,128]{1,0:T(2,128)}, u32[]{:S(2)}) copy-start(f32[2,128]{1,0:T(2,128)} %get-tuple-element.299) | copy-start | bytes 3076
  153.6 9.0 %copy-start.46 = (f32[2048]{0:T(1024)S(1)}, f32[2048]{0:T(1024)}, u32[]{:S(2)}) copy-start(f32[2048]{0:T(1024)} %param.20) | copy-start | bytes 24580
  162.6 13.3 %copy-start.47 = (s32[256]{0:T(256)S(1)}, s32[256]{0:T(256)}, u32[]{:S(2)}) copy-start(s32[256]{0:T(256)} %param.22) | copy-start | bytes 3076
  162.6 13.3 %copy-start.48 = (u32[32]{0:T(128)S(1)}, u32[32]{0:T(128)}, u32[]{:S(2)}) copy-start(u32[32]{0:T(128)} %constant.102) | copy-start | bytes 388
  162.6 22.1 %copy-start.33 = (s32[256]{0:T(256)S(1)}, s32[256]{0:T(256)}, u32[]{:S(2)}) copy-start(s32[256]{0:T(256)} %copy-done.32) | copy-start | bytes 3076
  162.7 34.5 %copy-start.45 = (s32[8]{0:T(128)S(1)}, s32[8]{0:T(128)}, u32[]{:S(2)}) copy-start(s32[8]{0:T(128)} %param.23) | copy-start | bytes 100
  166.5 8.1 %collective-permute-start.3 = (f32[128,512]{1,0:T(8,128)S(1)}, f32[128,512]{1,0:T(8,128)S(1)}, u32[]{:S(2)}, u32[]{:S(2)}) collective-permute-start(f32[128,512]{1,0:T(8,128)S(1)} %slice_select_fusion), channel_id=1, source_target_pairs={{0,2},{1,3},{2,0},{3,1},{4,6},{5,7},{6,4},{7,5},{8,10},{9,11},{10,... | collective-permute-start | bytes 786440 | tf_op jit(solution)/shard_map/ppermute | solution.py:32
  175.8 1.4 collective-permute-start.4
  184.7 13.0 %copy-start.42 = (f32[256]{0:T(256)}, f32[256]{0:T(256)S(1)}, u32[]{:S(2)}) copy-start(f32[256]{0:T(256)S(1)} %all-reduce) | copy-start | bytes 3076
  184.8 7.4 %collective-permute-start.5 = (f32[8]{0:T(128)S(1)}, f32[8]{0:T(128)S(1)}, u32[]{:S(2)}, u32[]{:S(2)}) collective-permute-start(f32[8]{0:T(128)S(1)} %select_reduce_fusion.1), channel_id=1, source_target_pairs={{0,4},{4,0},{8,12},{12,8},{1,5},{5,1},{9,13},{13,9},{2,6},{6,2},{1... | collective-permute-start | bytes 104 | tf_op jit(solution)/shard_map/ppermute | solution.py:43
  192.3 4.9 %collective-permute-start.6 = (f32[8]{0:T(128)S(1)}, f32[8]{0:T(128)S(1)}, u32[]{:S(2)}, u32[]{:S(2)}) collective-permute-start(f32[8]{0:T(128)S(1)} %add.293), channel_id=1, source_target_pairs={{0,8},{4,12},{8,0},{12,4},{1,9},{5,13},{9,1},{13,5},{2,10},{6,14},... | collective-permute-start | bytes 104 | tf_op jit(solution)/shard_map/ppermute | solution.py:43
  (34 other events, 107.9 us)

commit v11 on v9

--- a/solution.py
+++ b/solution.py
@@ -20,18 +20,18 @@
 
 def scatter_sum(part, axes):
     count = lax.axis_size(axes)
-    if count & (count - 1):
-        return lax.psum_scatter(part, axes, scatter_dimension=0, tiled=True)
     place = lax.axis_index(axes)
-    bit = count // 2
-    while bit >= 1:
+    bit = 1
+    piece_index = 0
+    while bit < count:
         half = part.shape[0] // 2
         upper = (place & bit) != 0
         keep = jnp.where(upper, part[half:], part[:half])
         give = jnp.where(upper, part[:half], part[half:])
         part = keep + lax.ppermute(give, axes, [(i, i ^ bit) for i in range(count)])
-        bit //= 2
-    return part
+        piece_index = piece_index * 2 + upper.astype(jnp.int32)
+        bit *= 2
+    return part, piece_index
 
 
 def sum_over(part, axis):
@@ -303,7 +303,7 @@
     long_cols = jnp.transpose(longconv, (1, 2, 0, 3)).reshape(chan_count, row_count)
     mixed = (query_proj.T.astype(jnp.float32) * long_cols).astype(jnp.bfloat16)
     mixed_wide = mixed.astype(jnp.float32)
-    squares = lax.psum(jnp.sum(mixed_wide * mixed_wide, axis=0), ("chan", "rep"))
+    squares = sum_over(jnp.sum(mixed_wide * mixed_wide, axis=0), ("chan", "rep"))
     normed = (mixed_wide * lax.rsqrt(squares / D + norm_eps)[None, :] * norm_gain[:, None]).astype(
         jnp.bfloat16
     )
@@ -311,10 +311,15 @@
     lanes = ("chan", "rep")
     lane_count = lax.axis_size(lanes)
     piece = row_count // lane_count
-    piece_at = lax.axis_index(lanes) * piece
-    logits = scatter_sum(partial_value, lanes)
+    logits, piece_index = scatter_sum(partial_value, lanes)
+    piece_at = piece_index * piece
     logprob_piece = log_probs(logits, lax.dynamic_slice_in_dim(token_ids, piece_at, piece, 0))
-    logprob = lax.all_gather(logprob_piece, lanes, tiled=True)
+    logprob = sum_over(
+        lax.dynamic_update_slice_in_dim(
+            jnp.zeros((row_count,), jnp.float32), logprob_piece, piece_at, 0
+        ),
+        lanes,
+    )
     genome_index = jnp.arange(genome_lengths.shape[0], dtype=jnp.int32)
     genome_part = jnp.sum(
         jnp.where(

time: 191 us -> 184 us (0.963)
  blocking collectives: 12.9 us -> 0 us
  waiting for transfers between devices: 11.5 us -> 17.1 us
  starting transfers between devices: 23 us -> 25.8 us
    unnamed x1 -> x0, blocking collectives: 7.2 us -> none
    ppermute x2 -> x6, waiting for transfers between devices: 3.04 us -> 9.46 us  [sum_over(): part = part + lax.ppermute(part, axis, [(i, i ^ bit) for i in range(count)])]
    psum x1 -> x0, blocking collectives: 5.66 us -> none  [per_device(): lax.psum(jnp.sum(mixed_wide * mixed_wide, axis=0), ('chan', 'rep'))]
    ppermute x2 -> x6, starting transfers between devices: 9.3 us -> 12.3 us  [sum_over(): part = part + lax.ppermute(part, axis, [(i, i ^ bit) for i in range(count)])]
    unnamed x112 -> x106, local copies, waits for them, and re-layouts: 27.7 us -> 27 us
  transfers between devices with their start and end apart: 7 -> 11, of which waited for: 4 -> 9; matrix products, arithmetic and copies ran while one was open for 43% -> 44% of each run, Pallas kernels for 0% -> 0%
where the time goes in v11:
time: 184 us
  local copies, waits for them, and re-layouts  55.5 us (30%)
  other arithmetic  42.9 us (23%)
  matrix products  40.8 us (22%)
  starting transfers between devices  25.8 us (14%)
  waiting for transfers between devices  17.1 us (9%)
    unnamed x106, local copies, waits for them, and re-layouts  27 us
    ppermute x6, starting transfers between devices, sum_over(): part = part + lax.ppermute(part, axis, [(i, i ^ bit) for i in range(count)])  12.3 us
    dot_general x2, matrix products, medium_block(): jnp.einsum('gts,gis->git', matrix, window, preferred_element_type=jnp.flo...  11.9 us
    ppermute x3, starting transfers between devices, from_behind(): return lax.ppermute(shard, axis, pairs)  11.9 us
    ppermute x6, waiting for transfers between devices, sum_over(): part = part + lax.ppermute(part, axis, [(i, i ^ bit) for i in range(count)])  9.46 us
    mul x1, other arithmetic, modal_tables(): power_im = magnitude * jnp.sin(powers * angles[None])  9.37 us
    select_n x1, other arithmetic, intra_block(): jnp.where(same_genome, toeplitz_upper, jnp.zeros_like(toeplitz_upper))  6.91 us
    dot_general x2, matrix products, intra_block(): jnp.einsum('gts,gis->git', upper, block_in, preferred_element_type=jnp.fl...  6.73 us
  transfers between devices with their start and end apart: 11, of which 9 were waited for; matrix products, arithmetic and copies ran while one was open for 44% of the time, Pallas kernels for 0%

profile of v11, /device:TPU:0, one launch (start us, length us, event | category | flops | bytes accessed | tf_op | source)
XLA Modules:
  0.0 183.5 jit_solution(14956565649540583321)
XLA Ops:
  3.2 5.9 %collective-permute-start = (bf16[2,136,2048]{2,1,0:T(8,128)(2,1)}, bf16[2,136,2048]{2,1,0:T(8,128)(2,1)}, u32[]{:S(2)}, u32[]{:S(2)}) collective-permute-start(bf16[2,136,2048]{2,1,0:T(8,128)(2,1)} %pad_maximum_fusion), channel_id=1, source_target_pairs={{0,4},{4,8},{8,12},{1,5},{5,9},{9,13},{2,6},{6,10},{10,14},{3,7},{... | collective-permute-start | bytes 3342344 | tf_op jit(solution)/shard_map/ppermute | solution.py:18
  10.7 9.4 %fusion.28 = (f32[129,128,16]{0,2,1:T(8,128)S(1)}, f32[129,128,16]{0,2,1:T(8,128)}, f32[129,128,16]{0,2,1:T(8,128)S(1)}) fusion(f32[128,16]{1,0:T(8,128)S(1)} %copy.89, f32[129]{0:T(256)S(1)} %iota_convert_fusion, f32[128,16]{1,0:T(8,128)S(1)} %copy.88, f32[129]{0:T(256)S(1)} %fusion.73, f32[128,16]{1,0:T(8,128)S(1)} %copy.90, f32[128,16]{1,0:T(8,128)S(1)} %copy.87), kind=kLoop, calls=%fused_computation.59 | loop fusion | flops 1849344 | bytes 3204104 | tf_op jit(solution)/shard_map/mul | solution.py:121
  26.7 3.2 %fusion.83 = (f32[128,128,16]{0,2,1:T(8,128)}, f32[128,128]{0,1:T(8,128)S(1)}) fusion(f32[129,128,16]{0,2,1:T(8,128)} %get-tuple-element.263), kind=kLoop, calls=%fused_computation.207 | loop fusion | flops 245760 | bytes 3211264 | tf_op jit(solution)/shard_map/slice | solution.py:126
  31.4 4.6 %convolution_convert_fusion = bf16[384,16384]{1,0:T(8,128)(2,1)S(1)} fusion(s32[16384]{0:T(1024)S(1)} %add_select_fusion, s32[128]{0:T(128)S(1)} %iota.77, bf16[128,128]{0,1:T(8,128)(2,1)S(1)} %get-tuple-element.224, bf16[128,128]{0,1:T(8,128)(2,1)} %get-tuple-element.225, bf16[128,128]{0,1:T(8,128)(2,1)S(1)} %copy.91), kind=kOutput, calls=%fused_computation.11 | convolution fusion | flops 1619296256 | bytes 12747264 | tf_op jit(solution)/shard_map/dot_general | solution.py:109
  36.0 3.9 %slice_bitcast_fusion = (bf16[16,8,128,128]{3,1,2,0:T(8,128)(2,1)}, bf16[16,8,128,128]{3,1,2,0:T(8,128)(2,1)}, bf16[16,8,128,128]{3,1,2,0:T(8,128)(2,1)S(1)}) fusion(bf16[384,16384]{1,0:T(8,128)(2,1)S(1)} %convolution_convert_fusion), kind=kLoop, calls=%fused_computation.23 | loop fusion | bytes 25165824
  54.4 5.6 %copy.106 = bf16[16,8,128,128]{3,2,1,0:T(8,128)(2,1)} copy(bf16[16,8,128,128]{3,1,2,0:T(8,128)(2,1)} %get-tuple-element.233) | data formatting | bytes 8388608
  59.9 3.2 %copy.107 = bf16[16,8,128,128]{3,2,1,0:T(8,128)(2,1)} copy(bf16[16,8,128,128]{3,1,2,0:T(8,128)(2,1)S(1)} %copy-done.3) | data formatting | bytes 8388608
  66.4 5.1 %constant_dynamic-update-slice_fusion = bf16[128,128,256]{2,1,0:T(8,128)(2,1)} fusion(bf16[128,128,256]{2,1,0:T(8,128)(2,1)} %constant_dynamic-update-slice_fusion.1, bf16[128,128,128]{2,1,0:T(8,128)(2,1)} %bitcast.151), kind=kLoop, calls=%fused_computation.163 | loop fusion | bytes 8388608 | tf_op jit(solution)/shard_map/concatenate | solution.py:211
  72.6 6.9 %bitcast_select_fusion.3 = (bf16[128,128,128]{2,1,0:T(8,128)(2,1)}, bf16[128,128,128]{2,1,0:T(8,128)(2,1)}, bf16[128,128,128]{2,1,0:T(8,128)(2,1)}, bf16[128,128,128]{2,1,0:T(8,128)(2,1)}) fusion(bf16[16,8,128,128]{3,2,1,0:T(8,128)(2,1)S(1)} %copy-done.4, pred[128,128]{1,0:T(8,128)(4,1)S(1)} %get-tuple-element.222, ...), kind=kLoop, calls=%fused_computation.22 | loop fusion | flops 8388608 | bytes 25198592 | tf_op jit(solution)/shard_map/jit(_where)/select_n | solution.py:242
  81.7 5.3 %fusion.36 = bf16[2048,384]{0,1:T(8,128)(2,1)} fusion(f32[384]{0:T(512)S(1)} %copy-done.35, f32[392,2048]{1,0:T(8,128)S(1)} %convert_multiply_fusion, f32[2048]{0:T(1024)S(1)} %bitcast.179, f32[384]{0:T(512)S(1)} %copy-done.31, f32[2048]{0:T(1024)S(1)} %bitcast.180, f32[384]{0:T(512)S(1)} %copy-done.32, f32[2048]{0:T(1024)S(1)} %bitcast.175, ...), kind=kLoop, calls=%fused_computation.75 | loop fusion | flops 15728640 | bytes 23659520 | tf_op jit(solution)/shard_map/transpose | solution.py:204
  89.6 6.1 %fusion.39 = bf16[128,16,128]{2,1,0:T(8,128)(2,1)S(1)} fusion(bf16[128,128,256]{2,1,0:T(8,128)(2,1)} %constant_dynamic-update-slice_fusion, pred[128,256]{1,0:T(8,128)(4,1)S(1)} %get-tuple-element.292, bf16[128,16,384]{2,1,0:T(8,128)(2,1)} %bitcast.162), kind=kOutput, calls=%fused_computation.80 | convolution fusion | flops 138674176 | bytes 9994240 | tf_op jit(solution)/shard_map/gts,gis->git/dot_general | solution.py:228
  95.7 5.8 %fusion.42 = bf16[128,16,128]{2,1,0:T(8,128)(2,1)S(1)} fusion(bf16[128,128,256]{2,1,0:T(8,128)(2,1)} %constant_dynamic-update-slice_fusion, pred[128,256]{1,0:T(8,128)(4,1)S(1)} %get-tuple-element.293, bf16[128,16,384]{2,1,0:T(8,128)(2,1)S(1)} %bitcast.163), kind=kOutput, calls=%fused_computation.81 | convolution fusion | flops 138674176 | bytes 9994240 | tf_op jit(solution)/shard_map/gts,gis->git/dot_general | solution.py:228
  104.2 3.5 %copy.96 = f32[2,128,16,32]{1,3,2,0:T(8,128)} copy(f32[2,128,16,32]{3,2,0,1:T(8,128)} %add_bitcast_fusion) | data formatting | bytes 1048576
  107.7 6.2 %while.25 = (s32[]{:T(128)}, f32[128,16]{0,1:T(8,128)S(1)}, f32[128,16]{0,1:T(8,128)S(1)}, f32[128,16,16]{0,2,1:T(8,128)S(1)}, f32[128,16,16]{0,2,1:T(8,128)S(1)...) while((s32[]{:T(128)}, f32[128,16]{0,1:T(8,128)S(1)}, ...), condition=%wide.region_7.8_spmd.clone, body=%wide.region_6.7_spmd.clone.sunk | while | flops 421891 | bytes 1999539 | solution.py:275
  116.8 4.5 %fusion.86 = f32[128,16,128]{2,1,0:T(8,128)S(1)} fusion(bf16[128,16,128]{2,1,0:T(8,128)(2,1)S(1)} %fusion.39, bf16[128,128,128]{2,1,0:T(8,128)(2,1)} %get-tuple-element.237), kind=kOutput, calls=%fused_computation.210 | convolution fusion | flops 67108864 | bytes 5767168 | tf_op jit(solution)/shard_map/gts,gis->git/dot_general | solution.py:244
  121.2 3.3 %fusion.38 = f32[1,128,16,128]{3,2,1,0:T(8,128)} fusion(f32[128,16,128]{2,1,0:T(8,128)S(1)} %fusion.86, bf16[128,16,128]{2,1,0:T(8,128)(2,1)S(1)} %fusion.39, bf16[128,128,128]{2,1,0:T(8,128)(2,1)S(1)} %copy-done.7), kind=kOutput, calls=%fused_computation.79 | convolution fusion | flops 67371008 | bytes 6815744 | tf_op jit(solution)/shard_map/gts,gis->git/dot_general | solution.py:246
  127.0 3.2 %collective-permute-start.2 = (f32[128,544]{0,1:T(8,128)S(1)}, f32[128,544]{0,1:T(8,128)S(1)}, u32[]{:S(2)}, u32[]{:S(2)}) collective-permute-start(f32[128,544]{0,1:T(8,128)S(1)} %pad_maximum_fusion.4), channel_id=1, source_target_pairs={{0,8},{4,12},{1,9},{5,13},{2,10},{6,14},{3,11},{7,15},{16,24},{20,... | collective-permute-start | bytes 835592 | tf_op jit(solution)/shard_map/ppermute | solution.py:18
  130.2 3.3 %fusion.37 = f32[1,128,16,128]{3,2,1,0:T(8,128)} fusion(f32[128,16,128]{2,1,0:T(8,128)S(1)} %fusion.87, bf16[128,16,128]{2,1,0:T(8,128)(2,1)S(1)} %fusion.42, bf16[128,128,128]{2,1,0:T(8,128)(2,1)S(1)} %copy-done.6), kind=kOutput, calls=%fused_computation.77 | convolution fusion | flops 67371008 | bytes 6815744 | tf_op jit(solution)/shard_map/gts,gis->git/dot_general | solution.py:246
  136.6 3.1 %copy.102 = f32[2,128,16,32]{3,2,1,0:T(8,128)} copy(f32[2,128,16,32]{1,3,2,0:T(8,128)} %pad_maximum_fusion.2) | data formatting | bytes 1048576 | tf_op jit(solution)/shard_map/concatenate | solution.py:293
  139.7 5.3 %fusion.31 = f32[128,16,2,128]{3,1,0,2:T(8,128)S(1)} fusion(f32[1,128,16,128]{3,2,1,0:T(8,128)} %fusion.37, f32[1,128,16,128]{3,2,1,0:T(8,128)} %fusion.38, f32[2,128,16,32]{3,2,1,0:T(8,128)} %copy.102, f32[128,128,16]{0,2,1:T(8,128)} %get-tuple-element.241, f32[128,128,16]{0,2,1:T(8,128)} %get-tuple-element.239, f32[128,16]{1,0:T(8,128)S(1)} %mul.576, ...), kind=kOutput, calls=%fused_computation.64 | convolution fusion | flops 205520896 | bytes 7873536 | tf_op jit(solution)/shard_map/gtm,jgim->jgit/dot_general | solution.py:290
  153.2 3.0 %fusion.50 = f32[256,512]{1,0:T(8,128)S(1)} fusion(bf16[2048,512]{1,0:T(8,128)(2,1)S(1)} %copy-done, f32[2048]{0:T(1024)S(1)} %copy-done.45, f32[256]{0:T(256)S(1)} %add_rsqrt_fusion, f32[256,8,2,128]{3,2,1,0:T(2,128)} %bitcast.161, bf16[256,2048]{0,1:T(8,128)(2,1)S(1)} %copy-done.11), kind=kOutput, calls=%fused_computation.86 | convolution fusion | flops 540540928 | bytes 5776384 | tf_op jit(solution)/shard_map/dot_general | solution.py:162
  161.4 4.0 %collective-permute-done.6 = f32[64,512]{1,0:T(8,128)S(1)} collective-permute-done((f32[64,512]{1,0:T(8,128)S(1)}, f32[64,512]{1,0:T(8,128)S(1)}, u32[]{:S(2)}, u32[]{:S(2)}) %collective-permute-start.6) | collective-permute-done | bytes 131104 | tf_op jit(solution)/shard_map/ppermute | solution.py:31
  170.7 5.9 %collective-permute-start.9 = (f32[8]{0:T(128)S(1)}, f32[8]{0:T(128)S(1)}, u32[]{:S(2)}, u32[]{:S(2)}) collective-permute-start(f32[8]{0:T(128)S(1)} %select_reduce_fusion.1), channel_id=1, source_target_pairs={{0,4},{4,0},{8,12},{12,8},{1,5},{5,1},{9,13},{13,9},{2,6},{6,2},{1... | collective-permute-start | bytes 104 | tf_op jit(solution)/shard_map/ppermute | solution.py:43
  178.1 3.4 %collective-permute-start.10 = (f32[8]{0:T(128)S(1)}, f32[8]{0:T(128)S(1)}, u32[]{:S(2)}, u32[]{:S(2)}) collective-permute-start(f32[8]{0:T(128)S(1)} %add.308), channel_id=1, source_target_pairs={{0,8},{4,12},{8,0},{12,4},{1,9},{5,13},{9,1},{13,5},{2,10},{6,14},... | collective-permute-start | bytes 104 | tf_op jit(solution)/shard_map/ppermute | solution.py:43
  (219 shorter events, 74.9 us)
Async XLA Ops:
  0.6 152.5 %copy-start = (bf16[2048,512]{1,0:T(8,128)(2,1)S(1)}, bf16[2048,512]{1,0:T(8,128)(2,1)}, u32[]{:S(2)}) copy-start(bf16[2048,512]{1,0:T(8,128)(2,1)} %param.21) | copy-start | bytes 6291460
  0.6 9.6 %copy-start.27 = (f32[4,128,16]{1,2,0:T(8,128)S(1)}, f32[4,128,16]{1,2,0:T(8,128)}, u32[]{:S(2)}) copy-start(f32[4,128,16]{1,2,0:T(8,128)} %param.18) | copy-start | bytes 98308
  3.2 76.3 %collective-permute-start = (bf16[2,136,2048]{2,1,0:T(8,128)(2,1)}, bf16[2,136,2048]{2,1,0:T(8,128)(2,1)}, u32[]{:S(2)}, u32[]{:S(2)}) collective-permute-start(bf16[2,136,2048]{2,1,0:T(8,128)(2,1)} %pad_maximum_fusion), channel_id=1, source_target_pairs={{0,4},{4,8},{8,12},{1,5},{5,9},{9,13},{2,6},{6,10},{10,14},{3,7},{... | collective-permute-start | bytes 3342344 | tf_op jit(solution)/shard_map/ppermute | solution.py:18
  66.4 6.2 %copy-start.5 = (bf16[16,8,128,128]{3,2,1,0:T(8,128)(2,1)S(1)}, bf16[16,8,128,128]{3,2,1,0:T(8,128)(2,1)}, u32[]{:S(2)}) copy-start(bf16[16,8,128,128]{3,2,1,0:T(8,128)(2,1)} %copy.107) | copy-start | bytes 12582916
  72.6 8.2 %copy-start.12 = (bf16[256,2048]{1,0:T(8,128)(2,1)S(1)}, bf16[256,2048]{1,0:T(8,128)(2,1)}, u32[]{:S(2)}) copy-start(bf16[256,2048]{1,0:T(8,128)(2,1)} %param.14) | copy-start | bytes 3145732
  72.6 8.2 %copy-start.13 = (bf16[256,2048]{1,0:T(8,128)(2,1)S(1)}, bf16[256,2048]{1,0:T(8,128)(2,1)}, u32[]{:S(2)}) copy-start(bf16[256,2048]{1,0:T(8,128)(2,1)} %param.15) | copy-start | bytes 3145732
  89.6 6.1 %copy-start.15 = (bf16[2048,384]{1,0:T(8,128)(2,1)S(1)}, bf16[2048,384]{1,0:T(8,128)(2,1)}, u32[]{:S(2)}) copy-start(bf16[2048,384]{1,0:T(8,128)(2,1)} %copy.86) | copy-start | bytes 4718596
  95.6 5.8 %copy-start.8 = (f32[128,128,16]{0,2,1:T(8,128)S(1)}, f32[128,128,16]{0,2,1:T(8,128)}, u32[]{:S(2)}) copy-start(f32[128,128,16]{0,2,1:T(8,128)} %rev.6) | copy-start | bytes 3145732
  113.9 7.3 %copy-start.7 = (bf16[128,128,128]{2,1,0:T(8,128)(2,1)S(1)}, bf16[128,128,128]{2,1,0:T(8,128)(2,1)}, u32[]{:S(2)}) copy-start(bf16[128,128,128]{2,1,0:T(8,128)(2,1)} %get-tuple-element.266) | copy-start | bytes 12582916
  114.0 12.9 %collective-permute-start.1 = (f32[128,544]{0,1:T(8,128)S(1)}, f32[128,544]{0,1:T(8,128)S(1)}, u32[]{:S(2)}, u32[]{:S(2)}) collective-permute-start(f32[128,544]{0,1:T(8,128)S(1)} %pad_maximum_fusion.3), channel_id=1, source_target_pairs={{0,4},{4,8},{8,12},{1,5},{5,9},{9,13},{2,6},{6,10},{10,14},{3,7},{... | collective-permute-start | bytes 835592 | tf_op jit(solution)/shard_map/ppermute | solution.py:18
  127.0 8.6 %collective-permute-start.2 = (f32[128,544]{0,1:T(8,128)S(1)}, f32[128,544]{0,1:T(8,128)S(1)}, u32[]{:S(2)}, u32[]{:S(2)}) collective-permute-start(f32[128,544]{0,1:T(8,128)S(1)} %pad_maximum_fusion.4), channel_id=1, source_target_pairs={{0,8},{4,12},{1,9},{5,13},{2,10},{6,14},{3,11},{7,15},{16,24},{20,... | collective-permute-start | bytes 835592 | tf_op jit(solution)/shard_map/ppermute | solution.py:18
  133.4 6.3 %copy-start.40 = (f32[2,128]{1,0:T(2,128)S(1)}, f32[2,128]{1,0:T(2,128)}, u32[]{:S(2)}) copy-start(f32[2,128]{1,0:T(2,128)} %get-tuple-element.286) | copy-start | bytes 3076
  145.0 8.1 %copy-start.45 = (f32[2048]{0:T(1024)S(1)}, f32[2048]{0:T(1024)}, u32[]{:S(2)}) copy-start(f32[2048]{0:T(1024)} %param.20) | copy-start | bytes 24580
  148.4 1.2 collective-permute-start.3
  149.6 3.6 %collective-permute-start.4 = (f32[256]{0:T(256)S(1)}, f32[256]{0:T(256)S(1)}, u32[]{:S(2)}, u32[]{:S(2)}) collective-permute-start(f32[256]{0:T(256)S(1)} %add.300), channel_id=1, source_target_pairs={{0,2},{1,3},{2,0},{3,1},{4,6},{5,7},{6,4},{7,5},{8,10},{9,11},{10,... | collective-permute-start | bytes 3080 | tf_op jit(solution)/shard_map/ppermute | solution.py:43
  153.2 8.2 %copy-start.46 = (s32[256]{0:T(256)S(1)}, s32[256]{0:T(256)}, u32[]{:S(2)}) copy-start(s32[256]{0:T(256)} %param.22) | copy-start | bytes 3076
  153.2 29.8 %copy-start.44 = (s32[8]{0:T(128)S(1)}, s32[8]{0:T(128)}, u32[]{:S(2)}) copy-start(s32[8]{0:T(128)} %param.23) | copy-start | bytes 100
  157.0 1.6 collective-permute-start.5
  159.8 5.6 %collective-permute-start.6 = (f32[64,512]{1,0:T(8,128)S(1)}, f32[64,512]{1,0:T(8,128)S(1)}, u32[]{:S(2)}, u32[]{:S(2)}) collective-permute-start(f32[64,512]{1,0:T(8,128)S(1)} %slice_select_fusion.5), channel_id=1, source_target_pairs={{0,2},{1,3},{2,0},{3,1},{4,6},{5,7},{6,4},{7,5},{8,10},{9,11},{10,... | collective-permute-start | bytes 393224 | tf_op jit(solution)/shard_map/ppermute | solution.py:31
  165.7 1.1 collective-permute-start.7
  167.0 3.6 %collective-permute-start.8 = (f32[256]{0:T(256)S(1)}, f32[256]{0:T(256)S(1)}, u32[]{:S(2)}, u32[]{:S(2)}) collective-permute-start(f32[256]{0:T(256)S(1)} %add_dynamic-update-slice_fusion), channel_id=1, source_target_pairs={{0,2},{1,3},{2,0},{3,1},{4,6},{5,7},{6,4},{7,5},{8,10},{9,11},{10,... | collective-permute-start | bytes 3080 | tf_op jit(solution)/shard_map/ppermute | solution.py:43
  170.5 13.0 %copy-start.41 = (f32[256]{0:T(256)}, f32[256]{0:T(256)S(1)}, u32[]{:S(2)}) copy-start(f32[256]{0:T(256)S(1)} %add.307) | copy-start | bytes 3076
  170.7 7.4 %collective-permute-start.9 = (f32[8]{0:T(128)S(1)}, f32[8]{0:T(128)S(1)}, u32[]{:S(2)}, u32[]{:S(2)}) collective-permute-start(f32[8]{0:T(128)S(1)} %select_reduce_fusion.1), channel_id=1, source_target_pairs={{0,4},{4,0},{8,12},{12,8},{1,5},{5,1},{9,13},{13,9},{2,6},{6,2},{1... | collective-permute-start | bytes 104 | tf_op jit(solution)/shard_map/ppermute | solution.py:43
  178.1 4.9 %collective-permute-start.10 = (f32[8]{0:T(128)S(1)}, f32[8]{0:T(128)S(1)}, u32[]{:S(2)}, u32[]{:S(2)}) collective-permute-start(f32[8]{0:T(128)S(1)} %add.308), channel_id=1, source_target_pairs={{0,8},{4,12},{8,0},{12,4},{1,9},{5,13},{9,1},{13,5},{2,10},{6,14},... | collective-permute-start | bytes 104 | tf_op jit(solution)/shard_map/ppermute | solution.py:43
  (36 other events, 103.3 us)

commit v12 on v11

--- a/solution.py
+++ b/solution.py
@@ -208,7 +208,7 @@
 
     long_toeplitz, outward, inward, decay_re, decay_im = modal_tables(modal_poles)
     circ = circulants(jnp.concatenate((medium_taps, long_toeplitz[0], long_toeplitz[1]), axis=1))
-    circ_medium = jnp.concatenate((circ[:group_count], circ[:group_count]), axis=2)
+    circ_medium = circ[:group_count]
     toeplitz_upper = circ[group_count : 2 * group_count]
     toeplitz_lower = circ[2 * group_count :]
     lag_band = (
@@ -224,9 +224,11 @@
         window_segs = lax.dynamic_slice_in_dim(medium_segs, start, 2 * tile_rows, 0)
         own_segs = lax.dynamic_slice_in_dim(segments, start, tile_rows, 0)
         same_genome = (own_segs[:, None] == window_segs[None, :]) & medium_band
-        matrix = jnp.where(same_genome[None], circ_medium, jnp.zeros_like(circ_medium))
+        halves = same_genome.reshape(tile_rows, 2, tile_rows).transpose(1, 0, 2)
+        matrix = jnp.where(halves[:, None], circ_medium[None], jnp.zeros_like(circ_medium)[None])
+        window2 = window.reshape(group_count, GROUP, 2, tile_rows)
         return jnp.einsum(
-            "gts,gis->git", matrix, window, preferred_element_type=jnp.float32
+            "hgts,gihs->git", matrix, window2, preferred_element_type=jnp.float32
         ).astype(jnp.bfloat16)
 
     signal = jnp.stack([medium_block(tile_index) for tile_index in range(tile_count)])

time: 184 us -> 197 us (1.071)
  local copies, waits for them, and re-layouts: 55.5 us -> 64.7 us
  other arithmetic: 42.9 us -> 51.4 us
  matrix products: 40.8 us -> 36.2 us
    convert_element_type x0 -> x1, other arithmetic: none -> 8.81 us  [short_filter(): return result.astype(jnp.bfloat16)]
    unnamed x106 -> x119, local copies, waits for them, and re-layouts: 27 us -> 33.8 us
    dynamic_slice x0 -> x3, local copies, waits for them, and re-layouts: none -> 5.37 us  [medium_block(): window = lax.dynamic_slice_in_dim(ext_short, start, 2 * tile_rows, 2)]
    transpose x1 -> x0, other arithmetic: 5.29 us -> none  [per_device(): ext_short = filtered.T.reshape(group_count, GROUP, row_count + tile_rows)]
    concatenate x1 -> x0, local copies, waits for them, and re-layouts: 5.06 us -> none  [per_device(): jnp.concatenate((circ[:group_count], circ[:group_count]), axis=2)]
    dot_general x2, matrix products: 11.9 us -> 7.21 us  [medium_block(): jnp.einsum('hgts,gihs->git', matrix, window2, preferred_element_type=jnp....]
    reshape x0 -> x2, local copies, waits for them, and re-layouts: none -> 3.41 us  [medium_block(): window2 = window.reshape(group_count, GROUP, 2, tile_rows)]
    mul x1, other arithmetic: 0.55 us -> 3.37 us  [short_filter(): gated = keys_in.astype(jnp.float32) * values_in.astype(jnp.float32)]
  transfers between devices with their start and end apart: 11 -> 11, of which waited for: 9 -> 9; matrix products, arithmetic and copies ran while one was open for 44% -> 41% of each run, Pallas kernels for 0% -> 0%
where the time goes in v12:
time: 197 us
  local copies, waits for them, and re-layouts  64.7 us (33%)
  other arithmetic  51.4 us (26%)
  matrix products  36.2 us (18%)
  starting transfers between devices  25.8 us (13%)
  waiting for transfers between devices  17.1 us (9%)
    unnamed x119, local copies, waits for them, and re-layouts  33.8 us
    ppermute x6, starting transfers between devices, sum_over(): part = part + lax.ppermute(part, axis, [(i, i ^ bit) for i in range(count)])  12.3 us
    ppermute x3, starting transfers between devices, from_behind(): return lax.ppermute(shard, axis, pairs)  11.9 us
    ppermute x6, waiting for transfers between devices, sum_over(): part = part + lax.ppermute(part, axis, [(i, i ^ bit) for i in range(count)])  9.45 us
    mul x1, other arithmetic, modal_tables(): power_im = magnitude * jnp.sin(powers * angles[None])  9.37 us
    convert_element_type x1, other arithmetic, short_filter(): return result.astype(jnp.bfloat16)  8.81 us
    select_n x1, other arithmetic, intra_block(): jnp.where(same_genome, toeplitz_upper, jnp.zeros_like(toeplitz_upper))  8.57 us
    dot_general x2, matrix products, medium_block(): jnp.einsum('hgts,gihs->git', matrix, window2, preferred_element_type=jnp....  7.21 us
  transfers between devices with their start and end apart: 11, of which 9 were waited for; matrix products, arithmetic and copies ran while one was open for 41% of the time, Pallas kernels for 0%

profile of v12, /device:TPU:0, one launch (start us, length us, event | category | flops | bytes accessed | tf_op | source)
XLA Modules:
  0.0 196.7 jit_solution(12557408006464404854)
XLA Ops:
  3.3 5.9 %collective-permute-start = (bf16[2,136,2048]{2,1,0:T(8,128)(2,1)}, bf16[2,136,2048]{2,1,0:T(8,128)(2,1)}, u32[]{:S(2)}, u32[]{:S(2)}) collective-permute-start(bf16[2,136,2048]{2,1,0:T(8,128)(2,1)} %pad_maximum_fusion), channel_id=1, source_target_pairs={{0,4},{4,8},{8,12},{1,5},{5,9},{9,13},{2,6},{6,10},{10,14},{3,7},{... | collective-permute-start | bytes 3342344 | tf_op jit(solution)/shard_map/ppermute | solution.py:18
  14.4 9.4 %fusion.30 = (f32[129,128,16]{0,2,1:T(8,128)S(1)}, f32[129,128,16]{0,2,1:T(8,128)}, f32[129,128,16]{0,2,1:T(8,128)S(1)}) fusion(f32[128,16]{1,0:T(8,128)S(1)} %copy.113, f32[129]{0:T(256)S(1)} %iota_convert_fusion, f32[128,16]{1,0:T(8,128)S(1)} %copy.112, f32[129]{0:T(256)S(1)} %fusion.80, f32[128,16]{1,0:T(8,128)S(1)} %copy.114, f32[128,16]{1,0:T(8,128)S(1)} %copy.111), kind=kLoop, calls=%fused_computation.61 | loop fusion | flops 1849344 | bytes 3204104 | tf_op jit(solution)/shard_map/mul | solution.py:121
  33.1 3.2 %fusion.90 = (f32[128,128,16]{0,2,1:T(8,128)}, f32[128,128]{0,1:T(8,128)S(1)}) fusion(f32[129,128,16]{0,2,1:T(8,128)} %get-tuple-element.263), kind=kLoop, calls=%fused_computation.209 | loop fusion | flops 245760 | bytes 3211264 | tf_op jit(solution)/shard_map/slice | solution.py:126
  37.8 4.6 %convolution_convert_fusion = bf16[384,16384]{1,0:T(8,128)(2,1)S(1)} fusion(s32[16384]{0:T(1024)S(1)} %add_select_fusion, s32[128]{0:T(128)S(1)} %iota.83, bf16[128,128]{0,1:T(8,128)(2,1)S(1)} %get-tuple-element.222, bf16[128,128]{0,1:T(8,128)(2,1)} %get-tuple-element.223, bf16[128,128]{0,1:T(8,128)(2,1)S(1)} %copy.115), kind=kOutput, calls=%fused_computation.11 | convolution fusion | flops 1619296256 | bytes 12747264 | tf_op jit(solution)/shard_map/dot_general | solution.py:109
  42.4 4.0 %slice_bitcast_fusion = (bf16[16,8,128,128]{3,1,2,0:T(8,128)(2,1)}, bf16[16,8,128,128]{3,1,2,0:T(8,128)(2,1)}, bf16[16,8,128,128]{3,1,2,0:T(8,128)(2,1)S(1)}) fusion(bf16[384,16384]{1,0:T(8,128)(2,1)S(1)} %convolution_convert_fusion), kind=kLoop, calls=%fused_computation.23 | loop fusion | bytes 25165824
  46.4 3.3 %copy.136 = bf16[16,8,128,128]{3,2,1,0:T(8,128)(2,1)} copy(bf16[16,8,128,128]{3,1,2,0:T(8,128)(2,1)S(1)} %get-tuple-element.232) | data formatting | bytes 8388608
  57.4 5.6 %copy.137 = bf16[16,8,128,128]{3,2,1,0:T(8,128)(2,1)} copy(bf16[16,8,128,128]{3,1,2,0:T(8,128)(2,1)} %get-tuple-element.231) | data formatting | bytes 8388608
  63.1 3.3 %copy.138 = bf16[16,8,128,128]{3,2,1,0:T(8,128)(2,1)} copy(bf16[16,8,128,128]{3,1,2,0:T(8,128)(2,1)S(1)} %copy-done.2) | data formatting | bytes 8388608
  70.7 8.6 %bitcast_select_fusion.3 = (bf16[128,128,128]{2,1,0:T(8,128)(2,1)}, bf16[128,128,128]{2,1,0:T(8,128)(2,1)}, bf16[128,128,128]{2,1,0:T(8,128)(2,1)}, bf16[128,128,128]{2,1,0:T(8,128)(2,1)}) fusion(bf16[16,8,128,128]{3,2,1,0:T(8,128)(2,1)} %copy.137, pred[128,128]{1,0:T(8,128)(4,1)S(1)} %get-tuple-element.294, pred[128,128]{1,0:T(8,128)(4,1)S(1)} %get-tuple-element.295, ...), kind=kLoop, calls=%fused_computation.22 | loop fusion | flops 8388608 | bytes 25198592 | tf_op jit(solution)/shard_map/jit(_where)/select_n | solution.py:244
  86.2 3.4 %convert_multiply_fusion = f32[392,2048]{0,1:T(8,128)S(1)} fusion(bf16[256,2048]{0,1:T(8,128)(2,1)S(1)} %copy-done.10, bf16[136,2048]{0,1:T(8,128)(2,1)} %bitcast.181, bf16[256,2048]{0,1:T(8,128)(2,1)} %copy.109, bf16[136,2048]{0,1:T(8,128)(2,1)} %bitcast.182), kind=kLoop, calls=%fused_computation.31 | loop fusion | flops 7225344 | bytes 6422528 | tf_op jit(solution)/shard_map/mul | solution.py:85
  89.7 8.8 %fusion.15 = bf16[384,2048]{0,1:T(8,128)(2,1)S(1)} fusion(f32[392,2048]{0,1:T(8,128)S(1)} %convert_multiply_fusion, f32[384]{0:T(512)S(1)} %copy-done.37, f32[2048]{0:T(1024)S(1)} %bitcast.198, f32[384]{0:T(512)S(1)} %copy-done.33, f32[2048]{0:T(1024)S(1)} %bitcast.199, f32[384]{0:T(512)S(1)} %copy-done.34, f32[2048]{0:T(1024)S(1)} %bitcast.194, ...), kind=kLoop, calls=%fused_computation.36 | loop fusion | flops 15728640 | bytes 23659520 | tf_op jit(solution)/shard_map/convert_element_type | solution.py:99
  107.3 4.9 %fusion.49 = bf16[128,16,128]{2,1,0:T(8,128)(2,1)S(1)} fusion(bf16[128,16,2,128]{3,1,2,0:T(8,128)(2,1)} %copy.116, pred[2,128,128]{2,1,0:T(8,128)(4,1)} %get-tuple-element.286, bf16[128,128,128]{2,1,0:T(8,128)(2,1)} %bitcast.177), kind=kOutput, calls=%fused_computation.84 | convolution fusion | flops 138674176 | bytes 5799936 | tf_op jit(solution)/shard_map/hgts,gihs->git/dot_general | solution.py:230
  117.4 3.4 %copy.123 = f32[2,128,16,32]{1,3,2,0:T(8,128)} copy(f32[2,128,16,32]{3,2,0,1:T(8,128)} %add_bitcast_fusion) | data formatting | bytes 1048576
  120.8 6.2 %while.25 = (s32[]{:T(128)}, f32[128,16]{0,1:T(8,128)S(1)}, f32[128,16]{0,1:T(8,128)S(1)}, f32[128,16,16]{0,2,1:T(8,128)S(1)}, f32[128,16,16]{0,2,1:T(8,128)S(1)...) while((s32[]{:T(128)}, f32[128,16]{0,1:T(8,128)S(1)}, ...), condition=%wide.region_7.8_spmd.clone, body=%wide.region_6.7_spmd.clone.sunk | while | flops 421891 | bytes 1999539 | solution.py:277
  129.9 4.5 %fusion.94 = f32[128,16,128]{2,1,0:T(8,128)S(1)} fusion(bf16[128,16,128]{2,1,0:T(8,128)(2,1)S(1)} %fusion.49, bf16[128,128,128]{2,1,0:T(8,128)(2,1)} %get-tuple-element.235), kind=kOutput, calls=%fused_computation.213 | convolution fusion | flops 67108864 | bytes 5767168 | tf_op jit(solution)/shard_map/gts,gis->git/dot_general | solution.py:246
  134.4 3.3 %fusion.45 = f32[1,128,16,128]{3,2,1,0:T(8,128)} fusion(f32[128,16,128]{2,1,0:T(8,128)S(1)} %fusion.94, bf16[128,16,128]{2,1,0:T(8,128)(2,1)S(1)} %fusion.49, bf16[128,128,128]{2,1,0:T(8,128)(2,1)S(1)} %copy-done.4), kind=kOutput, calls=%fused_computation.82 | convolution fusion | flops 67371008 | bytes 6815744 | tf_op jit(solution)/shard_map/gts,gis->git/dot_general | solution.py:248
  140.1 3.2 %collective-permute-start.2 = (f32[128,544]{0,1:T(8,128)S(1)}, f32[128,544]{0,1:T(8,128)S(1)}, u32[]{:S(2)}, u32[]{:S(2)}) collective-permute-start(f32[128,544]{0,1:T(8,128)S(1)} %pad_maximum_fusion.4), channel_id=1, source_target_pairs={{0,8},{4,12},{1,9},{5,13},{2,10},{6,14},{3,11},{7,15},{16,24},{20,... | collective-permute-start | bytes 835592 | tf_op jit(solution)/shard_map/ppermute | solution.py:18
  143.3 3.3 %fusion.44 = f32[1,128,16,128]{3,2,1,0:T(8,128)} fusion(f32[128,16,128]{2,1,0:T(8,128)S(1)} %fusion.95, bf16[128,16,128]{2,1,0:T(8,128)(2,1)S(1)} %fusion.46, bf16[128,128,128]{2,1,0:T(8,128)(2,1)S(1)} %copy-done.3), kind=kOutput, calls=%fused_computation.80 | convolution fusion | flops 67371008 | bytes 6815744 | tf_op jit(solution)/shard_map/gts,gis->git/dot_general | solution.py:248
  149.8 3.1 %copy.131 = f32[2,128,16,32]{3,2,1,0:T(8,128)} copy(f32[2,128,16,32]{1,3,2,0:T(8,128)} %pad_maximum_fusion.2) | data formatting | bytes 1048576 | tf_op jit(solution)/shard_map/concatenate | solution.py:295
  152.9 5.3 %fusion.33 = f32[128,16,2,128]{3,1,0,2:T(8,128)S(1)} fusion(f32[1,128,16,128]{3,2,1,0:T(8,128)} %fusion.44, f32[1,128,16,128]{3,2,1,0:T(8,128)} %fusion.45, f32[2,128,16,32]{3,2,1,0:T(8,128)} %copy.131, f32[128,128,16]{0,2,1:T(8,128)} %get-tuple-element.239, f32[128,128,16]{0,2,1:T(8,128)} %get-tuple-element.237, f32[128,16]{1,0:T(8,128)S(1)} %mul.576, ...), kind=kOutput, calls=%fused_computation.66 | convolution fusion | flops 205520896 | bytes 7873536 | tf_op jit(solution)/shard_map/gtm,jgim->jgit/dot_general | solution.py:292
  166.3 3.0 %fusion.57 = f32[256,512]{1,0:T(8,128)S(1)} fusion(bf16[2048,512]{1,0:T(8,128)(2,1)S(1)} %copy-done, f32[2048]{0:T(1024)S(1)} %copy-done.50, f32[256]{0:T(256)S(1)} %add_rsqrt_fusion, f32[256,8,2,128]{3,2,1,0:T(2,128)} %bitcast.176, bf16[256,2048]{0,1:T(8,128)(2,1)S(1)} %copy-done.9), kind=kOutput, calls=%fused_computation.89 | convolution fusion | flops 540540928 | bytes 5776384 | tf_op jit(solution)/shard_map/dot_general | solution.py:162
  174.5 4.0 %collective-permute-done.6 = f32[64,512]{1,0:T(8,128)S(1)} collective-permute-done((f32[64,512]{1,0:T(8,128)S(1)}, f32[64,512]{1,0:T(8,128)S(1)}, u32[]{:S(2)}, u32[]{:S(2)}) %collective-permute-start.6) | collective-permute-done | bytes 131104 | tf_op jit(solution)/shard_map/ppermute | solution.py:31
  183.8 5.9 %collective-permute-start.9 = (f32[8]{0:T(128)S(1)}, f32[8]{0:T(128)S(1)}, u32[]{:S(2)}, u32[]{:S(2)}) collective-permute-start(f32[8]{0:T(128)S(1)} %select_reduce_fusion.1), channel_id=1, source_target_pairs={{0,4},{4,0},{8,12},{12,8},{1,5},{5,1},{9,13},{13,9},{2,6},{6,2},{1... | collective-permute-start | bytes 104 | tf_op jit(solution)/shard_map/ppermute | solution.py:43
  191.2 3.4 %collective-permute-start.10 = (f32[8]{0:T(128)S(1)}, f32[8]{0:T(128)S(1)}, u32[]{:S(2)}, u32[]{:S(2)}) collective-permute-start(f32[8]{0:T(128)S(1)} %add.316), channel_id=1, source_target_pairs={{0,8},{4,12},{8,0},{12,4},{1,9},{5,13},{9,1},{13,5},{2,10},{6,14},... | collective-permute-start | bytes 104 | tf_op jit(solution)/shard_map/ppermute | solution.py:43
  (234 shorter events, 87.9 us)
Async XLA Ops:
  0.6 165.7 %copy-start = (bf16[2048,512]{1,0:T(8,128)(2,1)S(1)}, bf16[2048,512]{1,0:T(8,128)(2,1)}, u32[]{:S(2)}) copy-start(bf16[2048,512]{1,0:T(8,128)(2,1)} %param.21) | copy-start | bytes 6291460
  0.6 8.6 %copy-start.11 = (bf16[256,2048]{1,0:T(8,128)(2,1)S(1)}, bf16[256,2048]{1,0:T(8,128)(2,1)}, u32[]{:S(2)}) copy-start(bf16[256,2048]{1,0:T(8,128)(2,1)} %param.14) | copy-start | bytes 3145732
  2.2 11.8 %copy-start.25 = (f32[4,128,16]{1,2,0:T(8,128)S(1)}, f32[4,128,16]{1,2,0:T(8,128)}, u32[]{:S(2)}) copy-start(f32[4,128,16]{1,2,0:T(8,128)} %param.18) | copy-start | bytes 98308
  3.3 76.0 %collective-permute-start = (bf16[2,136,2048]{2,1,0:T(8,128)(2,1)}, bf16[2,136,2048]{2,1,0:T(8,128)(2,1)}, u32[]{:S(2)}, u32[]{:S(2)}) collective-permute-start(bf16[2,136,2048]{2,1,0:T(8,128)(2,1)} %pad_maximum_fusion), channel_id=1, source_target_pairs={{0,4},{4,8},{8,12},{1,5},{5,9},{9,13},{2,6},{6,10},{10,14},{3,7},{... | collective-permute-start | bytes 3342344 | tf_op jit(solution)/shard_map/ppermute | solution.py:18
  28.6 7.7 %copy-start.42 = (s32[8]{0:T(128)}, s32[8]{0:T(128)S(1)}, u32[]{:S(2)}) copy-start(s32[8]{0:T(128)S(1)} %bitcast_subtract_fusion) | copy-start | bytes 100
  53.4 14.4 %copy-start.47 = (s32[2]{0:T(128)}, s32[2]{0:T(128)S(1)}, u32[]{:S(2)}) copy-start(s32[2]{0:T(128)S(1)} %slice_reduce_fusion.1) | copy-start | bytes 28
  79.2 6.8 %copy-start.10 = (bf16[256,2048]{0,1:T(8,128)(2,1)S(1)}, bf16[256,2048]{0,1:T(8,128)(2,1)}, u32[]{:S(2)}) copy-start(bf16[256,2048]{0,1:T(8,128)(2,1)} %copy.107) | copy-start | bytes 3145732
  127.1 7.3 %copy-start.4 = (bf16[128,128,128]{2,1,0:T(8,128)(2,1)S(1)}, bf16[128,128,128]{2,1,0:T(8,128)(2,1)}, u32[]{:S(2)}) copy-start(bf16[128,128,128]{2,1,0:T(8,128)(2,1)} %get-tuple-element.266) | copy-start | bytes 12582916
  127.1 12.8 %collective-permute-start.1 = (f32[128,544]{0,1:T(8,128)S(1)}, f32[128,544]{0,1:T(8,128)S(1)}, u32[]{:S(2)}, u32[]{:S(2)}) collective-permute-start(f32[128,544]{0,1:T(8,128)S(1)} %pad_maximum_fusion.3), channel_id=1, source_target_pairs={{0,4},{4,8},{8,12},{1,5},{5,9},{9,13},{2,6},{6,10},{10,14},{3,7},{... | collective-permute-start | bytes 835592 | tf_op jit(solution)/shard_map/ppermute | solution.py:18
  140.1 8.6 %collective-permute-start.2 = (f32[128,544]{0,1:T(8,128)S(1)}, f32[128,544]{0,1:T(8,128)S(1)}, u32[]{:S(2)}, u32[]{:S(2)}) collective-permute-start(f32[128,544]{0,1:T(8,128)S(1)} %pad_maximum_fusion.4), channel_id=1, source_target_pairs={{0,8},{4,12},{1,9},{5,13},{2,10},{6,14},{3,11},{7,15},{16,24},{20,... | collective-permute-start | bytes 835592 | tf_op jit(solution)/shard_map/ppermute | solution.py:18
  146.6 6.3 %copy-start.44 = (f32[2,128]{1,0:T(2,128)S(1)}, f32[2,128]{1,0:T(2,128)}, u32[]{:S(2)}) copy-start(f32[2,128]{1,0:T(2,128)} %get-tuple-element.288) | copy-start | bytes 3076
  158.2 8.1 %copy-start.50 = (f32[2048]{0:T(1024)S(1)}, f32[2048]{0:T(1024)}, u32[]{:S(2)}) copy-start(f32[2048]{0:T(1024)} %param.20) | copy-start | bytes 24580
  161.5 1.2 collective-permute-start.3
  162.7 3.6 %collective-permute-start.4 = (f32[256]{0:T(256)S(1)}, f32[256]{0:T(256)S(1)}, u32[]{:S(2)}, u32[]{:S(2)}) collective-permute-start(f32[256]{0:T(256)S(1)} %add.308), channel_id=1, source_target_pairs={{0,2},{1,3},{2,0},{3,1},{4,6},{5,7},{6,4},{7,5},{8,10},{9,11},{10,... | collective-permute-start | bytes 3080 | tf_op jit(solution)/shard_map/ppermute | solution.py:43
  166.3 8.2 %copy-start.51 = (s32[256]{0:T(256)S(1)}, s32[256]{0:T(256)}, u32[]{:S(2)}) copy-start(s32[256]{0:T(256)} %param.22) | copy-start | bytes 3076
  166.3 17.4 %copy-start.31 = (s32[256]{0:T(256)S(1)}, s32[256]{0:T(256)}, u32[]{:S(2)}) copy-start(s32[256]{0:T(256)} %copy-done.30) | copy-start | bytes 3076
  166.3 29.8 %copy-start.49 = (s32[8]{0:T(128)S(1)}, s32[8]{0:T(128)}, u32[]{:S(2)}) copy-start(s32[8]{0:T(128)} %param.23) | copy-start | bytes 100
  170.2 1.6 collective-permute-start.5
  172.9 5.6 %collective-permute-start.6 = (f32[64,512]{1,0:T(8,128)S(1)}, f32[64,512]{1,0:T(8,128)S(1)}, u32[]{:S(2)}, u32[]{:S(2)}) collective-permute-start(f32[64,512]{1,0:T(8,128)S(1)} %slice_select_fusion.5), channel_id=1, source_target_pairs={{0,2},{1,3},{2,0},{3,1},{4,6},{5,7},{6,4},{7,5},{8,10},{9,11},{10,... | collective-permute-start | bytes 393224 | tf_op jit(solution)/shard_map/ppermute | solution.py:31
  178.8 1.1 collective-permute-start.7
  180.1 3.6 %collective-permute-start.8 = (f32[256]{0:T(256)S(1)}, f32[256]{0:T(256)S(1)}, u32[]{:S(2)}, u32[]{:S(2)}) collective-permute-start(f32[256]{0:T(256)S(1)} %add_dynamic-update-slice_fusion), channel_id=1, source_target_pairs={{0,2},{1,3},{2,0},{3,1},{4,6},{5,7},{6,4},{7,5},{8,10},{9,11},{10,... | collective-permute-start | bytes 3080 | tf_op jit(solution)/shard_map/ppermute | solution.py:43
  183.7 13.0 %copy-start.45 = (f32[256]{0:T(256)}, f32[256]{0:T(256)S(1)}, u32[]{:S(2)}) copy-start(f32[256]{0:T(256)S(1)} %add.315) | copy-start | bytes 3076
  183.8 7.4 %collective-permute-start.9 = (f32[8]{0:T(128)S(1)}, f32[8]{0:T(128)S(1)}, u32[]{:S(2)}, u32[]{:S(2)}) collective-permute-start(f32[8]{0:T(128)S(1)} %select_reduce_fusion.1), channel_id=1, source_target_pairs={{0,4},{4,0},{8,12},{12,8},{1,5},{5,1},{9,13},{13,9},{2,6},{6,2},{1... | collective-permute-start | bytes 104 | tf_op jit(solution)/shard_map/ppermute | solution.py:43
  191.2 4.9 %collective-permute-start.10 = (f32[8]{0:T(128)S(1)}, f32[8]{0:T(128)S(1)}, u32[]{:S(2)}, u32[]{:S(2)}) collective-permute-start(f32[8]{0:T(128)S(1)} %add.316), channel_id=1, source_target_pairs={{0,8},{4,12},{8,0},{12,4},{1,9},{5,13},{9,1},{13,5},{2,10},{6,14},... | collective-permute-start | bytes 104 | tf_op jit(solution)/shard_map/ppermute | solution.py:43
  (41 other events, 150.3 us)

commit v13 on v11

--- a/solution.py
+++ b/solution.py
@@ -272,7 +272,13 @@
         state_zero,
         state_zero,
     )
-    summary, entering = lax.scan(chain_link, start_carry, (states, carried))
+    carry = start_carry
+    entering_steps = []
+    for j in range(tile_count):
+        carry, seen = chain_link(carry, (states[j], carried[j]))
+        entering_steps.append(seen)
+    summary = carry
+    entering = tuple(jnp.stack(parts) for parts in zip(*entering_steps))
     incoming = entering_2(
         (summary[0], summary[1], summary[2], summary[3]),
         "seq",

time: 184 us -> 184 us (level)
  local copies, waits for them, and re-layouts: 55.5 us -> 61.6 us
  other arithmetic: 42.9 us -> 37 us
    dot_general x0 -> x2, local copies, waits for them, and re-layouts: none -> 6.89 us  [the longest x1 3.45 us: per_device(): jnp.einsum('gsm,jgis->jgim', inward_lower, masked_signal, preferred_eleme...]
    convert_element_type x0 -> x2, local copies, waits for them, and re-layouts: none -> 6.44 us  [the longest x1 3.23 us: split_table(): lower = (table - upper.astype(jnp.float32)).astype(jnp.bfloat16)]
    mul x1, other arithmetic: 9.37 us -> 4 us  [modal_tables(): power_re = magnitude * jnp.cos(powers * angles[None])]
    slice x5 -> x2, local copies, waits for them, and re-layouts: 5.6 us -> 0.76 us  [the longest x1 0.58 us: per_device(): carry, seen = chain_link(carry, (states[j], carried[j]))]
    transpose x0 -> x1, local copies, waits for them, and re-layouts: none -> 3.42 us  [modal_tables(): jnp.transpose(jnp.concatenate((kernel_re[1:], -kernel_im[1:]), axis=2), (...]
    sub x3, other arithmetic: 0.03 us -> 3.35 us  [complex_link(): late_are * early_are - late_aim * early_aim]
    slice x1 -> x0, other arithmetic: 3.19 us -> none  [modal_tables(): kernel_re[1:]]
    unnamed x106 -> x66, local copies, waits for them, and re-layouts: 27 us -> 24.2 us
  transfers between devices with their start and end apart: 11 -> 11, of which waited for: 9 -> 9; matrix products, arithmetic and copies ran while one was open for 44% -> 43% of each run, Pallas kernels for 0% -> 0%
where the time goes in v13:
time: 184 us; the launch traced here: 183 us
  local copies, waits for them, and re-layouts  61.6 us (33%)
  matrix products  40.6 us (22%)
  other arithmetic  37 us (20%)
  starting transfers between devices  26.1 us (14%)
  waiting for transfers between devices  16.8 us (9%)
    unnamed x66, local copies, waits for them, and re-layouts  24.2 us
    ppermute x6, starting transfers between devices, sum_over(): part = part + lax.ppermute(part, axis, [(i, i ^ bit) for i in range(count)])  12.3 us
    ppermute x3, starting transfers between devices, from_behind(): return lax.ppermute(shard, axis, pairs)  12.1 us
    dot_general x2, matrix products, medium_block(): jnp.einsum('gts,gis->git', matrix, window, preferred_element_type=jnp.flo...  11.9 us
    ppermute x6, waiting for transfers between devices, sum_over(): part = part + lax.ppermute(part, axis, [(i, i ^ bit) for i in range(count)])  9.45 us
    select_n x1, other arithmetic, intra_block(): jnp.where(same_genome, toeplitz_upper, jnp.zeros_like(toeplitz_upper))  6.9 us
    dot_general x2, matrix products, intra_block(): jnp.einsum('gts,gis->git', lower, block_in, preferred_element_type=jnp.fl...  6.6 us
    ppermute x2, waiting for transfers between devices, scatter_sum(): part = keep + lax.ppermute(give, axes, [(i, i ^ bit) for i in range(count)])  5.49 us
  transfers between devices with their start and end apart: 11, of which 9 were waited for; matrix products, arithmetic and copies ran while one was open for 43% of the time, Pallas kernels for 0%

profile of v13, /device:TPU:0, one launch (start us, length us, event | category | flops | bytes accessed | tf_op | source)
XLA Modules:
  0.0 183.2 jit_solution(10108608932633320040)
XLA Ops:
  3.3 6.0 %collective-permute-start = (bf16[2,136,2048]{2,1,0:T(8,128)(2,1)}, bf16[2,136,2048]{2,1,0:T(8,128)(2,1)}, u32[]{:S(2)}, u32[]{:S(2)}) collective-permute-start(bf16[2,136,2048]{2,1,0:T(8,128)(2,1)} %pad_maximum_fusion), channel_id=1, source_target_pairs={{0,4},{4,8},{8,12},{1,5},{5,9},{9,13},{2,6},{6,10},{10,14},{3,7},{... | collective-permute-start | bytes 3342344 | tf_op jit(solution)/shard_map/ppermute | solution.py:18
  9.3 4.0 %fusion.45 = (f32[129,128,16]{1,2,0:T(8,128)S(1)}, f32[129,128,16]{1,2,0:T(8,128)S(1)}, f32[129,128,16]{1,2,0:T(8,128)S(1)}) fusion(f32[128,16]{0,1:T(8,128)S(1)} %get-tuple-element.64, f32[129]{0:T(256)S(1)} %iota_convert_fusion, f32[128,16]{0,1:T(8,128)S(1)} %get-tuple-element.61, f32[129]{0:T(256)S(1)} %fusion.77, f32[128,16]{0,1:T(8,128)S(1)} %get-tuple-element.63, ...), kind=kLoop, calls=%fused_computation.67 | loop fusion | flops 1849344 | bytes 3204104 | tf_op jit(solution)/shard_map/mul | solution.py:120
  24.4 4.0 %convolution_convert_fusion = bf16[384,16384]{1,0:T(8,128)(2,1)S(1)} fusion(s32[16384]{0:T(1024)S(1)} %add_select_fusion, s32[128]{0:T(128)S(1)} %iota.77, bf16[128,128]{0,1:T(8,128)(2,1)S(1)} %get-tuple-element.9, bf16[128,128]{0,1:T(8,128)(2,1)S(1)} %get-tuple-element.10, bf16[128,128]{0,1:T(8,128)(2,1)S(1)} %copy.218), kind=kOutput, calls=%fused_computation | convolution fusion | flops 1619296256 | bytes 12747264 | tf_op jit(solution)/shard_map/dot_general | solution.py:109
  28.4 3.9 %slice_bitcast_fusion = (bf16[16,8,128,128]{3,1,2,0:T(8,128)(2,1)}, bf16[16,8,128,128]{3,1,2,0:T(8,128)(2,1)}, bf16[16,8,128,128]{3,1,2,0:T(8,128)(2,1)S(1)}) fusion(bf16[384,16384]{1,0:T(8,128)(2,1)S(1)} %convolution_convert_fusion), kind=kLoop, calls=%fused_computation.12 | loop fusion | bytes 25165824
  38.6 3.2 %copy.230 = bf16[128,128,32,1]{1,2,3,0:T(8,128)(2,1)} copy(bf16[128,128,32,1]{0,2,1,3:T(8,128)(2,1)} %fusion.47) | data formatting | bytes 2097152 | tf_op jit(solution)/shard_map/convert_element_type | solution.py:136
  42.3 3.2 %copy.229 = bf16[128,128,32,1]{1,2,3,0:T(8,128)(2,1)} copy(bf16[128,128,32,1]{0,2,1,3:T(8,128)(2,1)} %fusion.44) | data formatting | bytes 2097152 | tf_op jit(solution)/shard_map/convert_element_type | solution.py:135
  49.4 5.5 %copy.240 = bf16[16,8,128,128]{3,2,1,0:T(8,128)(2,1)} copy(bf16[16,8,128,128]{3,1,2,0:T(8,128)(2,1)} %get-tuple-element.12) | data formatting | bytes 8388608
  54.9 3.2 %copy.241 = bf16[16,8,128,128]{3,2,1,0:T(8,128)(2,1)} copy(bf16[16,8,128,128]{3,1,2,0:T(8,128)(2,1)S(1)} %copy-done.2) | data formatting | bytes 8388608
  60.0 3.4 %copy.226 = f32[128,128,32]{1,2,0:T(8,128)} copy(f32[128,128,32]{0,2,1:T(8,128)} %maximum_bitcast_fusion.1) | data formatting | bytes 4194304 | tf_op jit(solution)/shard_map/transpose | solution.py:126
  67.4 5.1 %constant_dynamic-update-slice_fusion = bf16[128,128,256]{2,1,0:T(8,128)(2,1)} fusion(bf16[128,128,256]{2,1,0:T(8,128)(2,1)} %constant_dynamic-update-slice_fusion.1, bf16[128,128,128]{2,1,0:T(8,128)(2,1)} %bitcast.174), kind=kLoop, calls=%fused_computation.174 | loop fusion | bytes 8388608 | tf_op jit(solution)/shard_map/concatenate | solution.py:211
  73.7 6.9 %bitcast_select_fusion.3 = (bf16[128,128,128]{2,1,0:T(8,128)(2,1)}, bf16[128,128,128]{2,1,0:T(8,128)(2,1)}, bf16[128,128,128]{2,1,0:T(8,128)(2,1)}, bf16[128,128,128]{2,1,0:T(8,128)(2,1)}) fusion(bf16[16,8,128,128]{3,2,1,0:T(8,128)(2,1)S(1)} %copy-done.5, pred[128,128]{1,0:T(8,128)(4,1)S(1)} %get-tuple-element.7, pred[128,128]{1,0:T(8,128)(4,1)S(1)} %compare_and_fusion.3, ...), kind=kLoop, calls=%fused_computation.11 | loop fusion | flops 8388608 | bytes 25198592 | tf_op jit(solution)/shard_map/jit(_where)/select_n | solution.py:242
  82.4 5.2 %fusion.35 = bf16[2048,384]{0,1:T(8,128)(2,1)} fusion(f32[384]{0:T(512)S(1)} %get-tuple-element.75, f32[392,2048]{1,0:T(8,128)S(1)} %convert_multiply_fusion, f32[2048]{0:T(1024)S(1)} %bitcast.200, f32[384]{0:T(512)S(1)} %get-tuple-element.71, f32[2048]{0:T(1024)S(1)} %bitcast.201, f32[384]{0:T(512)S(1)} %get-tuple-element.72, f32[2048]{0:T(1024)S(1)} %bitcast.196, ...), kind=kLoop, calls=%fused_computation.56 | loop fusion | flops 15728640 | bytes 23659520 | tf_op jit(solution)/shard_map/transpose | solution.py:204
  90.3 6.1 %fusion.38 = bf16[128,16,128]{2,1,0:T(8,128)(2,1)S(1)} fusion(bf16[128,128,256]{2,1,0:T(8,128)(2,1)} %constant_dynamic-update-slice_fusion, pred[128,256]{1,0:T(8,128)(4,1)S(1)} %get-tuple-element.84, bf16[128,16,384]{2,1,0:T(8,128)(2,1)} %bitcast.183), kind=kOutput, calls=%fused_computation.63 | convolution fusion | flops 138674176 | bytes 9994240 | tf_op jit(solution)/shard_map/gts,gis->git/dot_general | solution.py:228
  96.4 5.8 %fusion.41 = bf16[128,16,128]{2,1,0:T(8,128)(2,1)S(1)} fusion(bf16[128,128,256]{2,1,0:T(8,128)(2,1)} %constant_dynamic-update-slice_fusion, pred[128,256]{1,0:T(8,128)(4,1)S(1)} %get-tuple-element.85, bf16[128,16,384]{2,1,0:T(8,128)(2,1)S(1)} %bitcast.184), kind=kOutput, calls=%fused_computation.64 | convolution fusion | flops 138674176 | bytes 9994240 | tf_op jit(solution)/shard_map/gts,gis->git/dot_general | solution.py:228
  104.2 3.5 %copy.224 = f32[128,2,16,32]{0,3,2,1:T(8,128)} copy(f32[128,2,16,32]{3,2,1,0:T(8,128)} %fusion.56) | data formatting | bytes 1048576 | tf_op jit(solution)/shard_map/gsm,jgis->jgim/dot_general | solution.py:253
  107.7 3.2 %fusion.58 = f32[128,2,16,32]{3,2,1,0:T(8,128)} fusion(bf16[128,128,32,1]{1,2,3,0:T(8,128)(2,1)} %copy.229, pred[2,128]{1,0:T(4,128)(4,1)S(1)} %get-tuple-element.77, bf16[1,128,16,128]{3,2,1,0:T(8,128)(2,1)S(1)} %bitcast.181, bf16[1,128,16,128]{3,2,1,0:T(8,128)(2,1)S(1)} %bitcast.178), kind=kOutput, calls=%fused_computation.86 | convolution fusion | flops 34603008 | bytes 2621696 | tf_op jit(solution)/shard_map/gsm,jgis->jgim/dot_general | solution.py:251
  110.9 3.4 %copy.223 = f32[128,2,16,32]{0,3,2,1:T(8,128)} copy(f32[128,2,16,32]{3,2,1,0:T(8,128)} %fusion.58) | data formatting | bytes 1048576 | tf_op jit(solution)/shard_map/gsm,jgis->jgim/dot_general | solution.py:251
  121.0 3.3 %fusion.37 = f32[1,128,16,128]{3,2,1,0:T(8,128)} fusion(f32[128,16,128]{2,1,0:T(8,128)S(1)} %fusion.88, bf16[128,16,128]{2,1,0:T(8,128)(2,1)S(1)} %fusion.38, bf16[128,128,128]{2,1,0:T(8,128)(2,1)S(1)} %copy-done.8), kind=kOutput, calls=%fused_computation.62 | convolution fusion | flops 67371008 | bytes 6815744 | tf_op jit(solution)/shard_map/gts,gis->git/dot_general | solution.py:246
  126.7 3.4 %collective-permute-start.2 = (f32[128,544]{0,1:T(8,128)S(1)}, f32[128,544]{0,1:T(8,128)S(1)}, u32[]{:S(2)}, u32[]{:S(2)}) collective-permute-start(f32[128,544]{0,1:T(8,128)S(1)} %pad_maximum_fusion.4), channel_id=1, source_target_pairs={{0,8},{4,12},{1,9},{5,13},{2,10},{6,14},{3,11},{7,15},{16,24},{20,... | collective-permute-start | bytes 835592 | tf_op jit(solution)/shard_map/ppermute | solution.py:18
  130.1 3.3 %fusion.36 = f32[1,128,16,128]{3,2,1,0:T(8,128)} fusion(f32[128,16,128]{2,1,0:T(8,128)S(1)} %fusion.89, bf16[128,16,128]{2,1,0:T(8,128)(2,1)S(1)} %fusion.41, bf16[128,128,128]{2,1,0:T(8,128)(2,1)S(1)} %copy-done.7), kind=kOutput, calls=%fused_computation.60 | convolution fusion | flops 67371008 | bytes 6815744 | tf_op jit(solution)/shard_map/gts,gis->git/dot_general | solution.py:246
  139.4 5.3 %fusion.29 = f32[128,16,2,128]{3,1,0,2:T(8,128)S(1)} fusion(f32[1,128,16,128]{3,2,1,0:T(8,128)} %fusion.36, f32[1,128,16,128]{3,2,1,0:T(8,128)} %fusion.37, f32[2,128,16,32]{3,2,1,0:T(8,128)} %copy.231, f32[128,128,32]{1,2,0:T(8,128)} %copy.226, f32[128,16]{1,0:T(8,128)S(1)} %mul.724, f32[2,128]{1,0:T(2,128)S(1)} %get-tuple-element.76, ...), kind=kOutput, calls=%fused_computation.49 | convolution fusion | flops 204996608 | bytes 7873536 | tf_op jit(solution)/shard_map/gtm,jgim->jgit/dot_general | solution.py:296
  161.1 4.0 %collective-permute-done.6 = f32[64,512]{1,0:T(8,128)S(1)} collective-permute-done((f32[64,512]{1,0:T(8,128)S(1)}, f32[64,512]{1,0:T(8,128)S(1)}, u32[]{:S(2)}, u32[]{:S(2)}) %collective-permute-start.6) | collective-permute-done | bytes 131104 | tf_op jit(solution)/shard_map/ppermute | solution.py:31
  170.3 5.9 %collective-permute-start.9 = (f32[8]{0:T(128)S(1)}, f32[8]{0:T(128)S(1)}, u32[]{:S(2)}, u32[]{:S(2)}) collective-permute-start(f32[8]{0:T(128)S(1)} %select_reduce_fusion.1), channel_id=1, source_target_pairs={{0,4},{4,0},{8,12},{12,8},{1,5},{5,1},{9,13},{13,9},{2,6},{6,2},{1... | collective-permute-start | bytes 104 | tf_op jit(solution)/shard_map/ppermute | solution.py:43
  177.8 3.4 %collective-permute-start.10 = (f32[8]{0:T(128)S(1)}, f32[8]{0:T(128)S(1)}, u32[]{:S(2)}, u32[]{:S(2)}) collective-permute-start(f32[8]{0:T(128)S(1)} %add.349), channel_id=1, source_target_pairs={{0,8},{4,12},{8,0},{12,4},{1,9},{5,13},{9,1},{13,5},{2,10},{6,14},... | collective-permute-start | bytes 104 | tf_op jit(solution)/shard_map/ppermute | solution.py:43
  (162 shorter events, 77.8 us)
Async XLA Ops:
  0.6 152.2 %copy-start = (bf16[2048,512]{1,0:T(8,128)(2,1)S(1)}, bf16[2048,512]{1,0:T(8,128)(2,1)}, u32[]{:S(2)}) copy-start(bf16[2048,512]{1,0:T(8,128)(2,1)} %param.19) | copy-start | bytes 6291460
  0.6 8.6 %copy-start.22 = (f32[4,128,16]{1,2,0:T(8,128)S(1)}, f32[4,128,16]{1,2,0:T(8,128)}, u32[]{:S(2)}) copy-start(f32[4,128,16]{1,2,0:T(8,128)} %param.16) | copy-start | bytes 98308
  3.3 77.3 %collective-permute-start = (bf16[2,136,2048]{2,1,0:T(8,128)(2,1)}, bf16[2,136,2048]{2,1,0:T(8,128)(2,1)}, u32[]{:S(2)}, u32[]{:S(2)}) collective-permute-start(bf16[2,136,2048]{2,1,0:T(8,128)(2,1)} %pad_maximum_fusion), channel_id=1, source_target_pairs={{0,4},{4,8},{8,12},{1,5},{5,9},{9,13},{2,6},{6,10},{10,14},{3,7},{... | collective-permute-start | bytes 3342344 | tf_op jit(solution)/shard_map/ppermute | solution.py:18
  49.4 5.5 %copy-start.2 = (bf16[16,8,128,128]{3,1,2,0:T(8,128)(2,1)S(1)}, bf16[16,8,128,128]{3,1,2,0:T(8,128)(2,1)}, u32[]{:S(2)}) copy-start(bf16[16,8,128,128]{3,1,2,0:T(8,128)(2,1)} %get-tuple-element.11) | copy-start | bytes 12582916
  67.4 5.1 %copy-start.5 = (bf16[16,8,128,128]{3,2,1,0:T(8,128)(2,1)S(1)}, bf16[16,8,128,128]{3,2,1,0:T(8,128)(2,1)}, u32[]{:S(2)}) copy-start(bf16[16,8,128,128]{3,2,1,0:T(8,128)(2,1)} %copy.240) | copy-start | bytes 12582916
  67.4 6.2 %copy-start.6 = (bf16[16,8,128,128]{3,2,1,0:T(8,128)(2,1)S(1)}, bf16[16,8,128,128]{3,2,1,0:T(8,128)(2,1)}, u32[]{:S(2)}) copy-start(bf16[16,8,128,128]{3,2,1,0:T(8,128)(2,1)} %copy.241) | copy-start | bytes 12582916
  73.7 8.2 %copy-start.16 = (bf16[256,2048]{1,0:T(8,128)(2,1)S(1)}, bf16[256,2048]{1,0:T(8,128)(2,1)}, u32[]{:S(2)}) copy-start(bf16[256,2048]{1,0:T(8,128)(2,1)} %param.12) | copy-start | bytes 3145732
  73.7 8.2 %copy-start.17 = (bf16[256,2048]{1,0:T(8,128)(2,1)S(1)}, bf16[256,2048]{1,0:T(8,128)(2,1)}, u32[]{:S(2)}) copy-start(bf16[256,2048]{1,0:T(8,128)(2,1)} %param.13) | copy-start | bytes 3145732
  90.3 6.1 %copy-start.19 = (bf16[2048,384]{1,0:T(8,128)(2,1)S(1)}, bf16[2048,384]{1,0:T(8,128)(2,1)}, u32[]{:S(2)}) copy-start(bf16[2048,384]{1,0:T(8,128)(2,1)} %copy.216) | copy-start | bytes 4718596
  96.4 5.8 %copy-start.20 = (bf16[128,128,32,1]{1,2,3,0:T(8,128)(2,1)S(1)}, bf16[128,128,32,1]{1,2,3,0:T(8,128)(2,1)}, u32[]{:S(2)}) copy-start(bf16[128,128,32,1]{1,2,3,0:T(8,128)(2,1)} %copy.230) | copy-start | bytes 3145732
  115.9 10.6 %collective-permute-start.1 = (f32[128,544]{0,1:T(8,128)S(1)}, f32[128,544]{0,1:T(8,128)S(1)}, u32[]{:S(2)}, u32[]{:S(2)}) collective-permute-start(f32[128,544]{0,1:T(8,128)S(1)} %pad_maximum_fusion.3), channel_id=1, source_target_pairs={{0,4},{4,8},{8,12},{1,5},{5,9},{9,13},{2,6},{6,10},{10,14},{3,7},{... | collective-permute-start | bytes 835592 | tf_op jit(solution)/shard_map/ppermute | solution.py:18
  124.3 5.8 %copy-start.7 = (bf16[128,128,128]{2,1,0:T(8,128)(2,1)S(1)}, bf16[128,128,128]{2,1,0:T(8,128)(2,1)}, u32[]{:S(2)}) copy-start(bf16[128,128,128]{2,1,0:T(8,128)(2,1)} %get-tuple-element.52) | copy-start | bytes 12582916
  126.7 8.6 %collective-permute-start.2 = (f32[128,544]{0,1:T(8,128)S(1)}, f32[128,544]{0,1:T(8,128)S(1)}, u32[]{:S(2)}, u32[]{:S(2)}) collective-permute-start(f32[128,544]{0,1:T(8,128)S(1)} %pad_maximum_fusion.4), channel_id=1, source_target_pairs={{0,8},{4,12},{1,9},{5,13},{2,10},{6,14},{3,11},{7,15},{16,24},{20,... | collective-permute-start | bytes 835592 | tf_op jit(solution)/shard_map/ppermute | solution.py:18
  144.7 8.1 %copy-start.27 = (f32[2048]{0:T(1024)S(1)}, f32[2048]{0:T(1024)}, u32[]{:S(2)}) copy-start(f32[2048]{0:T(1024)} %param.18) | copy-start | bytes 24580
  148.1 1.2 collective-permute-start.3
  149.3 3.6 %collective-permute-start.4 = (f32[256]{0:T(256)S(1)}, f32[256]{0:T(256)S(1)}, u32[]{:S(2)}, u32[]{:S(2)}) collective-permute-start(f32[256]{0:T(256)S(1)} %add.341), channel_id=1, source_target_pairs={{0,2},{1,3},{2,0},{3,1},{4,6},{5,7},{6,4},{7,5},{8,10},{9,11},{10,... | collective-permute-start | bytes 3080 | tf_op jit(solution)/shard_map/ppermute | solution.py:43
  152.9 8.1 %copy-start.28 = (s32[256]{0:T(256)S(1)}, s32[256]{0:T(256)}, u32[]{:S(2)}) copy-start(s32[256]{0:T(256)} %param.20) | copy-start | bytes 3076
  156.7 1.6 collective-permute-start.5
  159.5 5.6 %collective-permute-start.6 = (f32[64,512]{1,0:T(8,128)S(1)}, f32[64,512]{1,0:T(8,128)S(1)}, u32[]{:S(2)}, u32[]{:S(2)}) collective-permute-start(f32[64,512]{1,0:T(8,128)S(1)} %slice_select_fusion.5), channel_id=1, source_target_pairs={{0,2},{1,3},{2,0},{3,1},{4,6},{5,7},{6,4},{7,5},{8,10},{9,11},{10,... | collective-permute-start | bytes 393224 | tf_op jit(solution)/shard_map/ppermute | solution.py:31
  165.3 1.1 collective-permute-start.7
  166.7 3.6 %collective-permute-start.8 = (f32[256]{0:T(256)S(1)}, f32[256]{0:T(256)S(1)}, u32[]{:S(2)}, u32[]{:S(2)}) collective-permute-start(f32[256]{0:T(256)S(1)} %add_dynamic-update-slice_fusion), channel_id=1, source_target_pairs={{0,2},{1,3},{2,0},{3,1},{4,6},{5,7},{6,4},{7,5},{8,10},{9,11},{10,... | collective-permute-start | bytes 3080 | tf_op jit(solution)/shard_map/ppermute | solution.py:43
  170.2 13.0 %copy-start.25 = (f32[256]{0:T(256)}, f32[256]{0:T(256)S(1)}, u32[]{:S(2)}) copy-start(f32[256]{0:T(256)S(1)} %add.348) | copy-start | bytes 3076
  170.3 7.4 %collective-permute-start.9 = (f32[8]{0:T(128)S(1)}, f32[8]{0:T(128)S(1)}, u32[]{:S(2)}, u32[]{:S(2)}) collective-permute-start(f32[8]{0:T(128)S(1)} %select_reduce_fusion.1), channel_id=1, source_target_pairs={{0,4},{4,0},{8,12},{12,8},{1,5},{5,1},{9,13},{13,9},{2,6},{6,2},{1... | collective-permute-start | bytes 104 | tf_op jit(solution)/shard_map/ppermute | solution.py:43
  177.8 4.9 %collective-permute-start.10 = (f32[8]{0:T(128)S(1)}, f32[8]{0:T(128)S(1)}, u32[]{:S(2)}, u32[]{:S(2)}) collective-permute-start(f32[8]{0:T(128)S(1)} %add.349), channel_id=1, source_target_pairs={{0,8},{4,12},{8,0},{12,4},{1,9},{5,13},{9,1},{13,5},{2,10},{6,14},... | collective-permute-start | bytes 104 | tf_op jit(solution)/shard_map/ppermute | solution.py:43
  (16 other events, 47.2 us)

commit v14 on v11

--- a/solution.py
+++ b/solution.py
@@ -99,15 +99,15 @@
     return result.astype(jnp.bfloat16)
 
 
-def circulants(table):
+def circulants(table, cols):
     lag_count, width = table.shape
     lag_ids = lax.optimization_barrier(jnp.arange(lag_count, dtype=jnp.int32))
     out_pos = jnp.arange(tile_rows, dtype=jnp.int32)[:, None]
-    in_pos = jnp.arange(tile_rows, dtype=jnp.int32)[None, :]
-    lag_grid = (out_pos - in_pos + tile_rows) % tile_rows
-    one_hot = (lag_grid.reshape(1, tile_rows * tile_rows) == lag_ids[:, None]).astype(table.dtype)
+    in_pos = jnp.arange(cols, dtype=jnp.int32)[None, :]
+    lag_grid = (out_pos - in_pos + cols) % tile_rows
+    one_hot = (lag_grid.reshape(1, tile_rows * cols) == lag_ids[:, None]).astype(table.dtype)
     picked = jnp.dot(table.T, one_hot, preferred_element_type=jnp.float32)
-    return picked.astype(table.dtype).reshape(width, tile_rows, tile_rows)
+    return picked.astype(table.dtype).reshape(width, tile_rows, cols)
 
 
 def modal_tables(modal_poles):
@@ -207,10 +207,12 @@
     )
 
     long_toeplitz, outward, inward, decay_re, decay_im = modal_tables(modal_poles)
-    circ = circulants(jnp.concatenate((medium_taps, long_toeplitz[0], long_toeplitz[1]), axis=1))
-    circ_medium = jnp.concatenate((circ[:group_count], circ[:group_count]), axis=2)
-    toeplitz_upper = circ[group_count : 2 * group_count]
-    toeplitz_lower = circ[2 * group_count :]
+    circ = circulants(
+        jnp.concatenate((medium_taps, long_toeplitz[0], long_toeplitz[1]), axis=1), 2 * tile_rows
+    )
+    circ_medium = circ[:group_count]
+    toeplitz_upper = circ[group_count : 2 * group_count, :, :tile_rows]
+    toeplitz_lower = circ[2 * group_count :, :, :tile_rows]
     lag_band = (
         jnp.arange(tile_rows, dtype=jnp.int32)[:, None] + tile_rows
         - jnp.arange(2 * tile_rows, dtype=jnp.int32)[None, :]

time: 184 us -> 216 us (1.17)
  local copies, waits for them, and re-layouts: 55.5 us -> 71.2 us
  matrix products: 40.8 us -> 54.2 us
  other arithmetic: 42.9 us -> 47.3 us
  waiting for transfers between devices: 17.1 us -> 14.9 us
    unnamed x106 -> x82, local copies, waits for them, and re-layouts: 27 us -> 39.9 us
    slice x0 -> x1, local copies, waits for them, and re-layouts: none -> 7.4 us  [per_device(): circ_medium = circ[:group_count]]
    dot_general x1, matrix products: 4.59 us -> 11.3 us  [circulants(): picked = jnp.dot(table.T, one_hot, preferred_element_type=jnp.float32)]
    concatenate x1 -> x0, local copies, waits for them, and re-layouts: 5.06 us -> none  [per_device(): jnp.concatenate((circ[:group_count], circ[:group_count]), axis=2)]
    dot_general x2, matrix products: 6.73 us -> 11 us  [intra_block(): jnp.einsum('gts,gis->git', upper, block_in, preferred_element_type=jnp.fl...]
    select_n x2, other arithmetic: 6.93 us -> 10 us  [the longest x1 9.99 us: medium_block(): jnp.where(same_genome[None], circ_medium, jnp.zeros_like(circ_medium))]
    dot_general x2, matrix products: 6.6 us -> 8.9 us  [intra_block(): jnp.einsum('gts,gis->git', lower, block_in, preferred_element_type=jnp.fl...]
  transfers between devices with their start and end apart: 11 -> 11, of which waited for: 9 -> 8; matrix products, arithmetic and copies ran while one was open for 44% -> 55% of each run, Pallas kernels for 0% -> 0%
where the time goes in v14:
time: 216 us; the launch traced here: 215 us
  local copies, waits for them, and re-layouts  71.2 us (33%)
  matrix products  54.2 us (25%)
  other arithmetic  47.3 us (22%)
  starting transfers between devices  25.7 us (12%)
  waiting for transfers between devices  14.9 us (7%)
    unnamed x82, local copies, waits for them, and re-layouts  39.9 us
    ppermute x6, starting transfers between devices, sum_over(): part = part + lax.ppermute(part, axis, [(i, i ^ bit) for i in range(count)])  12.3 us
    dot_general x2, matrix products, medium_block(): jnp.einsum('gts,gis->git', matrix, window, preferred_element_type=jnp.flo...  11.9 us
    ppermute x3, starting transfers between devices, from_behind(): return lax.ppermute(shard, axis, pairs)  11.7 us
    dot_general x1, matrix products, circulants(): picked = jnp.dot(table.T, one_hot, preferred_element_type=jnp.float32)  11.3 us
    dot_general x2, matrix products, intra_block(): jnp.einsum('gts,gis->git', upper, block_in, preferred_element_type=jnp.fl...  11 us
    select_n x1, other arithmetic, medium_block(): jnp.where(same_genome[None], circ_medium, jnp.zeros_like(circ_medium))  9.99 us
    ppermute x6, waiting for transfers between devices, sum_over(): part = part + lax.ppermute(part, axis, [(i, i ^ bit) for i in range(count)])  9.45 us
  transfers between devices with their start and end apart: 11, of which 8 were waited for; matrix products, arithmetic and copies ran while one was open for 55% of the time, Pallas kernels for 0%

profile of v14, /device:TPU:0, one launch (start us, length us, event | category | flops | bytes accessed | tf_op | source)
XLA Modules:
  0.0 214.7 jit_solution(17519981898012602223)
XLA Ops:
  3.3 5.9 %collective-permute-start = (bf16[2,136,2048]{2,1,0:T(8,128)(2,1)}, bf16[2,136,2048]{2,1,0:T(8,128)(2,1)}, u32[]{:S(2)}, u32[]{:S(2)}) collective-permute-start(bf16[2,136,2048]{2,1,0:T(8,128)(2,1)} %pad_maximum_fusion), channel_id=1, source_target_pairs={{0,4},{4,8},{8,12},{1,5},{5,9},{9,13},{2,6},{6,10},{10,14},{3,7},{... | collective-permute-start | bytes 3342344 | tf_op jit(solution)/shard_map/ppermute | solution.py:18
  9.7 9.4 %fusion.36 = (f32[129,128,16]{0,2,1:T(8,128)S(1)}, f32[129,128,16]{0,2,1:T(8,128)}, f32[129,128,16]{0,2,1:T(8,128)S(1)}) fusion(f32[128,16]{1,0:T(8,128)S(1)} %copy.89, f32[129]{0:T(256)S(1)} %iota_convert_fusion, f32[128,16]{1,0:T(8,128)S(1)} %copy.88, f32[129]{0:T(256)S(1)} %fusion.89, f32[128,16]{1,0:T(8,128)S(1)} %copy.90, f32[128,16]{1,0:T(8,128)S(1)} %copy.87), kind=kLoop, calls=%fused_computation.62 | loop fusion | flops 1849344 | bytes 3204104 | tf_op jit(solution)/shard_map/mul | solution.py:121
  25.3 3.2 %fusion.101 = (f32[128,128,16]{0,2,1:T(8,128)}, f32[128,128]{0,1:T(8,128)S(1)}) fusion(f32[129,128,16]{0,2,1:T(8,128)} %get-tuple-element.258), kind=kLoop, calls=%fused_computation.215 | loop fusion | flops 245760 | bytes 3211264 | tf_op jit(solution)/shard_map/slice | solution.py:126
  28.8 11.3 %convolution_convert_fusion = bf16[384,32768]{1,0:T(8,128)(2,1)} fusion(s32[32768]{0:T(1024)S(1)} %add_select_fusion, s32[128]{0:T(128)S(1)} %iota.75, bf16[128,128]{0,1:T(8,128)(2,1)S(1)} %get-tuple-element.224, bf16[128,128]{0,1:T(8,128)(2,1)S(1)} %get-tuple-element.225, bf16[128,128]{0,1:T(8,128)(2,1)S(1)} %copy.91), kind=kOutput, calls=%fused_computation.11 | convolution fusion | flops 3238297600 | bytes 25395712 | tf_op jit(solution)/shard_map/dot_general | solution.py:109
  40.1 7.4 %slice.240 = bf16[128,32768]{1,0:T(8,128)(2,1)} slice(bf16[384,32768]{1,0:T(8,128)(2,1)} %convolution_convert_fusion), slice={[0:128], [0:32768]} | slice | bytes 16777216 | tf_op jit(solution)/shard_map/slice | solution.py:213
  47.5 9.1 %copy.106 = bf16[16,8,128,256]{3,2,1,0:T(8,128)(2,1)} copy(bf16[16,8,128,256]{3,1,2,0:T(8,128)(2,1)} %bitcast.141) | data formatting | bytes 16777216
  66.7 23.2 %copy.107 = bf16[48,8,128,256]{3,2,1,0:T(8,128)(2,1)} copy(bf16[48,8,128,256]{3,1,2,0:T(8,128)(2,1)} %bitcast.140) | data formatting | bytes 50331648
  97.5 10.0 %bitcast_select_fusion.1 = (bf16[128,128,256]{2,1,0:T(8,128)(2,1)}, bf16[128,128,256]{2,1,0:T(8,128)(2,1)}) fusion(bf16[16,8,128,256]{3,2,1,0:T(8,128)(2,1)} %copy.106, pred[128,256]{1,0:T(8,128)(4,1)S(1)} %get-tuple-element.285, pred[128,256]{1,0:T(8,128)(4,1)S(1)} %get-tuple-element.286), kind=kLoop, calls=%fused_computation.14 | loop fusion | flops 8388608 | bytes 25231360 | tf_op jit(solution)/shard_map/jit(_where)/select_n | solution.py:229
  109.6 5.3 %fusion.48 = bf16[2048,384]{0,1:T(8,128)(2,1)} fusion(f32[384]{0:T(512)S(1)} %copy-done.29, f32[392,2048]{1,0:T(8,128)S(1)} %convert_multiply_fusion, f32[2048]{0:T(1024)S(1)} %bitcast.174, f32[384]{0:T(512)S(1)} %copy-done.25, f32[2048]{0:T(1024)S(1)} %bitcast.175, f32[384]{0:T(512)S(1)} %copy-done.26, f32[2048]{0:T(1024)S(1)} %bitcast.170, ...), kind=kLoop, calls=%fused_computation.82 | loop fusion | flops 15728640 | bytes 23659520 | tf_op jit(solution)/shard_map/transpose | solution.py:204
  117.5 6.1 %convolution_convert_fusion.2 = bf16[128,16,128]{2,1,0:T(8,128)(2,1)S(1)} fusion(bf16[128,128,256]{2,1,0:T(8,128)(2,1)} %get-tuple-element.232, bf16[128,16,384]{2,1,0:T(8,128)(2,1)} %bitcast.148), kind=kOutput, calls=%fused_computation.88 | convolution fusion | flops 134479872 | bytes 9961472 | tf_op jit(solution)/shard_map/gts,gis->git/dot_general | solution.py:230
  123.7 5.9 %convolution_convert_fusion.1 = bf16[128,16,128]{2,1,0:T(8,128)(2,1)S(1)} fusion(bf16[128,128,256]{2,1,0:T(8,128)(2,1)} %get-tuple-element.233, bf16[128,16,384]{2,1,0:T(8,128)(2,1)S(1)} %bitcast.149), kind=kOutput, calls=%fused_computation.87 | convolution fusion | flops 134479872 | bytes 9961472 | tf_op jit(solution)/shard_map/gts,gis->git/dot_general | solution.py:230
  132.4 2.7 %copy.96 = f32[2,128,16,32]{1,3,2,0:T(8,128)S(1)} copy(f32[2,128,16,32]{3,2,0,1:T(8,128)} %add_bitcast_fusion) | data formatting | bytes 1048576
  135.1 5.7 %while.25 = (s32[]{:T(128)}, f32[128,16]{0,1:T(8,128)S(1)}, f32[128,16]{0,1:T(8,128)S(1)}, f32[128,16,16]{0,2,1:T(8,128)S(1)}, f32[128,16,16]{0,2,1:T(8,128)S(1)...) while((s32[]{:T(128)}, f32[128,16]{0,1:T(8,128)S(1)}, ...), condition=%wide.region_7.8_spmd.clone, body=%wide.region_6.7_spmd.clone.sunk | while | flops 421891 | bytes 1999539 | solution.py:277
  143.4 4.5 %fusion.7 = f32[128,16,128]{2,1,0:T(8,128)S(1)} fusion(bf16[128,16,128]{2,1,0:T(8,128)(2,1)S(1)} %copy-done.5, pred[128,128]{1,0:T(8,128)(4,1)S(1)} %copy-done.20, bf16[384,128,256]{2,1,0:T(8,128)(2,1)} %bitcast.142), kind=kOutput, calls=%fused_computation.21 | convolution fusion | flops 69206016 | bytes 5783552 | tf_op jit(solution)/shard_map/gts,gis->git/dot_general | solution.py:248
  147.8 5.6 %fusion.52 = f32[1,128,16,128]{3,2,1,0:T(8,128)} fusion(f32[128,16,128]{2,1,0:T(8,128)S(1)} %fusion.7, bf16[128,16,128]{2,1,0:T(8,128)(2,1)S(1)} %copy-done.5, pred[128,128]{1,0:T(8,128)(4,1)S(1)} %copy-done.20, bf16[384,128,256]{2,1,0:T(8,128)(2,1)} %bitcast.143), kind=kOutput, calls=%fused_computation.84 | convolution fusion | flops 69468160 | bytes 6832128 | tf_op jit(solution)/shard_map/gts,gis->git/dot_general | solution.py:246
  153.4 4.5 %fusion.3 = f32[128,16,128]{2,1,0:T(8,128)S(1)} fusion(bf16[128,16,128]{2,1,0:T(8,128)(2,1)S(1)} %copy-done.7, pred[128,128]{1,0:T(8,128)(4,1)S(1)} %copy-done.21, bf16[384,128,256]{2,1,0:T(8,128)(2,1)} %bitcast.144), kind=kOutput, calls=%fused_computation.17 | convolution fusion | flops 69206016 | bytes 5783552 | tf_op jit(solution)/shard_map/gts,gis->git/dot_general | solution.py:248
  158.0 3.3 %collective-permute-start.2 = (f32[128,544]{0,1:T(8,128)S(1)}, f32[128,544]{0,1:T(8,128)S(1)}, u32[]{:S(2)}, u32[]{:S(2)}) collective-permute-start(f32[128,544]{0,1:T(8,128)S(1)} %pad_maximum_fusion.4), channel_id=1, source_target_pairs={{0,8},{4,12},{1,9},{5,13},{2,10},{6,14},{3,11},{7,15},{16,24},{20,... | collective-permute-start | bytes 835592 | tf_op jit(solution)/shard_map/ppermute | solution.py:18
  161.3 5.5 %fusion.58 = f32[1,128,16,128]{3,2,1,0:T(8,128)} fusion(f32[128,16,128]{2,1,0:T(8,128)S(1)} %fusion.3, bf16[128,16,128]{2,1,0:T(8,128)(2,1)S(1)} %copy-done.7, pred[128,128]{1,0:T(8,128)(4,1)S(1)} %copy-done.21, bf16[384,128,256]{2,1,0:T(8,128)(2,1)} %bitcast.145), kind=kOutput, calls=%fused_computation.86 | convolution fusion | flops 69468160 | bytes 6832128 | tf_op jit(solution)/shard_map/gts,gis->git/dot_general | solution.py:246
  167.9 3.1 %copy.102 = f32[2,128,16,32]{3,2,1,0:T(8,128)} copy(f32[2,128,16,32]{1,3,2,0:T(8,128)} %pad_maximum_fusion.2) | data formatting | bytes 1048576 | tf_op jit(solution)/shard_map/concatenate | solution.py:295
  171.0 5.3 %fusion.39 = f32[128,16,2,128]{3,1,0,2:T(8,128)S(1)} fusion(f32[1,128,16,128]{3,2,1,0:T(8,128)} %fusion.58, f32[1,128,16,128]{3,2,1,0:T(8,128)} %fusion.52, f32[2,128,16,32]{3,2,1,0:T(8,128)} %copy.102, f32[128,128,16]{0,2,1:T(8,128)} %get-tuple-element.236, f32[128,128,16]{0,2,1:T(8,128)} %get-tuple-element.234, f32[128,16]{1,0:T(8,128)S(1)} %mul.576, ...), kind=kOutput, calls=%fused_computation.67 | convolution fusion | flops 205520896 | bytes 7873536 | tf_op jit(solution)/shard_map/gtm,jgim->jgit/dot_general | solution.py:292
  184.4 3.0 %fusion.66 = f32[256,512]{1,0:T(8,128)S(1)} fusion(bf16[2048,512]{1,0:T(8,128)(2,1)S(1)} %copy-done, f32[2048]{0:T(1024)S(1)} %copy-done.36, f32[256]{0:T(256)S(1)} %add_rsqrt_fusion, f32[256,8,2,128]{3,2,1,0:T(2,128)} %bitcast.151, bf16[256,2048]{0,1:T(8,128)(2,1)S(1)} %copy-done.8), kind=kOutput, calls=%fused_computation.93 | convolution fusion | flops 540540928 | bytes 5776384 | tf_op jit(solution)/shard_map/dot_general | solution.py:162
  192.6 4.0 %collective-permute-done.6 = f32[64,512]{1,0:T(8,128)S(1)} collective-permute-done((f32[64,512]{1,0:T(8,128)S(1)}, f32[64,512]{1,0:T(8,128)S(1)}, u32[]{:S(2)}, u32[]{:S(2)}) %collective-permute-start.6) | collective-permute-done | bytes 131104 | tf_op jit(solution)/shard_map/ppermute | solution.py:31
  201.9 5.9 %collective-permute-start.9 = (f32[8]{0:T(128)S(1)}, f32[8]{0:T(128)S(1)}, u32[]{:S(2)}, u32[]{:S(2)}) collective-permute-start(f32[8]{0:T(128)S(1)} %select_reduce_fusion.1), channel_id=1, source_target_pairs={{0,4},{4,0},{8,12},{12,8},{1,5},{5,1},{9,13},{13,9},{2,6},{6,2},{1... | collective-permute-start | bytes 104 | tf_op jit(solution)/shard_map/ppermute | solution.py:43
  209.3 3.4 %collective-permute-start.10 = (f32[8]{0:T(128)S(1)}, f32[8]{0:T(128)S(1)}, u32[]{:S(2)}, u32[]{:S(2)}) collective-permute-start(f32[8]{0:T(128)S(1)} %add.305), channel_id=1, source_target_pairs={{0,8},{4,12},{8,0},{12,4},{1,9},{5,13},{9,1},{13,5},{2,10},{6,14},... | collective-permute-start | bytes 104 | tf_op jit(solution)/shard_map/ppermute | solution.py:43
  (196 shorter events, 66.0 us)
Async XLA Ops:
  0.6 183.8 %copy-start = (bf16[2048,512]{1,0:T(8,128)(2,1)S(1)}, bf16[2048,512]{1,0:T(8,128)(2,1)}, u32[]{:S(2)}) copy-start(bf16[2048,512]{1,0:T(8,128)(2,1)} %param.21) | copy-start | bytes 6291460
  0.6 8.6 %copy-start.16 = (f32[4,128,16]{1,2,0:T(8,128)S(1)}, f32[4,128,16]{1,2,0:T(8,128)}, u32[]{:S(2)}) copy-start(f32[4,128,16]{1,2,0:T(8,128)} %param.18) | copy-start | bytes 98308
  3.3 104.2 %collective-permute-start = (bf16[2,136,2048]{2,1,0:T(8,128)(2,1)}, bf16[2,136,2048]{2,1,0:T(8,128)(2,1)}, u32[]{:S(2)}, u32[]{:S(2)}) collective-permute-start(bf16[2,136,2048]{2,1,0:T(8,128)(2,1)} %pad_maximum_fusion), channel_id=1, source_target_pairs={{0,4},{4,8},{8,12},{1,5},{5,9},{9,13},{2,6},{6,10},{10,14},{3,7},{... | collective-permute-start | bytes 3342344 | tf_op jit(solution)/shard_map/ppermute | solution.py:18
  24.6 65.2 %copy-start.30 = (s32[128]{0:T(128)}, s32[128]{0:T(128)S(1)}, u32[]{:S(2)}) copy-start(s32[128]{0:T(128)S(1)} %get-tuple-element.287) | copy-start | bytes 1540
  47.5 9.9 %copy-start.14 = (bf16[7,2048]{1,0:T(8,128)(2,1)S(1)}, bf16[7,2048]{1,0:T(8,128)(2,1)}, u32[]{:S(2)}) copy-start(bf16[7,2048]{1,0:T(8,128)(2,1)} %param.16) | copy-start | bytes 86020
  97.4 11.4 %copy-start.9 = (bf16[256,2048]{1,0:T(8,128)(2,1)S(1)}, bf16[256,2048]{1,0:T(8,128)(2,1)}, u32[]{:S(2)}) copy-start(bf16[256,2048]{1,0:T(8,128)(2,1)} %param.14) | copy-start | bytes 3145732
  97.4 11.4 %copy-start.10 = (bf16[256,2048]{1,0:T(8,128)(2,1)S(1)}, bf16[256,2048]{1,0:T(8,128)(2,1)}, u32[]{:S(2)}) copy-start(bf16[256,2048]{1,0:T(8,128)(2,1)} %param.15) | copy-start | bytes 3145732
  135.0 8.3 %copy-start.5 = (bf16[128,16,128]{2,1,0:T(8,128)(2,1)S(1)}, bf16[128,16,128]{2,1,0:T(8,128)(2,1)}, u32[]{:S(2)}) copy-start(bf16[128,16,128]{2,1,0:T(8,128)(2,1)} %copy-done.4) | copy-start | bytes 1572868
  135.1 8.3 %copy-start.20 = (pred[128,128]{1,0:T(8,128)(4,1)S(1)}, pred[128,128]{1,0:T(8,128)(4,1)}, u32[]{:S(2)}) copy-start(pred[128,128]{1,0:T(8,128)(4,1)} %get-tuple-element.222) | copy-start | bytes 49156
  140.8 17.1 %collective-permute-start.1 = (f32[128,544]{0,1:T(8,128)S(1)}, f32[128,544]{0,1:T(8,128)S(1)}, u32[]{:S(2)}, u32[]{:S(2)}) collective-permute-start(f32[128,544]{0,1:T(8,128)S(1)} %pad_maximum_fusion.3), channel_id=1, source_target_pairs={{0,4},{4,8},{8,12},{1,5},{5,9},{9,13},{2,6},{6,10},{10,14},{3,7},{... | collective-permute-start | bytes 835592 | tf_op jit(solution)/shard_map/ppermute | solution.py:18
  158.0 8.9 %copy-start.12 = (f32[2,128,16,16]{1,3,2,0:T(8,128)S(1)}, f32[2,128,16,16]{1,3,2,0:T(8,128)}, u32[]{:S(2)}) copy-start(f32[2,128,16,16]{1,3,2,0:T(8,128)} %get-tuple-element.76) | copy-start | bytes 786436
  158.0 8.9 %copy-start.13 = (f32[2,128,16,16]{1,3,2,0:T(8,128)S(1)}, f32[2,128,16,16]{1,3,2,0:T(8,128)}, u32[]{:S(2)}) copy-start(f32[2,128,16,16]{1,3,2,0:T(8,128)} %get-tuple-element.83) | copy-start | bytes 786436
  158.0 8.8 %collective-permute-start.2 = (f32[128,544]{0,1:T(8,128)S(1)}, f32[128,544]{0,1:T(8,128)S(1)}, u32[]{:S(2)}, u32[]{:S(2)}) collective-permute-start(f32[128,544]{0,1:T(8,128)S(1)} %pad_maximum_fusion.4), channel_id=1, source_target_pairs={{0,8},{4,12},{1,9},{5,13},{2,10},{6,14},{3,11},{7,15},{16,24},{20,... | collective-permute-start | bytes 835592 | tf_op jit(solution)/shard_map/ppermute | solution.py:18
  179.6 1.2 collective-permute-start.3
  180.8 3.6 %collective-permute-start.4 = (f32[256]{0:T(256)S(1)}, f32[256]{0:T(256)S(1)}, u32[]{:S(2)}, u32[]{:S(2)}) collective-permute-start(f32[256]{0:T(256)S(1)} %add.297), channel_id=1, source_target_pairs={{0,2},{1,3},{2,0},{3,1},{4,6},{5,7},{6,4},{7,5},{8,10},{9,11},{10,... | collective-permute-start | bytes 3080 | tf_op jit(solution)/shard_map/ppermute | solution.py:43
  184.4 17.4 %copy-start.23 = (s32[256]{0:T(256)S(1)}, s32[256]{0:T(256)}, u32[]{:S(2)}) copy-start(s32[256]{0:T(256)} %copy-done.22) | copy-start | bytes 3076
  184.4 29.8 %copy-start.35 = (s32[8]{0:T(128)S(1)}, s32[8]{0:T(128)}, u32[]{:S(2)}) copy-start(s32[8]{0:T(128)} %param.23) | copy-start | bytes 100
  188.3 1.6 collective-permute-start.5
  191.0 5.6 %collective-permute-start.6 = (f32[64,512]{1,0:T(8,128)S(1)}, f32[64,512]{1,0:T(8,128)S(1)}, u32[]{:S(2)}, u32[]{:S(2)}) collective-permute-start(f32[64,512]{1,0:T(8,128)S(1)} %slice_select_fusion.5), channel_id=1, source_target_pairs={{0,2},{1,3},{2,0},{3,1},{4,6},{5,7},{6,4},{7,5},{8,10},{9,11},{10,... | collective-permute-start | bytes 393224 | tf_op jit(solution)/shard_map/ppermute | solution.py:31
  196.9 1.1 collective-permute-start.7
  198.2 3.6 %collective-permute-start.8 = (f32[256]{0:T(256)S(1)}, f32[256]{0:T(256)S(1)}, u32[]{:S(2)}, u32[]{:S(2)}) collective-permute-start(f32[256]{0:T(256)S(1)} %add_dynamic-update-slice_fusion), channel_id=1, source_target_pairs={{0,2},{1,3},{2,0},{3,1},{4,6},{5,7},{6,4},{7,5},{8,10},{9,11},{10,... | collective-permute-start | bytes 3080 | tf_op jit(solution)/shard_map/ppermute | solution.py:43
  201.8 13.0 %copy-start.33 = (f32[256]{0:T(256)}, f32[256]{0:T(256)S(1)}, u32[]{:S(2)}) copy-start(f32[256]{0:T(256)S(1)} %add.304) | copy-start | bytes 3076
  201.9 7.4 %collective-permute-start.9 = (f32[8]{0:T(128)S(1)}, f32[8]{0:T(128)S(1)}, u32[]{:S(2)}, u32[]{:S(2)}) collective-permute-start(f32[8]{0:T(128)S(1)} %select_reduce_fusion.1), channel_id=1, source_target_pairs={{0,4},{4,0},{8,12},{12,8},{1,5},{5,1},{9,13},{13,9},{2,6},{6,2},{1... | collective-permute-start | bytes 104 | tf_op jit(solution)/shard_map/ppermute | solution.py:43
  209.3 4.9 %collective-permute-start.10 = (f32[8]{0:T(128)S(1)}, f32[8]{0:T(128)S(1)}, u32[]{:S(2)}, u32[]{:S(2)}) collective-permute-start(f32[8]{0:T(128)S(1)} %add.305), channel_id=1, source_target_pairs={{0,8},{4,12},{8,0},{12,4},{1,9},{5,13},{9,1},{13,5},{2,10},{6,14},... | collective-permute-start | bytes 104 | tf_op jit(solution)/shard_map/ppermute | solution.py:43
  (25 other events, 87.2 us)

commit v15 on v13

--- a/solution.py
+++ b/solution.py
@@ -242,8 +242,11 @@
         upper = jnp.where(same_genome, toeplitz_upper, jnp.zeros_like(toeplitz_upper))
         lower = jnp.where(same_genome, toeplitz_lower, jnp.zeros_like(toeplitz_lower))
         return jnp.einsum(
-            "gts,gis->git", upper, block_in, preferred_element_type=jnp.float32
-        ) + jnp.einsum("gts,gis->git", lower, block_in, preferred_element_type=jnp.float32)
+            "gts,gis->git",
+            jnp.concatenate((upper, lower), axis=2),
+            jnp.concatenate((block_in, block_in), axis=2),
+            preferred_element_type=jnp.float32,
+        )
 
     local_part = jnp.stack([intra_block((signal[j], tile_segs[j])) for j in range(tile_count)])
     end_keep = (tile_segs == tile_segs[:, -1:])[:, None, None, :]

time: 184 us -> 180 us (0.978)
  other arithmetic: 37 us -> 34.7 us
  starting transfers between devices: 26.1 us -> 28.4 us
    dot_general x4 -> x2, matrix products: 11.2 us -> 9.43 us  [intra_block(): jnp.einsum('gts,gis->git', jnp.concatenate((upper, lower), axis=2), jnp.c...]
    unnamed x66 -> x72, local copies, waits for them, and re-layouts: 24.2 us -> 25.2 us
where the time goes in v15:
time: 180 us
  local copies, waits for them, and re-layouts  60 us (33%)
  matrix products  39.3 us (22%)
  other arithmetic  34.7 us (19%)
  starting transfers between devices  28.4 us (16%)
  waiting for transfers between devices  16.1 us (9%)
    unnamed x72, local copies, waits for them, and re-layouts  25.2 us
    ppermute x3, starting transfers between devices, from_behind(): return lax.ppermute(shard, axis, pairs)  13.8 us
    ppermute x6, starting transfers between devices, sum_over(): part = part + lax.ppermute(part, axis, [(i, i ^ bit) for i in range(count)])  13 us
    dot_general x2, matrix products, medium_block(): jnp.einsum('gts,gis->git', matrix, window, preferred_element_type=jnp.flo...  12 us
    ppermute x6, waiting for transfers between devices, sum_over(): part = part + lax.ppermute(part, axis, [(i, i ^ bit) for i in range(count)])  9.45 us
    dot_general x2, matrix products, intra_block(): jnp.einsum('gts,gis->git', jnp.concatenate((upper, lower), axis=2), jnp.c...  9.43 us
    select_n x1, other arithmetic, intra_block(): jnp.where(same_genome, toeplitz_lower, jnp.zeros_like(toeplitz_lower))  6.89 us
    ppermute x2, waiting for transfers between devices, scatter_sum(): part = keep + lax.ppermute(give, axes, [(i, i ^ bit) for i in range(count)])  5.49 us
  transfers between devices with their start and end apart: 11, of which 9 were waited for; matrix products, arithmetic and copies ran while one was open for 43% of the time, Pallas kernels for 0%

profile of v15, /device:TPU:0, one launch (start us, length us, event | category | flops | bytes accessed | tf_op | source)
XLA Modules:
  0.0 179.7 jit_solution(5174539027972594598)
XLA Ops:
  3.2 6.0 %collective-permute-start = (bf16[2,136,2048]{2,1,0:T(8,128)(2,1)}, bf16[2,136,2048]{2,1,0:T(8,128)(2,1)}, u32[]{:S(2)}, u32[]{:S(2)}) collective-permute-start(bf16[2,136,2048]{2,1,0:T(8,128)(2,1)} %pad_maximum_fusion), channel_id=1, source_target_pairs={{0,4},{4,8},{8,12},{1,5},{5,9},{9,13},{2,6},{6,10},{10,14},{3,7},{... | collective-permute-start | bytes 3342344 | tf_op jit(solution)/shard_map/ppermute | solution.py:18
  9.3 4.0 %fusion.57 = (f32[129,128,16]{1,2,0:T(8,128)S(1)}, f32[129,128,16]{1,2,0:T(8,128)S(1)}, f32[129,128,16]{1,2,0:T(8,128)S(1)}) fusion(f32[128,16]{0,1:T(8,128)S(1)} %get-tuple-element.64, f32[129]{0:T(256)S(1)} %iota_convert_fusion, f32[128,16]{0,1:T(8,128)S(1)} %get-tuple-element.61, f32[129]{0:T(256)S(1)} %fusion.95, f32[128,16]{0,1:T(8,128)S(1)} %get-tuple-element.63, ...), kind=kLoop, calls=%fused_computation.73 | loop fusion | flops 1849344 | bytes 3204104 | tf_op jit(solution)/shard_map/mul | solution.py:120
  20.1 2.9 %fusion.59 = bf16[128,128,32,1]{0,2,1,3:T(8,128)(2,1)} fusion(f32[128,128,16]{1,2,0:T(8,128)} %rev.7, f32[128,128,16]{1,2,0:T(8,128)} %rev.6), kind=kLoop, calls=%fused_computation.77 | loop fusion | flops 2621440 | bytes 3145728 | tf_op jit(solution)/shard_map/convert_element_type | solution.py:136
  24.4 4.0 %convolution_convert_fusion = bf16[384,16384]{1,0:T(8,128)(2,1)S(1)} fusion(s32[16384]{0:T(1024)S(1)} %add_select_fusion, s32[128]{0:T(128)S(1)} %iota.77, bf16[128,128]{0,1:T(8,128)(2,1)S(1)} %get-tuple-element.9, bf16[128,128]{0,1:T(8,128)(2,1)S(1)} %get-tuple-element.10, bf16[128,128]{0,1:T(8,128)(2,1)S(1)} %copy.218), kind=kOutput, calls=%fused_computation | convolution fusion | flops 1619296256 | bytes 12747264 | tf_op jit(solution)/shard_map/dot_general | solution.py:109
  28.4 4.0 %slice_bitcast_fusion.2 = (bf16[16,8,128,128]{3,1,2,0:T(8,128)(2,1)S(1)}, bf16[16,8,128,128]{3,1,2,0:T(8,128)(2,1)}, bf16[16,8,128,128]{3,1,2,0:T(8,128)(2,1)}) fusion(bf16[384,16384]{1,0:T(8,128)(2,1)S(1)} %convolution_convert_fusion), kind=kLoop, calls=%fused_computation.22 | loop fusion | bytes 25165824
  38.7 3.2 %copy.230 = bf16[128,128,32,1]{1,2,3,0:T(8,128)(2,1)} copy(bf16[128,128,32,1]{0,2,1,3:T(8,128)(2,1)} %fusion.59) | data formatting | bytes 2097152 | tf_op jit(solution)/shard_map/convert_element_type | solution.py:136
  42.4 3.2 %copy.229 = bf16[128,128,32,1]{1,2,3,0:T(8,128)(2,1)} copy(bf16[128,128,32,1]{0,2,1,3:T(8,128)(2,1)} %fusion.56) | data formatting | bytes 2097152 | tf_op jit(solution)/shard_map/convert_element_type | solution.py:135
  49.5 5.5 %copy.240 = bf16[16,8,128,128]{3,2,1,0:T(8,128)(2,1)} copy(bf16[16,8,128,128]{3,1,2,0:T(8,128)(2,1)} %get-tuple-element.13) | data formatting | bytes 8388608
  55.0 3.2 %copy.241 = bf16[16,8,128,128]{3,2,1,0:T(8,128)(2,1)} copy(bf16[16,8,128,128]{3,1,2,0:T(8,128)(2,1)S(1)} %copy-done.2) | data formatting | bytes 8388608
  60.1 3.4 %copy.226 = f32[128,128,32]{1,2,0:T(8,128)} copy(f32[128,128,32]{0,2,1:T(8,128)} %maximum_bitcast_fusion.1) | data formatting | bytes 4194304 | tf_op jit(solution)/shard_map/transpose | solution.py:126
  67.5 5.1 %constant_dynamic-update-slice_fusion = bf16[128,128,256]{2,1,0:T(8,128)(2,1)} fusion(bf16[128,128,256]{2,1,0:T(8,128)(2,1)} %constant_dynamic-update-slice_fusion.1, bf16[128,128,128]{2,1,0:T(8,128)(2,1)} %bitcast.166), kind=kLoop, calls=%fused_computation.186 | loop fusion | bytes 8388608 | tf_op jit(solution)/shard_map/concatenate | solution.py:211
  73.8 6.9 %bitcast_select_fusion.1 = (bf16[128,128,128]{2,1,0:T(8,128)(2,1)}, bf16[128,128,128]{2,1,0:T(8,128)(2,1)}, bf16[128,128,128]{2,1,0:T(8,128)(2,1)}, bf16[128,128,128]{2,1,0:T(8,128)(2,1)}) fusion(bf16[16,8,128,128]{3,2,1,0:T(8,128)(2,1)S(1)} %copy-done.4, pred[128,128]{1,0:T(8,128)(4,1)S(1)} %get-tuple-element.7, pred[128,128]{1,0:T(8,128)(4,1)S(1)} %compare_and_fusion.3, ...), kind=kLoop, calls=%fused_computation.17 | loop fusion | flops 8388608 | bytes 25198592 | tf_op jit(solution)/shard_map/jit(_where)/select_n | solution.py:243
  82.5 5.2 %fusion.43 = bf16[2048,384]{0,1:T(8,128)(2,1)} fusion(f32[384]{0:T(512)S(1)} %get-tuple-element.75, f32[392,2048]{1,0:T(8,128)S(1)} %convert_multiply_fusion, f32[2048]{0:T(1024)S(1)} %bitcast.192, f32[384]{0:T(512)S(1)} %get-tuple-element.71, f32[2048]{0:T(1024)S(1)} %bitcast.193, f32[384]{0:T(512)S(1)} %get-tuple-element.72, f32[2048]{0:T(1024)S(1)} %bitcast.188, ...), kind=kLoop, calls=%fused_computation.64 | loop fusion | flops 15728640 | bytes 23659520 | tf_op jit(solution)/shard_map/transpose | solution.py:204
  90.4 6.1 %fusion.50 = bf16[128,16,128]{2,1,0:T(8,128)(2,1)S(1)} fusion(bf16[128,128,256]{2,1,0:T(8,128)(2,1)} %constant_dynamic-update-slice_fusion, pred[128,256]{1,0:T(8,128)(4,1)S(1)} %get-tuple-element.84, bf16[128,16,384]{2,1,0:T(8,128)(2,1)} %bitcast.169), kind=kOutput, calls=%fused_computation.69 | convolution fusion | flops 138674176 | bytes 9994240 | tf_op jit(solution)/shard_map/gts,gis->git/dot_general | solution.py:228
  96.5 5.9 %fusion.53 = bf16[128,16,128]{2,1,0:T(8,128)(2,1)S(1)} fusion(bf16[128,128,256]{2,1,0:T(8,128)(2,1)} %constant_dynamic-update-slice_fusion, pred[128,256]{1,0:T(8,128)(4,1)S(1)} %get-tuple-element.85, bf16[128,16,384]{2,1,0:T(8,128)(2,1)S(1)} %bitcast.170), kind=kOutput, calls=%fused_computation.70 | convolution fusion | flops 138674176 | bytes 9994240 | tf_op jit(solution)/shard_map/gts,gis->git/dot_general | solution.py:228
  107.9 3.4 %fusion.76 = f32[128,2,16,32]{3,2,1,0:T(8,128)} fusion(bf16[128,128,32,1]{1,2,3,0:T(8,128)(2,1)} %copy.229, pred[2,128]{1,0:T(4,128)(4,1)S(1)} %get-tuple-element.77, bf16[1,128,16,128]{3,2,1,0:T(8,128)(2,1)} %bitcast.181, bf16[1,128,16,128]{3,2,1,0:T(8,128)(2,1)S(1)} %bitcast.178), kind=kOutput, calls=%fused_computation.98 | convolution fusion | flops 34603008 | bytes 2621696 | tf_op jit(solution)/shard_map/gsm,jgis->jgim/dot_general | solution.py:254
  117.0 5.9 %fusion.47 = f32[1,128,16,128]{3,2,1,0:T(8,128)} fusion(bf16[128,128,128]{2,1,0:T(8,128)(2,1)S(1)} %copy-done.14, bf16[128,128,128]{2,1,0:T(8,128)(2,1)} %get-tuple-element.53, bf16[128,16,128]{2,1,0:T(8,128)(2,1)} %copy-done.20), kind=kOutput, calls=%fused_computation.68 | convolution fusion | flops 153092096 | bytes 9961472 | tf_op jit(solution)/shard_map/gts,gis->git/dot_general | solution.py:244
  123.0 5.1 %collective-permute-start.2 = (f32[128,544]{0,1:T(8,128)S(1)}, f32[128,544]{0,1:T(8,128)S(1)}, u32[]{:S(2)}, u32[]{:S(2)}) collective-permute-start(f32[128,544]{0,1:T(8,128)S(1)} %pad_maximum_fusion.4), channel_id=1, source_target_pairs={{0,8},{4,12},{1,9},{5,13},{2,10},{6,14},{3,11},{7,15},{16,24},{20,... | collective-permute-start | bytes 835592 | tf_op jit(solution)/shard_map/ppermute | solution.py:18
  128.1 3.5 %fusion.44 = f32[1,128,16,128]{3,2,1,0:T(8,128)} fusion(bf16[128,128,128]{2,1,0:T(8,128)(2,1)S(1)} %copy-done.12, bf16[128,128,128]{2,1,0:T(8,128)(2,1)S(1)} %copy-done.13, bf16[128,16,128]{2,1,0:T(8,128)(2,1)S(1)} %copy-done.23), kind=kOutput, calls=%fused_computation.67 | convolution fusion | flops 153092096 | bytes 9961472 | tf_op jit(solution)/shard_map/gts,gis->git/dot_general | solution.py:244
  135.1 5.4 %fusion.37 = f32[128,16,2,128]{3,1,0,2:T(8,128)S(1)} fusion(f32[1,128,16,128]{3,2,1,0:T(8,128)} %fusion.44, f32[1,128,16,128]{3,2,1,0:T(8,128)} %fusion.47, f32[2,128,16,32]{3,2,1,0:T(8,128)} %copy.231, f32[128,128,32]{1,2,0:T(8,128)} %copy.226, f32[128,16]{1,0:T(8,128)S(1)} %mul.724, f32[2,128]{1,0:T(2,128)S(1)} %get-tuple-element.76, ...), kind=kOutput, calls=%fused_computation.57 | convolution fusion | flops 204996608 | bytes 7873536 | tf_op jit(solution)/shard_map/gtm,jgim->jgit/dot_general | solution.py:299
  148.7 3.0 %fusion.60 = f32[256,512]{1,0:T(8,128)S(1)} fusion(bf16[2048,512]{1,0:T(8,128)(2,1)S(1)} %copy-done, f32[2048]{0:T(1024)S(1)} %copy-done.30, f32[256]{0:T(256)S(1)} %add_rsqrt_fusion, f32[256,8,2,128]{3,2,1,0:T(2,128)} %bitcast.168, bf16[256,2048]{0,1:T(8,128)(2,1)S(1)} %copy-done.9), kind=kOutput, calls=%fused_computation.78 | convolution fusion | flops 540540928 | bytes 5776384 | tf_op jit(solution)/shard_map/dot_general | solution.py:162
  156.9 4.0 %collective-permute-done.6 = f32[64,512]{1,0:T(8,128)S(1)} collective-permute-done((f32[64,512]{1,0:T(8,128)S(1)}, f32[64,512]{1,0:T(8,128)S(1)}, u32[]{:S(2)}, u32[]{:S(2)}) %collective-permute-start.6) | collective-permute-done | bytes 131104 | tf_op jit(solution)/shard_map/ppermute | solution.py:31
  166.2 6.6 %collective-permute-start.9 = (f32[8]{0:T(128)S(1)}, f32[8]{0:T(128)S(1)}, u32[]{:S(2)}, u32[]{:S(2)}) collective-permute-start(f32[8]{0:T(128)S(1)} %select_reduce_fusion.1), channel_id=1, source_target_pairs={{0,4},{4,0},{8,12},{12,8},{1,5},{5,1},{9,13},{13,9},{2,6},{6,2},{1... | collective-permute-start | bytes 104 | tf_op jit(solution)/shard_map/ppermute | solution.py:43
  174.3 3.4 %collective-permute-start.10 = (f32[8]{0:T(128)S(1)}, f32[8]{0:T(128)S(1)}, u32[]{:S(2)}, u32[]{:S(2)}) collective-permute-start(f32[8]{0:T(128)S(1)} %add.341), channel_id=1, source_target_pairs={{0,8},{4,12},{8,0},{12,4},{1,9},{5,13},{9,1},{13,5},{2,10},{6,14},... | collective-permute-start | bytes 104 | tf_op jit(solution)/shard_map/ppermute | solution.py:43
  (166 shorter events, 69.6 us)
Async XLA Ops:
  0.6 148.1 %copy-start = (bf16[2048,512]{1,0:T(8,128)(2,1)S(1)}, bf16[2048,512]{1,0:T(8,128)(2,1)}, u32[]{:S(2)}) copy-start(bf16[2048,512]{1,0:T(8,128)(2,1)} %param.19) | copy-start | bytes 6291460
  0.6 8.6 %copy-start.25 = (f32[4,128,16]{1,2,0:T(8,128)S(1)}, f32[4,128,16]{1,2,0:T(8,128)}, u32[]{:S(2)}) copy-start(f32[4,128,16]{1,2,0:T(8,128)} %param.16) | copy-start | bytes 98308
  3.2 77.4 %collective-permute-start = (bf16[2,136,2048]{2,1,0:T(8,128)(2,1)}, bf16[2,136,2048]{2,1,0:T(8,128)(2,1)}, u32[]{:S(2)}, u32[]{:S(2)}) collective-permute-start(bf16[2,136,2048]{2,1,0:T(8,128)(2,1)} %pad_maximum_fusion), channel_id=1, source_target_pairs={{0,4},{4,8},{8,12},{1,5},{5,9},{9,13},{2,6},{6,10},{10,14},{3,7},{... | collective-permute-start | bytes 3342344 | tf_op jit(solution)/shard_map/ppermute | solution.py:18
  67.5 6.2 %copy-start.4 = (bf16[16,8,128,128]{3,2,1,0:T(8,128)(2,1)S(1)}, bf16[16,8,128,128]{3,2,1,0:T(8,128)(2,1)}, u32[]{:S(2)}) copy-start(bf16[16,8,128,128]{3,2,1,0:T(8,128)(2,1)} %copy.241) | copy-start | bytes 12582916
  73.8 8.2 %copy-start.15 = (bf16[256,2048]{1,0:T(8,128)(2,1)S(1)}, bf16[256,2048]{1,0:T(8,128)(2,1)}, u32[]{:S(2)}) copy-start(bf16[256,2048]{1,0:T(8,128)(2,1)} %param.12) | copy-start | bytes 3145732
  73.8 8.2 %copy-start.16 = (bf16[256,2048]{1,0:T(8,128)(2,1)S(1)}, bf16[256,2048]{1,0:T(8,128)(2,1)}, u32[]{:S(2)}) copy-start(bf16[256,2048]{1,0:T(8,128)(2,1)} %param.13) | copy-start | bytes 3145732
  96.5 11.4 %copy-start.20 = (bf16[128,16,128]{2,1,0:T(8,128)(2,1)}, bf16[128,16,128]{2,1,0:T(8,128)(2,1)S(1)}, u32[]{:S(2)}) copy-start(bf16[128,16,128]{2,1,0:T(8,128)(2,1)S(1)} %fusion.50) | copy-start | bytes 1572868
  96.5 6.7 %copy-start.19 = (bf16[128,128,32,1]{1,2,3,0:T(8,128)(2,1)S(1)}, bf16[128,128,32,1]{1,2,3,0:T(8,128)(2,1)}, u32[]{:S(2)}) copy-start(bf16[128,128,32,1]{1,2,3,0:T(8,128)(2,1)} %copy.230) | copy-start | bytes 3145732
  114.2 8.7 %collective-permute-start.1 = (f32[128,544]{0,1:T(8,128)S(1)}, f32[128,544]{0,1:T(8,128)S(1)}, u32[]{:S(2)}, u32[]{:S(2)}) collective-permute-start(f32[128,544]{0,1:T(8,128)S(1)} %pad_maximum_fusion.3), channel_id=1, source_target_pairs={{0,4},{4,8},{8,12},{1,5},{5,9},{9,13},{2,6},{6,10},{10,14},{3,7},{... | collective-permute-start | bytes 835592 | tf_op jit(solution)/shard_map/ppermute | solution.py:18
  116.9 11.1 %copy-start.12 = (bf16[128,128,128]{2,1,0:T(8,128)(2,1)S(1)}, bf16[128,128,128]{2,1,0:T(8,128)(2,1)}, u32[]{:S(2)}) copy-start(bf16[128,128,128]{2,1,0:T(8,128)(2,1)} %get-tuple-element.17) | copy-start | bytes 12582916
  117.0 11.1 %copy-start.13 = (bf16[128,128,128]{2,1,0:T(8,128)(2,1)S(1)}, bf16[128,128,128]{2,1,0:T(8,128)(2,1)}, u32[]{:S(2)}) copy-start(bf16[128,128,128]{2,1,0:T(8,128)(2,1)} %get-tuple-element.52) | copy-start | bytes 12582916
  117.0 11.1 %copy-start.23 = (bf16[128,16,128]{2,1,0:T(8,128)(2,1)S(1)}, bf16[128,16,128]{2,1,0:T(8,128)(2,1)}, u32[]{:S(2)}) copy-start(bf16[128,16,128]{2,1,0:T(8,128)(2,1)} %copy-done.22) | copy-start | bytes 1572868
  123.0 9.8 %collective-permute-start.2 = (f32[128,544]{0,1:T(8,128)S(1)}, f32[128,544]{0,1:T(8,128)S(1)}, u32[]{:S(2)}, u32[]{:S(2)}) collective-permute-start(f32[128,544]{0,1:T(8,128)S(1)} %pad_maximum_fusion.4), channel_id=1, source_target_pairs={{0,8},{4,12},{1,9},{5,13},{2,10},{6,14},{3,11},{7,15},{16,24},{20,... | collective-permute-start | bytes 835592 | tf_op jit(solution)/shard_map/ppermute | solution.py:18
  140.6 8.1 %copy-start.30 = (f32[2048]{0:T(1024)S(1)}, f32[2048]{0:T(1024)}, u32[]{:S(2)}) copy-start(f32[2048]{0:T(1024)} %param.18) | copy-start | bytes 24580
  143.9 1.2 collective-permute-start.3
  145.1 3.6 %collective-permute-start.4 = (f32[256]{0:T(256)S(1)}, f32[256]{0:T(256)S(1)}, u32[]{:S(2)}, u32[]{:S(2)}) collective-permute-start(f32[256]{0:T(256)S(1)} %add.333), channel_id=1, source_target_pairs={{0,2},{1,3},{2,0},{3,1},{4,6},{5,7},{6,4},{7,5},{8,10},{9,11},{10,... | collective-permute-start | bytes 3080 | tf_op jit(solution)/shard_map/ppermute | solution.py:43
  148.7 8.1 %copy-start.31 = (s32[256]{0:T(256)S(1)}, s32[256]{0:T(256)}, u32[]{:S(2)}) copy-start(s32[256]{0:T(256)} %param.20) | copy-start | bytes 3076
  152.6 1.6 collective-permute-start.5
  155.3 5.6 %collective-permute-start.6 = (f32[64,512]{1,0:T(8,128)S(1)}, f32[64,512]{1,0:T(8,128)S(1)}, u32[]{:S(2)}, u32[]{:S(2)}) collective-permute-start(f32[64,512]{1,0:T(8,128)S(1)} %slice_select_fusion.5), channel_id=1, source_target_pairs={{0,2},{1,3},{2,0},{3,1},{4,6},{5,7},{6,4},{7,5},{8,10},{9,11},{10,... | collective-permute-start | bytes 393224 | tf_op jit(solution)/shard_map/ppermute | solution.py:31
  161.2 1.1 collective-permute-start.7
  162.5 3.6 %collective-permute-start.8 = (f32[256]{0:T(256)S(1)}, f32[256]{0:T(256)S(1)}, u32[]{:S(2)}, u32[]{:S(2)}) collective-permute-start(f32[256]{0:T(256)S(1)} %add_dynamic-update-slice_fusion), channel_id=1, source_target_pairs={{0,2},{1,3},{2,0},{3,1},{4,6},{5,7},{6,4},{7,5},{8,10},{9,11},{10,... | collective-permute-start | bytes 3080 | tf_op jit(solution)/shard_map/ppermute | solution.py:43
  166.1 13.7 %copy-start.28 = (f32[256]{0:T(256)}, f32[256]{0:T(256)S(1)}, u32[]{:S(2)}) copy-start(f32[256]{0:T(256)S(1)} %add.340) | copy-start | bytes 3076
  166.2 8.1 %collective-permute-start.9 = (f32[8]{0:T(128)S(1)}, f32[8]{0:T(128)S(1)}, u32[]{:S(2)}, u32[]{:S(2)}) collective-permute-start(f32[8]{0:T(128)S(1)} %select_reduce_fusion.1), channel_id=1, source_target_pairs={{0,4},{4,0},{8,12},{12,8},{1,5},{5,1},{9,13},{13,9},{2,6},{6,2},{1... | collective-permute-start | bytes 104 | tf_op jit(solution)/shard_map/ppermute | solution.py:43
  174.3 4.9 %collective-permute-start.10 = (f32[8]{0:T(128)S(1)}, f32[8]{0:T(128)S(1)}, u32[]{:S(2)}, u32[]{:S(2)}) collective-permute-start(f32[8]{0:T(128)S(1)} %add.341), channel_id=1, source_target_pairs={{0,8},{4,12},{8,0},{12,4},{1,9},{5,13},{9,1},{13,5},{2,10},{6,14},... | collective-permute-start | bytes 104 | tf_op jit(solution)/shard_map/ppermute | solution.py:43
  (19 other events, 58.6 us)

commit v16 on v15

--- a/solution.py
+++ b/solution.py
@@ -252,9 +252,10 @@
     end_keep = (tile_segs == tile_segs[:, -1:])[:, None, None, :]
     masked_signal = jnp.where(end_keep, signal, jnp.zeros_like(signal))
     states = jnp.einsum(
-        "gsm,jgis->jgim", inward_upper, masked_signal, preferred_element_type=jnp.float32
-    ) + jnp.einsum(
-        "gsm,jgis->jgim", inward_lower, masked_signal, preferred_element_type=jnp.float32
+        "gsm,jgis->jgim",
+        jnp.concatenate((inward_upper, inward_lower), axis=1),
+        jnp.concatenate((masked_signal, masked_signal), axis=3),
+        preferred_element_type=jnp.float32,
     )
     carried = (tile_segs[:, -1] == before).astype(jnp.float32)
 

time: 180 us -> 180 us (level)
  other arithmetic: 34.7 us -> 38.8 us
  matrix products: 39.3 us -> 36.5 us
    convert_element_type x2 -> x0, local copies, waits for them, and re-layouts: 6.44 us -> none  [the longest x1 3.24 us: split_table(): lower = (table - upper.astype(jnp.float32)).astype(jnp.bfloat16)]
    concatenate x0 -> x1, local copies, waits for them, and re-layouts: none -> 4.92 us  [per_device(): jnp.concatenate((inward_upper, inward_lower), axis=1)]
    dot_general x2 -> x1, matrix products: 5.45 us -> 2.03 us  [per_device(): jnp.einsum('gsm,jgis->jgim', jnp.concatenate((inward_upper, inward_lower)...]
    concatenate x0 -> x1, other arithmetic: none -> 3.1 us  [per_device(): jnp.concatenate((inward_upper, inward_lower), axis=1)]
    dot_general x2 -> x1, local copies, waits for them, and re-layouts: 5.31 us -> 3.46 us  [per_device(): jnp.einsum('gsm,jgis->jgim', jnp.concatenate((inward_upper, inward_lower)...]
    unnamed x72 -> x62, local copies, waits for them, and re-layouts: 25.2 us -> 26.1 us
  transfers between devices with their start and end apart: 11 -> 11, of which waited for: 9 -> 9; matrix products, arithmetic and copies ran while one was open for 43% -> 45% of each run, Pallas kernels for 0% -> 0%
where the time goes in v16:
time: 180 us
  local copies, waits for them, and re-layouts  59.8 us (33%)
  other arithmetic  38.8 us (22%)
  matrix products  36.5 us (20%)
  starting transfers between devices  27.2 us (15%)
  waiting for transfers between devices  16.2 us (9%)
    unnamed x62, local copies, waits for them, and re-layouts  26.1 us
    ppermute x6, starting transfers between devices, sum_over(): part = part + lax.ppermute(part, axis, [(i, i ^ bit) for i in range(count)])  13 us
    ppermute x3, starting transfers between devices, from_behind(): return lax.ppermute(shard, axis, pairs)  12.6 us
    dot_general x2, matrix products, medium_block(): jnp.einsum('gts,gis->git', matrix, window, preferred_element_type=jnp.flo...  11.8 us
    dot_general x2, matrix products, intra_block(): jnp.einsum('gts,gis->git', jnp.concatenate((upper, lower), axis=2), jnp.c...  10.4 us
    ppermute x6, waiting for transfers between devices, sum_over(): part = part + lax.ppermute(part, axis, [(i, i ^ bit) for i in range(count)])  9.45 us
    select_n x1, other arithmetic, intra_block(): jnp.where(same_genome, toeplitz_lower, jnp.zeros_like(toeplitz_lower))  6.93 us
    ppermute x2, waiting for transfers between devices, scatter_sum(): part = keep + lax.ppermute(give, axes, [(i, i ^ bit) for i in range(count)])  5.49 us
  transfers between devices with their start and end apart: 11, of which 9 were waited for; matrix products, arithmetic and copies ran while one was open for 45% of the time, Pallas kernels for 0%

profile of v16, /device:TPU:0, one launch (start us, length us, event | category | flops | bytes accessed | tf_op | source)
XLA Modules:
  0.0 179.6 jit_solution(15969883616724416036)
XLA Ops:
  3.3 5.9 %collective-permute-start = (bf16[2,136,2048]{2,1,0:T(8,128)(2,1)}, bf16[2,136,2048]{2,1,0:T(8,128)(2,1)}, u32[]{:S(2)}, u32[]{:S(2)}) collective-permute-start(bf16[2,136,2048]{2,1,0:T(8,128)(2,1)} %pad_maximum_fusion.1), channel_id=1, source_target_pairs={{0,4},{4,8},{8,12},{1,5},{5,9},{9,13},{2,6},{6,10},{10,14},{3,7},{... | collective-permute-start | bytes 3342344 | tf_op jit(solution)/shard_map/ppermute | solution.py:18
  9.3 4.0 %fusion.58 = (f32[129,128,16]{1,2,0:T(8,128)S(1)}, f32[129,128,16]{1,2,0:T(8,128)S(1)}, f32[129,128,16]{1,2,0:T(8,128)S(1)}) fusion(f32[128,16]{0,1:T(8,128)S(1)} %get-tuple-element.64, f32[129]{0:T(256)S(1)} %iota_convert_fusion, f32[128,16]{0,1:T(8,128)S(1)} %get-tuple-element.61, f32[129]{0:T(256)S(1)} %fusion.91, f32[128,16]{0,1:T(8,128)S(1)} %get-tuple-element.63, ...), kind=kLoop, calls=%fused_computation.76 | loop fusion | flops 1849344 | bytes 3204104 | tf_op jit(solution)/shard_map/mul | solution.py:120
  24.4 4.0 %convolution_convert_fusion = bf16[384,16384]{1,0:T(8,128)(2,1)S(1)} fusion(s32[16384]{0:T(1024)S(1)} %add_select_fusion, s32[128]{0:T(128)S(1)} %iota.77, bf16[128,128]{0,1:T(8,128)(2,1)S(1)} %get-tuple-element.9, bf16[128,128]{0,1:T(8,128)(2,1)S(1)} %get-tuple-element.10, bf16[128,128]{0,1:T(8,128)(2,1)S(1)} %copy.212), kind=kOutput, calls=%fused_computation | convolution fusion | flops 1619296256 | bytes 12747264 | tf_op jit(solution)/shard_map/dot_general | solution.py:109
  28.4 4.0 %slice_bitcast_fusion.2 = (bf16[16,8,128,128]{3,1,2,0:T(8,128)(2,1)S(1)}, bf16[16,8,128,128]{3,1,2,0:T(8,128)(2,1)}, bf16[16,8,128,128]{3,1,2,0:T(8,128)(2,1)}) fusion(bf16[384,16384]{1,0:T(8,128)(2,1)S(1)} %convolution_convert_fusion), kind=kLoop, calls=%fused_computation.22 | loop fusion | bytes 25165824
  39.2 3.1 %maximum_bitcast_fusion.1 = bf16[128,256,32,1]{0,2,1,3:T(8,128)(2,1)} fusion(bf16[128,128,32]{0,2,1:T(8,128)(2,1)} %subtract_convert_fusion, bf16[128,128,32]{0,2,1:T(8,128)(2,1)} %fusion.42), kind=kLoop, calls=%fused_computation.60 | loop fusion | flops 1048576 | bytes 4194304 | tf_op jit(solution)/shard_map/concatenate | solution.py:256
  42.3 4.9 %copy.220 = bf16[128,256,32,1]{1,2,3,0:T(8,128)(2,1)} copy(bf16[128,256,32,1]{0,2,1,3:T(8,128)(2,1)} %maximum_bitcast_fusion.1) | data formatting | bytes 4194304 | tf_op jit(solution)/shard_map/concatenate | solution.py:256
  51.1 5.5 %copy.228 = bf16[16,8,128,128]{3,2,1,0:T(8,128)(2,1)} copy(bf16[16,8,128,128]{3,1,2,0:T(8,128)(2,1)} %get-tuple-element.13) | data formatting | bytes 8388608
  56.6 3.2 %copy.229 = bf16[16,8,128,128]{3,2,1,0:T(8,128)(2,1)} copy(bf16[16,8,128,128]{3,1,2,0:T(8,128)(2,1)S(1)} %copy-done.2) | data formatting | bytes 8388608
  61.6 3.4 %copy.217 = f32[128,128,32]{1,2,0:T(8,128)} copy(f32[128,128,32]{0,2,1:T(8,128)} %maximum_bitcast_fusion.2) | data formatting | bytes 4194304 | tf_op jit(solution)/shard_map/transpose | solution.py:126
  69.2 5.1 %constant_dynamic-update-slice_fusion = bf16[128,128,256]{2,1,0:T(8,128)(2,1)} fusion(bf16[128,128,256]{2,1,0:T(8,128)(2,1)} %constant_dynamic-update-slice_fusion.1, bf16[128,128,128]{2,1,0:T(8,128)(2,1)} %bitcast.158), kind=kLoop, calls=%fused_computation.183 | loop fusion | bytes 8388608 | tf_op jit(solution)/shard_map/concatenate | solution.py:211
  75.4 6.9 %bitcast_select_fusion.1 = (bf16[128,128,128]{2,1,0:T(8,128)(2,1)}, bf16[128,128,128]{2,1,0:T(8,128)(2,1)}, bf16[128,128,128]{2,1,0:T(8,128)(2,1)}, bf16[128,128,128]{2,1,0:T(8,128)(2,1)}) fusion(bf16[16,8,128,128]{3,2,1,0:T(8,128)(2,1)S(1)} %copy-done.4, pred[128,128]{1,0:T(8,128)(4,1)S(1)} %get-tuple-element.7, pred[128,128]{1,0:T(8,128)(4,1)S(1)} %compare_and_fusion.3, ...), kind=kLoop, calls=%fused_computation.17 | loop fusion | flops 8388608 | bytes 25198592 | tf_op jit(solution)/shard_map/jit(_where)/select_n | solution.py:243
  84.8 5.2 %fusion.45 = bf16[2048,384]{0,1:T(8,128)(2,1)} fusion(f32[384]{0:T(512)S(1)} %get-tuple-element.75, f32[392,2048]{1,0:T(8,128)S(1)} %convert_multiply_fusion, f32[2048]{0:T(1024)S(1)} %bitcast.183, f32[384]{0:T(512)S(1)} %get-tuple-element.71, f32[2048]{0:T(1024)S(1)} %bitcast.184, f32[384]{0:T(512)S(1)} %get-tuple-element.72, f32[2048]{0:T(1024)S(1)} %bitcast.179, ...), kind=kLoop, calls=%fused_computation.68 | loop fusion | flops 15728640 | bytes 23659520 | tf_op jit(solution)/shard_map/transpose | solution.py:204
  92.6 6.1 %fusion.52 = bf16[128,16,128]{2,1,0:T(8,128)(2,1)S(1)} fusion(bf16[128,128,256]{2,1,0:T(8,128)(2,1)} %constant_dynamic-update-slice_fusion, pred[128,256]{1,0:T(8,128)(4,1)S(1)} %get-tuple-element.84, bf16[128,16,384]{2,1,0:T(8,128)(2,1)} %bitcast.166), kind=kOutput, calls=%fused_computation.73 | convolution fusion | flops 138674176 | bytes 9994240 | tf_op jit(solution)/shard_map/gts,gis->git/dot_general | solution.py:228
  98.7 5.7 %fusion.55 = bf16[128,16,128]{2,1,0:T(8,128)(2,1)S(1)} fusion(bf16[128,128,256]{2,1,0:T(8,128)(2,1)} %constant_dynamic-update-slice_fusion, pred[128,256]{1,0:T(8,128)(4,1)S(1)} %get-tuple-element.85, bf16[128,16,384]{2,1,0:T(8,128)(2,1)S(1)} %bitcast.167), kind=kOutput, calls=%fused_computation.74 | convolution fusion | flops 138674176 | bytes 9994240 | tf_op jit(solution)/shard_map/gts,gis->git/dot_general | solution.py:228
  108.0 3.5 %copy.215 = f32[128,2,16,32]{0,3,2,1:T(8,128)} copy(f32[128,2,16,32]{3,2,1,0:T(8,128)} %fusion.40) | data formatting | bytes 1048576 | tf_op jit(solution)/shard_map/gsm,jgis->jgim/dot_general | solution.py:254
  115.2 6.9 %fusion.49 = f32[1,128,16,128]{3,2,1,0:T(8,128)} fusion(bf16[128,128,128]{2,1,0:T(8,128)(2,1)} %get-tuple-element.16, bf16[128,128,128]{2,1,0:T(8,128)(2,1)} %get-tuple-element.53, bf16[128,16,128]{2,1,0:T(8,128)(2,1)S(1)} %fusion.52), kind=kOutput, calls=%fused_computation.72 | convolution fusion | flops 153092096 | bytes 9961472 | tf_op jit(solution)/shard_map/gts,gis->git/dot_general | solution.py:244
  122.2 4.1 %collective-permute-start.2 = (f32[128,544]{0,1:T(8,128)S(1)}, f32[128,544]{0,1:T(8,128)S(1)}, u32[]{:S(2)}, u32[]{:S(2)}) collective-permute-start(f32[128,544]{0,1:T(8,128)S(1)} %pad_maximum_fusion.5), channel_id=1, source_target_pairs={{0,8},{4,12},{1,9},{5,13},{2,10},{6,14},{3,11},{7,15},{16,24},{20,... | collective-permute-start | bytes 835592 | tf_op jit(solution)/shard_map/ppermute | solution.py:18
  126.3 3.5 %fusion.46 = f32[1,128,16,128]{3,2,1,0:T(8,128)} fusion(bf16[128,128,128]{2,1,0:T(8,128)(2,1)S(1)} %copy-done.12, bf16[128,128,128]{2,1,0:T(8,128)(2,1)S(1)} %copy-done.13, bf16[128,16,128]{2,1,0:T(8,128)(2,1)S(1)} %fusion.55), kind=kOutput, calls=%fused_computation.71 | convolution fusion | flops 153092096 | bytes 9961472 | tf_op jit(solution)/shard_map/gts,gis->git/dot_general | solution.py:244
  132.1 3.1 %copy.221 = f32[2,128,16,32]{3,2,1,0:T(8,128)} copy(f32[2,128,16,32]{1,3,2,0:T(8,128)} %pad_maximum_fusion.3) | data formatting | bytes 1048576 | tf_op jit(solution)/shard_map/concatenate | solution.py:303
  135.2 5.3 %fusion.37 = f32[128,16,2,128]{3,1,0,2:T(8,128)S(1)} fusion(f32[1,128,16,128]{3,2,1,0:T(8,128)} %fusion.46, f32[1,128,16,128]{3,2,1,0:T(8,128)} %fusion.49, f32[2,128,16,32]{3,2,1,0:T(8,128)} %copy.221, f32[128,128,32]{1,2,0:T(8,128)} %copy.217, f32[128,16]{1,0:T(8,128)S(1)} %mul.724, f32[2,128]{1,0:T(2,128)S(1)} %get-tuple-element.76, ...), kind=kOutput, calls=%fused_computation.57 | convolution fusion | flops 204996608 | bytes 7873536 | tf_op jit(solution)/shard_map/gtm,jgim->jgit/dot_general | solution.py:300
  148.6 3.0 %fusion.60 = f32[256,512]{1,0:T(8,128)S(1)} fusion(bf16[2048,512]{1,0:T(8,128)(2,1)S(1)} %copy-done, f32[2048]{0:T(1024)S(1)} %copy-done.25, f32[256]{0:T(256)S(1)} %add_rsqrt_fusion, f32[256,8,2,128]{3,2,1,0:T(2,128)} %bitcast.160, bf16[256,2048]{0,1:T(8,128)(2,1)S(1)} %copy-done.9), kind=kOutput, calls=%fused_computation.80 | convolution fusion | flops 540540928 | bytes 5776384 | tf_op jit(solution)/shard_map/dot_general | solution.py:162
  156.8 4.0 %collective-permute-done.6 = f32[64,512]{1,0:T(8,128)S(1)} collective-permute-done((f32[64,512]{1,0:T(8,128)S(1)}, f32[64,512]{1,0:T(8,128)S(1)}, u32[]{:S(2)}, u32[]{:S(2)}) %collective-permute-start.6) | collective-permute-done | bytes 131104 | tf_op jit(solution)/shard_map/ppermute | solution.py:31
  166.1 6.6 %collective-permute-start.9 = (f32[8]{0:T(128)S(1)}, f32[8]{0:T(128)S(1)}, u32[]{:S(2)}, u32[]{:S(2)}) collective-permute-start(f32[8]{0:T(128)S(1)} %select_reduce_fusion.1), channel_id=1, source_target_pairs={{0,4},{4,0},{8,12},{12,8},{1,5},{5,1},{9,13},{13,9},{2,6},{6,2},{1... | collective-permute-start | bytes 104 | tf_op jit(solution)/shard_map/ppermute | solution.py:43
  174.2 3.4 %collective-permute-start.10 = (f32[8]{0:T(128)S(1)}, f32[8]{0:T(128)S(1)}, u32[]{:S(2)}, u32[]{:S(2)}) collective-permute-start(f32[8]{0:T(128)S(1)} %add.333), channel_id=1, source_target_pairs={{0,8},{4,12},{8,0},{12,4},{1,9},{5,13},{9,1},{13,5},{2,10},{6,14},... | collective-permute-start | bytes 104 | tf_op jit(solution)/shard_map/ppermute | solution.py:43
  (154 shorter events, 68.0 us)
Async XLA Ops:
  0.6 148.0 %copy-start = (bf16[2048,512]{1,0:T(8,128)(2,1)S(1)}, bf16[2048,512]{1,0:T(8,128)(2,1)}, u32[]{:S(2)}) copy-start(bf16[2048,512]{1,0:T(8,128)(2,1)} %param.19) | copy-start | bytes 6291460
  0.6 8.6 %copy-start.20 = (f32[4,128,16]{1,2,0:T(8,128)S(1)}, f32[4,128,16]{1,2,0:T(8,128)}, u32[]{:S(2)}) copy-start(f32[4,128,16]{1,2,0:T(8,128)} %param.16) | copy-start | bytes 98308
  3.3 79.1 %collective-permute-start = (bf16[2,136,2048]{2,1,0:T(8,128)(2,1)}, bf16[2,136,2048]{2,1,0:T(8,128)(2,1)}, u32[]{:S(2)}, u32[]{:S(2)}) collective-permute-start(bf16[2,136,2048]{2,1,0:T(8,128)(2,1)} %pad_maximum_fusion.1), channel_id=1, source_target_pairs={{0,4},{4,8},{8,12},{1,5},{5,9},{9,13},{2,6},{6,10},{10,14},{3,7},{... | collective-permute-start | bytes 3342344 | tf_op jit(solution)/shard_map/ppermute | solution.py:18
  51.1 5.5 %copy-start.2 = (bf16[16,8,128,128]{3,1,2,0:T(8,128)(2,1)S(1)}, bf16[16,8,128,128]{3,1,2,0:T(8,128)(2,1)}, u32[]{:S(2)}) copy-start(bf16[16,8,128,128]{3,1,2,0:T(8,128)(2,1)} %get-tuple-element.12) | copy-start | bytes 12582916
  56.6 3.3 %copy-start.11 = (f32[128,128,16]{1,2,0:T(8,128)S(1)}, f32[128,128,16]{1,2,0:T(8,128)}, u32[]{:S(2)}) copy-start(f32[128,128,16]{1,2,0:T(8,128)} %get-tuple-element.87) | copy-start | bytes 3145732
  61.6 3.4 %copy-start.22 = (f32[2048]{0:T(1024)S(1)}, f32[2048]{0:T(1024)}, u32[]{:S(2)}) copy-start(f32[2048]{0:T(1024)} %param.17) | copy-start | bytes 24580
  69.1 5.1 %copy-start.3 = (bf16[16,8,128,128]{3,2,1,0:T(8,128)(2,1)S(1)}, bf16[16,8,128,128]{3,2,1,0:T(8,128)(2,1)}, u32[]{:S(2)}) copy-start(bf16[16,8,128,128]{3,2,1,0:T(8,128)(2,1)} %copy.228) | copy-start | bytes 12582916
  69.1 6.2 %copy-start.4 = (bf16[16,8,128,128]{3,2,1,0:T(8,128)(2,1)S(1)}, bf16[16,8,128,128]{3,2,1,0:T(8,128)(2,1)}, u32[]{:S(2)}) copy-start(bf16[16,8,128,128]{3,2,1,0:T(8,128)(2,1)} %copy.229) | copy-start | bytes 12582916
  92.6 6.1 %copy-start.18 = (bf16[2048,384]{1,0:T(8,128)(2,1)S(1)}, bf16[2048,384]{1,0:T(8,128)(2,1)}, u32[]{:S(2)}) copy-start(bf16[2048,384]{1,0:T(8,128)(2,1)} %copy.210) | copy-start | bytes 4718596
  112.6 9.4 %collective-permute-start.1 = (f32[128,544]{0,1:T(8,128)S(1)}, f32[128,544]{0,1:T(8,128)S(1)}, u32[]{:S(2)}, u32[]{:S(2)}) collective-permute-start(f32[128,544]{0,1:T(8,128)S(1)} %pad_maximum_fusion.4), channel_id=1, source_target_pairs={{0,4},{4,8},{8,12},{1,5},{5,9},{9,13},{2,6},{6,10},{10,14},{3,7},{... | collective-permute-start | bytes 835592 | tf_op jit(solution)/shard_map/ppermute | solution.py:18
  115.1 11.1 %copy-start.12 = (bf16[128,128,128]{2,1,0:T(8,128)(2,1)S(1)}, bf16[128,128,128]{2,1,0:T(8,128)(2,1)}, u32[]{:S(2)}) copy-start(bf16[128,128,128]{2,1,0:T(8,128)(2,1)} %get-tuple-element.17) | copy-start | bytes 12582916
  115.2 11.1 %copy-start.13 = (bf16[128,128,128]{2,1,0:T(8,128)(2,1)S(1)}, bf16[128,128,128]{2,1,0:T(8,128)(2,1)}, u32[]{:S(2)}) copy-start(bf16[128,128,128]{2,1,0:T(8,128)(2,1)} %get-tuple-element.52) | copy-start | bytes 12582916
  122.2 8.9 %collective-permute-start.2 = (f32[128,544]{0,1:T(8,128)S(1)}, f32[128,544]{0,1:T(8,128)S(1)}, u32[]{:S(2)}, u32[]{:S(2)}) collective-permute-start(f32[128,544]{0,1:T(8,128)S(1)} %pad_maximum_fusion.5), channel_id=1, source_target_pairs={{0,8},{4,12},{1,9},{5,13},{2,10},{6,14},{3,11},{7,15},{16,24},{20,... | collective-permute-start | bytes 835592 | tf_op jit(solution)/shard_map/ppermute | solution.py:18
  142.2 6.5 %copy-start.25 = (f32[2048]{0:T(1024)S(1)}, f32[2048]{0:T(1024)}, u32[]{:S(2)}) copy-start(f32[2048]{0:T(1024)} %param.18) | copy-start | bytes 24580
  143.8 1.2 collective-permute-start.3
  145.0 3.6 %collective-permute-start.4 = (f32[256]{0:T(256)S(1)}, f32[256]{0:T(256)S(1)}, u32[]{:S(2)}, u32[]{:S(2)}) collective-permute-start(f32[256]{0:T(256)S(1)} %add.325), channel_id=1, source_target_pairs={{0,2},{1,3},{2,0},{3,1},{4,6},{5,7},{6,4},{7,5},{8,10},{9,11},{10,... | collective-permute-start | bytes 3080 | tf_op jit(solution)/shard_map/ppermute | solution.py:43
  152.4 4.3 %copy-start.26 = (s32[256]{0:T(256)S(1)}, s32[256]{0:T(256)}, u32[]{:S(2)}) copy-start(s32[256]{0:T(256)} %param.20) | copy-start | bytes 3076
  152.5 1.6 collective-permute-start.5
  155.2 5.6 %collective-permute-start.6 = (f32[64,512]{1,0:T(8,128)S(1)}, f32[64,512]{1,0:T(8,128)S(1)}, u32[]{:S(2)}, u32[]{:S(2)}) collective-permute-start(f32[64,512]{1,0:T(8,128)S(1)} %slice_select_fusion.5), channel_id=1, source_target_pairs={{0,2},{1,3},{2,0},{3,1},{4,6},{5,7},{6,4},{7,5},{8,10},{9,11},{10,... | collective-permute-start | bytes 393224 | tf_op jit(solution)/shard_map/ppermute | solution.py:31
  161.1 1.1 collective-permute-start.7
  162.4 3.6 %collective-permute-start.8 = (f32[256]{0:T(256)S(1)}, f32[256]{0:T(256)S(1)}, u32[]{:S(2)}, u32[]{:S(2)}) collective-permute-start(f32[256]{0:T(256)S(1)} %add_dynamic-update-slice_fusion), channel_id=1, source_target_pairs={{0,2},{1,3},{2,0},{3,1},{4,6},{5,7},{6,4},{7,5},{8,10},{9,11},{10,... | collective-permute-start | bytes 3080 | tf_op jit(solution)/shard_map/ppermute | solution.py:43
  166.0 13.7 %copy-start.23 = (f32[256]{0:T(256)}, f32[256]{0:T(256)S(1)}, u32[]{:S(2)}) copy-start(f32[256]{0:T(256)S(1)} %add.332) | copy-start | bytes 3076
  166.1 8.1 %collective-permute-start.9 = (f32[8]{0:T(128)S(1)}, f32[8]{0:T(128)S(1)}, u32[]{:S(2)}, u32[]{:S(2)}) collective-permute-start(f32[8]{0:T(128)S(1)} %select_reduce_fusion.1), channel_id=1, source_target_pairs={{0,4},{4,0},{8,12},{12,8},{1,5},{5,1},{9,13},{13,9},{2,6},{6,2},{1... | collective-permute-start | bytes 104 | tf_op jit(solution)/shard_map/ppermute | solution.py:43
  174.2 4.9 %collective-permute-start.10 = (f32[8]{0:T(128)S(1)}, f32[8]{0:T(128)S(1)}, u32[]{:S(2)}, u32[]{:S(2)}) collective-permute-start(f32[8]{0:T(128)S(1)} %add.333), channel_id=1, source_target_pairs={{0,8},{4,12},{8,0},{12,4},{1,9},{5,13},{9,1},{13,5},{2,10},{6,14},... | collective-permute-start | bytes 104 | tf_op jit(solution)/shard_map/ppermute | solution.py:43
  (14 other events, 30.0 us)

commit v17 on v16

--- a/solution.py
+++ b/solution.py
@@ -313,15 +313,15 @@
     long_cols = jnp.transpose(longconv, (1, 2, 0, 3)).reshape(chan_count, row_count)
     mixed = (query_proj.T.astype(jnp.float32) * long_cols).astype(jnp.bfloat16)
     mixed_wide = mixed.astype(jnp.float32)
-    squares = sum_over(jnp.sum(mixed_wide * mixed_wide, axis=0), ("chan", "rep"))
-    normed = (mixed_wide * lax.rsqrt(squares / D + norm_eps)[None, :] * norm_gain[:, None]).astype(
-        jnp.bfloat16
-    )
-    partial_value = channel_logits(normed, unembed)
+    squares = jnp.sum(mixed_wide * mixed_wide, axis=0)
+    gained = (mixed_wide * norm_gain[:, None]).astype(jnp.bfloat16)
+    partial_value = jnp.concatenate((channel_logits(gained, unembed), squares[:, None]), axis=1)
     lanes = ("chan", "rep")
     lane_count = lax.axis_size(lanes)
     piece = row_count // lane_count
-    logits, piece_index = scatter_sum(partial_value, lanes)
+    summed, piece_index = scatter_sum(partial_value, lanes)
+    vocab = unembed.shape[1]
+    logits = summed[:, :vocab] * lax.rsqrt(summed[:, vocab] / D + norm_eps)[:, None]
     piece_at = piece_index * piece
     logprob_piece = log_probs(logits, lax.dynamic_slice_in_dim(token_ids, piece_at, piece, 0))
     logprob = sum_over(

time: 180 us -> 177 us (0.983)
  waiting for transfers between devices: 16.2 us -> 13.7 us
    ppermute x6 -> x4, waiting for transfers between devices: 9.45 us -> 6.24 us  [sum_over(): part = part + lax.ppermute(part, axis, [(i, i ^ bit) for i in range(count)])]
    ppermute x6 -> x4, starting transfers between devices: 13 us -> 11.5 us  [sum_over(): part = part + lax.ppermute(part, axis, [(i, i ^ bit) for i in range(count)])]
  transfers between devices with their start and end apart: 11 -> 9, of which waited for: 9 -> 7; matrix products, arithmetic and copies ran while one was open for 45% -> 45% of each run, Pallas kernels for 0% -> 0%
where the time goes in v17:
time: 177 us; the launch traced here: 176 us
  local copies, waits for them, and re-layouts  59.9 us (34%)
  other arithmetic  39.1 us (22%)
  matrix products  36.5 us (21%)
  starting transfers between devices  25.7 us (15%)
  waiting for transfers between devices  13.7 us (8%)
    unnamed x62, local copies, waits for them, and re-layouts  26.1 us
    ppermute x3, starting transfers between devices, from_behind(): return lax.ppermute(shard, axis, pairs)  12.6 us
    dot_general x2, matrix products, medium_block(): jnp.einsum('gts,gis->git', matrix, window, preferred_element_type=jnp.flo...  11.8 us
    ppermute x4, starting transfers between devices, sum_over(): part = part + lax.ppermute(part, axis, [(i, i ^ bit) for i in range(count)])  11.5 us
    dot_general x2, matrix products, intra_block(): jnp.einsum('gts,gis->git', jnp.concatenate((upper, lower), axis=2), jnp.c...  10.4 us
    select_n x1, other arithmetic, intra_block(): jnp.where(same_genome, toeplitz_lower, jnp.zeros_like(toeplitz_lower))  6.97 us
    ppermute x2, waiting for transfers between devices, scatter_sum(): part = keep + lax.ppermute(give, axes, [(i, i ^ bit) for i in range(count)])  6.28 us
    ppermute x4, waiting for transfers between devices, sum_over(): part = part + lax.ppermute(part, axis, [(i, i ^ bit) for i in range(count)])  6.24 us
  transfers between devices with their start and end apart: 9, of which 7 were waited for; matrix products, arithmetic and copies ran while one was open for 45% of the time, Pallas kernels for 0%

profile of v17, /device:TPU:0, one launch (start us, length us, event | category | flops | bytes accessed | tf_op | source)
XLA Modules:
  0.0 176.0 jit_solution(4428395736063886951)
XLA Ops:
  3.3 5.9 %collective-permute-start = (bf16[2,136,2048]{2,1,0:T(8,128)(2,1)}, bf16[2,136,2048]{2,1,0:T(8,128)(2,1)}, u32[]{:S(2)}, u32[]{:S(2)}) collective-permute-start(bf16[2,136,2048]{2,1,0:T(8,128)(2,1)} %pad_maximum_fusion.1), channel_id=1, source_target_pairs={{0,4},{4,8},{8,12},{1,5},{5,9},{9,13},{2,6},{6,10},{10,14},{3,7},{... | collective-permute-start | bytes 3342344 | tf_op jit(solution)/shard_map/ppermute | solution.py:18
  9.3 4.0 %fusion.57 = (f32[129,128,16]{1,2,0:T(8,128)S(1)}, f32[129,128,16]{1,2,0:T(8,128)S(1)}, f32[129,128,16]{1,2,0:T(8,128)S(1)}) fusion(f32[128,16]{0,1:T(8,128)S(1)} %get-tuple-element.64, f32[129]{0:T(256)S(1)} %iota_convert_fusion, f32[128,16]{0,1:T(8,128)S(1)} %get-tuple-element.61, f32[129]{0:T(256)S(1)} %fusion.93, f32[128,16]{0,1:T(8,128)S(1)} %get-tuple-element.63, ...), kind=kLoop, calls=%fused_computation.75 | loop fusion | flops 1849344 | bytes 3204104 | tf_op jit(solution)/shard_map/mul | solution.py:120
  24.4 4.0 %convolution_convert_fusion = bf16[384,16384]{1,0:T(8,128)(2,1)S(1)} fusion(s32[16384]{0:T(1024)S(1)} %add_select_fusion, s32[128]{0:T(128)S(1)} %iota.77, bf16[128,128]{0,1:T(8,128)(2,1)S(1)} %get-tuple-element.9, bf16[128,128]{0,1:T(8,128)(2,1)S(1)} %get-tuple-element.10, bf16[128,128]{0,1:T(8,128)(2,1)S(1)} %copy.217), kind=kOutput, calls=%fused_computation | convolution fusion | flops 1619296256 | bytes 12747264 | tf_op jit(solution)/shard_map/dot_general | solution.py:109
  28.4 4.0 %slice_bitcast_fusion.2 = (bf16[16,8,128,128]{3,1,2,0:T(8,128)(2,1)S(1)}, bf16[16,8,128,128]{3,1,2,0:T(8,128)(2,1)}, bf16[16,8,128,128]{3,1,2,0:T(8,128)(2,1)}) fusion(bf16[384,16384]{1,0:T(8,128)(2,1)S(1)} %convolution_convert_fusion), kind=kLoop, calls=%fused_computation.22 | loop fusion | bytes 25165824
  39.1 3.1 %maximum_bitcast_fusion.1 = bf16[128,256,32,1]{0,2,1,3:T(8,128)(2,1)} fusion(bf16[128,128,32]{0,2,1:T(8,128)(2,1)} %subtract_convert_fusion, bf16[128,128,32]{0,2,1:T(8,128)(2,1)} %fusion.41), kind=kLoop, calls=%fused_computation.59 | loop fusion | flops 1048576 | bytes 4194304 | tf_op jit(solution)/shard_map/concatenate | solution.py:256
  42.2 4.9 %copy.226 = bf16[128,256,32,1]{1,2,3,0:T(8,128)(2,1)} copy(bf16[128,256,32,1]{0,2,1,3:T(8,128)(2,1)} %maximum_bitcast_fusion.1) | data formatting | bytes 4194304 | tf_op jit(solution)/shard_map/concatenate | solution.py:256
  51.1 5.5 %copy.234 = bf16[16,8,128,128]{3,2,1,0:T(8,128)(2,1)} copy(bf16[16,8,128,128]{3,1,2,0:T(8,128)(2,1)} %get-tuple-element.13) | data formatting | bytes 8388608
  56.6 3.2 %copy.235 = bf16[16,8,128,128]{3,2,1,0:T(8,128)(2,1)} copy(bf16[16,8,128,128]{3,1,2,0:T(8,128)(2,1)S(1)} %copy-done.3) | data formatting | bytes 8388608
  61.6 3.4 %copy.222 = f32[128,128,32]{1,2,0:T(8,128)} copy(f32[128,128,32]{0,2,1:T(8,128)} %maximum_bitcast_fusion.2) | data formatting | bytes 4194304 | tf_op jit(solution)/shard_map/transpose | solution.py:126
  69.1 5.1 %constant_dynamic-update-slice_fusion = bf16[128,128,256]{2,1,0:T(8,128)(2,1)} fusion(bf16[128,128,256]{2,1,0:T(8,128)(2,1)} %constant_dynamic-update-slice_fusion.1, bf16[128,128,128]{2,1,0:T(8,128)(2,1)} %bitcast.159), kind=kLoop, calls=%fused_computation.190 | loop fusion | bytes 8388608 | tf_op jit(solution)/shard_map/concatenate | solution.py:211
  75.3 7.0 %bitcast_select_fusion.1 = (bf16[128,128,128]{2,1,0:T(8,128)(2,1)}, bf16[128,128,128]{2,1,0:T(8,128)(2,1)}, bf16[128,128,128]{2,1,0:T(8,128)(2,1)}, bf16[128,128,128]{2,1,0:T(8,128)(2,1)}) fusion(bf16[16,8,128,128]{3,2,1,0:T(8,128)(2,1)S(1)} %copy-done.5, pred[128,128]{1,0:T(8,128)(4,1)S(1)} %get-tuple-element.7, pred[128,128]{1,0:T(8,128)(4,1)S(1)} %compare_and_fusion.3, ...), kind=kLoop, calls=%fused_computation.17 | loop fusion | flops 8388608 | bytes 25198592 | tf_op jit(solution)/shard_map/jit(_where)/select_n | solution.py:243
  84.7 5.2 %fusion.44 = bf16[2048,384]{0,1:T(8,128)(2,1)} fusion(f32[384]{0:T(512)S(1)} %get-tuple-element.75, f32[392,2048]{1,0:T(8,128)S(1)} %convert_multiply_fusion, f32[2048]{0:T(1024)S(1)} %bitcast.184, f32[384]{0:T(512)S(1)} %get-tuple-element.71, f32[2048]{0:T(1024)S(1)} %bitcast.185, f32[384]{0:T(512)S(1)} %get-tuple-element.72, f32[2048]{0:T(1024)S(1)} %bitcast.180, ...), kind=kLoop, calls=%fused_computation.67 | loop fusion | flops 15728640 | bytes 23659520 | tf_op jit(solution)/shard_map/transpose | solution.py:204
  92.6 6.1 %fusion.51 = bf16[128,16,128]{2,1,0:T(8,128)(2,1)S(1)} fusion(bf16[128,128,256]{2,1,0:T(8,128)(2,1)} %constant_dynamic-update-slice_fusion, pred[128,256]{1,0:T(8,128)(4,1)S(1)} %get-tuple-element.84, bf16[128,16,384]{2,1,0:T(8,128)(2,1)} %bitcast.167), kind=kOutput, calls=%fused_computation.72 | convolution fusion | flops 138674176 | bytes 9994240 | tf_op jit(solution)/shard_map/gts,gis->git/dot_general | solution.py:228
  98.6 5.7 %fusion.54 = bf16[128,16,128]{2,1,0:T(8,128)(2,1)S(1)} fusion(bf16[128,128,256]{2,1,0:T(8,128)(2,1)} %constant_dynamic-update-slice_fusion, pred[128,256]{1,0:T(8,128)(4,1)S(1)} %get-tuple-element.85, bf16[128,16,384]{2,1,0:T(8,128)(2,1)S(1)} %bitcast.168), kind=kOutput, calls=%fused_computation.73 | convolution fusion | flops 138674176 | bytes 9994240 | tf_op jit(solution)/shard_map/gts,gis->git/dot_general | solution.py:228
  108.0 3.5 %copy.220 = f32[128,2,16,32]{0,3,2,1:T(8,128)} copy(f32[128,2,16,32]{3,2,1,0:T(8,128)} %fusion.39) | data formatting | bytes 1048576 | tf_op jit(solution)/shard_map/gsm,jgis->jgim/dot_general | solution.py:254
  115.1 6.9 %fusion.48 = f32[1,128,16,128]{3,2,1,0:T(8,128)} fusion(bf16[128,128,128]{2,1,0:T(8,128)(2,1)} %get-tuple-element.16, bf16[128,128,128]{2,1,0:T(8,128)(2,1)} %get-tuple-element.53, bf16[128,16,128]{2,1,0:T(8,128)(2,1)S(1)} %fusion.51), kind=kOutput, calls=%fused_computation.71 | convolution fusion | flops 153092096 | bytes 9961472 | tf_op jit(solution)/shard_map/gts,gis->git/dot_general | solution.py:244
  122.1 4.1 %collective-permute-start.2 = (f32[128,544]{0,1:T(8,128)S(1)}, f32[128,544]{0,1:T(8,128)S(1)}, u32[]{:S(2)}, u32[]{:S(2)}) collective-permute-start(f32[128,544]{0,1:T(8,128)S(1)} %pad_maximum_fusion.6), channel_id=1, source_target_pairs={{0,8},{4,12},{1,9},{5,13},{2,10},{6,14},{3,11},{7,15},{16,24},{20,... | collective-permute-start | bytes 835592 | tf_op jit(solution)/shard_map/ppermute | solution.py:18
  126.3 3.5 %fusion.45 = f32[1,128,16,128]{3,2,1,0:T(8,128)} fusion(bf16[128,128,128]{2,1,0:T(8,128)(2,1)S(1)} %copy-done.13, bf16[128,128,128]{2,1,0:T(8,128)(2,1)S(1)} %copy-done.14, bf16[128,16,128]{2,1,0:T(8,128)(2,1)S(1)} %fusion.54), kind=kOutput, calls=%fused_computation.70 | convolution fusion | flops 153092096 | bytes 9961472 | tf_op jit(solution)/shard_map/gts,gis->git/dot_general | solution.py:244
  132.1 3.1 %copy.227 = f32[2,128,16,32]{3,2,1,0:T(8,128)} copy(f32[2,128,16,32]{1,3,2,0:T(8,128)} %pad_maximum_fusion.3) | data formatting | bytes 1048576 | tf_op jit(solution)/shard_map/concatenate | solution.py:303
  135.2 5.3 %fusion.36 = f32[128,16,2,128]{3,1,0,2:T(8,128)S(1)} fusion(f32[1,128,16,128]{3,2,1,0:T(8,128)} %fusion.45, f32[1,128,16,128]{3,2,1,0:T(8,128)} %fusion.48, f32[2,128,16,32]{3,2,1,0:T(8,128)} %copy.227, f32[128,128,32]{1,2,0:T(8,128)} %copy.222, f32[128,16]{1,0:T(8,128)S(1)} %mul.726, f32[2,128]{1,0:T(2,128)S(1)} %get-tuple-element.76, ...), kind=kOutput, calls=%fused_computation.56 | convolution fusion | flops 204996608 | bytes 7873536 | tf_op jit(solution)/shard_map/gtm,jgim->jgit/dot_general | solution.py:300
  144.0 3.0 %fusion.59 = f32[256,512]{1,0:T(8,128)S(1)} fusion(bf16[2048,512]{1,0:T(8,128)(2,1)S(1)} %copy-done, f32[2048]{0:T(1024)S(1)} %copy-done.22, f32[256,8,2,128]{3,2,1,0:T(2,128)} %bitcast.161, bf16[256,2048]{0,1:T(8,128)(2,1)S(1)} %copy-done.9), kind=kOutput, calls=%fused_computation.79 | convolution fusion | flops 540016640 | bytes 5775360 | tf_op jit(solution)/shard_map/dot_general | solution.py:162
  152.3 4.7 %collective-permute-done.4 = f32[64,513]{1,0:T(8,128)S(1)} collective-permute-done((f32[64,513]{1,0:T(8,128)S(1)}, f32[64,513]{1,0:T(8,128)S(1)}, u32[]{:S(2)}, u32[]{:S(2)}) %collective-permute-start.4) | collective-permute-done | bytes 131360 | tf_op jit(solution)/shard_map/ppermute | solution.py:31
  162.4 6.6 %collective-permute-start.7 = (f32[8]{0:T(128)S(1)}, f32[8]{0:T(128)S(1)}, u32[]{:S(2)}, u32[]{:S(2)}) collective-permute-start(f32[8]{0:T(128)S(1)} %select_reduce_fusion.1), channel_id=1, source_target_pairs={{0,4},{4,0},{8,12},{12,8},{1,5},{5,1},{9,13},{13,9},{2,6},{6,2},{1... | collective-permute-start | bytes 104 | tf_op jit(solution)/shard_map/ppermute | solution.py:43
  170.6 3.4 %collective-permute-start.8 = (f32[8]{0:T(128)S(1)}, f32[8]{0:T(128)S(1)}, u32[]{:S(2)}, u32[]{:S(2)}) collective-permute-start(f32[8]{0:T(128)S(1)} %add.326), channel_id=1, source_target_pairs={{0,8},{4,12},{8,0},{12,4},{1,9},{5,13},{9,1},{13,5},{2,10},{6,14},... | collective-permute-start | bytes 104 | tf_op jit(solution)/shard_map/ppermute | solution.py:43
  (151 shorter events, 63.7 us)
Async XLA Ops:
  0.6 143.3 %copy-start = (bf16[2048,512]{1,0:T(8,128)(2,1)S(1)}, bf16[2048,512]{1,0:T(8,128)(2,1)}, u32[]{:S(2)}) copy-start(bf16[2048,512]{1,0:T(8,128)(2,1)} %param.19) | copy-start | bytes 6291460
  0.6 8.6 %copy-start.20 = (f32[4,128,16]{1,2,0:T(8,128)S(1)}, f32[4,128,16]{1,2,0:T(8,128)}, u32[]{:S(2)}) copy-start(f32[4,128,16]{1,2,0:T(8,128)} %param.16) | copy-start | bytes 98308
  3.3 79.0 %collective-permute-start = (bf16[2,136,2048]{2,1,0:T(8,128)(2,1)}, bf16[2,136,2048]{2,1,0:T(8,128)(2,1)}, u32[]{:S(2)}, u32[]{:S(2)}) collective-permute-start(bf16[2,136,2048]{2,1,0:T(8,128)(2,1)} %pad_maximum_fusion.1), channel_id=1, source_target_pairs={{0,4},{4,8},{8,12},{1,5},{5,9},{9,13},{2,6},{6,10},{10,14},{3,7},{... | collective-permute-start | bytes 3342344 | tf_op jit(solution)/shard_map/ppermute | solution.py:18
  20.1 2.9 %copy-start.8 = (f32[128,128,16]{1,2,0:T(8,128)S(1)}, f32[128,128,16]{1,2,0:T(8,128)}, u32[]{:S(2)}) copy-start(f32[128,128,16]{1,2,0:T(8,128)} %rev.7) | copy-start | bytes 3145732
  51.1 5.5 %copy-start.3 = (bf16[16,8,128,128]{3,1,2,0:T(8,128)(2,1)S(1)}, bf16[16,8,128,128]{3,1,2,0:T(8,128)(2,1)}, u32[]{:S(2)}) copy-start(bf16[16,8,128,128]{3,1,2,0:T(8,128)(2,1)} %get-tuple-element.12) | copy-start | bytes 12582916
  56.6 3.3 %copy-start.11 = (f32[128,128,16]{1,2,0:T(8,128)S(1)}, f32[128,128,16]{1,2,0:T(8,128)}, u32[]{:S(2)}) copy-start(f32[128,128,16]{1,2,0:T(8,128)} %get-tuple-element.27) | copy-start | bytes 3145732
  56.6 3.3 %copy-start.12 = (f32[128,128,16]{1,2,0:T(8,128)S(1)}, f32[128,128,16]{1,2,0:T(8,128)}, u32[]{:S(2)}) copy-start(f32[128,128,16]{1,2,0:T(8,128)} %get-tuple-element.87) | copy-start | bytes 3145732
  61.6 3.4 %copy-start.23 = (f32[2048]{0:T(1024)S(1)}, f32[2048]{0:T(1024)}, u32[]{:S(2)}) copy-start(f32[2048]{0:T(1024)} %param.17) | copy-start | bytes 24580
  69.1 5.1 %copy-start.4 = (bf16[16,8,128,128]{3,2,1,0:T(8,128)(2,1)S(1)}, bf16[16,8,128,128]{3,2,1,0:T(8,128)(2,1)}, u32[]{:S(2)}) copy-start(bf16[16,8,128,128]{3,2,1,0:T(8,128)(2,1)} %copy.234) | copy-start | bytes 12582916
  69.1 6.2 %copy-start.5 = (bf16[16,8,128,128]{3,2,1,0:T(8,128)(2,1)S(1)}, bf16[16,8,128,128]{3,2,1,0:T(8,128)(2,1)}, u32[]{:S(2)}) copy-start(bf16[16,8,128,128]{3,2,1,0:T(8,128)(2,1)} %copy.235) | copy-start | bytes 12582916
  92.6 6.1 %copy-start.18 = (bf16[2048,384]{1,0:T(8,128)(2,1)S(1)}, bf16[2048,384]{1,0:T(8,128)(2,1)}, u32[]{:S(2)}) copy-start(bf16[2048,384]{1,0:T(8,128)(2,1)} %copy.215) | copy-start | bytes 4718596
  112.6 9.4 %collective-permute-start.1 = (f32[128,544]{0,1:T(8,128)S(1)}, f32[128,544]{0,1:T(8,128)S(1)}, u32[]{:S(2)}, u32[]{:S(2)}) collective-permute-start(f32[128,544]{0,1:T(8,128)S(1)} %pad_maximum_fusion.5), channel_id=1, source_target_pairs={{0,4},{4,8},{8,12},{1,5},{5,9},{9,13},{2,6},{6,10},{10,14},{3,7},{... | collective-permute-start | bytes 835592 | tf_op jit(solution)/shard_map/ppermute | solution.py:18
  115.1 11.2 %copy-start.13 = (bf16[128,128,128]{2,1,0:T(8,128)(2,1)S(1)}, bf16[128,128,128]{2,1,0:T(8,128)(2,1)}, u32[]{:S(2)}) copy-start(bf16[128,128,128]{2,1,0:T(8,128)(2,1)} %get-tuple-element.17) | copy-start | bytes 12582916
  115.1 11.2 %copy-start.14 = (bf16[128,128,128]{2,1,0:T(8,128)(2,1)S(1)}, bf16[128,128,128]{2,1,0:T(8,128)(2,1)}, u32[]{:S(2)}) copy-start(bf16[128,128,128]{2,1,0:T(8,128)(2,1)} %get-tuple-element.52) | copy-start | bytes 12582916
  122.1 8.9 %collective-permute-start.2 = (f32[128,544]{0,1:T(8,128)S(1)}, f32[128,544]{0,1:T(8,128)S(1)}, u32[]{:S(2)}, u32[]{:S(2)}) collective-permute-start(f32[128,544]{0,1:T(8,128)S(1)} %pad_maximum_fusion.6), channel_id=1, source_target_pairs={{0,8},{4,12},{1,9},{5,13},{2,10},{6,14},{3,11},{7,15},{16,24},{20,... | collective-permute-start | bytes 835592 | tf_op jit(solution)/shard_map/ppermute | solution.py:18
  140.5 3.0 %copy-start.9 = (bf16[256,2048]{0,1:T(8,128)(2,1)S(1)}, bf16[256,2048]{0,1:T(8,128)(2,1)}, u32[]{:S(2)}) copy-start(bf16[256,2048]{0,1:T(8,128)(2,1)} %copy.214) | copy-start | bytes 3145732
  147.8 4.4 %copy-start.26 = (s32[256]{0:T(256)S(1)}, s32[256]{0:T(256)}, u32[]{:S(2)}) copy-start(s32[256]{0:T(256)} %param.20) | copy-start | bytes 3076
  147.9 1.7 collective-permute-start.3
  150.7 6.3 %collective-permute-start.4 = (f32[64,513]{1,0:T(8,128)S(1)}, f32[64,513]{1,0:T(8,128)S(1)}, u32[]{:S(2)}, u32[]{:S(2)}) collective-permute-start(f32[64,513]{1,0:T(8,128)S(1)} %slice_select_fusion), channel_id=1, source_target_pairs={{0,2},{1,3},{2,0},{3,1},{4,6},{5,7},{6,4},{7,5},{8,10},{9,11},{10,... | collective-permute-start | bytes 393992 | tf_op jit(solution)/shard_map/ppermute | solution.py:31
  157.5 1.1 collective-permute-start.5
  158.8 3.6 %collective-permute-start.6 = (f32[256]{0:T(256)S(1)}, f32[256]{0:T(256)S(1)}, u32[]{:S(2)}, u32[]{:S(2)}) collective-permute-start(f32[256]{0:T(256)S(1)} %add_dynamic-update-slice_fusion), channel_id=1, source_target_pairs={{0,2},{1,3},{2,0},{3,1},{4,6},{5,7},{6,4},{7,5},{8,10},{9,11},{10,... | collective-permute-start | bytes 3080 | tf_op jit(solution)/shard_map/ppermute | solution.py:43
  162.3 13.6 %copy-start.24 = (f32[256]{0:T(256)}, f32[256]{0:T(256)S(1)}, u32[]{:S(2)}) copy-start(f32[256]{0:T(256)S(1)} %add.325) | copy-start | bytes 3076
  162.4 8.1 %collective-permute-start.7 = (f32[8]{0:T(128)S(1)}, f32[8]{0:T(128)S(1)}, u32[]{:S(2)}, u32[]{:S(2)}) collective-permute-start(f32[8]{0:T(128)S(1)} %select_reduce_fusion.1), channel_id=1, source_target_pairs={{0,4},{4,0},{8,12},{12,8},{1,5},{5,1},{9,13},{13,9},{2,6},{6,2},{1... | collective-permute-start | bytes 104 | tf_op jit(solution)/shard_map/ppermute | solution.py:43
  170.6 4.9 %collective-permute-start.8 = (f32[8]{0:T(128)S(1)}, f32[8]{0:T(128)S(1)}, u32[]{:S(2)}, u32[]{:S(2)}) collective-permute-start(f32[8]{0:T(128)S(1)} %add.326), channel_id=1, source_target_pairs={{0,8},{4,12},{8,0},{12,4},{1,9},{5,13},{9,1},{13,5},{2,10},{6,14},... | collective-permute-start | bytes 104 | tf_op jit(solution)/shard_map/ppermute | solution.py:43
  (12 other events, 22.6 us)

commit v18 on v17

--- a/solution.py
+++ b/solution.py
@@ -310,12 +310,14 @@
         + carried_part
         + skip_gain.reshape(group_count, GROUP)[None, :, :, None] * signal.astype(jnp.float32)
     )
-    long_cols = jnp.transpose(longconv, (1, 2, 0, 3)).reshape(chan_count, row_count)
-    mixed = (query_proj.T.astype(jnp.float32) * long_cols).astype(jnp.bfloat16)
+    long_rows = jnp.transpose(longconv, (0, 3, 1, 2)).reshape(row_count, chan_count)
+    mixed = (query_proj.astype(jnp.float32) * long_rows).astype(jnp.bfloat16)
     mixed_wide = mixed.astype(jnp.float32)
-    squares = jnp.sum(mixed_wide * mixed_wide, axis=0)
-    gained = (mixed_wide * norm_gain[:, None]).astype(jnp.bfloat16)
-    partial_value = jnp.concatenate((channel_logits(gained, unembed), squares[:, None]), axis=1)
+    squares = jnp.sum(mixed_wide * mixed_wide, axis=1)
+    gained = (mixed_wide * norm_gain[None, :]).astype(jnp.bfloat16)
+    partial_value = jnp.concatenate(
+        (jnp.dot(gained, unembed, preferred_element_type=jnp.float32), squares[:, None]), axis=1
+    )
     lanes = ("chan", "rep")
     lane_count = lax.axis_size(lanes)
     piece = row_count // lane_count

time: 177 us -> 177 us (level)
  no operation moved by 1% of the time
where the time goes in v18:
time: 177 us; the launch traced here: 176 us
  local copies, waits for them, and re-layouts  59.9 us (34%)
  other arithmetic  39.1 us (22%)
  matrix products  36.5 us (21%)
  starting transfers between devices  25.7 us (15%)
  waiting for transfers between devices  13.7 us (8%)
    unnamed x62, local copies, waits for them, and re-layouts  26.1 us
    ppermute x3, starting transfers between devices, from_behind(): return lax.ppermute(shard, axis, pairs)  12.6 us
    dot_general x2, matrix products, medium_block(): jnp.einsum('gts,gis->git', matrix, window, preferred_element_type=jnp.flo...  11.8 us
    ppermute x4, starting transfers between devices, sum_over(): part = part + lax.ppermute(part, axis, [(i, i ^ bit) for i in range(count)])  11.5 us
    dot_general x2, matrix products, intra_block(): jnp.einsum('gts,gis->git', jnp.concatenate((upper, lower), axis=2), jnp.c...  10.4 us
    select_n x1, other arithmetic, intra_block(): jnp.where(same_genome, toeplitz_lower, jnp.zeros_like(toeplitz_lower))  6.97 us
    ppermute x2, waiting for transfers between devices, scatter_sum(): part = keep + lax.ppermute(give, axes, [(i, i ^ bit) for i in range(count)])  6.28 us
    ppermute x4, waiting for transfers between devices, sum_over(): part = part + lax.ppermute(part, axis, [(i, i ^ bit) for i in range(count)])  6.24 us
  transfers between devices with their start and end apart: 9, of which 7 were waited for; matrix products, arithmetic and copies ran while one was open for 45% of the time, Pallas kernels for 0%

profile of v18, /device:TPU:0, one launch (start us, length us, event | category | flops | bytes accessed | tf_op | source)
XLA Modules:
  0.0 176.0 jit_solution(4428395736063886951)
XLA Ops:
  3.3 5.9 %collective-permute-start = (bf16[2,136,2048]{2,1,0:T(8,128)(2,1)}, bf16[2,136,2048]{2,1,0:T(8,128)(2,1)}, u32[]{:S(2)}, u32[]{:S(2)}) collective-permute-start(bf16[2,136,2048]{2,1,0:T(8,128)(2,1)} %pad_maximum_fusion.1), channel_id=1, source_target_pairs={{0,4},{4,8},{8,12},{1,5},{5,9},{9,13},{2,6},{6,10},{10,14},{3,7},{... | collective-permute-start | bytes 3342344 | tf_op jit(solution)/shard_map/ppermute | solution.py:18
  9.3 4.0 %fusion.57 = (f32[129,128,16]{1,2,0:T(8,128)S(1)}, f32[129,128,16]{1,2,0:T(8,128)S(1)}, f32[129,128,16]{1,2,0:T(8,128)S(1)}) fusion(f32[128,16]{0,1:T(8,128)S(1)} %get-tuple-element.64, f32[129]{0:T(256)S(1)} %iota_convert_fusion, f32[128,16]{0,1:T(8,128)S(1)} %get-tuple-element.61, f32[129]{0:T(256)S(1)} %fusion.93, f32[128,16]{0,1:T(8,128)S(1)} %get-tuple-element.63, ...), kind=kLoop, calls=%fused_computation.75 | loop fusion | flops 1849344 | bytes 3204104 | tf_op jit(solution)/shard_map/mul | solution.py:120
  24.4 4.0 %convolution_convert_fusion = bf16[384,16384]{1,0:T(8,128)(2,1)S(1)} fusion(s32[16384]{0:T(1024)S(1)} %add_select_fusion, s32[128]{0:T(128)S(1)} %iota.77, bf16[128,128]{0,1:T(8,128)(2,1)S(1)} %get-tuple-element.9, bf16[128,128]{0,1:T(8,128)(2,1)S(1)} %get-tuple-element.10, bf16[128,128]{0,1:T(8,128)(2,1)S(1)} %copy.217), kind=kOutput, calls=%fused_computation | convolution fusion | flops 1619296256 | bytes 12747264 | tf_op jit(solution)/shard_map/dot_general | solution.py:109
  28.4 4.0 %slice_bitcast_fusion.2 = (bf16[16,8,128,128]{3,1,2,0:T(8,128)(2,1)S(1)}, bf16[16,8,128,128]{3,1,2,0:T(8,128)(2,1)}, bf16[16,8,128,128]{3,1,2,0:T(8,128)(2,1)}) fusion(bf16[384,16384]{1,0:T(8,128)(2,1)S(1)} %convolution_convert_fusion), kind=kLoop, calls=%fused_computation.22 | loop fusion | bytes 25165824
  39.1 3.1 %maximum_bitcast_fusion.1 = bf16[128,256,32,1]{0,2,1,3:T(8,128)(2,1)} fusion(bf16[128,128,32]{0,2,1:T(8,128)(2,1)} %subtract_convert_fusion, bf16[128,128,32]{0,2,1:T(8,128)(2,1)} %fusion.41), kind=kLoop, calls=%fused_computation.59 | loop fusion | flops 1048576 | bytes 4194304 | tf_op jit(solution)/shard_map/concatenate | solution.py:256
  42.2 4.9 %copy.226 = bf16[128,256,32,1]{1,2,3,0:T(8,128)(2,1)} copy(bf16[128,256,32,1]{0,2,1,3:T(8,128)(2,1)} %maximum_bitcast_fusion.1) | data formatting | bytes 4194304 | tf_op jit(solution)/shard_map/concatenate | solution.py:256
  51.1 5.5 %copy.234 = bf16[16,8,128,128]{3,2,1,0:T(8,128)(2,1)} copy(bf16[16,8,128,128]{3,1,2,0:T(8,128)(2,1)} %get-tuple-element.13) | data formatting | bytes 8388608
  56.6 3.2 %copy.235 = bf16[16,8,128,128]{3,2,1,0:T(8,128)(2,1)} copy(bf16[16,8,128,128]{3,1,2,0:T(8,128)(2,1)S(1)} %copy-done.3) | data formatting | bytes 8388608
  61.6 3.4 %copy.222 = f32[128,128,32]{1,2,0:T(8,128)} copy(f32[128,128,32]{0,2,1:T(8,128)} %maximum_bitcast_fusion.2) | data formatting | bytes 4194304 | tf_op jit(solution)/shard_map/transpose | solution.py:126
  69.1 5.1 %constant_dynamic-update-slice_fusion = bf16[128,128,256]{2,1,0:T(8,128)(2,1)} fusion(bf16[128,128,256]{2,1,0:T(8,128)(2,1)} %constant_dynamic-update-slice_fusion.1, bf16[128,128,128]{2,1,0:T(8,128)(2,1)} %bitcast.154), kind=kLoop, calls=%fused_computation.190 | loop fusion | bytes 8388608 | tf_op jit(solution)/shard_map/concatenate | solution.py:211
  75.3 7.0 %bitcast_select_fusion.1 = (bf16[128,128,128]{2,1,0:T(8,128)(2,1)}, bf16[128,128,128]{2,1,0:T(8,128)(2,1)}, bf16[128,128,128]{2,1,0:T(8,128)(2,1)}, bf16[128,128,128]{2,1,0:T(8,128)(2,1)}) fusion(bf16[16,8,128,128]{3,2,1,0:T(8,128)(2,1)S(1)} %copy-done.5, pred[128,128]{1,0:T(8,128)(4,1)S(1)} %get-tuple-element.7, pred[128,128]{1,0:T(8,128)(4,1)S(1)} %compare_and_fusion.3, ...), kind=kLoop, calls=%fused_computation.17 | loop fusion | flops 8388608 | bytes 25198592 | tf_op jit(solution)/shard_map/jit(_where)/select_n | solution.py:243
  84.7 5.2 %fusion.44 = bf16[2048,384]{0,1:T(8,128)(2,1)} fusion(f32[384]{0:T(512)S(1)} %get-tuple-element.75, f32[392,2048]{1,0:T(8,128)S(1)} %convert_multiply_fusion, f32[2048]{0:T(1024)S(1)} %bitcast.179, f32[384]{0:T(512)S(1)} %get-tuple-element.71, f32[2048]{0:T(1024)S(1)} %bitcast.180, f32[384]{0:T(512)S(1)} %get-tuple-element.72, f32[2048]{0:T(1024)S(1)} %bitcast.175, ...), kind=kLoop, calls=%fused_computation.67 | loop fusion | flops 15728640 | bytes 23659520 | tf_op jit(solution)/shard_map/transpose | solution.py:204
  92.6 6.1 %fusion.51 = bf16[128,16,128]{2,1,0:T(8,128)(2,1)S(1)} fusion(bf16[128,128,256]{2,1,0:T(8,128)(2,1)} %constant_dynamic-update-slice_fusion, pred[128,256]{1,0:T(8,128)(4,1)S(1)} %get-tuple-element.84, bf16[128,16,384]{2,1,0:T(8,128)(2,1)} %bitcast.162), kind=kOutput, calls=%fused_computation.72 | convolution fusion | flops 138674176 | bytes 9994240 | tf_op jit(solution)/shard_map/gts,gis->git/dot_general | solution.py:228
  98.6 5.7 %fusion.54 = bf16[128,16,128]{2,1,0:T(8,128)(2,1)S(1)} fusion(bf16[128,128,256]{2,1,0:T(8,128)(2,1)} %constant_dynamic-update-slice_fusion, pred[128,256]{1,0:T(8,128)(4,1)S(1)} %get-tuple-element.85, bf16[128,16,384]{2,1,0:T(8,128)(2,1)S(1)} %bitcast.163), kind=kOutput, calls=%fused_computation.73 | convolution fusion | flops 138674176 | bytes 9994240 | tf_op jit(solution)/shard_map/gts,gis->git/dot_general | solution.py:228
  108.0 3.5 %copy.220 = f32[128,2,16,32]{0,3,2,1:T(8,128)} copy(f32[128,2,16,32]{3,2,1,0:T(8,128)} %fusion.39) | data formatting | bytes 1048576 | tf_op jit(solution)/shard_map/gsm,jgis->jgim/dot_general | solution.py:254
  115.1 6.9 %fusion.48 = f32[1,128,16,128]{3,2,1,0:T(8,128)} fusion(bf16[128,128,128]{2,1,0:T(8,128)(2,1)} %get-tuple-element.16, bf16[128,128,128]{2,1,0:T(8,128)(2,1)} %get-tuple-element.53, bf16[128,16,128]{2,1,0:T(8,128)(2,1)S(1)} %fusion.51), kind=kOutput, calls=%fused_computation.71 | convolution fusion | flops 153092096 | bytes 9961472 | tf_op jit(solution)/shard_map/gts,gis->git/dot_general | solution.py:244
  122.1 4.1 %collective-permute-start.2 = (f32[128,544]{0,1:T(8,128)S(1)}, f32[128,544]{0,1:T(8,128)S(1)}, u32[]{:S(2)}, u32[]{:S(2)}) collective-permute-start(f32[128,544]{0,1:T(8,128)S(1)} %pad_maximum_fusion.6), channel_id=1, source_target_pairs={{0,8},{4,12},{1,9},{5,13},{2,10},{6,14},{3,11},{7,15},{16,24},{20,... | collective-permute-start | bytes 835592 | tf_op jit(solution)/shard_map/ppermute | solution.py:18
  126.3 3.5 %fusion.45 = f32[1,128,16,128]{3,2,1,0:T(8,128)} fusion(bf16[128,128,128]{2,1,0:T(8,128)(2,1)S(1)} %copy-done.13, bf16[128,128,128]{2,1,0:T(8,128)(2,1)S(1)} %copy-done.14, bf16[128,16,128]{2,1,0:T(8,128)(2,1)S(1)} %fusion.54), kind=kOutput, calls=%fused_computation.70 | convolution fusion | flops 153092096 | bytes 9961472 | tf_op jit(solution)/shard_map/gts,gis->git/dot_general | solution.py:244
  132.1 3.1 %copy.227 = f32[2,128,16,32]{3,2,1,0:T(8,128)} copy(f32[2,128,16,32]{1,3,2,0:T(8,128)} %pad_maximum_fusion.3) | data formatting | bytes 1048576 | tf_op jit(solution)/shard_map/concatenate | solution.py:303
  135.2 5.3 %fusion.36 = f32[2,128,128,16]{1,3,2,0:T(8,128)S(1)} fusion(f32[1,128,16,128]{3,2,1,0:T(8,128)} %fusion.45, f32[1,128,16,128]{3,2,1,0:T(8,128)} %fusion.48, f32[2,128,16,32]{3,2,1,0:T(8,128)} %copy.227, f32[128,128,32]{1,2,0:T(8,128)} %copy.222, f32[128,16]{1,0:T(8,128)S(1)} %mul.726, f32[2,128]{1,0:T(2,128)S(1)} %get-tuple-element.76, ...), kind=kOutput, calls=%fused_computation.56 | convolution fusion | flops 204996608 | bytes 7873536 | tf_op jit(solution)/shard_map/gtm,jgim->jgit/dot_general | solution.py:300
  144.0 3.0 %fusion.59 = f32[256,512]{1,0:T(8,128)S(1)} fusion(bf16[2048,512]{1,0:T(8,128)(2,1)S(1)} %copy-done, f32[2048]{0:T(1024)S(1)} %copy-done.22, f32[256,8,2,128]{3,2,1,0:T(2,128)} %bitcast.156, bf16[256,2048]{0,1:T(8,128)(2,1)S(1)} %copy-done.9), kind=kOutput, calls=%fused_computation.79 | convolution fusion | flops 540016640 | bytes 5775360 | tf_op jit(solution)/shard_map/dot_general | solution.py:319
  152.3 4.7 %collective-permute-done.4 = f32[64,513]{1,0:T(8,128)S(1)} collective-permute-done((f32[64,513]{1,0:T(8,128)S(1)}, f32[64,513]{1,0:T(8,128)S(1)}, u32[]{:S(2)}, u32[]{:S(2)}) %collective-permute-start.4) | collective-permute-done | bytes 131360 | tf_op jit(solution)/shard_map/ppermute | solution.py:31
  162.4 6.6 %collective-permute-start.7 = (f32[8]{0:T(128)S(1)}, f32[8]{0:T(128)S(1)}, u32[]{:S(2)}, u32[]{:S(2)}) collective-permute-start(f32[8]{0:T(128)S(1)} %select_reduce_fusion.1), channel_id=1, source_target_pairs={{0,4},{4,0},{8,12},{12,8},{1,5},{5,1},{9,13},{13,9},{2,6},{6,2},{1... | collective-permute-start | bytes 104 | tf_op jit(solution)/shard_map/ppermute | solution.py:43
  170.6 3.4 %collective-permute-start.8 = (f32[8]{0:T(128)S(1)}, f32[8]{0:T(128)S(1)}, u32[]{:S(2)}, u32[]{:S(2)}) collective-permute-start(f32[8]{0:T(128)S(1)} %add.326), channel_id=1, source_target_pairs={{0,8},{4,12},{8,0},{12,4},{1,9},{5,13},{9,1},{13,5},{2,10},{6,14},... | collective-permute-start | bytes 104 | tf_op jit(solution)/shard_map/ppermute | solution.py:43
  (151 shorter events, 63.7 us)
Async XLA Ops:
  0.6 143.3 %copy-start = (bf16[2048,512]{1,0:T(8,128)(2,1)S(1)}, bf16[2048,512]{1,0:T(8,128)(2,1)}, u32[]{:S(2)}) copy-start(bf16[2048,512]{1,0:T(8,128)(2,1)} %param.19) | copy-start | bytes 6291460
  0.6 8.6 %copy-start.20 = (f32[4,128,16]{1,2,0:T(8,128)S(1)}, f32[4,128,16]{1,2,0:T(8,128)}, u32[]{:S(2)}) copy-start(f32[4,128,16]{1,2,0:T(8,128)} %param.16) | copy-start | bytes 98308
  3.3 79.0 %collective-permute-start = (bf16[2,136,2048]{2,1,0:T(8,128)(2,1)}, bf16[2,136,2048]{2,1,0:T(8,128)(2,1)}, u32[]{:S(2)}, u32[]{:S(2)}) collective-permute-start(bf16[2,136,2048]{2,1,0:T(8,128)(2,1)} %pad_maximum_fusion.1), channel_id=1, source_target_pairs={{0,4},{4,8},{8,12},{1,5},{5,9},{9,13},{2,6},{6,10},{10,14},{3,7},{... | collective-permute-start | bytes 3342344 | tf_op jit(solution)/shard_map/ppermute | solution.py:18
  20.1 2.9 %copy-start.8 = (f32[128,128,16]{1,2,0:T(8,128)S(1)}, f32[128,128,16]{1,2,0:T(8,128)}, u32[]{:S(2)}) copy-start(f32[128,128,16]{1,2,0:T(8,128)} %rev.7) | copy-start | bytes 3145732
  51.1 5.5 %copy-start.3 = (bf16[16,8,128,128]{3,1,2,0:T(8,128)(2,1)S(1)}, bf16[16,8,128,128]{3,1,2,0:T(8,128)(2,1)}, u32[]{:S(2)}) copy-start(bf16[16,8,128,128]{3,1,2,0:T(8,128)(2,1)} %get-tuple-element.12) | copy-start | bytes 12582916
  56.6 3.3 %copy-start.11 = (f32[128,128,16]{1,2,0:T(8,128)S(1)}, f32[128,128,16]{1,2,0:T(8,128)}, u32[]{:S(2)}) copy-start(f32[128,128,16]{1,2,0:T(8,128)} %get-tuple-element.27) | copy-start | bytes 3145732
  56.6 3.3 %copy-start.12 = (f32[128,128,16]{1,2,0:T(8,128)S(1)}, f32[128,128,16]{1,2,0:T(8,128)}, u32[]{:S(2)}) copy-start(f32[128,128,16]{1,2,0:T(8,128)} %get-tuple-element.87) | copy-start | bytes 3145732
  61.6 3.4 %copy-start.23 = (f32[2048]{0:T(1024)S(1)}, f32[2048]{0:T(1024)}, u32[]{:S(2)}) copy-start(f32[2048]{0:T(1024)} %param.17) | copy-start | bytes 24580
  69.1 5.1 %copy-start.4 = (bf16[16,8,128,128]{3,2,1,0:T(8,128)(2,1)S(1)}, bf16[16,8,128,128]{3,2,1,0:T(8,128)(2,1)}, u32[]{:S(2)}) copy-start(bf16[16,8,128,128]{3,2,1,0:T(8,128)(2,1)} %copy.234) | copy-start | bytes 12582916
  69.1 6.2 %copy-start.5 = (bf16[16,8,128,128]{3,2,1,0:T(8,128)(2,1)S(1)}, bf16[16,8,128,128]{3,2,1,0:T(8,128)(2,1)}, u32[]{:S(2)}) copy-start(bf16[16,8,128,128]{3,2,1,0:T(8,128)(2,1)} %copy.235) | copy-start | bytes 12582916
  92.6 6.1 %copy-start.18 = (bf16[2048,384]{1,0:T(8,128)(2,1)S(1)}, bf16[2048,384]{1,0:T(8,128)(2,1)}, u32[]{:S(2)}) copy-start(bf16[2048,384]{1,0:T(8,128)(2,1)} %copy.215) | copy-start | bytes 4718596
  112.6 9.4 %collective-permute-start.1 = (f32[128,544]{0,1:T(8,128)S(1)}, f32[128,544]{0,1:T(8,128)S(1)}, u32[]{:S(2)}, u32[]{:S(2)}) collective-permute-start(f32[128,544]{0,1:T(8,128)S(1)} %pad_maximum_fusion.5), channel_id=1, source_target_pairs={{0,4},{4,8},{8,12},{1,5},{5,9},{9,13},{2,6},{6,10},{10,14},{3,7},{... | collective-permute-start | bytes 835592 | tf_op jit(solution)/shard_map/ppermute | solution.py:18
  115.1 11.2 %copy-start.13 = (bf16[128,128,128]{2,1,0:T(8,128)(2,1)S(1)}, bf16[128,128,128]{2,1,0:T(8,128)(2,1)}, u32[]{:S(2)}) copy-start(bf16[128,128,128]{2,1,0:T(8,128)(2,1)} %get-tuple-element.17) | copy-start | bytes 12582916
  115.1 11.2 %copy-start.14 = (bf16[128,128,128]{2,1,0:T(8,128)(2,1)S(1)}, bf16[128,128,128]{2,1,0:T(8,128)(2,1)}, u32[]{:S(2)}) copy-start(bf16[128,128,128]{2,1,0:T(8,128)(2,1)} %get-tuple-element.52) | copy-start | bytes 12582916
  122.1 8.9 %collective-permute-start.2 = (f32[128,544]{0,1:T(8,128)S(1)}, f32[128,544]{0,1:T(8,128)S(1)}, u32[]{:S(2)}, u32[]{:S(2)}) collective-permute-start(f32[128,544]{0,1:T(8,128)S(1)} %pad_maximum_fusion.6), channel_id=1, source_target_pairs={{0,8},{4,12},{1,9},{5,13},{2,10},{6,14},{3,11},{7,15},{16,24},{20,... | collective-permute-start | bytes 835592 | tf_op jit(solution)/shard_map/ppermute | solution.py:18
  140.5 3.0 %copy-start.9 = (bf16[256,2048]{0,1:T(8,128)(2,1)S(1)}, bf16[256,2048]{0,1:T(8,128)(2,1)}, u32[]{:S(2)}) copy-start(bf16[256,2048]{0,1:T(8,128)(2,1)} %copy.214) | copy-start | bytes 3145732
  147.8 4.4 %copy-start.26 = (s32[256]{0:T(256)S(1)}, s32[256]{0:T(256)}, u32[]{:S(2)}) copy-start(s32[256]{0:T(256)} %param.20) | copy-start | bytes 3076
  147.9 1.7 collective-permute-start.3
  150.7 6.3 %collective-permute-start.4 = (f32[64,513]{1,0:T(8,128)S(1)}, f32[64,513]{1,0:T(8,128)S(1)}, u32[]{:S(2)}, u32[]{:S(2)}) collective-permute-start(f32[64,513]{1,0:T(8,128)S(1)} %slice_select_fusion), channel_id=1, source_target_pairs={{0,2},{1,3},{2,0},{3,1},{4,6},{5,7},{6,4},{7,5},{8,10},{9,11},{10,... | collective-permute-start | bytes 393992 | tf_op jit(solution)/shard_map/ppermute | solution.py:31
  157.5 1.1 collective-permute-start.5
  158.8 3.6 %collective-permute-start.6 = (f32[256]{0:T(256)S(1)}, f32[256]{0:T(256)S(1)}, u32[]{:S(2)}, u32[]{:S(2)}) collective-permute-start(f32[256]{0:T(256)S(1)} %add_dynamic-update-slice_fusion), channel_id=1, source_target_pairs={{0,2},{1,3},{2,0},{3,1},{4,6},{5,7},{6,4},{7,5},{8,10},{9,11},{10,... | collective-permute-start | bytes 3080 | tf_op jit(solution)/shard_map/ppermute | solution.py:43
  162.3 13.6 %copy-start.24 = (f32[256]{0:T(256)}, f32[256]{0:T(256)S(1)}, u32[]{:S(2)}) copy-start(f32[256]{0:T(256)S(1)} %add.325) | copy-start | bytes 3076
  162.4 8.1 %collective-permute-start.7 = (f32[8]{0:T(128)S(1)}, f32[8]{0:T(128)S(1)}, u32[]{:S(2)}, u32[]{:S(2)}) collective-permute-start(f32[8]{0:T(128)S(1)} %select_reduce_fusion.1), channel_id=1, source_target_pairs={{0,4},{4,0},{8,12},{12,8},{1,5},{5,1},{9,13},{13,9},{2,6},{6,2},{1... | collective-permute-start | bytes 104 | tf_op jit(solution)/shard_map/ppermute | solution.py:43
  170.6 4.9 %collective-permute-start.8 = (f32[8]{0:T(128)S(1)}, f32[8]{0:T(128)S(1)}, u32[]{:S(2)}, u32[]{:S(2)}) collective-permute-start(f32[8]{0:T(128)S(1)} %add.326), channel_id=1, source_target_pairs={{0,8},{4,12},{8,0},{12,4},{1,9},{5,13},{9,1},{13,5},{2,10},{6,14},... | collective-permute-start | bytes 104 | tf_op jit(solution)/shard_map/ppermute | solution.py:43
  (12 other events, 22.6 us)

commit v19 on v18

--- a/solution.py
+++ b/solution.py
@@ -185,10 +185,9 @@
     first_row = lax.axis_index("seq") * row_count
     segments = segment_ids(first_row + jnp.arange(row_count, dtype=jnp.int32), genome_lengths)
     halo = tile_rows + short_margin
-    edge_pair = from_behind(
-        jnp.stack((key_proj[row_count - halo :], value_proj[row_count - halo :])),
-        "seq",
-        1,
+    edge_pair = (
+        from_behind(key_proj[row_count - halo :], "seq", 1),
+        from_behind(value_proj[row_count - halo :], "seq", 1),
     )
     ext_segs = segment_ids(
         first_row - halo + jnp.arange(row_count + halo, dtype=jnp.int32),

time: 177 us -> 170 us (0.960)
  local copies, waits for them, and re-layouts: 59.9 us -> 49.9 us
    unnamed x62 -> x54, local copies, waits for them, and re-layouts: 26.1 us -> 17.1 us
    slice x0 -> x2, local copies, waits for them, and re-layouts: none -> 3.97 us  [the longest x1 2.06 us: per_device(): key_proj[row_count - halo:]]
    concatenate x1, local copies, waits for them, and re-layouts: 5.06 us -> 2.41 us  [per_device(): jnp.concatenate((circ[:group_count], circ[:group_count]), axis=2)]
    mul x1, other arithmetic: 0.56 us -> 2.42 us  [short_filter(): gated = keys_in.astype(jnp.float32) * values_in.astype(jnp.float32)]
    ppermute x3 -> x4, starting transfers between devices: 12.6 us -> 14.2 us  [from_behind(): return lax.ppermute(shard, axis, pairs)]
  transfers between devices with their start and end apart: 9 -> 10, of which waited for: 7 -> 7; matrix products, arithmetic and copies ran while one was open for 45% -> 45% of each run, Pallas kernels for 0% -> 0%
where the time goes in v19:
time: 170 us; the launch traced here: 169 us
  local copies, waits for them, and re-layouts  49.9 us (29%)
  other arithmetic  39.7 us (23%)
  matrix products  37.2 us (22%)
  starting transfers between devices  27.2 us (16%)
  waiting for transfers between devices  13.8 us (8%)
    unnamed x54, local copies, waits for them, and re-layouts  17.1 us
    ppermute x4, starting transfers between devices, from_behind(): return lax.ppermute(shard, axis, pairs)  14.2 us
    dot_general x2, matrix products, medium_block(): jnp.einsum('gts,gis->git', matrix, window, preferred_element_type=jnp.flo...  12 us
    ppermute x4, starting transfers between devices, sum_over(): part = part + lax.ppermute(part, axis, [(i, i ^ bit) for i in range(count)])  11.4 us
    dot_general x2, matrix products, intra_block(): jnp.einsum('gts,gis->git', jnp.concatenate((upper, lower), axis=2), jnp.c...  10.7 us
    select_n x1, other arithmetic, intra_block(): jnp.where(same_genome, toeplitz_lower, jnp.zeros_like(toeplitz_lower))  6.93 us
    ppermute x2, waiting for transfers between devices, scatter_sum(): part = keep + lax.ppermute(give, axes, [(i, i ^ bit) for i in range(count)])  6.28 us
    ppermute x4, waiting for transfers between devices, sum_over(): part = part + lax.ppermute(part, axis, [(i, i ^ bit) for i in range(count)])  6.24 us
  transfers between devices with their start and end apart: 10, of which 7 were waited for; matrix products, arithmetic and copies ran while one was open for 45% of the time, Pallas kernels for 0%

profile of v19, /device:TPU:0, one launch (start us, length us, event | category | flops | bytes accessed | tf_op | source)
XLA Modules:
  0.0 169.1 jit_solution(9178293094229448805)
XLA Ops:
  2.7 5.7 %collective-permute-start = (bf16[136,2048]{1,0:T(8,128)(2,1)}, bf16[136,2048]{1,0:T(8,128)(2,1)}, u32[]{:S(2)}, u32[]{:S(2)}) collective-permute-start(bf16[136,2048]{1,0:T(8,128)(2,1)} %slice.200), channel_id=1, source_target_pairs={{0,4},{4,8},{8,12},{1,5},{5,9},{9,13},{2,6},{6,10},{10,14},{3,7},{... | collective-permute-start | bytes 1671176 | tf_op jit(solution)/shard_map/ppermute | solution.py:18
  10.4 3.5 %collective-permute-start.1 = (bf16[136,2048]{1,0:T(8,128)(2,1)}, bf16[136,2048]{1,0:T(8,128)(2,1)}, u32[]{:S(2)}, u32[]{:S(2)}) collective-permute-start(bf16[136,2048]{1,0:T(8,128)(2,1)} %slice.201), channel_id=1, source_target_pairs={{0,4},{4,8},{8,12},{1,5},{5,9},{9,13},{2,6},{6,10},{10,14},{3,7},{... | collective-permute-start | bytes 1671176 | tf_op jit(solution)/shard_map/ppermute | solution.py:18
  14.7 4.0 %fusion.57 = (f32[129,128,16]{1,2,0:T(8,128)S(1)}, f32[129,128,16]{1,2,0:T(8,128)S(1)}, f32[129,128,16]{1,2,0:T(8,128)S(1)}) fusion(f32[128,16]{0,1:T(8,128)S(1)} %get-tuple-element.62, f32[129]{0:T(256)S(1)} %iota_convert_fusion, f32[128,16]{0,1:T(8,128)S(1)} %get-tuple-element.59, f32[129]{0:T(256)S(1)} %fusion.93, f32[128,16]{0,1:T(8,128)S(1)} %get-tuple-element.61, ...), kind=kLoop, calls=%fused_computation.74 | loop fusion | flops 1849344 | bytes 3204104 | tf_op jit(solution)/shard_map/mul | solution.py:120
  25.7 2.8 %fusion.41 = bf16[128,128,32]{0,2,1:T(8,128)(2,1)} fusion(f32[128,128,16]{1,2,0:T(8,128)} %rev.7, f32[128,128,16]{1,2,0:T(8,128)} %rev.6), kind=kLoop, calls=%fused_computation.66 | loop fusion | flops 2097152 | bytes 3145728 | tf_op jit(solution)/shard_map/convert_element_type | solution.py:135
  30.0 4.0 %convolution_convert_fusion = bf16[384,16384]{1,0:T(8,128)(2,1)S(1)} fusion(s32[16384]{0:T(1024)S(1)} %add_select_fusion, s32[128]{0:T(128)S(1)} %iota.77, bf16[128,128]{0,1:T(8,128)(2,1)S(1)} %get-tuple-element.9, bf16[128,128]{0,1:T(8,128)(2,1)S(1)} %get-tuple-element.10, bf16[128,128]{0,1:T(8,128)(2,1)S(1)} %copy.217), kind=kOutput, calls=%fused_computation | convolution fusion | flops 1619296256 | bytes 12747264 | tf_op jit(solution)/shard_map/dot_general | solution.py:109
  34.0 3.9 %slice_bitcast_fusion.2 = (bf16[16,8,128,128]{3,1,2,0:T(8,128)(2,1)S(1)}, bf16[16,8,128,128]{3,1,2,0:T(8,128)(2,1)}, bf16[16,8,128,128]{3,1,2,0:T(8,128)(2,1)}) fusion(bf16[384,16384]{1,0:T(8,128)(2,1)S(1)} %convolution_convert_fusion), kind=kLoop, calls=%fused_computation.22 | loop fusion | bytes 25165824
  45.1 3.1 %maximum_bitcast_fusion.1 = bf16[128,256,32,1]{0,2,1,3:T(8,128)(2,1)} fusion(bf16[128,128,32]{0,2,1:T(8,128)(2,1)} %subtract_convert_fusion, bf16[128,128,32]{0,2,1:T(8,128)(2,1)} %fusion.41), kind=kLoop, calls=%fused_computation.59 | loop fusion | flops 1048576 | bytes 4194304 | tf_op jit(solution)/shard_map/concatenate | solution.py:255
  48.1 4.9 %copy.226 = bf16[128,256,32,1]{1,2,3,0:T(8,128)(2,1)} copy(bf16[128,256,32,1]{0,2,1,3:T(8,128)(2,1)} %maximum_bitcast_fusion.1) | data formatting | bytes 4194304 | tf_op jit(solution)/shard_map/concatenate | solution.py:255
  56.9 3.6 %copy.234 = bf16[16,8,128,128]{3,2,1,0:T(8,128)(2,1)S(1)} copy(bf16[16,8,128,128]{3,1,2,0:T(8,128)(2,1)} %get-tuple-element.13) | data formatting | bytes 8388608
  63.5 6.9 %bitcast_select_fusion.1 = (bf16[128,128,128]{2,1,0:T(8,128)(2,1)}, bf16[128,128,128]{2,1,0:T(8,128)(2,1)}, bf16[128,128,128]{2,1,0:T(8,128)(2,1)}, bf16[128,128,128]{2,1,0:T(8,128)(2,1)}) fusion(bf16[16,8,128,128]{3,2,1,0:T(8,128)(2,1)S(1)} %copy.235, pred[128,128]{1,0:T(8,128)(4,1)S(1)} %get-tuple-element.7, pred[128,128]{1,0:T(8,128)(4,1)S(1)} %compare_and_fusion.3, ...), kind=kLoop, calls=%fused_computation.17 | loop fusion | flops 8388608 | bytes 25198592 | tf_op jit(solution)/shard_map/jit(_where)/select_n | solution.py:242
  72.1 3.4 %copy.222 = f32[128,128,32]{1,2,0:T(8,128)} copy(f32[128,128,32]{0,2,1:T(8,128)} %maximum_bitcast_fusion.2) | data formatting | bytes 4194304 | tf_op jit(solution)/shard_map/transpose | solution.py:126
  79.7 5.1 %fusion.44 = bf16[2048,384]{0,1:T(8,128)(2,1)} fusion(f32[384]{0:T(512)S(1)} %get-tuple-element.73, f32[392,2048]{1,0:T(8,128)S(1)} %convert_multiply_fusion, f32[2048]{0:T(1024)S(1)} %bitcast.171, f32[384]{0:T(512)S(1)} %get-tuple-element.69, f32[2048]{0:T(1024)S(1)} %bitcast.172, f32[384]{0:T(512)S(1)} %get-tuple-element.70, f32[2048]{0:T(1024)S(1)} %bitcast.167, ...), kind=kLoop, calls=%fused_computation.67 | loop fusion | flops 15728640 | bytes 23659520 | tf_op jit(solution)/shard_map/transpose | solution.py:203
  87.4 6.1 %fusion.51 = bf16[128,16,128]{2,1,0:T(8,128)(2,1)S(1)} fusion(bf16[128,128,256]{2,1,0:T(8,128)(2,1)} %constant_dynamic-update-slice_fusion, pred[128,256]{1,0:T(8,128)(4,1)S(1)} %get-tuple-element.82, bf16[128,16,384]{2,1,0:T(8,128)(2,1)} %bitcast.154), kind=kOutput, calls=%fused_computation.72 | convolution fusion | flops 138674176 | bytes 9994240 | tf_op jit(solution)/shard_map/gts,gis->git/dot_general | solution.py:227
  93.5 5.9 %fusion.54 = bf16[128,16,128]{2,1,0:T(8,128)(2,1)S(1)} fusion(bf16[128,128,256]{2,1,0:T(8,128)(2,1)} %constant_dynamic-update-slice_fusion, pred[128,256]{1,0:T(8,128)(4,1)S(1)} %get-tuple-element.83, bf16[128,16,384]{2,1,0:T(8,128)(2,1)S(1)} %bitcast.155), kind=kOutput, calls=%fused_computation.73 | convolution fusion | flops 138674176 | bytes 9994240 | tf_op jit(solution)/shard_map/gts,gis->git/dot_general | solution.py:227
  102.3 3.4 %copy.220 = f32[128,2,16,32]{0,3,2,1:T(8,128)} copy(f32[128,2,16,32]{3,2,1,0:T(8,128)} %fusion.39) | data formatting | bytes 1048576 | tf_op jit(solution)/shard_map/gsm,jgis->jgim/dot_general | solution.py:253
  106.9 2.7 %collective-permute-start.2 = (f32[128,544]{0,1:T(8,128)S(1)}, f32[128,544]{0,1:T(8,128)S(1)}, u32[]{:S(2)}, u32[]{:S(2)}) collective-permute-start(f32[128,544]{0,1:T(8,128)S(1)} %pad_maximum_fusion.4), channel_id=1, source_target_pairs={{0,4},{4,8},{8,12},{1,5},{5,9},{9,13},{2,6},{6,10},{10,14},{3,7},{... | collective-permute-start | bytes 835592 | tf_op jit(solution)/shard_map/ppermute | solution.py:18
  109.6 7.2 %fusion.48 = f32[1,128,16,128]{3,2,1,0:T(8,128)} fusion(bf16[128,128,128]{2,1,0:T(8,128)(2,1)} %get-tuple-element.16, bf16[128,128,128]{2,1,0:T(8,128)(2,1)} %get-tuple-element.51, bf16[128,16,128]{2,1,0:T(8,128)(2,1)} %copy-done.11), kind=kOutput, calls=%fused_computation.71 | convolution fusion | flops 153092096 | bytes 9961472 | tf_op jit(solution)/shard_map/gts,gis->git/dot_general | solution.py:243
  119.2 3.5 %fusion.45 = f32[1,128,16,128]{3,2,1,0:T(8,128)} fusion(bf16[128,128,128]{2,1,0:T(8,128)(2,1)S(1)} %copy-done.9, bf16[128,128,128]{2,1,0:T(8,128)(2,1)S(1)} %copy-done.10, bf16[128,16,128]{2,1,0:T(8,128)(2,1)S(1)} %copy-done.13), kind=kOutput, calls=%fused_computation.70 | convolution fusion | flops 153092096 | bytes 9961472 | tf_op jit(solution)/shard_map/gts,gis->git/dot_general | solution.py:243
  125.0 3.1 %copy.227 = f32[2,128,16,32]{3,2,1,0:T(8,128)} copy(f32[2,128,16,32]{1,3,2,0:T(8,128)} %pad_maximum_fusion.2) | data formatting | bytes 1048576 | tf_op jit(solution)/shard_map/concatenate | solution.py:302
  128.1 5.5 %fusion.36 = f32[2,128,128,16]{1,3,2,0:T(8,128)S(1)} fusion(f32[1,128,16,128]{3,2,1,0:T(8,128)} %fusion.45, f32[1,128,16,128]{3,2,1,0:T(8,128)} %fusion.48, f32[2,128,16,32]{3,2,1,0:T(8,128)} %copy.227, f32[128,128,32]{1,2,0:T(8,128)} %copy.222, f32[128,16]{1,0:T(8,128)S(1)} %mul.726, f32[2,128]{1,0:T(2,128)S(1)} %get-tuple-element.74, ...), kind=kOutput, calls=%fused_computation.56 | convolution fusion | flops 204996608 | bytes 7873536 | tf_op jit(solution)/shard_map/gtm,jgim->jgit/dot_general | solution.py:299
  137.1 3.0 %fusion.59 = f32[256,512]{1,0:T(8,128)S(1)} fusion(bf16[2048,512]{1,0:T(8,128)(2,1)S(1)} %copy-done, f32[2048]{0:T(1024)S(1)} %copy-done.18, f32[256,8,2,128]{3,2,1,0:T(2,128)} %bitcast.148, bf16[256,2048]{0,1:T(8,128)(2,1)S(1)} %copy.214), kind=kOutput, calls=%fused_computation.78 | convolution fusion | flops 540016640 | bytes 5775360 | tf_op jit(solution)/shard_map/dot_general | solution.py:318
  145.4 4.7 %collective-permute-done.5 = f32[64,513]{1,0:T(8,128)S(1)} collective-permute-done((f32[64,513]{1,0:T(8,128)S(1)}, f32[64,513]{1,0:T(8,128)S(1)}, u32[]{:S(2)}, u32[]{:S(2)}) %collective-permute-start.5) | collective-permute-done | bytes 131360 | tf_op jit(solution)/shard_map/ppermute | solution.py:31
  155.6 6.5 %collective-permute-start.8 = (f32[8]{0:T(128)S(1)}, f32[8]{0:T(128)S(1)}, u32[]{:S(2)}, u32[]{:S(2)}) collective-permute-start(f32[8]{0:T(128)S(1)} %select_reduce_fusion.1), channel_id=1, source_target_pairs={{0,4},{4,0},{8,12},{12,8},{1,5},{5,1},{9,13},{13,9},{2,6},{6,2},{1... | collective-permute-start | bytes 104 | tf_op jit(solution)/shard_map/ppermute | solution.py:43
  163.6 3.4 %collective-permute-start.9 = (f32[8]{0:T(128)S(1)}, f32[8]{0:T(128)S(1)}, u32[]{:S(2)}, u32[]{:S(2)}) collective-permute-start(f32[8]{0:T(128)S(1)} %add.326), channel_id=1, source_target_pairs={{0,8},{4,12},{8,0},{12,4},{1,9},{5,13},{9,1},{13,5},{2,10},{6,14},... | collective-permute-start | bytes 104 | tf_op jit(solution)/shard_map/ppermute | solution.py:43
  (144 shorter events, 61.9 us)
Async XLA Ops:
  0.6 136.5 %copy-start = (bf16[2048,512]{1,0:T(8,128)(2,1)S(1)}, bf16[2048,512]{1,0:T(8,128)(2,1)}, u32[]{:S(2)}) copy-start(bf16[2048,512]{1,0:T(8,128)(2,1)} %param.19) | copy-start | bytes 6291460
  2.7 74.5 %collective-permute-start = (bf16[136,2048]{1,0:T(8,128)(2,1)}, bf16[136,2048]{1,0:T(8,128)(2,1)}, u32[]{:S(2)}, u32[]{:S(2)}) collective-permute-start(bf16[136,2048]{1,0:T(8,128)(2,1)} %slice.200), channel_id=1, source_target_pairs={{0,4},{4,8},{8,12},{1,5},{5,9},{9,13},{2,6},{6,10},{10,14},{3,7},{... | collective-permute-start | bytes 1671176 | tf_op jit(solution)/shard_map/ppermute | solution.py:18
  10.4 66.9 %collective-permute-start.1 = (bf16[136,2048]{1,0:T(8,128)(2,1)}, bf16[136,2048]{1,0:T(8,128)(2,1)}, u32[]{:S(2)}, u32[]{:S(2)}) collective-permute-start(bf16[136,2048]{1,0:T(8,128)(2,1)} %slice.201), channel_id=1, source_target_pairs={{0,4},{4,8},{8,12},{1,5},{5,9},{9,13},{2,6},{6,10},{10,14},{3,7},{... | collective-permute-start | bytes 1671176 | tf_op jit(solution)/shard_map/ppermute | solution.py:18
  25.7 4.1 %copy-start.17 = (bf16[128,128]{1,0:T(8,128)(2,1)S(1)}, bf16[128,128]{1,0:T(8,128)(2,1)}, u32[]{:S(2)}) copy-start(bf16[128,128]{1,0:T(8,128)(2,1)} %param.15) | copy-start | bytes 98308
  56.9 3.6 %copy-start.2 = (bf16[16,8,128,128]{3,1,2,0:T(8,128)(2,1)S(1)}, bf16[16,8,128,128]{3,1,2,0:T(8,128)(2,1)}, u32[]{:S(2)}) copy-start(bf16[16,8,128,128]{3,1,2,0:T(8,128)(2,1)} %get-tuple-element.12) | copy-start | bytes 12582916
  63.5 6.9 %copy-start.7 = (f32[128,128,16]{1,2,0:T(8,128)S(1)}, f32[128,128,16]{1,2,0:T(8,128)}, u32[]{:S(2)}) copy-start(f32[128,128,16]{1,2,0:T(8,128)} %get-tuple-element.25) | copy-start | bytes 3145732
  63.5 6.9 %copy-start.8 = (f32[128,128,16]{1,2,0:T(8,128)S(1)}, f32[128,128,16]{1,2,0:T(8,128)}, u32[]{:S(2)}) copy-start(f32[128,128,16]{1,2,0:T(8,128)} %get-tuple-element.85) | copy-start | bytes 3145732
  72.1 5.0 %copy-start.16 = (bf16[7,2048]{1,0:T(8,128)(2,1)S(1)}, bf16[7,2048]{1,0:T(8,128)(2,1)}, u32[]{:S(2)}) copy-start(bf16[7,2048]{1,0:T(8,128)(2,1)} %param.14) | copy-start | bytes 86020
  87.4 6.1 %copy-start.15 = (bf16[2048,384]{1,0:T(8,128)(2,1)S(1)}, bf16[2048,384]{1,0:T(8,128)(2,1)}, u32[]{:S(2)}) copy-start(bf16[2048,384]{1,0:T(8,128)(2,1)} %copy.215) | copy-start | bytes 4718596
  93.5 5.9 %copy-start.11 = (bf16[128,16,128]{2,1,0:T(8,128)(2,1)}, bf16[128,16,128]{2,1,0:T(8,128)(2,1)S(1)}, u32[]{:S(2)}) copy-start(bf16[128,16,128]{2,1,0:T(8,128)(2,1)S(1)} %fusion.51) | copy-start | bytes 1572868
  93.5 6.8 %copy-start.14 = (bf16[128,256,32,1]{1,2,3,0:T(8,128)(2,1)S(1)}, bf16[128,256,32,1]{1,2,3,0:T(8,128)(2,1)}, u32[]{:S(2)}) copy-start(bf16[128,256,32,1]{1,2,3,0:T(8,128)(2,1)} %copy.226) | copy-start | bytes 6291460
  106.9 9.9 %collective-permute-start.2 = (f32[128,544]{0,1:T(8,128)S(1)}, f32[128,544]{0,1:T(8,128)S(1)}, u32[]{:S(2)}, u32[]{:S(2)}) collective-permute-start(f32[128,544]{0,1:T(8,128)S(1)} %pad_maximum_fusion.4), channel_id=1, source_target_pairs={{0,4},{4,8},{8,12},{1,5},{5,9},{9,13},{2,6},{6,10},{10,14},{3,7},{... | collective-permute-start | bytes 835592 | tf_op jit(solution)/shard_map/ppermute | solution.py:18
  109.6 9.6 %copy-start.9 = (bf16[128,128,128]{2,1,0:T(8,128)(2,1)S(1)}, bf16[128,128,128]{2,1,0:T(8,128)(2,1)}, u32[]{:S(2)}) copy-start(bf16[128,128,128]{2,1,0:T(8,128)(2,1)} %get-tuple-element.17) | copy-start | bytes 12582916
  109.6 9.6 %copy-start.10 = (bf16[128,128,128]{2,1,0:T(8,128)(2,1)S(1)}, bf16[128,128,128]{2,1,0:T(8,128)(2,1)}, u32[]{:S(2)}) copy-start(bf16[128,128,128]{2,1,0:T(8,128)(2,1)} %get-tuple-element.50) | copy-start | bytes 12582916
  109.6 9.6 %copy-start.13 = (bf16[128,16,128]{2,1,0:T(8,128)(2,1)S(1)}, bf16[128,16,128]{2,1,0:T(8,128)(2,1)}, u32[]{:S(2)}) copy-start(bf16[128,16,128]{2,1,0:T(8,128)(2,1)} %copy-done.12) | copy-start | bytes 1572868
  116.9 7.0 %collective-permute-start.3 = (f32[128,544]{0,1:T(8,128)S(1)}, f32[128,544]{0,1:T(8,128)S(1)}, u32[]{:S(2)}, u32[]{:S(2)}) collective-permute-start(f32[128,544]{0,1:T(8,128)S(1)} %pad_maximum_fusion.5), channel_id=1, source_target_pairs={{0,8},{4,12},{1,9},{5,13},{2,10},{6,14},{3,11},{7,15},{16,24},{20,... | collective-permute-start | bytes 835592 | tf_op jit(solution)/shard_map/ppermute | solution.py:18
  137.1 8.3 %copy-start.22 = (s32[256]{0:T(256)S(1)}, s32[256]{0:T(256)}, u32[]{:S(2)}) copy-start(s32[256]{0:T(256)} %param.20) | copy-start | bytes 3076
  141.0 1.7 %collective-permute-start.4 = (f32[128,513]{1,0:T(8,128)S(1)}, f32[128,513]{1,0:T(8,128)S(1)}, u32[]{:S(2)}, u32[]{:S(2)}) collective-permute-start(f32[128,513]{1,0:T(8,128)S(1)} %broadcast_select_fusion.1), channel_id=1, source_target_pairs={{0,1},{1,0},{2,3},{3,2},{4,5},{5,4},{6,7},{7,6},{8,9},{9,8},{10,11... | collective-permute-start | bytes 787976 | tf_op jit(solution)/shard_map/ppermute | solution.py:31
  143.8 6.3 %collective-permute-start.5 = (f32[64,513]{1,0:T(8,128)S(1)}, f32[64,513]{1,0:T(8,128)S(1)}, u32[]{:S(2)}, u32[]{:S(2)}) collective-permute-start(f32[64,513]{1,0:T(8,128)S(1)} %slice_select_fusion), channel_id=1, source_target_pairs={{0,2},{1,3},{2,0},{3,1},{4,6},{5,7},{6,4},{7,5},{8,10},{9,11},{10,... | collective-permute-start | bytes 393992 | tf_op jit(solution)/shard_map/ppermute | solution.py:31
  150.6 1.1 collective-permute-start.6
  151.9 3.6 %collective-permute-start.7 = (f32[256]{0:T(256)S(1)}, f32[256]{0:T(256)S(1)}, u32[]{:S(2)}, u32[]{:S(2)}) collective-permute-start(f32[256]{0:T(256)S(1)} %add_dynamic-update-slice_fusion), channel_id=1, source_target_pairs={{0,2},{1,3},{2,0},{3,1},{4,6},{5,7},{6,4},{7,5},{8,10},{9,11},{10,... | collective-permute-start | bytes 3080 | tf_op jit(solution)/shard_map/ppermute | solution.py:43
  155.5 13.6 %copy-start.20 = (f32[256]{0:T(256)}, f32[256]{0:T(256)S(1)}, u32[]{:S(2)}) copy-start(f32[256]{0:T(256)S(1)} %add.325) | copy-start | bytes 3076
  155.6 8.0 %collective-permute-start.8 = (f32[8]{0:T(128)S(1)}, f32[8]{0:T(128)S(1)}, u32[]{:S(2)}, u32[]{:S(2)}) collective-permute-start(f32[8]{0:T(128)S(1)} %select_reduce_fusion.1), channel_id=1, source_target_pairs={{0,4},{4,0},{8,12},{12,8},{1,5},{5,1},{9,13},{13,9},{2,6},{6,2},{1... | collective-permute-start | bytes 104 | tf_op jit(solution)/shard_map/ppermute | solution.py:43
  163.6 4.9 %collective-permute-start.9 = (f32[8]{0:T(128)S(1)}, f32[8]{0:T(128)S(1)}, u32[]{:S(2)}, u32[]{:S(2)}) collective-permute-start(f32[8]{0:T(128)S(1)} %add.326), channel_id=1, source_target_pairs={{0,8},{4,12},{8,0},{12,4},{1,9},{5,13},{9,1},{13,5},{2,10},{6,14},... | collective-permute-start | bytes 104 | tf_op jit(solution)/shard_map/ppermute | solution.py:43
  (9 other events, 20.6 us)

commit v20 on v19

--- a/solution.py
+++ b/solution.py
@@ -67,7 +67,7 @@
     upto = tuple(part)
     shift = 1
     while shift < count:
-        arrived = unpack(from_behind(pack(upto), axis, shift))
+        arrived = tuple(from_behind(a, axis, shift) for a in upto)
         arrived = tuple(jnp.where(place >= shift, r, i) for r, i in zip(arrived, ident))
         before = combine(arrived, before)
         upto = combine(arrived, upto)

time: 170 us -> 168 us (0.988)
  other arithmetic: 39.7 us -> 33.4 us
  starting transfers between devices: 27.2 us -> 32.6 us
    ppermute x4 -> x8, starting transfers between devices: 14.2 us -> 20.5 us  [from_behind(): return lax.ppermute(shard, axis, pairs)]
    convert_element_type x1, other arithmetic: 2.85 us -> 0.14 us  [split_table(): upper = table.astype(jnp.bfloat16)]
    unnamed x54 -> x50, local copies, waits for them, and re-layouts: 17.1 us -> 17.4 us
  transfers between devices with their start and end apart: 10 -> 14, of which waited for: 7 -> 7; matrix products, arithmetic and copies ran while one was open for 45% -> 41% of each run, Pallas kernels for 0% -> 0%
where the time goes in v20:
time: 168 us; the launch traced here: 167 us
  local copies, waits for them, and re-layouts  49.3 us (29%)
  matrix products  36.8 us (22%)
  other arithmetic  33.4 us (20%)
  starting transfers between devices  32.6 us (19%)
  waiting for transfers between devices  13.3 us (8%)
    ppermute x8, starting transfers between devices, from_behind(): return lax.ppermute(shard, axis, pairs)  20.5 us
    unnamed x50, local copies, waits for them, and re-layouts  17.4 us
    dot_general x2, matrix products, medium_block(): jnp.einsum('gts,gis->git', matrix, window, preferred_element_type=jnp.flo...  12 us
    ppermute x4, starting transfers between devices, sum_over(): part = part + lax.ppermute(part, axis, [(i, i ^ bit) for i in range(count)])  10.4 us
    dot_general x2, matrix products, intra_block(): jnp.einsum('gts,gis->git', jnp.concatenate((upper, lower), axis=2), jnp.c...  10.4 us
    select_n x1, other arithmetic, intra_block(): jnp.where(same_genome, toeplitz_lower, jnp.zeros_like(toeplitz_lower))  6.93 us
    ppermute x2, waiting for transfers between devices, scatter_sum(): part = keep + lax.ppermute(give, axes, [(i, i ^ bit) for i in range(count)])  6.28 us
    ppermute x4, waiting for transfers between devices, sum_over(): part = part + lax.ppermute(part, axis, [(i, i ^ bit) for i in range(count)])  6.24 us
  transfers between devices with their start and end apart: 14, of which 7 were waited for; matrix products, arithmetic and copies ran while one was open for 41% of the time, Pallas kernels for 0%

profile of v20, /device:TPU:0, one launch (start us, length us, event | category | flops | bytes accessed | tf_op | source)
XLA Modules:
  0.0 166.7 jit_solution(557815387321037437)
XLA Ops:
  2.7 5.7 %collective-permute-start = (bf16[136,2048]{1,0:T(8,128)(2,1)}, bf16[136,2048]{1,0:T(8,128)(2,1)}, u32[]{:S(2)}, u32[]{:S(2)}) collective-permute-start(bf16[136,2048]{1,0:T(8,128)(2,1)} %slice.182), channel_id=1, source_target_pairs={{0,4},{4,8},{8,12},{1,5},{5,9},{9,13},{2,6},{6,10},{10,14},{3,7},{... | collective-permute-start | bytes 1671176 | tf_op jit(solution)/shard_map/ppermute | solution.py:18
  10.4 3.5 %collective-permute-start.1 = (bf16[136,2048]{1,0:T(8,128)(2,1)}, bf16[136,2048]{1,0:T(8,128)(2,1)}, u32[]{:S(2)}, u32[]{:S(2)}) collective-permute-start(bf16[136,2048]{1,0:T(8,128)(2,1)} %slice.183), channel_id=1, source_target_pairs={{0,4},{4,8},{8,12},{1,5},{5,9},{9,13},{2,6},{6,10},{10,14},{3,7},{... | collective-permute-start | bytes 1671176 | tf_op jit(solution)/shard_map/ppermute | solution.py:18
  17.2 4.0 %fusion.57 = (f32[129,128,16]{1,2,0:T(8,128)S(1)}, f32[129,128,16]{1,2,0:T(8,128)S(1)}, f32[129,128,16]{1,2,0:T(8,128)S(1)}) fusion(f32[128,16]{0,1:T(8,128)S(1)} %get-tuple-element.52, f32[129]{0:T(256)S(1)} %iota_convert_fusion, f32[128,16]{0,1:T(8,128)S(1)} %get-tuple-element.49, f32[129]{0:T(256)S(1)} %fusion.93, f32[128,16]{0,1:T(8,128)S(1)} %get-tuple-element.51, ...), kind=kLoop, calls=%fused_computation.74 | loop fusion | flops 1849344 | bytes 3204104 | tf_op jit(solution)/shard_map/mul | solution.py:120
  23.2 2.7 %collective-permute-start.3 = (f32[128,16]{0,1:T(8,128)S(1)}, f32[128,16]{0,1:T(8,128)S(1)}, u32[]{:S(2)}, u32[]{:S(2)}) collective-permute-start(f32[128,16]{0,1:T(8,128)S(1)} %get-tuple-element.20), channel_id=1, source_target_pairs={{0,4},{4,8},{8,12},{1,5},{5,9},{9,13},{2,6},{6,10},{10,14},{3,7},{... | collective-permute-start | bytes 24584 | tf_op jit(solution)/shard_map/ppermute | solution.py:18
  31.1 3.8 %convolution_convert_fusion = bf16[384,16384]{1,0:T(8,128)(2,1)S(1)} fusion(s32[16384]{0:T(1024)S(1)} %add_select_fusion, s32[128]{0:T(128)S(1)} %iota.77, bf16[128,128]{0,1:T(8,128)(2,1)S(1)} %get-tuple-element.9, bf16[128,128]{0,1:T(8,128)(2,1)S(1)} %get-tuple-element.10, bf16[128,128]{0,1:T(8,128)(2,1)S(1)} %copy.169), kind=kOutput, calls=%fused_computation | convolution fusion | flops 1619296256 | bytes 12747264 | tf_op jit(solution)/shard_map/dot_general | solution.py:109
  34.9 3.9 %slice_bitcast_fusion.2 = (bf16[16,8,128,128]{3,1,2,0:T(8,128)(2,1)S(1)}, bf16[16,8,128,128]{3,1,2,0:T(8,128)(2,1)}, bf16[16,8,128,128]{3,1,2,0:T(8,128)(2,1)}) fusion(bf16[384,16384]{1,0:T(8,128)(2,1)S(1)} %convolution_convert_fusion), kind=kLoop, calls=%fused_computation.22 | loop fusion | bytes 25165824
  48.9 3.6 %copy.186 = bf16[16,8,128,128]{3,2,1,0:T(8,128)(2,1)S(1)} copy(bf16[16,8,128,128]{3,1,2,0:T(8,128)(2,1)} %get-tuple-element.13) | data formatting | bytes 8388608
  54.3 6.9 %bitcast_select_fusion.1 = (bf16[128,128,128]{2,1,0:T(8,128)(2,1)}, bf16[128,128,128]{2,1,0:T(8,128)(2,1)}, bf16[128,128,128]{2,1,0:T(8,128)(2,1)}, bf16[128,128,128]{2,1,0:T(8,128)(2,1)}) fusion(bf16[16,8,128,128]{3,2,1,0:T(8,128)(2,1)S(1)} %copy.187, pred[128,128]{1,0:T(8,128)(4,1)S(1)} %get-tuple-element.7, pred[128,128]{1,0:T(8,128)(4,1)S(1)} %compare_and_fusion.3, ...), kind=kLoop, calls=%fused_computation.17 | loop fusion | flops 8388608 | bytes 25198592 | tf_op jit(solution)/shard_map/jit(_where)/select_n | solution.py:242
  65.0 4.9 %copy.178 = bf16[128,256,32,1]{1,2,3,0:T(8,128)(2,1)} copy(bf16[128,256,32,1]{0,2,1,3:T(8,128)(2,1)} %maximum_bitcast_fusion.1) | data formatting | bytes 4194304 | tf_op jit(solution)/shard_map/concatenate | solution.py:255
  69.9 3.4 %copy.174 = f32[128,128,32]{1,2,0:T(8,128)} copy(f32[128,128,32]{0,2,1:T(8,128)} %maximum_bitcast_fusion.2) | data formatting | bytes 4194304 | tf_op jit(solution)/shard_map/transpose | solution.py:126
  75.0 2.4 %convert_multiply_fusion = f32[392,2048]{1,0:T(8,128)S(1)} fusion(bf16[256,2048]{1,0:T(8,128)(2,1)} %param.12, bf16[136,2048]{1,0:T(8,128)(2,1)} %collective-permute-done, bf16[256,2048]{1,0:T(8,128)(2,1)} %param.13, bf16[136,2048]{1,0:T(8,128)(2,1)} %collective-permute-done.1), kind=kLoop, calls=%fused_computation.27 | loop fusion | flops 7225344 | bytes 6422528 | tf_op jit(solution)/shard_map/mul | solution.py:85
  77.4 5.3 %fusion.44 = bf16[2048,384]{0,1:T(8,128)(2,1)} fusion(f32[384]{0:T(512)S(1)} %get-tuple-element.65, f32[392,2048]{1,0:T(8,128)S(1)} %convert_multiply_fusion, f32[2048]{0:T(1024)S(1)} %bitcast.153, f32[384]{0:T(512)S(1)} %get-tuple-element.61, f32[2048]{0:T(1024)S(1)} %bitcast.154, f32[384]{0:T(512)S(1)} %get-tuple-element.62, f32[2048]{0:T(1024)S(1)} %bitcast.149, ...), kind=kLoop, calls=%fused_computation.67 | loop fusion | flops 15728640 | bytes 23659520 | tf_op jit(solution)/shard_map/transpose | solution.py:203
  82.7 2.6 %copy.167 = bf16[2048,384]{1,0:T(8,128)(2,1)} copy(bf16[2048,384]{0,1:T(8,128)(2,1)} %fusion.44) | data formatting | bytes 3145728 | tf_op jit(solution)/shard_map/transpose | solution.py:203
  85.3 6.1 %fusion.51 = bf16[128,16,128]{2,1,0:T(8,128)(2,1)S(1)} fusion(bf16[128,128,256]{2,1,0:T(8,128)(2,1)} %constant_dynamic-update-slice_fusion, pred[128,256]{1,0:T(8,128)(4,1)S(1)} %get-tuple-element.74, bf16[128,16,384]{2,1,0:T(8,128)(2,1)} %bitcast.146), kind=kOutput, calls=%fused_computation.72 | convolution fusion | flops 138674176 | bytes 9994240 | tf_op jit(solution)/shard_map/gts,gis->git/dot_general | solution.py:227
  91.4 5.9 %fusion.54 = bf16[128,16,128]{2,1,0:T(8,128)(2,1)S(1)} fusion(bf16[128,128,256]{2,1,0:T(8,128)(2,1)} %constant_dynamic-update-slice_fusion, pred[128,256]{1,0:T(8,128)(4,1)S(1)} %get-tuple-element.75, bf16[128,16,384]{2,1,0:T(8,128)(2,1)S(1)} %bitcast.147), kind=kOutput, calls=%fused_computation.73 | convolution fusion | flops 138674176 | bytes 9994240 | tf_op jit(solution)/shard_map/gts,gis->git/dot_general | solution.py:227
  100.2 3.4 %copy.172 = f32[128,2,16,32]{0,3,2,1:T(8,128)} copy(f32[128,2,16,32]{3,2,1,0:T(8,128)} %fusion.39) | data formatting | bytes 1048576 | tf_op jit(solution)/shard_map/gsm,jgis->jgim/dot_general | solution.py:253
  108.7 7.2 %fusion.48 = f32[1,128,16,128]{3,2,1,0:T(8,128)} fusion(bf16[128,128,128]{2,1,0:T(8,128)(2,1)} %get-tuple-element.16, bf16[128,128,128]{2,1,0:T(8,128)(2,1)} %get-tuple-element.41, bf16[128,16,128]{2,1,0:T(8,128)(2,1)} %copy-done.9), kind=kOutput, calls=%fused_computation.71 | convolution fusion | flops 153092096 | bytes 9961472 | tf_op jit(solution)/shard_map/gts,gis->git/dot_general | solution.py:243
  118.6 3.2 %fusion.45 = f32[1,128,16,128]{3,2,1,0:T(8,128)} fusion(bf16[128,128,128]{2,1,0:T(8,128)(2,1)S(1)} %copy-done.7, bf16[128,128,128]{2,1,0:T(8,128)(2,1)S(1)} %copy-done.8, bf16[128,16,128]{2,1,0:T(8,128)(2,1)S(1)} %copy-done.11), kind=kOutput, calls=%fused_computation.70 | convolution fusion | flops 153092096 | bytes 9961472 | tf_op jit(solution)/shard_map/gts,gis->git/dot_general | solution.py:243
  123.6 3.1 %copy.179 = f32[2,128,16,32]{3,2,1,0:T(8,128)} copy(f32[2,128,16,32]{1,3,2,0:T(8,128)} %pad_maximum_fusion.2) | data formatting | bytes 1048576 | tf_op jit(solution)/shard_map/concatenate | solution.py:302
  126.7 5.5 %fusion.36 = f32[2,128,128,16]{1,3,2,0:T(8,128)S(1)} fusion(f32[1,128,16,128]{3,2,1,0:T(8,128)} %fusion.45, f32[1,128,16,128]{3,2,1,0:T(8,128)} %fusion.48, f32[2,128,16,32]{3,2,1,0:T(8,128)} %copy.179, f32[128,128,32]{1,2,0:T(8,128)} %copy.174, f32[128,16]{1,0:T(8,128)S(1)} %mul.686, f32[2,128]{1,0:T(2,128)S(1)} %get-tuple-element.66, ...), kind=kOutput, calls=%fused_computation.56 | convolution fusion | flops 204996608 | bytes 7873536 | tf_op jit(solution)/shard_map/gtm,jgim->jgit/dot_general | solution.py:299
  135.7 3.0 %fusion.59 = f32[256,512]{1,0:T(8,128)S(1)} fusion(bf16[2048,512]{1,0:T(8,128)(2,1)S(1)} %copy-done, f32[2048]{0:T(1024)S(1)} %copy-done.16, f32[256,8,2,128]{3,2,1,0:T(2,128)} %bitcast.140, bf16[256,2048]{0,1:T(8,128)(2,1)S(1)} %copy.166), kind=kOutput, calls=%fused_computation.78 | convolution fusion | flops 540016640 | bytes 5775360 | tf_op jit(solution)/shard_map/dot_general | solution.py:318
  144.0 4.7 %collective-permute-done.9 = f32[64,513]{1,0:T(8,128)S(1)} collective-permute-done((f32[64,513]{1,0:T(8,128)S(1)}, f32[64,513]{1,0:T(8,128)S(1)}, u32[]{:S(2)}, u32[]{:S(2)}) %collective-permute-start.9) | collective-permute-done | bytes 131360 | tf_op jit(solution)/shard_map/ppermute | solution.py:31
  154.2 5.6 %collective-permute-start.12 = (f32[8]{0:T(128)S(1)}, f32[8]{0:T(128)S(1)}, u32[]{:S(2)}, u32[]{:S(2)}) collective-permute-start(f32[8]{0:T(128)S(1)} %select_reduce_fusion.1), channel_id=1, source_target_pairs={{0,4},{4,0},{8,12},{12,8},{1,5},{5,1},{9,13},{13,9},{2,6},{6,2},{1... | collective-permute-start | bytes 104 | tf_op jit(solution)/shard_map/ppermute | solution.py:43
  161.3 3.4 %collective-permute-start.13 = (f32[8]{0:T(128)S(1)}, f32[8]{0:T(128)S(1)}, u32[]{:S(2)}, u32[]{:S(2)}) collective-permute-start(f32[8]{0:T(128)S(1)} %add.306), channel_id=1, source_target_pairs={{0,8},{4,12},{8,0},{12,4},{1,9},{5,13},{9,1},{13,5},{2,10},{6,14},... | collective-permute-start | bytes 104 | tf_op jit(solution)/shard_map/ppermute | solution.py:43
  (144 shorter events, 61.6 us)
Async XLA Ops:
  0.6 135.1 %copy-start = (bf16[2048,512]{1,0:T(8,128)(2,1)S(1)}, bf16[2048,512]{1,0:T(8,128)(2,1)}, u32[]{:S(2)}) copy-start(bf16[2048,512]{1,0:T(8,128)(2,1)} %param.19) | copy-start | bytes 6291460
  2.7 72.3 %collective-permute-start = (bf16[136,2048]{1,0:T(8,128)(2,1)}, bf16[136,2048]{1,0:T(8,128)(2,1)}, u32[]{:S(2)}, u32[]{:S(2)}) collective-permute-start(bf16[136,2048]{1,0:T(8,128)(2,1)} %slice.182), channel_id=1, source_target_pairs={{0,4},{4,8},{8,12},{1,5},{5,9},{9,13},{2,6},{6,10},{10,14},{3,7},{... | collective-permute-start | bytes 1671176 | tf_op jit(solution)/shard_map/ppermute | solution.py:18
  10.4 64.6 %collective-permute-start.1 = (bf16[136,2048]{1,0:T(8,128)(2,1)}, bf16[136,2048]{1,0:T(8,128)(2,1)}, u32[]{:S(2)}, u32[]{:S(2)}) collective-permute-start(bf16[136,2048]{1,0:T(8,128)(2,1)} %slice.183), channel_id=1, source_target_pairs={{0,4},{4,8},{8,12},{1,5},{5,9},{9,13},{2,6},{6,10},{10,14},{3,7},{... | collective-permute-start | bytes 1671176 | tf_op jit(solution)/shard_map/ppermute | solution.py:18
  23.2 51.8 %collective-permute-start.3 = (f32[128,16]{0,1:T(8,128)S(1)}, f32[128,16]{0,1:T(8,128)S(1)}, u32[]{:S(2)}, u32[]{:S(2)}) collective-permute-start(f32[128,16]{0,1:T(8,128)S(1)} %get-tuple-element.20), channel_id=1, source_target_pairs={{0,4},{4,8},{8,12},{1,5},{5,9},{9,13},{2,6},{6,10},{10,14},{3,7},{... | collective-permute-start | bytes 24584 | tf_op jit(solution)/shard_map/ppermute | solution.py:18
  25.8 49.1 %collective-permute-start.2 = (f32[128,16]{0,1:T(8,128)S(1)}, f32[128,16]{0,1:T(8,128)S(1)}, u32[]{:S(2)}, u32[]{:S(2)}) collective-permute-start(f32[128,16]{0,1:T(8,128)S(1)} %get-tuple-element.4), channel_id=1, source_target_pairs={{0,4},{4,8},{8,12},{1,5},{5,9},{9,13},{2,6},{6,10},{10,14},{3,7},{... | collective-permute-start | bytes 24584 | tf_op jit(solution)/shard_map/ppermute | solution.py:18
  85.3 6.1 %copy-start.13 = (bf16[2048,384]{1,0:T(8,128)(2,1)S(1)}, bf16[2048,384]{1,0:T(8,128)(2,1)}, u32[]{:S(2)}) copy-start(bf16[2048,384]{1,0:T(8,128)(2,1)} %copy.167) | copy-start | bytes 4718596
  91.3 5.9 %copy-start.9 = (bf16[128,16,128]{2,1,0:T(8,128)(2,1)}, bf16[128,16,128]{2,1,0:T(8,128)(2,1)S(1)}, u32[]{:S(2)}) copy-start(bf16[128,16,128]{2,1,0:T(8,128)(2,1)S(1)} %fusion.51) | copy-start | bytes 1572868
  91.4 6.8 %copy-start.12 = (bf16[128,256,32,1]{1,2,3,0:T(8,128)(2,1)S(1)}, bf16[128,256,32,1]{1,2,3,0:T(8,128)(2,1)}, u32[]{:S(2)}) copy-start(bf16[128,256,32,1]{1,2,3,0:T(8,128)(2,1)} %copy.178) | copy-start | bytes 6291460
  104.8 11.1 %collective-permute-start.4 = (f32[128,16,16]{0,2,1:T(8,128)S(1)}, f32[128,16,16]{0,2,1:T(8,128)S(1)}, u32[]{:S(2)}, u32[]{:S(2)}) collective-permute-start(f32[128,16,16]{0,2,1:T(8,128)S(1)} %get-tuple-element.28), channel_id=1, source_target_pairs={{0,4},{4,8},{8,12},{1,5},{5,9},{9,13},{2,6},{6,10},{10,14},{3,7},{... | collective-permute-start | bytes 393224 | tf_op jit(solution)/shard_map/ppermute | solution.py:18
  106.7 9.2 %collective-permute-start.5 = (f32[128,16,16]{0,2,1:T(8,128)S(1)}, f32[128,16,16]{0,2,1:T(8,128)S(1)}, u32[]{:S(2)}, u32[]{:S(2)}) collective-permute-start(f32[128,16,16]{0,2,1:T(8,128)S(1)} %get-tuple-element.29), channel_id=1, source_target_pairs={{0,4},{4,8},{8,12},{1,5},{5,9},{9,13},{2,6},{6,10},{10,14},{3,7},{... | collective-permute-start | bytes 393224 | tf_op jit(solution)/shard_map/ppermute | solution.py:18
  108.6 10.0 %copy-start.7 = (bf16[128,128,128]{2,1,0:T(8,128)(2,1)S(1)}, bf16[128,128,128]{2,1,0:T(8,128)(2,1)}, u32[]{:S(2)}) copy-start(bf16[128,128,128]{2,1,0:T(8,128)(2,1)} %get-tuple-element.17) | copy-start | bytes 12582916
  108.6 10.0 %copy-start.8 = (bf16[128,128,128]{2,1,0:T(8,128)(2,1)S(1)}, bf16[128,128,128]{2,1,0:T(8,128)(2,1)}, u32[]{:S(2)}) copy-start(bf16[128,128,128]{2,1,0:T(8,128)(2,1)} %get-tuple-element.40) | copy-start | bytes 12582916
  108.6 10.0 %copy-start.11 = (bf16[128,16,128]{2,1,0:T(8,128)(2,1)S(1)}, bf16[128,16,128]{2,1,0:T(8,128)(2,1)}, u32[]{:S(2)}) copy-start(bf16[128,16,128]{2,1,0:T(8,128)(2,1)} %copy-done.10) | copy-start | bytes 1572868
  115.9 5.9 %collective-permute-start.6 = (f32[128,16,16]{0,2,1:T(8,128)S(1)}, f32[128,16,16]{0,2,1:T(8,128)S(1)}, u32[]{:S(2)}, u32[]{:S(2)}) collective-permute-start(f32[128,16,16]{0,2,1:T(8,128)S(1)} %get-tuple-element.36), channel_id=1, source_target_pairs={{0,8},{4,12},{1,9},{5,13},{2,10},{6,14},{3,11},{7,15},{16,24},{20,... | collective-permute-start | bytes 393224 | tf_op jit(solution)/shard_map/ppermute | solution.py:18
  117.3 5.3 %collective-permute-start.7 = (f32[128,16,16]{0,2,1:T(8,128)S(1)}, f32[128,16,16]{0,2,1:T(8,128)S(1)}, u32[]{:S(2)}, u32[]{:S(2)}) collective-permute-start(f32[128,16,16]{0,2,1:T(8,128)S(1)} %get-tuple-element.37), channel_id=1, source_target_pairs={{0,8},{4,12},{1,9},{5,13},{2,10},{6,14},{3,11},{7,15},{16,24},{20,... | collective-permute-start | bytes 393224 | tf_op jit(solution)/shard_map/ppermute | solution.py:18
  135.7 8.2 %copy-start.20 = (s32[256]{0:T(256)S(1)}, s32[256]{0:T(256)}, u32[]{:S(2)}) copy-start(s32[256]{0:T(256)} %param.20) | copy-start | bytes 3076
  139.5 26.6 %copy-start.19 = (s32[8]{0:T(128)S(1)}, s32[8]{0:T(128)}, u32[]{:S(2)}) copy-start(s32[8]{0:T(128)} %param.21) | copy-start | bytes 100
  139.6 1.7 %collective-permute-start.8 = (f32[128,513]{1,0:T(8,128)S(1)}, f32[128,513]{1,0:T(8,128)S(1)}, u32[]{:S(2)}, u32[]{:S(2)}) collective-permute-start(f32[128,513]{1,0:T(8,128)S(1)} %broadcast_select_fusion.1), channel_id=1, source_target_pairs={{0,1},{1,0},{2,3},{3,2},{4,5},{5,4},{6,7},{7,6},{8,9},{9,8},{10,11... | collective-permute-start | bytes 787976 | tf_op jit(solution)/shard_map/ppermute | solution.py:31
  142.4 6.3 %collective-permute-start.9 = (f32[64,513]{1,0:T(8,128)S(1)}, f32[64,513]{1,0:T(8,128)S(1)}, u32[]{:S(2)}, u32[]{:S(2)}) collective-permute-start(f32[64,513]{1,0:T(8,128)S(1)} %slice_select_fusion), channel_id=1, source_target_pairs={{0,2},{1,3},{2,0},{3,1},{4,6},{5,7},{6,4},{7,5},{8,10},{9,11},{10,... | collective-permute-start | bytes 393992 | tf_op jit(solution)/shard_map/ppermute | solution.py:31
  149.2 1.1 collective-permute-start.10
  150.5 3.6 %collective-permute-start.11 = (f32[256]{0:T(256)S(1)}, f32[256]{0:T(256)S(1)}, u32[]{:S(2)}, u32[]{:S(2)}) collective-permute-start(f32[256]{0:T(256)S(1)} %add_dynamic-update-slice_fusion), channel_id=1, source_target_pairs={{0,2},{1,3},{2,0},{3,1},{4,6},{5,7},{6,4},{7,5},{8,10},{9,11},{10,... | collective-permute-start | bytes 3080 | tf_op jit(solution)/shard_map/ppermute | solution.py:43
  154.1 12.6 %copy-start.18 = (f32[256]{0:T(256)}, f32[256]{0:T(256)S(1)}, u32[]{:S(2)}) copy-start(f32[256]{0:T(256)S(1)} %add.305) | copy-start | bytes 3076
  154.2 7.1 %collective-permute-start.12 = (f32[8]{0:T(128)S(1)}, f32[8]{0:T(128)S(1)}, u32[]{:S(2)}, u32[]{:S(2)}) collective-permute-start(f32[8]{0:T(128)S(1)} %select_reduce_fusion.1), channel_id=1, source_target_pairs={{0,4},{4,0},{8,12},{12,8},{1,5},{5,1},{9,13},{13,9},{2,6},{6,2},{1... | collective-permute-start | bytes 104 | tf_op jit(solution)/shard_map/ppermute | solution.py:43
  161.3 4.9 %collective-permute-start.13 = (f32[8]{0:T(128)S(1)}, f32[8]{0:T(128)S(1)}, u32[]{:S(2)}, u32[]{:S(2)}) collective-permute-start(f32[8]{0:T(128)S(1)} %add.306), channel_id=1, source_target_pairs={{0,8},{4,12},{8,0},{12,4},{1,9},{5,13},{9,1},{13,5},{2,10},{6,14},... | collective-permute-start | bytes 104 | tf_op jit(solution)/shard_map/ppermute | solution.py:43
  (11 other events, 24.0 us)
